TPU v7x, 256 devices: a whole 4x4x8 slice. The times are simulated.
256 devices in a mesh: seq: 64 (over x, z, core), tensor: 4 (over y).
Axes of the slice: x: 4, y: 4, z: 8, core: 2. Of those that a mesh axis runs over, the one named last changes fastest.
Arguments:
- hidden: bfloat16 [512, 1280], P('seq', 'tensor'), may hold values from -20 to 20
- inward_weight: bfloat16 [1280, 3, 1280], P(None, None, 'tensor'), may hold values from -0.15625 to 0.15625
- output_weight: bfloat16 [1280, 1280], P('tensor'), may hold values from -0.559017 to 0.559017
- score_gain: float32 [1280], P('tensor'), may hold values from 0.5 to 9
- eigen_rate: float32 [1280], replicated, may hold values from 0.1 to 0.6
- lengths: int32 [512], replicated, may hold values from 1 to 16384, as said below
- page_request: int32 [1536], P('seq'), may hold values from 0 to 511, as said below
- page_number: int32 [1536], P('seq'), may hold values from 0 to 128, as said below
- page_cache: bfloat16 [1536, 128, 2, 1280], P('seq', None, None, 'tensor'), may hold values from -6 to 6
Outputs:
- new_hidden: bfloat16 [512, 1280], P('seq', 'tensor')
Inputs may be any that keep to these rules, and one draw needn't show every extreme that they name: `lengths`: exactly 4 requests have more than 256 cached positions; they have more than 16256, one has exactly 16384. Every other request has at most 256, one exactly 256. `page_request`: each page of each request stands in exactly one slot: pages 0 to 1 of every short request, pages 0 to 127 of every long request. The remaining 2 * 4 slots name a long request with page number 128 and hold nothing live. `page_number`: see page_request.
All inputs are finite; a program needn't handle non-finite values.
Results may differ from a plain program's by a relative error of at most 0.012.
The roundings to bfloat16 on the way count: a program that leaves them out, or rounds other values in their place, can miss the bound.
Values may be sent and summed in bfloat16 or wider, within the bound.
No kernel may reach another device: no remote copies, remote signals or barrier semaphores. Data moves between devices by JAX's collectives and lax.ppermute only.
A program may use at most 192 MiB of HBM per device.

v0:
```python
import math

import jax
import jax.numpy as jnp
from jax import lax
from jax.sharding import PartitionSpec as P

HEAD_DIM = 64


epsilon = 1e-06
far_below = -1e30


def merged_2(part, axis, combine):
    gathered = jax.tree.map(lambda a: lax.all_gather(a, axis), part)

    def take(source):
        return jax.tree.map(lambda a: lax.dynamic_index_in_dim(a, source, 0, False), gathered)

    return lax.fori_loop(
        1, lax.axis_size(axis), lambda source, state: combine(state, take(source)), take(0)
    )


def head_norm(values, gain):
    shaped = values.reshape(values.shape[:-1] + (-1, HEAD_DIM))
    normed = shaped / jnp.sqrt(jnp.mean(shaped * shaped, axis=-1, keepdims=True) + epsilon)
    return normed * gain.reshape(-1, HEAD_DIM)


def scale_heads(summed, factor):
    shaped = summed.reshape(summed.shape[:-1] + (factor.shape[-1], -1))
    return (shaped * factor[..., None]).reshape(summed.shape)


def join_parts(first, second):
    first_max, first_total, first_acc = first
    second_max, second_total, second_acc = second
    top = jnp.maximum(first_max, second_max)
    first_factor = jnp.exp(first_max - top)
    second_factor = jnp.exp(second_max - top)
    return (
        top,
        first_total * first_factor + second_total * second_factor,
        scale_heads(first_acc, first_factor) + scale_heads(second_acc, second_factor),
    )


def local(
    hidden,
    inward_weight,
    output_weight,
    score_gain,
    eigen_rate,
    lengths,
    page_request,
    page_number,
    page_cache,
):
    rows, width_local = hidden.shape
    heads_local = width_local // HEAD_DIM
    gathered = lax.all_gather(hidden, "tensor", axis=1, tiled=True)
    projected = jnp.dot(
        gathered,
        inward_weight.reshape(inward_weight.shape[0], -1),
        preferred_element_type=jnp.float32,
    )
    query = head_norm(projected[:, :width_local], score_gain).astype(jnp.bfloat16)
    key_new = head_norm(projected[:, width_local : 2 * width_local], score_gain).astype(
        jnp.bfloat16
    )
    value_own = projected[:, 2 * width_local :].astype(jnp.bfloat16)
    own_score = jnp.sum(
        query.astype(jnp.float32) * key_new.astype(jnp.float32), axis=-1
    ) / math.sqrt(HEAD_DIM)
    all_queries = lax.all_gather(query.reshape(rows, width_local), "seq", axis=0, tiled=True)
    pages, page_len = (page_cache.shape[0], page_cache.shape[1])
    owner_query = all_queries[page_request].reshape(pages, heads_local, HEAD_DIM)
    keys_scaled = head_norm(page_cache[:, :, 0, :].astype(jnp.float32), score_gain).astype(
        jnp.bfloat16
    )
    values_paged = page_cache[:, :, 1, :].reshape(pages, page_len, heads_local, HEAD_DIM)
    scores = jnp.einsum(
        "sphd,shd->shp", keys_scaled, owner_query, preferred_element_type=jnp.float32
    ) / math.sqrt(HEAD_DIM)
    positions = page_number[:, None] * page_len + jnp.arange(page_len, dtype=jnp.int32)[None, :]
    live_mask = positions < lengths[page_request][:, None]
    page_max = jnp.max(jnp.where(live_mask[:, None, :], scores, far_below), axis=-1)
    weights = jnp.where(live_mask[:, None, :], jnp.exp(scores - page_max[..., None]), 0.0).astype(
        jnp.bfloat16
    )
    page_total = jnp.sum(weights.astype(jnp.float32), axis=-1)
    page_acc = jnp.einsum(
        "shp,sphd->shd", weights, values_paged, preferred_element_type=jnp.float32
    ).reshape(pages, width_local)
    requests = lengths.shape[0]
    onehot = page_request[:, None] == jnp.arange(requests, dtype=jnp.int32)[None, :]
    request_max = jnp.max(jnp.where(onehot[:, :, None], page_max[:, None, :], far_below), axis=0)
    factor = jnp.exp(page_max - request_max[page_request])
    selector = onehot.astype(jnp.float32)
    request_total = jnp.dot(selector.T, page_total * factor, precision=lax.Precision.HIGHEST)
    request_acc = jnp.dot(
        selector.T, scale_heads(page_acc, factor), precision=lax.Precision.HIGHEST
    )
    first_row = lax.axis_index("seq") * rows
    merged = merged_2((request_max, request_total, request_acc), "seq", join_parts)
    home_max = lax.dynamic_slice_in_dim(merged[0], first_row, rows, 0)
    home_total = lax.dynamic_slice_in_dim(merged[1], first_row, rows, 0)
    home_acc = lax.dynamic_slice_in_dim(merged[2], first_row, rows, 0)
    final_max = jnp.maximum(home_max, own_score)
    stored_factor = jnp.exp(home_max - final_max)
    own_factor = jnp.exp(own_score - final_max)
    total = home_total * stored_factor + own_factor
    summed = scale_heads(home_acc, stored_factor) + scale_heads(
        value_own.astype(jnp.float32), own_factor
    )
    attended = (
        (summed.reshape(rows, heads_local, HEAD_DIM) / total[..., None])
        .reshape(rows, width_local)
        .astype(jnp.bfloat16)
    )
    partial_out = jnp.dot(attended, output_weight, preferred_element_type=jnp.float32)
    first_col = lax.axis_index("tensor") * width_local
    rate = lax.dynamic_slice_in_dim(eigen_rate, first_col, width_local, 0)
    state = hidden.astype(jnp.float32)
    width = partial_out.shape[1]
    attn_local = lax.psum_scatter(partial_out, "tensor", scatter_dimension=1, tiled=True)
    attn_square = lax.psum(jnp.sum(attn_local * attn_local, axis=-1), "tensor")
    unit = attn_local / jnp.sqrt(attn_square / width + epsilon)[:, None]
    mixed = state + rate * (unit - state)
    mixed_square = lax.psum(jnp.sum(mixed * mixed, axis=-1), "tensor")
    return (mixed / jnp.sqrt(mixed_square / width + epsilon)[:, None]).astype(jnp.bfloat16)


def solution(mesh):
    placed = (
        P("seq", "tensor"),
        P(None, None, "tensor"),
        P("tensor", None),
        P("tensor"),
        P(),
        P(),
        P("seq"),
        P("seq"),
        P("seq", None, None, "tensor"),
    )
    return jax.shard_map(
        local, mesh=mesh, in_specs=placed, out_specs=P("seq", "tensor"), check_vma=False
    )
```

profile of v0, /device:TPU:6, one launch (start us, length us, event | category | flops | bytes accessed | tf_op | source)
XLA Modules:
  0.0 608.3 jit_solution(11876755678239287850)
XLA Ops:
  8.1 12.7 %all-gather.3 = bf16[4,320,8]{1,2,0:T(8,128)(2,1)S(1)} all-gather(bf16[1,320,8]{1,2,0:T(8,128)(2,1)} %bitcast.78), channel_id=1, replica_groups=mesh['seq'=64,'tensor'=4] {'tensor'}, dimensions={0}, use_global_device_ids=true | all-gather | bytes 25600 | tf_op jit(solution)/shard_map/all_gather | solution.py:63
  22.1 50.4 %all_gather.25 = bf16[512,320]{1,0:T(8,128)(2,1)S(1)} all-gather(bf16[8,320]{1,0:T(8,128)(2,1)S(1)} %get-tuple-element.242), channel_id=1, replica_groups=mesh['seq'=64,'tensor'=4] {'seq'}, dimensions={0}, use_global_device_ids=true | all-gather | bytes 332800 | tf_op jit(solution)/shard_map/all_gather | solution.py:77
  73.3 3.7 fusion.24
  85.0 49.6 %all-gather.1 = f32[32768,5]{0,1:T(8,128)S(1)} all-gather(f32[512,5]{0,1:T(8,128)S(1)} %fusion.12), channel_id=3, replica_groups=mesh['seq'=64,'tensor'=4] {'seq'}, dimensions={0}, use_global_device_ids=true | all-gather | bytes 665600 | tf_op jit(solution)/shard_map/all_gather | solution.py:16
  134.6 50.9 %all-gather = f32[32768,5]{0,1:T(8,128)S(1)} all-gather(f32[512,5]{0,1:T(8,128)S(1)} %select_reduce_fusion), channel_id=2, replica_groups=mesh['seq'=64,'tensor'=4] {'seq'}, dimensions={0}, use_global_device_ids=true | all-gather | bytes 665600 | tf_op jit(solution)/shard_map/all_gather | solution.py:16
  186.9 61.7 %all-gather.6.cloned.1.call-done = f32[32768,320]{0,1:T(8,128)} async-done(((f32[512,320]{0,1:T(8,128)}), f32[32768,320]{0,1:T(8,128)}) %all-gather.6.cloned.1.call-update) | async-done | bytes 41943056 | tf_op jit(solution)/shard_map/all_gather | solution.py:16
  248.6 38.8 %copy.54 = f32[40,8,64,512]{3,2,1,0:T(8,128)} copy(f32[40,8,64,512]{3,1,2,0:T(8,128)} %bitcast.71) | data formatting | bytes 83886080
  288.5 265.0 %while.19 = (s32[]{:T(128)}, f32[512,5]{0,1:T(8,128)S(1)}, f32[512,5]{0,1:T(8,128)S(1)}, f32[512,320]{0,1:T(8,128)S(1)}, f32[64,512,5]{1,2,0:T(8,128)}, /*index=...) while((s32[]{:T(128)}, f32[512,5]{0,1:T(8,128)S(1)}, ...), condition=%wide.region_6.7_spmd, body=%wide.region_5.6_spmd.sunk | while | flops 506885 | bytes 3379351 | solution.py:21
  289.2 3.1 constant_dynamic-slice_fusion.2
  293.4 3.1 constant_dynamic-slice_fusion.2
  297.6 3.1 constant_dynamic-slice_fusion.2
  301.8 3.1 constant_dynamic-slice_fusion.2
  306.0 3.1 constant_dynamic-slice_fusion.2
  310.3 3.1 constant_dynamic-slice_fusion.2
  314.5 3.1 constant_dynamic-slice_fusion.2
  318.7 3.1 constant_dynamic-slice_fusion.2
  322.9 3.1 constant_dynamic-slice_fusion.2
  331.3 3.1 constant_dynamic-slice_fusion.2
  339.7 3.1 constant_dynamic-slice_fusion.2
  348.1 3.1 constant_dynamic-slice_fusion.2
  356.5 3.1 constant_dynamic-slice_fusion.2
  364.9 3.1 constant_dynamic-slice_fusion.2
  373.3 3.1 constant_dynamic-slice_fusion.2
  377.5 3.1 constant_dynamic-slice_fusion.2
  386.0 3.1 constant_dynamic-slice_fusion.2
  394.4 3.1 constant_dynamic-slice_fusion.2
  402.8 3.1 constant_dynamic-slice_fusion.2
  411.2 3.1 constant_dynamic-slice_fusion.2
  419.6 3.1 constant_dynamic-slice_fusion.2
  428.0 3.1 constant_dynamic-slice_fusion.2
  436.4 3.1 constant_dynamic-slice_fusion.2
  444.8 3.1 constant_dynamic-slice_fusion.2
  453.3 3.1 constant_dynamic-slice_fusion.2
  457.5 3.1 constant_dynamic-slice_fusion.2
  465.9 3.1 constant_dynamic-slice_fusion.2
  474.3 3.1 constant_dynamic-slice_fusion.2
  482.7 3.1 constant_dynamic-slice_fusion.2
  491.1 3.1 constant_dynamic-slice_fusion.2
  499.5 3.1 constant_dynamic-slice_fusion.2
  507.9 3.1 constant_dynamic-slice_fusion.2
  516.3 3.1 constant_dynamic-slice_fusion.2
  524.7 3.1 constant_dynamic-slice_fusion.2
  533.2 3.1 constant_dynamic-slice_fusion.2
  537.4 3.1 constant_dynamic-slice_fusion.2
  545.8 3.1 constant_dynamic-slice_fusion.2
  557.9 23.2 %reduce-scatter.4.cloned.1.call-done = f32[320,8]{1,0:T(8,128)} async-done(((f32[1280,8]{1,0:T(8,128)}), f32[320,8]{1,0:T(8,128)}) %reduce-scatter.4.cloned.1.call-update) | async-done | bytes 10256
  583.1 8.2 %psum.14 = f32[8]{0:T(128)S(1)} all-reduce(f32[8]{0:T(128)S(1)} %multiply_reduce_fusion.4), channel_id=1, replica_groups=mesh['seq'=64,'tensor'=4] {'tensor'}, use_global_device_ids=true, to_apply=%region_11.12 | all-reduce | flops 8 | bytes 64 | tf_op jit(solution)/shard_map/psum | solution.py:129
  591.5 9.2 %psum.15 = f32[8]{0:T(128)S(1)} all-reduce(f32[8]{0:T(128)S(1)} %get-tuple-element.232), channel_id=1, replica_groups=mesh['seq'=64,'tensor'=4] {'tensor'}, use_global_device_ids=true, to_apply=%region_13.14 | all-reduce | flops 8 | bytes 64 | tf_op jit(solution)/shard_map/psum | solution.py:132
  (232 shorter events, 168.2 us)
Async XLA Ops:
  6.5 14.3 %copy-start = (bf16[1280,3,320]{0,2,1:T(8,128)(2,1)S(1)}, bf16[1280,3,320]{0,2,1:T(8,128)(2,1)}, u32[]{:S(2)}) copy-start(bf16[1280,3,320]{0,2,1:T(8,128)(2,1)} %param.12) | copy-start | bytes 7372804
  6.5 15.5 %copy-start.5 = (f32[320]{0:T(512)S(1)}, f32[320]{0:T(512)}, u32[]{:S(2)}) copy-start(f32[320]{0:T(512)} %param.14) | copy-start | bytes 3844
  6.5 242.0 %all-gather.6.cloned.1.call-start = ((), (), s32[]{:S(2)}) async-start(), calls=%async_computation.1 | async-start | bytes 42598400 | tf_op jit(solution)/shard_map/all_gather | solution.py:16
  77.0 0.7 copy-start.2
  77.0 1.5 copy-start.7
  79.2 4.1 copy-start.6
  84.7 496.5 %reduce-scatter.4.cloned.1.call-start = ((), (), s32[]{:S(2)}) async-start(), calls=%async_computation.2 | async-start | bytes 819200
  185.6 1.0 copy-start.3
  553.4 37.9 %copy-start.4 = (bf16[8,320]{1,0:T(8,128)(2,1)S(1)}, bf16[8,320]{1,0:T(8,128)(2,1)}, u32[]{:S(2)}) copy-start(bf16[8,320]{1,0:T(8,128)(2,1)} %param.11) | copy-start | bytes 15364
  553.4 48.0 %copy-start.1 = (bf16[1280,3,320]{0,2,1:T(8,128)(2,1)S(1)}, bf16[1280,3,320]{0,2,1:T(8,128)(2,1)}, u32[]{:S(2)}) copy-start(bf16[1280,3,320]{0,2,1:T(8,128)(2,1)} %param.12) | copy-start | bytes 7372804
Sparse Core Ops, SparseCore 0:
  84.8 163.7 all-gather.5
  558.1 23.0 reduce-scatter.3
where the time goes:
time: 615 us; the launch traced here: 608 us
  local copies, waits for them, and re-layouts  249 us (40%)
  blocking collectives  181 us (29%)
  waiting for transfers between devices  84.9 us (14%)
  other arithmetic  69.5 us (11%)
  between operations  13.6 us (2%)
  matrix products  8.18 us (1%)
    dynamic_slice x66, local copies, waits for them, and re-layouts, take(): lax.dynamic_index_in_dim(a, source, 0, False)  199 us
    all_gather x2, blocking collectives, merged_2(): gathered = jax.tree.map(lambda a: lax.all_gather(a, axis), part)  101 us
    all_gather x1, waiting for transfers between devices, merged_2(): gathered = jax.tree.map(lambda a: lax.all_gather(a, axis), part)  61.7 us
    all_gather x1, blocking collectives, local(): lax.all_gather(query.reshape(rows, width_local), 'seq', axis=0, tiled=True)  50.4 us
    add x63, other arithmetic, join_parts(): first_total * first_factor + second_total * second_factor  46.9 us
    unnamed x19, local copies, waits for them, and re-layouts  40.9 us
    unnamed x3, waiting for transfers between devices  23.3 us
    add x63, other arithmetic, join_parts(): scale_heads(first_acc, first_factor)  18.3 us
  transfers between devices with their start and end apart: 2, of which 2 were waited for; matrix products, arithmetic and copies ran while one was open for 0% of the time, Pallas kernels for 0%

commit v1 on v0

v1 whole, which is shorter than its diff:
```python
import math

import jax
import jax.numpy as jnp
from jax import lax
from jax.sharding import PartitionSpec as P

HEAD_DIM = 64


epsilon = 1e-06
far_below = -1e30


def head_norm(values, gain):
    shaped = values.reshape(values.shape[:-1] + (-1, HEAD_DIM))
    normed = shaped / jnp.sqrt(jnp.mean(shaped * shaped, axis=-1, keepdims=True) + epsilon)
    return normed * gain.reshape(-1, HEAD_DIM)


def scale_heads(summed, factor):
    shaped = summed.reshape(summed.shape[:-1] + (factor.shape[-1], -1))
    return (shaped * factor[..., None]).reshape(summed.shape)


def local(
    hidden,
    inward_weight,
    output_weight,
    score_gain,
    eigen_rate,
    lengths,
    page_request,
    page_number,
    page_cache,
):
    rows, width_local = hidden.shape
    heads_local = width_local // HEAD_DIM
    gathered = lax.all_gather(hidden, "tensor", axis=1, tiled=True)
    projected = jnp.dot(
        gathered,
        inward_weight.reshape(inward_weight.shape[0], -1),
        preferred_element_type=jnp.float32,
    )
    query = head_norm(projected[:, :width_local], score_gain).astype(jnp.bfloat16)
    key_new = head_norm(projected[:, width_local : 2 * width_local], score_gain).astype(
        jnp.bfloat16
    )
    value_own = projected[:, 2 * width_local :].astype(jnp.bfloat16)
    own_score = jnp.sum(
        (query.astype(jnp.float32) * key_new.astype(jnp.float32)).reshape(
            rows, heads_local, HEAD_DIM
        ),
        axis=-1,
    ) / math.sqrt(HEAD_DIM)

    all_queries = lax.all_gather(query, "seq", axis=0, tiled=True)
    pages, page_len = (page_cache.shape[0], page_cache.shape[1])
    owner_query = all_queries[page_request].reshape(pages, heads_local, HEAD_DIM)
    keys_scaled = head_norm(page_cache[:, :, 0, :].astype(jnp.float32), score_gain).astype(
        jnp.bfloat16
    )
    values_paged = page_cache[:, :, 1, :].reshape(pages, page_len, heads_local, HEAD_DIM)
    scores = jnp.einsum(
        "sphd,shd->shp", keys_scaled, owner_query, preferred_element_type=jnp.float32
    ) / math.sqrt(HEAD_DIM)
    positions = page_number[:, None] * page_len + jnp.arange(page_len, dtype=jnp.int32)[None, :]
    live_mask = positions < lengths[page_request][:, None]
    page_max = jnp.max(jnp.where(live_mask[:, None, :], scores, far_below), axis=-1)
    weights = jnp.where(live_mask[:, None, :], jnp.exp(scores - page_max[..., None]), 0.0).astype(
        jnp.bfloat16
    )
    page_total = jnp.sum(weights.astype(jnp.float32), axis=-1)
    page_acc = jnp.einsum(
        "shp,sphd->shd", weights, values_paged, preferred_element_type=jnp.float32
    ).reshape(pages, width_local)

    packed = jnp.concatenate(
        [page_acc, page_total, page_max, page_request.astype(jnp.float32)[:, None]], axis=1
    )
    all_parts = lax.all_gather(packed, "seq", axis=0, tiled=True)
    acc_all = all_parts[:, :width_local]
    total_all = all_parts[:, width_local : width_local + heads_local]
    max_all = all_parts[:, width_local + heads_local : width_local + 2 * heads_local]
    owner_all = all_parts[:, width_local + 2 * heads_local]

    first_row = lax.axis_index("seq") * rows
    row_ids = (first_row + jnp.arange(rows, dtype=jnp.int32)).astype(jnp.float32)
    mine = owner_all[None, :] == row_ids[:, None]
    masked_max = jnp.max(jnp.where(mine[:, :, None], max_all[None], far_below), axis=1)
    final_max = jnp.maximum(masked_max, own_score)
    factor = jnp.where(
        mine[:, :, None], jnp.exp(max_all[None] - final_max[:, None, :]), 0.0
    )
    own_factor = jnp.exp(own_score - final_max)
    total = jnp.sum(factor * total_all[None], axis=1) + own_factor
    stored = jnp.einsum(
        "rsh,shd->rhd",
        factor,
        acc_all.reshape(-1, heads_local, HEAD_DIM),
        precision=lax.Precision.HIGHEST,
    ).reshape(rows, width_local)
    summed = stored + scale_heads(value_own.astype(jnp.float32), own_factor)
    attended = (
        (summed.reshape(rows, heads_local, HEAD_DIM) / total[..., None])
        .reshape(rows, width_local)
        .astype(jnp.bfloat16)
    )
    partial_out = jnp.dot(attended, output_weight, preferred_element_type=jnp.float32)
    attn_out = lax.psum(partial_out, "tensor")
    width = attn_out.shape[1]
    state = gathered.astype(jnp.float32)
    unit = attn_out / jnp.sqrt(jnp.sum(attn_out * attn_out, axis=-1, keepdims=True) / width + epsilon)
    mixed = state + eigen_rate * (unit - state)
    result = mixed / jnp.sqrt(jnp.sum(mixed * mixed, axis=-1, keepdims=True) / width + epsilon)
    first_col = lax.axis_index("tensor") * width_local
    return lax.dynamic_slice_in_dim(result, first_col, width_local, 1).astype(jnp.bfloat16)


def solution(mesh):
    placed = (
        P("seq", "tensor"),
        P(None, None, "tensor"),
        P("tensor", None),
        P("tensor"),
        P(),
        P(),
        P("seq"),
        P("seq"),
        P("seq", None, None, "tensor"),
    )
    return jax.shard_map(
        local, mesh=mesh, in_specs=placed, out_specs=P("seq", "tensor"), check_vma=False
    )
```

time: 615 us -> 203 us (0.33); the launches traced: 608 us -> 202 us
  local copies, waits for them, and re-layouts: 249 us -> 18 us
  blocking collectives: 181 us -> 83.3 us
  other arithmetic: 69.5 us -> 5.14 us
  waiting for transfers between devices: 84.9 us -> 74.1 us
    dynamic_slice x67 -> x0, local copies, waits for them, and re-layouts: 200 us -> none  [the longest x66 199 us: take(): lax.dynamic_index_in_dim(a, source, 0, False)]
    all_gather x3 -> x1, blocking collectives: 151 us -> 53.2 us  [local(): all_queries = lax.all_gather(query, 'seq', axis=0, tiled=True)]
    add x127 -> x1, other arithmetic: 65.2 us -> 0.01 us  [local(): total = jnp.sum(factor * total_all[None], axis=1) + own_factor]
    unnamed x19 -> x13, local copies, waits for them, and re-layouts: 40.9 us -> 0.68 us
    unnamed x3 -> x1, waiting for transfers between devices: 23.3 us -> 0.02 us
    all_gather x1, waiting for transfers between devices: 61.7 us -> 74.1 us  [local(): all_parts = lax.all_gather(packed, 'seq', axis=0, tiled=True)]
    slice x0 -> x5, local copies, waits for them, and re-layouts: none -> 9.32 us  [the longest x2 4.38 us: local(): all_parts[:, width_local + heads_local:width_local + 2 * heads_local]]
    psum x2 -> x1, blocking collectives: 17.5 us -> 17.4 us  [local(): attn_out = lax.psum(partial_out, 'tensor')]
  transfers between devices with their start and end apart: 2 -> 1, of which waited for: 2 -> 1; matrix products, arithmetic and copies ran while one was open for 0% -> 0% of each run, Pallas kernels for 0% -> 0%
where the time goes in v1:
time: 203 us; the launch traced here: 202 us
  blocking collectives  83.3 us (41%)
  waiting for transfers between devices  74.1 us (37%)
  local copies, waits for them, and re-layouts  18 us (9%)
  between operations  13.5 us (7%)
  matrix products  8.35 us (4%)
  other arithmetic  5.14 us (3%)
    all_gather x1, waiting for transfers between devices, local(): all_parts = lax.all_gather(packed, 'seq', axis=0, tiled=True)  74.1 us
    all_gather x1, blocking collectives, local(): all_queries = lax.all_gather(query, 'seq', axis=0, tiled=True)  53.2 us
    psum x1, blocking collectives, local(): attn_out = lax.psum(partial_out, 'tensor')  17.4 us
    all_gather x1, blocking collectives, local(): gathered = lax.all_gather(hidden, 'tensor', axis=1, tiled=True)  12.7 us
    slice x2, local copies, waits for them, and re-layouts, local(): all_parts[:, width_local + heads_local:width_local + 2 * heads_local]  4.38 us
  transfers between devices with their start and end apart: 1, of which 1 were waited for; matrix products, arithmetic and copies ran while one was open for 0% of the time, Pallas kernels for 0%

profile of v1, /device:TPU:6, one launch (start us, length us, event | category | flops | bytes accessed | tf_op | source)
XLA Modules:
  0.0 202.4 jit_solution(14112942308790230901)
XLA Ops:
  6.5 0.8 broadcast_multiply_fusion
  7.3 0.7 compare_select_fusion
  8.1 0.8 mul.86
  8.8 12.7 %all-gather = bf16[4,320,8]{1,2,0:T(8,128)(2,1)S(1)} all-gather(bf16[1,320,8]{1,2,0:T(8,128)(2,1)} %bitcast.52), channel_id=1, replica_groups=mesh['seq'=64,'tensor'=4] {'tensor'}, dimensions={0}, use_global_device_ids=true | all-gather | bytes 25600 | tf_op jit(solution)/shard_map/all_gather | solution.py:39
  21.5 0.1 reshape.184
  21.7 0.7 fusion.21
  22.5 0.6 copy-done.3
  23.1 0.1 multiply_reduce_fusion.5
  23.3 0.1 multiply_reduce_fusion.4
  23.4 0.2 multiply_reduce_fusion.3
  23.6 53.2 %all_gather.10 = bf16[512,5,64]{2,0,1:T(8,128)(2,1)S(1)} all-gather(bf16[8,5,64]{2,0,1:T(8,128)(2,1)S(1)} %copy.50), channel_id=1, replica_groups=mesh['seq'=64,'tensor'=4] {'seq'}, dimensions={0}, use_global_device_ids=true | all-gather | bytes 332800 | tf_op jit(solution)/shard_map/all_gather | solution.py:57
  76.8 0.5 copy.51
  77.3 0.7 gather_fusion
  78.0 1.2 gather_fusion.1
  79.2 3.7 %fusion.18 = (bf16[24,128,1,320]{1,3,2,0:T(8,128)(2,1)}, bf16[24,128,1,320]{1,3,2,0:T(8,128)(2,1)S(1)}) fusion(bf16[24,128,2,320]{1,3,2,0:T(8,128)(2,1)} %param.17), kind=kLoop, calls=%fused_computation.58 | loop fusion | bytes 7864320 | tf_op jit(solution)/shard_map/slice | solution.py:63
  82.8 0.7 fusion
  83.6 0.1 add_compare_fusion
  83.7 0.7 fusion.3
  84.4 0.1 select_reduce_fusion.1
  84.5 0.2 fusion.16
  84.7 0.1 copy.53
  84.8 0.1 copy.54
  84.9 0.1 copy.52
  85.0 2.6 %fusion.9 = f32[24,5,1,64]{3,2,1,0:T(1,128)S(1)} fusion(bf16[24,128,5,64]{1,3,2,0:T(8,128)(2,1)} %bitcast.49, bf16[24,5,128,1]{2,0,1,3:T(8,128)(2,1)S(1)} %get-tuple-element.15), kind=kOutput, calls=%fused_computation.20 | convolution fusion | flops 1966080 | bytes 2027520 | tf_op jit(solution)/shard_map/shp,sphd->shd/dot_general | solution.py:74
  87.6 0.1 reshape.160
  87.7 0.7 pad_maximum_fusion
  88.5 0.1 copy.57
  88.5 74.1 %all-gather.3.cloned.1.call-done = f32[1536,331]{1,0:T(8,128)} async-done(((f32[24,331]{1,0:T(8,128)}), f32[1536,331]{1,0:T(8,128)}) %all-gather.3.cloned.1.call-update) | async-done | bytes 2033680 | tf_op jit(solution)/shard_map/all_gather | solution.py:81
  162.6 3.0 %fusion.19 = (f32[1536,5]{1,0:T(8,128)}, f32[1536,5]{1,0:T(8,128)S(1)}) fusion(f32[1536,331]{1,0:T(8,128)} %all-gather.3.cloned.1.call-done), kind=kLoop, calls=%fused_computation.59 | loop fusion | bytes 122880 | tf_op jit(solution)/shard_map/slice | solution.py:84
  165.6 1.4 copy.56
  167.0 0.3 copy.60
  167.3 1.6 slice_reduce_fusion
  168.9 0.1 broadcast_compare_fusion
  169.0 0.1 select_reduce_fusion
  169.1 0.2 multiply_reduce_fusion
  169.3 0.1 copy.61
  169.4 0.1 copy.59
  169.5 0.1 mul.96
  169.6 0.1 mul.97
  169.7 0.1 div.96
  169.8 3.0 %copy.55 = f32[1536,320]{0,1:T(8,128)} copy(f32[1536,320]{1,0:T(8,128)} %bitcast.45) | data formatting | bytes 3932160 | tf_op jit(solution)/shard_map/slice | solution.py:82
  172.9 3.3 %convolution_bitcast_fusion = f32[8,5,64]{2,0,1:T(8,128)S(1)} fusion(f32[1536,5,64]{0,2,1:T(8,128)} %bitcast.46, f32[8,5]{0,1:T(8,128)S(1)} %multiply_maximum_fusion, f32[1536,5]{0,1:T(8,128)S(1)} %copy.56, pred[8,1536]{1,0:T(8,128)(4,1)S(1)} %broadcast_compare_fusion), kind=kOutput, calls=%fused_computation.8 | convolution fusion | flops 47308800 | bytes 2019488 | tf_op jit(solution)/shard_map/rsh,shd->rhd/dot_general | solution.py:97
  176.2 0.1 reshape.163
  176.3 0.9 fusion.14
  177.2 17.4 %psum.7 = f32[8,1280]{1,0:T(8,128)S(1)} all-reduce(f32[8,1280]{1,0:T(8,128)S(1)} %fusion.14), channel_id=1, replica_groups=mesh['seq'=64,'tensor'=4] {'tensor'}, use_global_device_ids=true, to_apply=%region_8.9 | all-reduce | flops 10240 | bytes 81920 | tf_op jit(solution)/shard_map/psum | solution.py:110
  194.6 0.1 multiply_reduce_fusion.2
  194.7 0.2 multiply_reduce_fusion.1
  194.9 0.7 fusion.13
  (29 shorter events, 0.5 us)
Async XLA Ops:
  6.5 15.1 %copy-start = (bf16[1280,3,320]{0,2,1:T(8,128)(2,1)S(1)}, bf16[1280,3,320]{0,2,1:T(8,128)(2,1)}, u32[]{:S(2)}) copy-start(bf16[1280,3,320]{0,2,1:T(8,128)(2,1)} %param.10) | copy-start | bytes 7372804
  6.5 156.1 %all-gather.3.cloned.1.call-start = ((), (), s32[]{:S(2)}) async-start(), calls=%async_computation | async-start | bytes 2396160 | tf_op jit(solution)/shard_map/all_gather | solution.py:81
  21.6 55.6 %copy-start.1 = (s32[512]{0:T(512)S(1)}, s32[512]{0:T(512)}, u32[]{:S(2)}) copy-start(s32[512]{0:T(512)} %param.14) | copy-start | bytes 6148
  22.4 0.6 copy-start.3
  79.2 4.5 %copy-start.4 = (bf16[24,5,64]{2,1,0:T(8,128)(2,1)S(1)}, bf16[24,5,64]{2,1,0:T(8,128)(2,1)}, u32[]{:S(2)}) copy-start(bf16[24,5,64]{2,1,0:T(8,128)(2,1)} %gather_fusion.1) | copy-start | bytes 46084
  169.8 6.5 %copy-start.2 = (bf16[320,1280]{1,0:T(8,128)(2,1)S(1)}, bf16[320,1280]{1,0:T(8,128)(2,1)}, u32[]{:S(2)}) copy-start(bf16[320,1280]{1,0:T(8,128)(2,1)} %param.11) | copy-start | bytes 2457604
  172.9 21.8 %copy-start.5 = (f32[1280]{0:T(1024)S(1)}, f32[1280]{0:T(1024)}, u32[]{:S(2)}) copy-start(f32[1280]{0:T(1024)} %param.13) | copy-start | bytes 15364
Sparse Core Ops, SparseCore 0:
  88.6 74.0 all-gather.2

commit v2 on v1

--- a/solution.py
+++ b/solution.py
@@ -23,6 +23,70 @@
     return (shaped * factor[..., None]).reshape(summed.shape)
 
 
+def xor_partner(axis, size, bit):
+    return [(i, i ^ bit) for i in range(size)]
+
+
+def gather_doubling(value, axis):
+    size = lax.axis_size(axis)
+    index = lax.axis_index(axis)
+    held = value[None]
+    bit = 1
+    while bit < size:
+        other = lax.ppermute(held, axis, perm=xor_partner(axis, size, bit))
+        high = (index & bit) != 0
+        held = jnp.where(high, jnp.stack([other, held]), jnp.stack([held, other]))
+        held = held.reshape((-1,) + value.shape)
+        bit *= 2
+    return held
+
+
+def sum_doubling(value, axis):
+    size = lax.axis_size(axis)
+    bit = 1
+    while bit < size:
+        value = value + lax.ppermute(value, axis, perm=xor_partner(axis, size, bit))
+        bit *= 2
+    return value
+
+
+def merge_packed(first, second, width, heads):
+    first_acc, first_total, first_max = (
+        first[..., :width], first[..., width : width + heads], first[..., width + heads :]
+    )
+    second_acc, second_total, second_max = (
+        second[..., :width], second[..., width : width + heads], second[..., width + heads :]
+    )
+    top = jnp.maximum(first_max, second_max)
+    first_factor = jnp.exp(first_max - top)
+    second_factor = jnp.exp(second_max - top)
+    return jnp.concatenate(
+        [
+            scale_heads(first_acc, first_factor) + scale_heads(second_acc, second_factor),
+            first_total * first_factor + second_total * second_factor,
+            top,
+        ],
+        axis=-1,
+    )
+
+
+def scatter_halving(packed, axis, width, heads):
+    size = lax.axis_size(axis)
+    index = lax.axis_index(axis)
+    bit = 1
+    step = 0
+    while bit < size:
+        paired = packed.reshape((packed.shape[0] // 2, 2) + packed.shape[1:])
+        mine = (index >> step) & 1
+        keep = lax.dynamic_index_in_dim(paired, mine, 1, False)
+        send = lax.dynamic_index_in_dim(paired, 1 - mine, 1, False)
+        other = lax.ppermute(send, axis, perm=xor_partner(axis, size, bit))
+        packed = merge_packed(keep, other, width, heads)
+        bit *= 2
+        step += 1
+    return packed[0]
+
+
 def local(
     hidden,
     inward_weight,
@@ -36,7 +100,7 @@
 ):
     rows, width_local = hidden.shape
     heads_local = width_local // HEAD_DIM
-    gathered = lax.all_gather(hidden, "tensor", axis=1, tiled=True)
+    gathered = jnp.moveaxis(gather_doubling(hidden, "tensor"), 0, 1).reshape(rows, -1)
     projected = jnp.dot(
         gathered,
         inward_weight.reshape(inward_weight.shape[0], -1),
@@ -54,7 +118,7 @@
         axis=-1,
     ) / math.sqrt(HEAD_DIM)
 
-    all_queries = lax.all_gather(query, "seq", axis=0, tiled=True)
+    all_queries = gather_doubling(query, "seq").reshape(-1, width_local)
     pages, page_len = (page_cache.shape[0], page_cache.shape[1])
     owner_query = all_queries[page_request].reshape(pages, heads_local, HEAD_DIM)
     keys_scaled = head_norm(page_cache[:, :, 0, :].astype(jnp.float32), score_gain).astype(
@@ -75,31 +139,27 @@
         "shp,sphd->shd", weights, values_paged, preferred_element_type=jnp.float32
     ).reshape(pages, width_local)
 
-    packed = jnp.concatenate(
-        [page_acc, page_total, page_max, page_request.astype(jnp.float32)[:, None]], axis=1
+    requests = lengths.shape[0]
+    onehot = page_request[:, None] == jnp.arange(requests, dtype=jnp.int32)[None, :]
+    request_max = jnp.max(jnp.where(onehot[:, :, None], page_max[:, None, :], far_below), axis=0)
+    factor = jnp.exp(page_max - request_max[page_request])
+    selector = onehot.astype(jnp.float32)
+    request_total = jnp.dot(selector.T, page_total * factor, precision=lax.Precision.HIGHEST)
+    request_acc = jnp.dot(
+        selector.T, scale_heads(page_acc, factor), precision=lax.Precision.HIGHEST
     )
-    all_parts = lax.all_gather(packed, "seq", axis=0, tiled=True)
-    acc_all = all_parts[:, :width_local]
-    total_all = all_parts[:, width_local : width_local + heads_local]
-    max_all = all_parts[:, width_local + heads_local : width_local + 2 * heads_local]
-    owner_all = all_parts[:, width_local + 2 * heads_local]
-
-    first_row = lax.axis_index("seq") * rows
-    row_ids = (first_row + jnp.arange(rows, dtype=jnp.int32)).astype(jnp.float32)
-    mine = owner_all[None, :] == row_ids[:, None]
-    masked_max = jnp.max(jnp.where(mine[:, :, None], max_all[None], far_below), axis=1)
-    final_max = jnp.maximum(masked_max, own_score)
-    factor = jnp.where(
-        mine[:, :, None], jnp.exp(max_all[None] - final_max[:, None, :]), 0.0
-    )
+    packed = jnp.concatenate([request_acc, request_total, request_max], axis=1)
+    packed = packed.reshape(lax.axis_size("seq"), rows, packed.shape[-1])
+    home = scatter_halving(packed, "seq", width_local, heads_local)
+    home_acc = home[:, :width_local]
+    home_total = home[:, width_local : width_local + heads_local]
+    home_max = home[:, width_local + heads_local :]
+    final_max = jnp.maximum(home_max, own_score)
+    stored_factor = jnp.exp(home_max - final_max)
+    total_stored = home_total * stored_factor
+    stored = scale_heads(home_acc, stored_factor)
     own_factor = jnp.exp(own_score - final_max)
-    total = jnp.sum(factor * total_all[None], axis=1) + own_factor
-    stored = jnp.einsum(
-        "rsh,shd->rhd",
-        factor,
-        acc_all.reshape(-1, heads_local, HEAD_DIM),
-        precision=lax.Precision.HIGHEST,
-    ).reshape(rows, width_local)
+    total = total_stored + own_factor
     summed = stored + scale_heads(value_own.astype(jnp.float32), own_factor)
     attended = (
         (summed.reshape(rows, heads_local, HEAD_DIM) / total[..., None])
@@ -107,7 +167,7 @@
         .astype(jnp.bfloat16)
     )
     partial_out = jnp.dot(attended, output_weight, preferred_element_type=jnp.float32)
-    attn_out = lax.psum(partial_out, "tensor")
+    attn_out = sum_doubling(partial_out, "tensor")
     width = attn_out.shape[1]
     state = gathered.astype(jnp.float32)
     unit = attn_out / jnp.sqrt(jnp.sum(attn_out * attn_out, axis=-1, keepdims=True) / width + epsilon)

time: 203 us -> 143 us (0.70)
  blocking collectives: 83.3 us -> 0 us
  starting transfers between devices: 0.01 us -> 28 us
  other arithmetic: 5.14 us -> 19.8 us
  between operations: 13.5 us -> 0.39 us
  waiting for transfers between devices: 74.1 us -> 62.3 us
  local copies, waits for them, and re-layouts: 18 us -> 24.3 us
    all_gather x1 -> x0, waiting for transfers between devices: 74.1 us -> none  [local(): all_parts = lax.all_gather(packed, 'seq', axis=0, tiled=True)]
    all_gather x2 -> x0, blocking collectives: 65.9 us -> none  [the longest x1 53.2 us: local(): all_queries = lax.all_gather(query, 'seq', axis=0, tiled=True)]
    ppermute x0 -> x16, waiting for transfers between devices: none -> 62.3 us  [the longest x8 30.5 us: gather_doubling(): other = lax.ppermute(held, axis, perm=xor_partner(axis, size, bit))]
    ppermute x0 -> x16, starting transfers between devices: none -> 28 us  [the longest x8 18.5 us: gather_doubling(): other = lax.ppermute(held, axis, perm=xor_partner(axis, size, bit))]
    psum x1 -> x0, blocking collectives: 17.4 us -> none  [local(): attn_out = lax.psum(partial_out, 'tensor')]
    mul x2 -> x28, local copies, waits for them, and re-layouts: 0.15 us -> 9.74 us  [scale_heads(): return (shaped * factor[..., None]).reshape(summed.shape)]
    add x1 -> x13, other arithmetic: 0.01 us -> 9.57 us  [the longest x6 5.18 us: merge_packed(): scale_heads(first_acc, first_factor)]
    slice x6 -> x1, local copies, waits for them, and re-layouts: 9.4 us -> 0.07 us  [local(): projected[:, width_local:2 * width_local]]
  transfers between devices with their start and end apart: 1 -> 16, of which waited for: 1 -> 15; matrix products, arithmetic and copies ran while one was open for 0% -> 6% of each run, Pallas kernels for 0% -> 0%
where the time goes in v2:
time: 143 us; the launch traced here: 142 us
  waiting for transfers between devices  62.3 us (44%)
  starting transfers between devices  28 us (20%)
  local copies, waits for them, and re-layouts  24.3 us (17%)
  other arithmetic  19.8 us (14%)
  matrix products  7.3 us (5%)
    ppermute x8, waiting for transfers between devices, gather_doubling(): other = lax.ppermute(held, axis, perm=xor_partner(axis, size, bit))  30.5 us
    ppermute x6, waiting for transfers between devices, scatter_halving(): other = lax.ppermute(send, axis, perm=xor_partner(axis, size, bit))  25.6 us
    ppermute x8, starting transfers between devices, gather_doubling(): other = lax.ppermute(held, axis, perm=xor_partner(axis, size, bit))  18.5 us
    mul x28, local copies, waits for them, and re-layouts, scale_heads(): return (shaped * factor[..., None]).reshape(summed.shape)  9.74 us
    ppermute x6, starting transfers between devices, scatter_halving(): other = lax.ppermute(send, axis, perm=xor_partner(axis, size, bit))  6.14 us
    ppermute x2, waiting for transfers between devices, sum_doubling(): value = value + lax.ppermute(value, axis, perm=xor_partner(axis, size, bit))  6.14 us
    add x6, other arithmetic, merge_packed(): scale_heads(first_acc, first_factor)  5.18 us
    add x5, other arithmetic, merge_packed(): first_total * first_factor + second_total * second_factor  4.3 us
  transfers between devices with their start and end apart: 16, of which 15 were waited for; matrix products, arithmetic and copies ran while one was open for 6% of the time, Pallas kernels for 0%

profile of v2, /device:TPU:6, one launch (start us, length us, event | category | flops | bytes accessed | tf_op | source)
XLA Modules:
  0.0 142.1 jit_solution(6711512934012523242)
XLA Ops:
  0.0 1.7 %collective-permute-start = (bf16[1,8,320]{2,1,0:T(8,128)(2,1)}, bf16[1,8,320]{2,1,0:T(8,128)(2,1)S(1)}, u32[]{:S(2)}, u32[]{:S(2)}) collective-permute-start(bf16[1,8,320]{2,1,0:T(8,128)(2,1)} %bitcast.104), channel_id=1, source_target_pairs={{0,1},{1,0},{2,3},{3,2},{4,5},{5,4},{6,7},{7,6},{8,9},{9,8},{10,11... | collective-permute-start | bytes 15368 | tf_op jit(solution)/shard_map/ppermute | solution.py:36
  1.7 3.7 %fusion.39 = (bf16[24,128,1,320]{1,3,2,0:T(8,128)(2,1)}, bf16[24,128,1,320]{1,3,2,0:T(8,128)(2,1)S(1)}) fusion(bf16[24,128,2,320]{1,3,2,0:T(8,128)(2,1)} %param.17), kind=kLoop, calls=%fused_computation.145 | loop fusion | bytes 7864320 | tf_op jit(solution)/shard_map/slice | solution.py:127
  5.4 1.3 copy-done.2
  8.3 3.0 %collective-permute-start.1 = (bf16[2,8,320]{2,1,0:T(8,128)(2,1)S(1)}, bf16[2,8,320]{2,1,0:T(8,128)(2,1)S(1)}, u32[]{:S(2)}, u32[]{:S(2)}) collective-permute-start(bf16[2,8,320]{2,1,0:T(8,128)(2,1)S(1)} %maximum_select_fusion.8), channel_id=1, source_target_pairs={{0,2},{1,3},{2,0},{3,1},{4,6},{5,7},{6,4},{7,5},{8,10},{9,11},{10,... | collective-permute-start | bytes 30728 | tf_op jit(solution)/shard_map/ppermute | solution.py:36
  11.3 2.3 %collective-permute-done.1 = bf16[2,8,320]{2,1,0:T(8,128)(2,1)S(1)} collective-permute-done((bf16[2,8,320]{2,1,0:T(8,128)(2,1)S(1)}, bf16[2,8,320]{2,1,0:T(8,128)(2,1)S(1)}, u32[]{:S(2)}, u32[]{:S(2)}) %collective-permute-start.1) | collective-permute-done | bytes 10272 | tf_op jit(solution)/shard_map/ppermute | solution.py:36
  15.6 1.1 collective-permute-done.2
  16.7 2.0 %collective-permute-start.3 = (bf16[2,8,5,64]{3,2,1,0:T(8,128)(2,1)S(1)}, bf16[2,8,5,64]{3,2,1,0:T(8,128)(2,1)S(1)}, u32[]{:S(2)}, u32[]{:S(2)}) collective-permute-start(bf16[2,8,5,64]{3,2,1,0:T(8,128)(2,1)S(1)} %maximum_select_fusion.5), channel_id=1, source_target_pairs={{0,8},{4,12},{8,0},{12,4},{16,24},{20,28},{24,16},{28,20},{32,40},... | collective-permute-start | bytes 30728 | tf_op jit(solution)/shard_map/ppermute | solution.py:36
  18.7 2.0 %collective-permute-done.3 = bf16[2,8,5,64]{3,2,1,0:T(8,128)(2,1)S(1)} collective-permute-done((bf16[2,8,5,64]{3,2,1,0:T(8,128)(2,1)S(1)}, bf16[2,8,5,64]{3,2,1,0:T(8,128)(2,1)S(1)}, u32[]{:S(2)}, u32[]{:S(2)}) %collective-permute-start.3) | collective-permute-done | bytes 10272 | tf_op jit(solution)/shard_map/ppermute | solution.py:36
  20.8 3.4 %collective-permute-start.4 = (bf16[4,8,5,64]{3,2,1,0:T(8,128)(2,1)S(1)}, bf16[4,8,5,64]{3,2,1,0:T(8,128)(2,1)S(1)}, u32[]{:S(2)}, u32[]{:S(2)}) collective-permute-start(bf16[4,8,5,64]{3,2,1,0:T(8,128)(2,1)S(1)} %bitcast.94), channel_id=1, source_target_pairs={{0,16},{4,20},{8,24},{12,28},{16,0},{20,4},{24,8},{28,12},{32,48},... | collective-permute-start | bytes 61448 | tf_op jit(solution)/shard_map/ppermute | solution.py:36
  24.1 2.6 %collective-permute-done.4 = bf16[4,8,5,64]{3,2,1,0:T(8,128)(2,1)S(1)} collective-permute-done((bf16[4,8,5,64]{3,2,1,0:T(8,128)(2,1)S(1)}, bf16[4,8,5,64]{3,2,1,0:T(8,128)(2,1)S(1)}, u32[]{:S(2)}, u32[]{:S(2)}) %collective-permute-start.4) | collective-permute-done | bytes 20512 | tf_op jit(solution)/shard_map/ppermute | solution.py:36
  26.8 7.4 %collective-permute-start.5 = (bf16[8,8,5,64]{3,2,1,0:T(8,128)(2,1)S(1)}, bf16[8,8,5,64]{3,2,1,0:T(8,128)(2,1)S(1)}, u32[]{:S(2)}, u32[]{:S(2)}) collective-permute-start(bf16[8,8,5,64]{3,2,1,0:T(8,128)(2,1)S(1)} %bitcast.91), channel_id=1, source_target_pairs={{0,32},{4,36},{8,40},{12,44},{16,48},{20,52},{24,56},{28,60},{32,0... | collective-permute-start | bytes 122888 | tf_op jit(solution)/shard_map/ppermute | solution.py:36
  34.2 4.3 %collective-permute-done.5 = bf16[8,8,5,64]{3,2,1,0:T(8,128)(2,1)S(1)} collective-permute-done((bf16[8,8,5,64]{3,2,1,0:T(8,128)(2,1)S(1)}, bf16[8,8,5,64]{3,2,1,0:T(8,128)(2,1)S(1)}, u32[]{:S(2)}, u32[]{:S(2)}) %collective-permute-start.5) | collective-permute-done | bytes 40992 | tf_op jit(solution)/shard_map/ppermute | solution.py:36
  38.6 0.9 collective-permute-start.6
  40.3 7.6 %collective-permute-done.6 = bf16[16,8,5,64]{3,2,1,0:T(8,128)(2,1)S(1)} collective-permute-done((bf16[16,8,5,64]{3,2,1,0:T(8,128)(2,1)S(1)}, bf16[16,8,5,64]{3,2,1,0:T(8,128)(2,1)S(1)}, u32[]{:S(2)}, u32[]{:S(2)}) %collective-permute-start.6) | collective-permute-done | bytes 81952 | tf_op jit(solution)/shard_map/ppermute | solution.py:36
  48.3 10.6 %collective-permute-done.7 = bf16[32,8,5,64]{3,2,1,0:T(8,128)(2,1)S(1)} collective-permute-done((bf16[32,8,5,64]{3,2,1,0:T(8,128)(2,1)S(1)}, bf16[32,8,5,64]{3,2,1,0:T(8,128)(2,1)S(1)}, u32[]{:S(2)}, u32[]{:S(2)}) %collective-permute-start.7) | collective-permute-done | bytes 163872 | tf_op jit(solution)/shard_map/ppermute | solution.py:36
  59.4 1.3 select_n.247
  60.7 1.7 %gather_fusion.1 = bf16[24,320]{1,0:T(8,128)(2,1)S(1)} fusion(bf16[512,320]{1,0:T(8,128)(2,1)} %select_n.247, s32[1024]{0:T(1024)S(1)} %pad_clamp_fusion), kind=kCustom, calls=%fused_computation.1 | custom fusion | bytes 30816 | tf_op jit(solution)/shard_map/gather | solution.py:123
  62.5 2.3 %fusion.3 = f32[24,5,1,128]{3,2,1,0:T(1,128)S(1)} fusion(bf16[24,5,64,1]{2,3,1,0:T(2,128)(2,1)S(1)} %reshape.542, bf16[24,128,5,64]{1,3,2,0:T(8,128)(2,1)} %bitcast.81, f32[5,64]{1,0:T(8,128)S(1)} %mul.301, f32[24,128,5]{1,2,0:T(8,128)} %add_sqrt_fusion), kind=kOutput, calls=%fused_computation.8 | convolution fusion | flops 5898240 | bytes 2105600 | tf_op jit(solution)/shard_map/sphd,shd->shp/dot_general | solution.py:128
  66.0 2.6 %fusion.10 = f32[24,5,1,64]{3,2,1,0:T(1,128)S(1)} fusion(bf16[24,128,5,64]{1,3,2,0:T(8,128)(2,1)} %bitcast.85, bf16[24,5,128,1]{2,0,1,3:T(8,128)(2,1)S(1)} %get-tuple-element.44), kind=kOutput, calls=%fused_computation.49 | convolution fusion | flops 1966080 | bytes 2027520 | tf_op jit(solution)/shard_map/shp,sphd->shd/dot_general | solution.py:138
  69.6 0.9 pad_maximum_fusion
  70.5 1.4 copy.22
  71.9 1.0 dynamic-slice_bitcast_fusion.1
  72.8 1.9 %collective-permute-done.8 = f32[32,8,330]{2,1,0:T(8,128)S(1)} collective-permute-done((f32[32,8,330]{2,1,0:T(8,128)}, f32[32,8,330]{2,1,0:T(8,128)S(1)}, u32[]{:S(2)}, u32[]{:S(2)}) %collective-permute-start.8) | collective-permute-done | bytes 337952 | tf_op jit(solution)/shard_map/ppermute | solution.py:83
  74.8 2.1 %fusion.7 = (f32[32,8,5]{2,1,0:T(8,128)}, f32[32,8,5]{2,1,0:T(8,128)S(1)}, f32[32,8,5]{2,1,0:T(8,128)}, f32[32,8,5]{2,1,0:T(8,128)}) fusion(f32[32,8,330]{2,1,0:T(8,128)S(1)} %collective-permute-done.8, f32[32,8,330]{2,1,0:T(8,128)} %get-tuple-element.36), kind=kLoop, calls=%fused_computation.27 | loop fusion | flops 7680 | bytes 40960 | tf_op jit(solution)/shard_map/add | solution.py:66
  77.2 1.0 mul.311
  78.1 1.2 mul.313
  79.4 1.0 mul.314
  80.3 1.4 %fusion.5 = f32[32,8,320]{2,1,0:T(8,128)S(1)} fusion(f32[32,8,320]{2,1,0:T(8,128)} %mul.314, f32[32,8,330]{2,1,0:T(8,128)} %copy-done.3, f32[32,8,320]{2,1,0:T(8,128)} %mul.311, f32[32,8,330]{2,1,0:T(8,128)} %get-tuple-element.36), kind=kLoop, calls=%fused_computation.13 | loop fusion | flops 245760 | bytes 1638400 | tf_op jit(solution)/shard_map/add | solution.py:65
  81.8 1.1 pad_maximum_fusion.1
  83.2 6.9 %collective-permute-done.9 = f32[16,8,330]{2,1,0:T(8,128)S(1)} collective-permute-done((f32[16,8,330]{2,1,0:T(8,128)S(1)}, f32[16,8,330]{2,1,0:T(8,128)S(1)}, u32[]{:S(2)}, u32[]{:S(2)}) %collective-permute-start.9) | collective-permute-done | bytes 168992 | tf_op jit(solution)/shard_map/ppermute | solution.py:83
  92.2 1.1 fusion.6
  93.3 0.9 pad_maximum_fusion.2
  94.2 1.5 %collective-permute-start.10 = (f32[8,8,330]{2,1,0:T(8,128)S(1)}, f32[8,8,330]{2,1,0:T(8,128)S(1)}, u32[]{:S(2)}, u32[]{:S(2)}) collective-permute-start(f32[8,8,330]{2,1,0:T(8,128)S(1)} %get-tuple-element.41), channel_id=1, source_target_pairs={{0,16},{4,20},{8,24},{12,28},{16,0},{20,4},{24,8},{28,12},{32,48},... | collective-permute-start | bytes 253448 | tf_op jit(solution)/shard_map/ppermute | solution.py:83
  96.4 4.9 %collective-permute-done.10 = f32[8,8,330]{2,1,0:T(8,128)S(1)} collective-permute-done((f32[8,8,330]{2,1,0:T(8,128)S(1)}, f32[8,8,330]{2,1,0:T(8,128)S(1)}, u32[]{:S(2)}, u32[]{:S(2)}) %collective-permute-start.10) | collective-permute-done | bytes 84512 | tf_op jit(solution)/shard_map/ppermute | solution.py:83
  102.9 0.9 mul.329
  104.5 1.1 fusion.8
  105.6 0.9 pad_maximum_fusion.3
  106.5 3.5 %collective-permute-start.11 = (f32[4,8,330]{2,1,0:T(8,128)S(1)}, f32[4,8,330]{2,1,0:T(8,128)S(1)}, u32[]{:S(2)}, u32[]{:S(2)}) collective-permute-start(f32[4,8,330]{2,1,0:T(8,128)S(1)} %get-tuple-element.43), channel_id=1, source_target_pairs={{0,32},{4,36},{8,40},{12,44},{16,48},{20,52},{24,56},{28,60},{32,0... | collective-permute-start | bytes 126728 | tf_op jit(solution)/shard_map/ppermute | solution.py:83
  110.0 0.8 multiply_reduce_fusion.3
  110.9 3.7 %collective-permute-done.11 = f32[4,8,330]{2,1,0:T(8,128)S(1)} collective-permute-done((f32[4,8,330]{2,1,0:T(8,128)S(1)}, f32[4,8,330]{2,1,0:T(8,128)S(1)}, u32[]{:S(2)}, u32[]{:S(2)}) %collective-permute-start.11) | collective-permute-done | bytes 42272 | tf_op jit(solution)/shard_map/ppermute | solution.py:83
  116.8 0.9 fusion.12
  117.7 0.8 pad_maximum_fusion.4
  118.8 3.6 %collective-permute-done.12 = f32[2,8,330]{2,1,0:T(8,128)S(1)} collective-permute-done((f32[2,8,330]{2,1,0:T(8,128)S(1)}, f32[2,8,330]{2,1,0:T(8,128)S(1)}, u32[]{:S(2)}, u32[]{:S(2)}) %collective-permute-start.12) | collective-permute-done | bytes 21152 | tf_op jit(solution)/shard_map/ppermute | solution.py:83
  124.9 4.5 %collective-permute-done.13 = f32[1,8,330]{2,1,0:T(8,128)S(1)} collective-permute-done((f32[1,8,330]{2,1,0:T(8,128)S(1)}, f32[1,8,330]{2,1,0:T(8,128)S(1)}, u32[]{:S(2)}, u32[]{:S(2)}) %collective-permute-start.13) | collective-permute-done | bytes 10592 | tf_op jit(solution)/shard_map/ppermute | solution.py:83
  130.5 0.9 fusion.28
  132.0 3.5 %collective-permute-done.14 = f32[8,1280]{1,0:T(8,128)S(1)} collective-permute-done((f32[8,1280]{1,0:T(8,128)S(1)}, f32[8,1280]{1,0:T(8,128)S(1)}, u32[]{:S(2)}, u32[]{:S(2)}) %collective-permute-start.14) | collective-permute-done | bytes 40992 | tf_op jit(solution)/shard_map/ppermute | solution.py:48
  135.5 2.9 %collective-permute-start.15 = (f32[8,1280]{1,0:T(8,128)S(1)}, f32[8,1280]{1,0:T(8,128)S(1)}, u32[]{:S(2)}, u32[]{:S(2)}) collective-permute-start(f32[8,1280]{1,0:T(8,128)S(1)} %add.203), channel_id=1, source_target_pairs={{0,2},{1,3},{2,0},{3,1},{4,6},{5,7},{6,4},{7,5},{8,10},{9,11},{10,... | collective-permute-start | bytes 122888 | tf_op jit(solution)/shard_map/ppermute | solution.py:48
  138.4 2.6 %collective-permute-done.15 = f32[8,1280]{1,0:T(8,128)S(1)} collective-permute-done((f32[8,1280]{1,0:T(8,128)S(1)}, f32[8,1280]{1,0:T(8,128)S(1)}, u32[]{:S(2)}, u32[]{:S(2)}) %collective-permute-start.15) | collective-permute-done | bytes 40992 | tf_op jit(solution)/shard_map/ppermute | solution.py:48
  (142 shorter events, 21.1 us)
Async XLA Ops:
  0.0 13.7 %copy-start = (bf16[1280,3,320]{0,2,1:T(8,128)(2,1)S(1)}, bf16[1280,3,320]{0,2,1:T(8,128)(2,1)}, u32[]{:S(2)}) copy-start(bf16[1280,3,320]{0,2,1:T(8,128)(2,1)} %param.10) | copy-start | bytes 7372804
  0.0 8.1 %copy-start.18 = (s32[24]{0:T(128)S(1)}, s32[24]{0:T(128)}, u32[]{:S(2)}) copy-start(s32[24]{0:T(128)} %param.15) | copy-start | bytes 292
  0.0 8.2 %copy-start.19 = (f32[320]{0:T(512)S(1)}, f32[320]{0:T(512)}, u32[]{:S(2)}) copy-start(f32[320]{0:T(512)} %param.12) | copy-start | bytes 3844
  0.0 8.2 %copy-start.16 = (bf16[8,320]{1,0:T(8,128)(2,1)S(1)}, bf16[8,320]{1,0:T(8,128)(2,1)}, u32[]{:S(2)}) copy-start(bf16[8,320]{1,0:T(8,128)(2,1)} %param.9) | copy-start | bytes 15364
  0.0 8.2 %collective-permute-start = (bf16[1,8,320]{2,1,0:T(8,128)(2,1)}, bf16[1,8,320]{2,1,0:T(8,128)(2,1)S(1)}, u32[]{:S(2)}, u32[]{:S(2)}) collective-permute-start(bf16[1,8,320]{2,1,0:T(8,128)(2,1)} %bitcast.104), channel_id=1, source_target_pairs={{0,1},{1,0},{2,3},{3,2},{4,5},{5,4},{6,7},{7,6},{8,9},{9,8},{10,11... | collective-permute-start | bytes 15368 | tf_op jit(solution)/shard_map/ppermute | solution.py:36
  5.4 1.3 copy-start.2
  6.7 27.5 %copy-start.20 = (s32[24]{0:T(128)S(1)}, s32[24]{0:T(128)}, u32[]{:S(2)}) copy-start(s32[24]{0:T(128)} %param.16) | copy-start | bytes 292
  7.4 32.2 %copy-start.1 = (s32[512]{0:T(512)S(1)}, s32[512]{0:T(512)}, u32[]{:S(2)}) copy-start(s32[512]{0:T(512)} %param.14) | copy-start | bytes 6148
  8.3 5.3 %collective-permute-start.1 = (bf16[2,8,320]{2,1,0:T(8,128)(2,1)S(1)}, bf16[2,8,320]{2,1,0:T(8,128)(2,1)S(1)}, u32[]{:S(2)}, u32[]{:S(2)}) collective-permute-start(bf16[2,8,320]{2,1,0:T(8,128)(2,1)S(1)} %maximum_select_fusion.8), channel_id=1, source_target_pairs={{0,2},{1,3},{2,0},{3,1},{4,6},{5,7},{6,4},{7,5},{8,10},{9,11},{10,... | collective-permute-start | bytes 30728 | tf_op jit(solution)/shard_map/ppermute | solution.py:36
  13.7 1.4 copy-start.11
  14.4 0.6 copy-start.13
  15.2 23.4 %copy-start.7 = (f32[8,5,64]{2,1,0:T(8,128)}, f32[8,5,64]{2,1,0:T(8,128)S(1)}, u32[]{:S(2)}) copy-start(f32[8,5,64]{2,1,0:T(8,128)S(1)} %reshape.501) | copy-start | bytes 30724
  15.4 1.3 collective-permute-start.2
  16.7 4.0 %collective-permute-start.3 = (bf16[2,8,5,64]{3,2,1,0:T(8,128)(2,1)S(1)}, bf16[2,8,5,64]{3,2,1,0:T(8,128)(2,1)S(1)}, u32[]{:S(2)}, u32[]{:S(2)}) collective-permute-start(bf16[2,8,5,64]{3,2,1,0:T(8,128)(2,1)S(1)} %maximum_select_fusion.5), channel_id=1, source_target_pairs={{0,8},{4,12},{8,0},{12,4},{16,24},{20,28},{24,16},{28,20},{32,40},... | collective-permute-start | bytes 30728 | tf_op jit(solution)/shard_map/ppermute | solution.py:36
  20.8 6.0 %collective-permute-start.4 = (bf16[4,8,5,64]{3,2,1,0:T(8,128)(2,1)S(1)}, bf16[4,8,5,64]{3,2,1,0:T(8,128)(2,1)S(1)}, u32[]{:S(2)}, u32[]{:S(2)}) collective-permute-start(bf16[4,8,5,64]{3,2,1,0:T(8,128)(2,1)S(1)} %bitcast.94), channel_id=1, source_target_pairs={{0,16},{4,20},{8,24},{12,28},{16,0},{20,4},{24,8},{28,12},{32,48},... | collective-permute-start | bytes 61448 | tf_op jit(solution)/shard_map/ppermute | solution.py:36
  26.8 11.7 %collective-permute-start.5 = (bf16[8,8,5,64]{3,2,1,0:T(8,128)(2,1)S(1)}, bf16[8,8,5,64]{3,2,1,0:T(8,128)(2,1)S(1)}, u32[]{:S(2)}, u32[]{:S(2)}) collective-permute-start(bf16[8,8,5,64]{3,2,1,0:T(8,128)(2,1)S(1)} %bitcast.91), channel_id=1, source_target_pairs={{0,32},{4,36},{8,40},{12,44},{16,48},{20,52},{24,56},{28,60},{32,0... | collective-permute-start | bytes 122888 | tf_op jit(solution)/shard_map/ppermute | solution.py:36
  38.6 9.3 %collective-permute-start.6 = (bf16[16,8,5,64]{3,2,1,0:T(8,128)(2,1)S(1)}, bf16[16,8,5,64]{3,2,1,0:T(8,128)(2,1)S(1)}, u32[]{:S(2)}, u32[]{:S(2)}) collective-permute-start(bf16[16,8,5,64]{3,2,1,0:T(8,128)(2,1)S(1)} %bitcast.87), channel_id=1, source_target_pairs={{0,64},{4,68},{8,72},{12,76},{16,80},{20,84},{24,88},{28,92},{32,9... | collective-permute-start | bytes 245768 | tf_op jit(solution)/shard_map/ppermute | solution.py:36
  48.1 10.8 %collective-permute-start.7 = (bf16[32,8,5,64]{3,2,1,0:T(8,128)(2,1)S(1)}, bf16[32,8,5,64]{3,2,1,0:T(8,128)(2,1)S(1)}, u32[]{:S(2)}, u32[]{:S(2)}) collective-permute-start(bf16[32,8,5,64]{3,2,1,0:T(8,128)(2,1)S(1)} %bitcast.83), channel_id=1, source_target_pairs={{0,128},{4,132},{8,136},{12,140},{16,144},{20,148},{24,152},{28,15... | collective-permute-start | bytes 491528 | tf_op jit(solution)/shard_map/ppermute | solution.py:36
  72.8 1.9 %collective-permute-start.8 = (f32[32,8,330]{2,1,0:T(8,128)}, f32[32,8,330]{2,1,0:T(8,128)S(1)}, u32[]{:S(2)}, u32[]{:S(2)}) collective-permute-start(f32[32,8,330]{2,1,0:T(8,128)} %get-tuple-element.37), channel_id=1, source_target_pairs={{0,4},{4,0},{8,12},{12,8},{16,20},{20,16},{24,28},{28,24},{32,36},... | collective-permute-start | bytes 1013768 | tf_op jit(solution)/shard_map/ppermute | solution.py:83
  74.8 2.1 %copy-start.3 = (f32[32,8,330]{2,1,0:T(8,128)}, f32[32,8,330]{2,1,0:T(8,128)S(1)}, u32[]{:S(2)}) copy-start(f32[32,8,330]{2,1,0:T(8,128)S(1)} %collective-permute-done.8) | copy-start | bytes 1013764
  82.9 7.2 %collective-permute-start.9 = (f32[16,8,330]{2,1,0:T(8,128)S(1)}, f32[16,8,330]{2,1,0:T(8,128)S(1)}, u32[]{:S(2)}, u32[]{:S(2)}) collective-permute-start(f32[16,8,330]{2,1,0:T(8,128)S(1)} %get-tuple-element.39), channel_id=1, source_target_pairs={{0,8},{4,12},{8,0},{12,4},{16,24},{20,28},{24,16},{28,20},{32,40},... | collective-permute-start | bytes 506888 | tf_op jit(solution)/shard_map/ppermute | solution.py:83
  90.1 0.7 copy-start.6
  94.2 7.8 %copy-start.5 = (f32[8,8,330]{2,1,0:T(8,128)}, f32[8,8,330]{2,1,0:T(8,128)S(1)}, u32[]{:S(2)}) copy-start(f32[8,8,330]{2,1,0:T(8,128)S(1)} %get-tuple-element.40) | copy-start | bytes 253444
  94.2 7.1 %collective-permute-start.10 = (f32[8,8,330]{2,1,0:T(8,128)S(1)}, f32[8,8,330]{2,1,0:T(8,128)S(1)}, u32[]{:S(2)}, u32[]{:S(2)}) collective-permute-start(f32[8,8,330]{2,1,0:T(8,128)S(1)} %get-tuple-element.41), channel_id=1, source_target_pairs={{0,16},{4,20},{8,24},{12,28},{16,0},{20,4},{24,8},{28,12},{32,48},... | collective-permute-start | bytes 253448 | tf_op jit(solution)/shard_map/ppermute | solution.py:83
  101.3 0.7 copy-start.10
  102.0 28.5 %copy-start.4 = (bf16[320,1280]{1,0:T(8,128)(2,1)S(1)}, bf16[320,1280]{1,0:T(8,128)(2,1)}, u32[]{:S(2)}) copy-start(bf16[320,1280]{1,0:T(8,128)(2,1)} %param.11) | copy-start | bytes 2457604
  104.5 20.3 %copy-start.8 = (f32[8,5,64]{2,1,0:T(8,128)S(1)}, f32[8,5,64]{2,1,0:T(8,128)}, u32[]{:S(2)}) copy-start(f32[8,5,64]{2,1,0:T(8,128)} %copy-done.7) | copy-start | bytes 30724
  104.5 20.3 %copy-start.9 = (f32[8,5,64]{2,1,0:T(8,128)S(1)}, f32[8,5,64]{2,1,0:T(8,128)}, u32[]{:S(2)}) copy-start(f32[8,5,64]{2,1,0:T(8,128)} %reshape.508) | copy-start | bytes 30724
  106.5 8.1 %collective-permute-start.11 = (f32[4,8,330]{2,1,0:T(8,128)S(1)}, f32[4,8,330]{2,1,0:T(8,128)S(1)}, u32[]{:S(2)}, u32[]{:S(2)}) collective-permute-start(f32[4,8,330]{2,1,0:T(8,128)S(1)} %get-tuple-element.43), channel_id=1, source_target_pairs={{0,32},{4,36},{8,40},{12,44},{16,48},{20,52},{24,56},{28,60},{32,0... | collective-permute-start | bytes 126728 | tf_op jit(solution)/shard_map/ppermute | solution.py:83
  114.6 0.7 copy-start.14
  116.8 24.3 %copy-start.12 = (bf16[8,1280]{1,0:T(8,128)(2,1)S(1)}, bf16[8,1280]{1,0:T(8,128)(2,1)}, u32[]{:S(2)}) copy-start(bf16[8,1280]{1,0:T(8,128)(2,1)} %copy-done.11) | copy-start | bytes 61444
  118.5 3.9 %collective-permute-start.12 = (f32[2,8,330]{2,1,0:T(8,128)S(1)}, f32[2,8,330]{2,1,0:T(8,128)S(1)}, u32[]{:S(2)}, u32[]{:S(2)}) collective-permute-start(f32[2,8,330]{2,1,0:T(8,128)S(1)} %get-tuple-element.47), channel_id=1, source_target_pairs={{0,64},{4,68},{8,72},{12,76},{16,80},{20,84},{24,88},{28,92},{32,9... | collective-permute-start | bytes 63368 | tf_op jit(solution)/shard_map/ppermute | solution.py:83
  118.8 22.3 %copy-start.17 = (f32[1280]{0:T(1024)S(1)}, f32[1280]{0:T(1024)}, u32[]{:S(2)}) copy-start(f32[1280]{0:T(1024)} %param.13) | copy-start | bytes 15364
  122.5 0.6 copy-start.15
  124.2 5.2 %collective-permute-start.13 = (f32[1,8,330]{2,1,0:T(8,128)S(1)}, f32[1,8,330]{2,1,0:T(8,128)S(1)}, u32[]{:S(2)}, u32[]{:S(2)}) collective-permute-start(f32[1,8,330]{2,1,0:T(8,128)S(1)} %constant_dynamic-slice_fusion.1), channel_id=1, source_target_pairs={{0,128},{4,132},{8,136},{12,140},{16,144},{20,148},{24,152},{28,15... | collective-permute-start | bytes 31688 | tf_op jit(solution)/shard_map/ppermute | solution.py:83
  131.5 4.1 %collective-permute-start.14 = (f32[8,1280]{1,0:T(8,128)S(1)}, f32[8,1280]{1,0:T(8,128)S(1)}, u32[]{:S(2)}, u32[]{:S(2)}) collective-permute-start(f32[8,1280]{1,0:T(8,128)S(1)} %fusion.28), channel_id=1, source_target_pairs={{0,1},{1,0},{2,3},{3,2},{4,5},{5,4},{6,7},{7,6},{8,9},{9,8},{10,11... | collective-permute-start | bytes 122888 | tf_op jit(solution)/shard_map/ppermute | solution.py:48
  135.5 5.5 %collective-permute-start.15 = (f32[8,1280]{1,0:T(8,128)S(1)}, f32[8,1280]{1,0:T(8,128)S(1)}, u32[]{:S(2)}, u32[]{:S(2)}) collective-permute-start(f32[8,1280]{1,0:T(8,128)S(1)} %add.203), channel_id=1, source_target_pairs={{0,2},{1,3},{2,0},{3,1},{4,6},{5,7},{6,4},{7,5},{8,10},{9,11},{10,... | collective-permute-start | bytes 122888 | tf_op jit(solution)/shard_map/ppermute | solution.py:48

commit v3 on v2

--- a/solution.py
+++ b/solution.py
@@ -27,63 +27,68 @@
     return [(i, i ^ bit) for i in range(size)]
 
 
-def gather_doubling(value, axis):
+def digit_groups(size):
+    groups = []
+    while size > 1:
+        width = 2 if size % 4 == 0 else 1
+        groups.append(width)
+        size >>= width
+    return groups
+
+
+def exchange(held, axis, low, width):
     size = lax.axis_size(axis)
-    index = lax.axis_index(axis)
+    mine = (lax.axis_index(axis) >> low) & ((1 << width) - 1)
+    got = [held] + [
+        lax.ppermute(held, axis, perm=xor_partner(axis, size, digit << low))
+        for digit in range(1, 1 << width)
+    ]
+    order = jnp.arange(1 << width, dtype=jnp.int32) ^ mine
+    return jnp.take(jnp.stack(got), order, axis=0)
+
+
+def gather_radix(value, axis):
     held = value[None]
-    bit = 1
-    while bit < size:
-        other = lax.ppermute(held, axis, perm=xor_partner(axis, size, bit))
-        high = (index & bit) != 0
-        held = jnp.where(high, jnp.stack([other, held]), jnp.stack([held, other]))
-        held = held.reshape((-1,) + value.shape)
-        bit *= 2
+    low = 0
+    for width in digit_groups(lax.axis_size(axis)):
+        held = exchange(held, axis, low, width).reshape((-1,) + value.shape)
+        low += width
     return held
 
 
-def sum_doubling(value, axis):
-    size = lax.axis_size(axis)
-    bit = 1
-    while bit < size:
-        value = value + lax.ppermute(value, axis, perm=xor_partner(axis, size, bit))
-        bit *= 2
+def sum_radix(value, axis):
+    low = 0
+    for width in digit_groups(lax.axis_size(axis)):
+        stacked = exchange(value, axis, low, width)
+        value = stacked[0]
+        for digit in range(1, stacked.shape[0]):
+            value = value + stacked[digit]
+        low += width
     return value
 
 
-def merge_packed(first, second, width, heads):
-    first_acc, first_total, first_max = (
-        first[..., :width], first[..., width : width + heads], first[..., width + heads :]
-    )
-    second_acc, second_total, second_max = (
-        second[..., :width], second[..., width : width + heads], second[..., width + heads :]
-    )
-    top = jnp.maximum(first_max, second_max)
-    first_factor = jnp.exp(first_max - top)
-    second_factor = jnp.exp(second_max - top)
-    return jnp.concatenate(
-        [
-            scale_heads(first_acc, first_factor) + scale_heads(second_acc, second_factor),
-            first_total * first_factor + second_total * second_factor,
-            top,
-        ],
-        axis=-1,
-    )
-
-
-def scatter_halving(packed, axis, width, heads):
+def scatter_radix(packed, axis, width_acc, heads):
     size = lax.axis_size(axis)
     index = lax.axis_index(axis)
-    bit = 1
-    step = 0
-    while bit < size:
-        paired = packed.reshape((packed.shape[0] // 2, 2) + packed.shape[1:])
-        mine = (index >> step) & 1
-        keep = lax.dynamic_index_in_dim(paired, mine, 1, False)
-        send = lax.dynamic_index_in_dim(paired, 1 - mine, 1, False)
-        other = lax.ppermute(send, axis, perm=xor_partner(axis, size, bit))
-        packed = merge_packed(keep, other, width, heads)
-        bit *= 2
-        step += 1
+    low = 0
+    for width in digit_groups(size):
+        count = 1 << width
+        mine = (index >> low) & (count - 1)
+        grouped = packed.reshape((packed.shape[0] // count, count) + packed.shape[1:])
+        pieces = [lax.dynamic_index_in_dim(grouped, mine, 1, False)]
+        for digit in range(1, count):
+            send = lax.dynamic_index_in_dim(grouped, mine ^ digit, 1, False)
+            pieces.append(lax.ppermute(send, axis, perm=xor_partner(axis, size, digit << low)))
+        stacked = jnp.stack(pieces)
+        acc = stacked[..., :width_acc]
+        total = stacked[..., width_acc : width_acc + heads]
+        top_each = stacked[..., width_acc + heads :]
+        top = jnp.max(top_each, axis=0)
+        factor = jnp.exp(top_each - top[None])
+        acc = jnp.sum(scale_heads(acc, factor), axis=0)
+        total = jnp.sum(total * factor, axis=0)
+        packed = jnp.concatenate([acc, total, top], axis=-1)
+        low += width
     return packed[0]
 
 
@@ -100,7 +105,7 @@
 ):
     rows, width_local = hidden.shape
     heads_local = width_local // HEAD_DIM
-    gathered = jnp.moveaxis(gather_doubling(hidden, "tensor"), 0, 1).reshape(rows, -1)
+    gathered = jnp.moveaxis(gather_radix(hidden, "tensor"), 0, 1).reshape(rows, -1)
     projected = jnp.dot(
         gathered,
         inward_weight.reshape(inward_weight.shape[0], -1),
@@ -118,7 +123,7 @@
         axis=-1,
     ) / math.sqrt(HEAD_DIM)
 
-    all_queries = gather_doubling(query, "seq").reshape(-1, width_local)
+    all_queries = gather_radix(query, "seq").reshape(-1, width_local)
     pages, page_len = (page_cache.shape[0], page_cache.shape[1])
     owner_query = all_queries[page_request].reshape(pages, heads_local, HEAD_DIM)
     keys_scaled = head_norm(page_cache[:, :, 0, :].astype(jnp.float32), score_gain).astype(
@@ -150,7 +155,7 @@
     )
     packed = jnp.concatenate([request_acc, request_total, request_max], axis=1)
     packed = packed.reshape(lax.axis_size("seq"), rows, packed.shape[-1])
-    home = scatter_halving(packed, "seq", width_local, heads_local)
+    home = scatter_radix(packed, "seq", width_local, heads_local)
     home_acc = home[:, :width_local]
     home_total = home[:, width_local : width_local + heads_local]
     home_max = home[:, width_local + heads_local :]
@@ -167,7 +172,7 @@
         .astype(jnp.bfloat16)
     )
     partial_out = jnp.dot(attended, output_weight, preferred_element_type=jnp.float32)
-    attn_out = sum_doubling(partial_out, "tensor")
+    attn_out = sum_radix(partial_out, "tensor")
     width = attn_out.shape[1]
     state = gathered.astype(jnp.float32)
     unit = attn_out / jnp.sqrt(jnp.sum(attn_out * attn_out, axis=-1, keepdims=True) / width + epsilon)

time: 143 us -> 126 us (0.88)
  waiting for transfers between devices: 62.3 us -> 40.5 us
  starting transfers between devices: 28 us -> 35.7 us
  other arithmetic: 19.8 us -> 15.6 us
    ppermute x16 -> x24, waiting for transfers between devices: 62.3 us -> 40.5 us  [the longest x15 24 us: exchange(): lax.ppermute(held, axis, perm=xor_partner(axis, size, digit << low))]
    add x12 -> x0, other arithmetic: 9.49 us -> none  [the longest x6 5.18 us: merge_packed(): scale_heads(first_acc, first_factor)]
    ppermute x16 -> x24, starting transfers between devices: 28 us -> 35.7 us  [the longest x15 22.9 us: exchange(): lax.ppermute(held, axis, perm=xor_partner(axis, size, digit << low))]
    gather x0 -> x6, local copies, waits for them, and re-layouts: none -> 5.95 us  [exchange(): return jnp.take(jnp.stack(got), order, axis=0)]
    mul x28 -> x10, local copies, waits for them, and re-layouts: 9.74 us -> 5.28 us  [scale_heads(): return (shaped * factor[..., None]).reshape(summed.shape)]
    concatenate x5 -> x2, other arithmetic: 3.79 us -> 0.9 us  [scatter_radix(): packed = jnp.concatenate([acc, total, top], axis=-1)]
    reduce_sum x0 -> x5, other arithmetic: none -> 2.18 us  [the longest x3 1.27 us: scatter_radix(): acc = jnp.sum(scale_heads(acc, factor), axis=0)]
    another operation x1 -> x8, other arithmetic: 0.08 us -> 1.67 us  [the longest x3 1.19 us: scatter_radix(): stacked = jnp.stack(pieces)]
  transfers between devices with their start and end apart: 16 -> 24, of which waited for: 15 -> 14; matrix products, arithmetic and copies ran while one was open for 6% -> 9% of each run, Pallas kernels for 0% -> 0%
where the time goes in v3:
time: 126 us; the launch traced here: 125 us
  waiting for transfers between devices  40.5 us (32%)
  starting transfers between devices  35.7 us (28%)
  local copies, waits for them, and re-layouts  24.7 us (20%)
  other arithmetic  15.6 us (12%)
  matrix products  7.73 us (6%)
    ppermute x15, waiting for transfers between devices, exchange(): lax.ppermute(held, axis, perm=xor_partner(axis, size, digit << low))  24 us
    ppermute x15, starting transfers between devices, exchange(): lax.ppermute(held, axis, perm=xor_partner(axis, size, digit << low))  22.9 us
    ppermute x9, waiting for transfers between devices, scatter_radix(): lax.ppermute(send, axis, perm=xor_partner(axis, size, digit << low))  16.6 us
    ppermute x9, starting transfers between devices, scatter_radix(): lax.ppermute(send, axis, perm=xor_partner(axis, size, digit << low))  12.8 us
    gather x6, local copies, waits for them, and re-layouts, exchange(): return jnp.take(jnp.stack(got), order, axis=0)  5.95 us
    mul x10, local copies, waits for them, and re-layouts, scale_heads(): return (shaped * factor[..., None]).reshape(summed.shape)  5.28 us
    slice x1, local copies, waits for them, and re-layouts, local(): page_cache[:, :, 1, :].reshape(pages, page_len, heads_local, HEAD_DIM)  3.69 us
    unnamed x40, local copies, waits for them, and re-layouts  2.66 us
  transfers between devices with their start and end apart: 24, of which 14 were waited for; matrix products, arithmetic and copies ran while one was open for 9% of the time, Pallas kernels for 0%

profile of v3, /device:TPU:6, one launch (start us, length us, event | category | flops | bytes accessed | tf_op | source)
XLA Modules:
  0.0 124.7 jit_solution(12377668714008188212)
XLA Ops:
  0.0 3.0 %collective-permute-start.2 = (bf16[1,8,320]{2,1,0:T(8,128)(2,1)}, bf16[1,8,320]{2,1,0:T(8,128)(2,1)S(1)}, u32[]{:S(2)}, u32[]{:S(2)}) collective-permute-start(bf16[1,8,320]{2,1,0:T(8,128)(2,1)} %bitcast.140), channel_id=1, source_target_pairs={{0,3},{1,2},{2,1},{3,0},{4,7},{5,6},{6,5},{7,4},{8,11},{9,10},{10,... | collective-permute-start | bytes 15368 | tf_op jit(solution)/shard_map/ppermute | solution.py:43
  4.8 1.3 %iota_compare_fusion = pred[24,512]{1,0:T(8,128)(4,1)} fusion(s32[24]{0:T(128)} %param.15), kind=kLoop, calls=%fused_computation.67 | loop fusion | flops 12288 | bytes 12384 | tf_op jit(solution)/shard_map/eq | solution.py:148
  7.4 3.7 %fusion.40 = (bf16[24,128,1,320]{1,3,2,0:T(8,128)(2,1)}, bf16[24,128,1,320]{1,3,2,0:T(8,128)(2,1)S(1)}) fusion(bf16[24,128,2,320]{1,3,2,0:T(8,128)(2,1)} %param.17), kind=kLoop, calls=%fused_computation.144 | loop fusion | bytes 7864320 | tf_op jit(solution)/shard_map/slice | solution.py:132
  11.1 1.2 copy-done.2
  12.4 0.7 fusion
  13.8 0.7 gather_fusion.1
  17.0 0.7 fusion.42
  18.9 0.8 collective-permute-start.5
  19.6 1.4 %collective-permute-start.4 = (bf16[1,8,5,64]{3,2,1,0:T(8,128)(2,1)S(1)}, bf16[1,8,5,64]{3,2,1,0:T(8,128)(2,1)S(1)}, u32[]{:S(2)}, u32[]{:S(2)}) collective-permute-start(bf16[1,8,5,64]{3,2,1,0:T(8,128)(2,1)S(1)} %multiply_convert_fusion.2), channel_id=1, source_target_pairs={{0,8},{4,12},{8,0},{12,4},{16,24},{20,28},{24,16},{28,20},{32,40},... | collective-permute-start | bytes 15368 | tf_op jit(solution)/shard_map/ppermute | solution.py:43
  21.1 1.0 collective-permute-done.5
  22.1 1.2 collective-permute-done.4
  24.0 5.9 %collective-permute-start.8 = (bf16[4,8,5,64]{3,2,1,0:T(8,128)(2,1)S(1)}, bf16[4,8,5,64]{3,2,1,0:T(8,128)(2,1)S(1)}, u32[]{:S(2)}, u32[]{:S(2)}) collective-permute-start(bf16[4,8,5,64]{3,2,1,0:T(8,128)(2,1)S(1)} %broadcast_select_fusion.2), channel_id=1, source_target_pairs={{0,48},{4,52},{8,56},{12,60},{16,32},{20,36},{24,40},{28,44},{32,1... | collective-permute-start | bytes 61448 | tf_op jit(solution)/shard_map/ppermute | solution.py:43
  29.9 1.0 collective-permute-start.7
  30.9 1.5 %collective-permute-start.6 = (bf16[4,8,5,64]{3,2,1,0:T(8,128)(2,1)S(1)}, bf16[4,8,5,64]{3,2,1,0:T(8,128)(2,1)S(1)}, u32[]{:S(2)}, u32[]{:S(2)}) collective-permute-start(bf16[4,8,5,64]{3,2,1,0:T(8,128)(2,1)S(1)} %broadcast_select_fusion.2), channel_id=1, source_target_pairs={{0,16},{4,20},{8,24},{12,28},{16,0},{20,4},{24,8},{28,12},{32,48},... | collective-permute-start | bytes 61448 | tf_op jit(solution)/shard_map/ppermute | solution.py:43
  32.5 3.3 %collective-permute-done.8 = bf16[4,8,5,64]{3,2,1,0:T(8,128)(2,1)S(1)} collective-permute-done((bf16[4,8,5,64]{3,2,1,0:T(8,128)(2,1)S(1)}, bf16[4,8,5,64]{3,2,1,0:T(8,128)(2,1)S(1)}, u32[]{:S(2)}, u32[]{:S(2)}) %collective-permute-start.8) | collective-permute-done | bytes 20512 | tf_op jit(solution)/shard_map/ppermute | solution.py:43
  35.8 4.7 %collective-permute-done.7 = bf16[4,8,5,64]{3,2,1,0:T(8,128)(2,1)S(1)} collective-permute-done((bf16[4,8,5,64]{3,2,1,0:T(8,128)(2,1)S(1)}, bf16[4,8,5,64]{3,2,1,0:T(8,128)(2,1)S(1)}, u32[]{:S(2)}, u32[]{:S(2)}) %collective-permute-start.7) | collective-permute-done | bytes 20512 | tf_op jit(solution)/shard_map/ppermute | solution.py:43
  41.9 2.4 %collective-permute-start.10 = (bf16[16,8,5,64]{3,2,1,0:T(8,128)(2,1)S(1)}, bf16[16,8,5,64]{3,2,1,0:T(8,128)(2,1)S(1)}, u32[]{:S(2)}, u32[]{:S(2)}) collective-permute-start(bf16[16,8,5,64]{3,2,1,0:T(8,128)(2,1)S(1)} %bitcast_select_fusion), channel_id=1, source_target_pairs={{0,128},{4,132},{8,136},{12,140},{16,144},{20,148},{24,152},{28,15... | collective-permute-start | bytes 245768 | tf_op jit(solution)/shard_map/ppermute | solution.py:43
  44.3 1.2 collective-permute-start.9
  45.6 8.8 %collective-permute-done.11 = bf16[16,8,5,64]{3,2,1,0:T(8,128)(2,1)S(1)} collective-permute-done((bf16[16,8,5,64]{3,2,1,0:T(8,128)(2,1)S(1)}, bf16[16,8,5,64]{3,2,1,0:T(8,128)(2,1)S(1)}, u32[]{:S(2)}, u32[]{:S(2)}) %collective-permute-start.11) | collective-permute-done | bytes 81952 | tf_op jit(solution)/shard_map/ppermute | solution.py:43
  55.3 1.8 %gather_fusion.4 = bf16[4,16,8,5,64]{4,3,2,1,0:T(8,128)(2,1)} fusion(bf16[4,16,8,5,64]{4,3,2,1,0:T(8,128)(2,1)S(1)} %pad_maximum_fusion, s32[1024]{0:T(1024)} %pad_clamp_fusion), kind=kCustom, calls=%fused_computation.4 | custom fusion | bytes 655376 | tf_op jit(solution)/shard_map/jit(_take)/gather | solution.py:47
  57.1 1.8 %gather.51 = bf16[512,320]{1,0:T(8,128)(2,1)S(1)} reshape(bf16[4,16,8,5,64]{4,3,2,1,0:T(8,128)(2,1)} %gather_fusion.4) | data formatting | bytes 655360 | tf_op jit(solution)/shard_map/jit(_take)/gather | solution.py:47
  58.9 0.8 broadcast_select_fusion
  60.4 2.3 %fusion.3 = f32[24,5,1,128]{3,2,1,0:T(1,128)S(1)} fusion(bf16[24,5,64,1]{2,3,1,0:T(2,128)(2,1)S(1)} %reshape.438, bf16[24,128,5,64]{1,3,2,0:T(8,128)(2,1)} %bitcast.109, f32[5,64]{1,0:T(8,128)S(1)} %mul.176, f32[24,128,5]{1,2,0:T(8,128)S(1)} %copy-done.10), kind=kOutput, calls=%fused_computation.13 | convolution fusion | flops 5898240 | bytes 2105600 | tf_op jit(solution)/shard_map/sphd,shd->shp/dot_general | solution.py:133
  63.9 2.6 %fusion.9 = f32[24,5,1,64]{3,2,1,0:T(1,128)S(1)} fusion(bf16[24,128,5,64]{1,3,2,0:T(8,128)(2,1)} %bitcast.112, bf16[24,5,128,1]{2,0,1,3:T(8,128)(2,1)S(1)} %get-tuple-element.24), kind=kOutput, calls=%fused_computation.48 | convolution fusion | flops 1966080 | bytes 2027520 | tf_op jit(solution)/shard_map/shp,sphd->shd/dot_general | solution.py:143
  67.5 0.9 pad_maximum_fusion.2
  68.4 1.4 %copy.30 = f32[512,330]{1,0:T(8,128)S(1)} copy(f32[512,330]{0,1:T(8,128)} %pad_maximum_fusion.2) | data formatting | bytes 1351680 | tf_op jit(solution)/shard_map/concatenate | solution.py:156
  69.8 0.9 dynamic-slice_bitcast_fusion.3
  71.2 1.3 %collective-permute-start.12 = (f32[16,8,330]{2,1,0:T(8,128)}, f32[16,8,330]{2,1,0:T(8,128)S(1)}, u32[]{:S(2)}, u32[]{:S(2)}) collective-permute-start(f32[16,8,330]{2,1,0:T(8,128)} %get-tuple-element.19), channel_id=1, source_target_pairs={{0,4},{4,0},{8,12},{12,8},{16,20},{20,16},{24,28},{28,24},{32,36},... | collective-permute-start | bytes 506888 | tf_op jit(solution)/shard_map/ppermute | solution.py:81
  72.7 5.4 %collective-permute-done.14 = f32[16,8,330]{2,1,0:T(8,128)S(1)} collective-permute-done((f32[16,8,330]{2,1,0:T(8,128)}, f32[16,8,330]{2,1,0:T(8,128)S(1)}, u32[]{:S(2)}, u32[]{:S(2)}) %collective-permute-start.14) | collective-permute-done | bytes 168992 | tf_op jit(solution)/shard_map/ppermute | solution.py:81
  78.1 2.4 %collective-permute-done.13 = f32[16,8,330]{2,1,0:T(8,128)S(1)} collective-permute-done((f32[16,8,330]{2,1,0:T(8,128)}, f32[16,8,330]{2,1,0:T(8,128)S(1)}, u32[]{:S(2)}, u32[]{:S(2)}) %collective-permute-start.13) | collective-permute-done | bytes 168992 | tf_op jit(solution)/shard_map/ppermute | solution.py:81
  81.2 1.2 pad_maximum_fusion.1
  82.7 1.9 %mul.187 = f32[4,16,8,5,64]{4,3,2,1,0:T(8,128)} broadcast(f32[4,16,8,5]{3,2,1,0:T(8,128)S(1)} %get-tuple-element.13), dimensions={0,1,2,3} | broadcast | bytes 665600 | tf_op jit(solution)/shard_map/mul | solution.py:23
  84.6 2.6 %mul.188 = f32[4,16,8,320]{3,2,1,0:T(8,128)} reshape(f32[4,16,8,5,64]{4,3,2,1,0:T(8,128)} %mul.187) | data formatting | bytes 1310720 | tf_op jit(solution)/shard_map/mul | solution.py:23
  87.2 1.2 fusion.5
  88.6 4.3 %collective-permute-start.17 = (f32[4,8,330]{2,1,0:T(8,128)S(1)}, f32[4,8,330]{2,1,0:T(8,128)S(1)}, u32[]{:S(2)}, u32[]{:S(2)}) collective-permute-start(f32[4,8,330]{2,1,0:T(8,128)S(1)} %get-tuple-element.21), channel_id=1, source_target_pairs={{0,48},{4,52},{8,56},{12,60},{16,32},{20,36},{24,40},{28,44},{32,1... | collective-permute-start | bytes 126728 | tf_op jit(solution)/shard_map/ppermute | solution.py:81
  92.9 1.5 %collective-permute-start.16 = (f32[4,8,330]{2,1,0:T(8,128)S(1)}, f32[4,8,330]{2,1,0:T(8,128)S(1)}, u32[]{:S(2)}, u32[]{:S(2)}) collective-permute-start(f32[4,8,330]{2,1,0:T(8,128)S(1)} %get-tuple-element.22), channel_id=1, source_target_pairs={{0,32},{4,36},{8,40},{12,44},{16,48},{20,52},{24,56},{28,60},{32,0... | collective-permute-start | bytes 126728 | tf_op jit(solution)/shard_map/ppermute | solution.py:81
  94.4 1.0 collective-permute-start.15
  95.4 6.7 %collective-permute-done.16 = f32[4,8,330]{2,1,0:T(8,128)S(1)} collective-permute-done((f32[4,8,330]{2,1,0:T(8,128)S(1)}, f32[4,8,330]{2,1,0:T(8,128)S(1)}, u32[]{:S(2)}, u32[]{:S(2)}) %collective-permute-start.16) | collective-permute-done | bytes 42272 | tf_op jit(solution)/shard_map/ppermute | solution.py:81
  102.2 0.7 fusion.8
  103.2 0.8 pad_maximum_fusion.7
  104.4 2.4 %collective-permute-start.19 = (f32[1,8,330]{2,1,0:T(8,128)S(1)}, f32[1,8,330]{2,1,0:T(8,128)S(1)}, u32[]{:S(2)}, u32[]{:S(2)}) collective-permute-start(f32[1,8,330]{2,1,0:T(8,128)S(1)} %get-tuple-element.30), channel_id=1, source_target_pairs={{0,128},{4,132},{8,136},{12,140},{16,144},{20,148},{24,152},{28,15... | collective-permute-start | bytes 31688 | tf_op jit(solution)/shard_map/ppermute | solution.py:81
  106.8 1.4 %collective-permute-start.18 = (f32[1,8,330]{2,1,0:T(8,128)S(1)}, f32[1,8,330]{2,1,0:T(8,128)S(1)}, u32[]{:S(2)}, u32[]{:S(2)}) collective-permute-start(f32[1,8,330]{2,1,0:T(8,128)S(1)} %get-tuple-element.31), channel_id=1, source_target_pairs={{0,64},{4,68},{8,72},{12,76},{16,80},{20,84},{24,88},{28,92},{32,9... | collective-permute-start | bytes 31688 | tf_op jit(solution)/shard_map/ppermute | solution.py:81
  109.6 0.9 collective-permute-done.18
  111.5 1.4 %fusion.28 = f32[8,1280]{1,0:T(8,128)S(1)} fusion(bf16[320,1280]{1,0:T(8,128)(2,1)} %param.11, f32[8,320]{1,0:T(8,128)S(1)} %div.127, f32[8,320]{1,0:T(8,128)S(1)} %mul.209, f32[8,320]{1,0:T(8,128)S(1)} %mul.206, f32[8,330]{1,0:T(8,128)S(1)} %maximum_bitcast_fusion.2, f32[8,960]{1,0:T(8,128)} %copy-done.8), kind=kOutput, calls=%fused_computation.106 | convolution fusion | flops 6568960 | bytes 907584 | tf_op jit(solution)/shard_map/dot_general | solution.py:174
  112.9 3.1 %collective-permute-start.23 = (f32[8,1280]{1,0:T(8,128)S(1)}, f32[8,1280]{1,0:T(8,128)S(1)}, u32[]{:S(2)}, u32[]{:S(2)}) collective-permute-start(f32[8,1280]{1,0:T(8,128)S(1)} %fusion.28), channel_id=1, source_target_pairs={{0,3},{1,2},{2,1},{3,0},{4,7},{5,6},{6,5},{7,4},{8,11},{9,10},{10,... | collective-permute-start | bytes 122888 | tf_op jit(solution)/shard_map/ppermute | solution.py:43
  117.2 1.4 %collective-permute-done.23 = f32[8,1280]{1,0:T(8,128)S(1)} collective-permute-done((f32[8,1280]{1,0:T(8,128)S(1)}, f32[8,1280]{1,0:T(8,128)S(1)}, u32[]{:S(2)}, u32[]{:S(2)}) %collective-permute-start.23) | collective-permute-done | bytes 40992 | tf_op jit(solution)/shard_map/ppermute | solution.py:43
  118.6 2.9 %collective-permute-done.22 = f32[8,1280]{1,0:T(8,128)S(1)} collective-permute-done((f32[8,1280]{1,0:T(8,128)S(1)}, f32[8,1280]{1,0:T(8,128)S(1)}, u32[]{:S(2)}, u32[]{:S(2)}) %collective-permute-start.22) | collective-permute-done | bytes 40992 | tf_op jit(solution)/shard_map/ppermute | solution.py:43
  123.3 1.4 %fusion.27 = bf16[8,320]{1,0:T(8,128)(2,1)} fusion(f32[8,1280]{1,0:T(8,128)S(1)} %bitcast.117, s32[]{:T(128)S(6)} %select_n.198, f32[8]{0:T(128)S(1)} %add_sqrt_fusion.3, f32[320]{0:T(512)S(1)} %dynamic-slice.7, f32[8]{0:T(128)S(1)} %add_sqrt_fusion.4, bf16[8,1280]{1,0:T(8,128)(2,1)} %copy-done.9), kind=kLoop, calls=%fused_computation.105 | loop fusion | flops 17920 | bytes 21828 | tf_op jit(solution)/shard_map/convert_element_type | solution.py:182
  (155 shorter events, 21.5 us)
Async XLA Ops:
  0.0 16.4 %copy-start = (bf16[1280,3,320]{0,2,1:T(8,128)(2,1)S(1)}, bf16[1280,3,320]{0,2,1:T(8,128)(2,1)}, u32[]{:S(2)}) copy-start(bf16[1280,3,320]{0,2,1:T(8,128)(2,1)} %param.10) | copy-start | bytes 7372804
  0.0 15.6 %collective-permute-start.2 = (bf16[1,8,320]{2,1,0:T(8,128)(2,1)}, bf16[1,8,320]{2,1,0:T(8,128)(2,1)S(1)}, u32[]{:S(2)}, u32[]{:S(2)}) collective-permute-start(bf16[1,8,320]{2,1,0:T(8,128)(2,1)} %bitcast.140), channel_id=1, source_target_pairs={{0,3},{1,2},{2,1},{3,0},{4,7},{5,6},{6,5},{7,4},{8,11},{9,10},{10,... | collective-permute-start | bytes 15368 | tf_op jit(solution)/shard_map/ppermute | solution.py:43
  3.0 12.6 %collective-permute-start.1 = (bf16[1,8,320]{2,1,0:T(8,128)(2,1)}, bf16[1,8,320]{2,1,0:T(8,128)(2,1)S(1)}, u32[]{:S(2)}, u32[]{:S(2)}) collective-permute-start(bf16[1,8,320]{2,1,0:T(8,128)(2,1)} %bitcast.141), channel_id=1, source_target_pairs={{0,2},{1,3},{2,0},{3,1},{4,6},{5,7},{6,4},{7,5},{8,10},{9,11},{10,... | collective-permute-start | bytes 15368 | tf_op jit(solution)/shard_map/ppermute | solution.py:43
  3.6 11.9 %collective-permute-start = (bf16[1,8,320]{2,1,0:T(8,128)(2,1)}, bf16[1,8,320]{2,1,0:T(8,128)(2,1)S(1)}, u32[]{:S(2)}, u32[]{:S(2)}) collective-permute-start(bf16[1,8,320]{2,1,0:T(8,128)(2,1)} %bitcast.142), channel_id=1, source_target_pairs={{0,1},{1,0},{2,3},{3,2},{4,5},{5,4},{6,7},{7,6},{8,9},{9,8},{10,11... | collective-permute-start | bytes 15368 | tf_op jit(solution)/shard_map/ppermute | solution.py:43
  6.8 8.8 %copy-start.16 = (s32[1024]{0:T(1024)}, s32[1024]{0:T(1024)S(1)}, u32[]{:S(2)}) copy-start(s32[1024]{0:T(1024)S(1)} %pad_clamp_fusion.4) | copy-start | bytes 12292
  11.1 1.3 %copy-start.2 = (bf16[24,128,1,320]{1,3,2,0:T(8,128)(2,1)}, bf16[24,128,1,320]{1,3,2,0:T(8,128)(2,1)S(1)}, u32[]{:S(2)}) copy-start(bf16[24,128,1,320]{1,3,2,0:T(8,128)(2,1)S(1)} %get-tuple-element.15) | copy-start | bytes 5898244
  11.1 2.7 %copy-start.1 = (s32[512]{0:T(512)S(1)}, s32[512]{0:T(512)}, u32[]{:S(2)}) copy-start(s32[512]{0:T(512)} %param.14) | copy-start | bytes 6148
  11.1 3.7 %copy-start.19 = (f32[320]{0:T(512)S(1)}, f32[320]{0:T(512)}, u32[]{:S(2)}) copy-start(f32[320]{0:T(512)} %param.12) | copy-start | bytes 3844
  11.1 4.5 %copy-start.17 = (bf16[8,320]{1,0:T(8,128)(2,1)S(1)}, bf16[8,320]{1,0:T(8,128)(2,1)}, u32[]{:S(2)}) copy-start(bf16[8,320]{1,0:T(8,128)(2,1)} %param.9) | copy-start | bytes 15364
  14.6 4.1 %copy-start.14 = (pred[4]{0:T(512)(128)(4,1)}, pred[4]{0:T(512)(128)(4,1)S(1)}, u32[]{:S(2)}) copy-start(pred[4]{0:T(512)(128)(4,1)S(1)} %get-tuple-element.35) | copy-start | bytes 16
  16.2 7.2 %copy-start.3 = (bf16[4,8,320]{2,1,0:T(8,128)(2,1)}, bf16[4,8,320]{2,1,0:T(8,128)(2,1)S(1)}, u32[]{:S(2)}) copy-start(bf16[4,8,320]{2,1,0:T(8,128)(2,1)S(1)} %gather_fusion) | copy-start | bytes 61444
  16.4 0.6 copy-start.9
  17.7 0.7 copy-start.8
  18.9 3.3 %collective-permute-start.5 = (bf16[1,8,5,64]{3,2,1,0:T(8,128)(2,1)S(1)}, bf16[1,8,5,64]{3,2,1,0:T(8,128)(2,1)S(1)}, u32[]{:S(2)}, u32[]{:S(2)}) collective-permute-start(bf16[1,8,5,64]{3,2,1,0:T(8,128)(2,1)S(1)} %multiply_convert_fusion.2), channel_id=1, source_target_pairs={{0,12},{4,8},{8,4},{12,0},{16,28},{20,24},{24,20},{28,16},{32,44},... | collective-permute-start | bytes 15368 | tf_op jit(solution)/shard_map/ppermute | solution.py:43
  19.6 3.7 %collective-permute-start.4 = (bf16[1,8,5,64]{3,2,1,0:T(8,128)(2,1)S(1)}, bf16[1,8,5,64]{3,2,1,0:T(8,128)(2,1)S(1)}, u32[]{:S(2)}, u32[]{:S(2)}) collective-permute-start(bf16[1,8,5,64]{3,2,1,0:T(8,128)(2,1)S(1)} %multiply_convert_fusion.2), channel_id=1, source_target_pairs={{0,8},{4,12},{8,0},{12,4},{16,24},{20,28},{24,16},{28,20},{32,40},... | collective-permute-start | bytes 15368 | tf_op jit(solution)/shard_map/ppermute | solution.py:43
  21.0 2.4 %collective-permute-start.3 = (bf16[1,8,5,64]{3,2,1,0:T(8,128)(2,1)S(1)}, bf16[1,8,5,64]{3,2,1,0:T(8,128)(2,1)S(1)}, u32[]{:S(2)}, u32[]{:S(2)}) collective-permute-start(bf16[1,8,5,64]{3,2,1,0:T(8,128)(2,1)S(1)} %multiply_convert_fusion.2), channel_id=1, source_target_pairs={{0,4},{4,0},{8,12},{12,8},{16,20},{20,16},{24,28},{28,24},{32,36},... | collective-permute-start | bytes 15368 | tf_op jit(solution)/shard_map/ppermute | solution.py:43
  24.0 11.8 %collective-permute-start.8 = (bf16[4,8,5,64]{3,2,1,0:T(8,128)(2,1)S(1)}, bf16[4,8,5,64]{3,2,1,0:T(8,128)(2,1)S(1)}, u32[]{:S(2)}, u32[]{:S(2)}) collective-permute-start(bf16[4,8,5,64]{3,2,1,0:T(8,128)(2,1)S(1)} %broadcast_select_fusion.2), channel_id=1, source_target_pairs={{0,48},{4,52},{8,56},{12,60},{16,32},{20,36},{24,40},{28,44},{32,1... | collective-permute-start | bytes 61448 | tf_op jit(solution)/shard_map/ppermute | solution.py:43
  29.9 10.6 %collective-permute-start.7 = (bf16[4,8,5,64]{3,2,1,0:T(8,128)(2,1)S(1)}, bf16[4,8,5,64]{3,2,1,0:T(8,128)(2,1)S(1)}, u32[]{:S(2)}, u32[]{:S(2)}) collective-permute-start(bf16[4,8,5,64]{3,2,1,0:T(8,128)(2,1)S(1)} %broadcast_select_fusion.2), channel_id=1, source_target_pairs={{0,32},{4,36},{8,40},{12,44},{16,48},{20,52},{24,56},{28,60},{32,0... | collective-permute-start | bytes 61448 | tf_op jit(solution)/shard_map/ppermute | solution.py:43
  30.9 9.6 %collective-permute-start.6 = (bf16[4,8,5,64]{3,2,1,0:T(8,128)(2,1)S(1)}, bf16[4,8,5,64]{3,2,1,0:T(8,128)(2,1)S(1)}, u32[]{:S(2)}, u32[]{:S(2)}) collective-permute-start(bf16[4,8,5,64]{3,2,1,0:T(8,128)(2,1)S(1)} %broadcast_select_fusion.2), channel_id=1, source_target_pairs={{0,16},{4,20},{8,24},{12,28},{16,0},{20,4},{24,8},{28,12},{32,48},... | collective-permute-start | bytes 61448 | tf_op jit(solution)/shard_map/ppermute | solution.py:43
  41.3 13.0 %collective-permute-start.11 = (bf16[16,8,5,64]{3,2,1,0:T(8,128)(2,1)S(1)}, bf16[16,8,5,64]{3,2,1,0:T(8,128)(2,1)S(1)}, u32[]{:S(2)}, u32[]{:S(2)}) collective-permute-start(bf16[16,8,5,64]{3,2,1,0:T(8,128)(2,1)S(1)} %bitcast_select_fusion), channel_id=1, source_target_pairs={{0,192},{4,196},{8,200},{12,204},{16,208},{20,212},{24,216},{28,22... | collective-permute-start | bytes 245768 | tf_op jit(solution)/shard_map/ppermute | solution.py:43
  41.9 12.5 %collective-permute-start.10 = (bf16[16,8,5,64]{3,2,1,0:T(8,128)(2,1)S(1)}, bf16[16,8,5,64]{3,2,1,0:T(8,128)(2,1)S(1)}, u32[]{:S(2)}, u32[]{:S(2)}) collective-permute-start(bf16[16,8,5,64]{3,2,1,0:T(8,128)(2,1)S(1)} %bitcast_select_fusion), channel_id=1, source_target_pairs={{0,128},{4,132},{8,136},{12,140},{16,144},{20,148},{24,152},{28,15... | collective-permute-start | bytes 245768 | tf_op jit(solution)/shard_map/ppermute | solution.py:43
  44.3 10.7 %collective-permute-start.9 = (bf16[16,8,5,64]{3,2,1,0:T(8,128)(2,1)S(1)}, bf16[16,8,5,64]{3,2,1,0:T(8,128)(2,1)S(1)}, u32[]{:S(2)}, u32[]{:S(2)}) collective-permute-start(bf16[16,8,5,64]{3,2,1,0:T(8,128)(2,1)S(1)} %bitcast_select_fusion), channel_id=1, source_target_pairs={{0,64},{4,68},{8,72},{12,76},{16,80},{20,84},{24,88},{28,92},{32,9... | collective-permute-start | bytes 245768 | tf_op jit(solution)/shard_map/ppermute | solution.py:43
  57.1 3.3 %copy-start.10 = (f32[24,128,5]{1,2,0:T(8,128)S(1)}, f32[24,128,5]{1,2,0:T(8,128)}, u32[]{:S(2)}) copy-start(f32[24,128,5]{1,2,0:T(8,128)} %add_sqrt_fusion) | copy-start | bytes 184324
  60.4 2.6 %copy-start.11 = (pred[24,512]{1,0:T(8,128)(4,1)S(1)}, pred[24,512]{1,0:T(8,128)(4,1)}, u32[]{:S(2)}) copy-start(pred[24,512]{1,0:T(8,128)(4,1)} %iota_compare_fusion) | copy-start | bytes 36868
  62.6 4.0 %copy-start.18 = (s32[24]{0:T(128)S(1)}, s32[24]{0:T(128)}, u32[]{:S(2)}) copy-start(s32[24]{0:T(128)} %param.15) | copy-start | bytes 292
  67.0 5.5 %copy-start.12 = (f32[8,320]{1,0:T(8,128)S(1)}, f32[8,320]{1,0:T(8,128)}, u32[]{:S(2)}) copy-start(f32[8,320]{1,0:T(8,128)} %get-tuple-element.32) | copy-start | bytes 30724
  70.6 7.4 %collective-permute-start.14 = (f32[16,8,330]{2,1,0:T(8,128)}, f32[16,8,330]{2,1,0:T(8,128)S(1)}, u32[]{:S(2)}, u32[]{:S(2)}) collective-permute-start(f32[16,8,330]{2,1,0:T(8,128)} %get-tuple-element.17), channel_id=1, source_target_pairs={{0,12},{4,8},{8,4},{12,0},{16,28},{20,24},{24,20},{28,16},{32,44},... | collective-permute-start | bytes 506888 | tf_op jit(solution)/shard_map/ppermute | solution.py:81
  70.6 9.8 %collective-permute-start.13 = (f32[16,8,330]{2,1,0:T(8,128)}, f32[16,8,330]{2,1,0:T(8,128)S(1)}, u32[]{:S(2)}, u32[]{:S(2)}) collective-permute-start(f32[16,8,330]{2,1,0:T(8,128)} %get-tuple-element.18), channel_id=1, source_target_pairs={{0,8},{4,12},{8,0},{12,4},{16,24},{20,28},{24,16},{28,20},{32,40},... | collective-permute-start | bytes 506888 | tf_op jit(solution)/shard_map/ppermute | solution.py:81
  71.2 9.3 %collective-permute-start.12 = (f32[16,8,330]{2,1,0:T(8,128)}, f32[16,8,330]{2,1,0:T(8,128)S(1)}, u32[]{:S(2)}, u32[]{:S(2)}) collective-permute-start(f32[16,8,330]{2,1,0:T(8,128)} %get-tuple-element.19), channel_id=1, source_target_pairs={{0,4},{4,0},{8,12},{12,8},{16,20},{20,16},{24,28},{28,24},{32,36},... | collective-permute-start | bytes 506888 | tf_op jit(solution)/shard_map/ppermute | solution.py:81
  78.1 2.4 %copy-start.5 = (f32[16,8,330]{2,1,0:T(8,128)}, f32[16,8,330]{2,1,0:T(8,128)S(1)}, u32[]{:S(2)}) copy-start(f32[16,8,330]{2,1,0:T(8,128)S(1)} %collective-permute-done.14) | copy-start | bytes 506884
  80.4 0.7 copy-start.6
  80.4 0.7 copy-start.7
  88.5 28.5 %copy-start.13 = (f32[1280]{0:T(1024)S(1)}, f32[1280]{0:T(1024)}, u32[]{:S(2)}) copy-start(f32[1280]{0:T(1024)} %param.13) | copy-start | bytes 15364
  88.6 6.8 %collective-permute-start.17 = (f32[4,8,330]{2,1,0:T(8,128)S(1)}, f32[4,8,330]{2,1,0:T(8,128)S(1)}, u32[]{:S(2)}, u32[]{:S(2)}) collective-permute-start(f32[4,8,330]{2,1,0:T(8,128)S(1)} %get-tuple-element.21), channel_id=1, source_target_pairs={{0,48},{4,52},{8,56},{12,60},{16,32},{20,36},{24,40},{28,44},{32,1... | collective-permute-start | bytes 126728 | tf_op jit(solution)/shard_map/ppermute | solution.py:81
  92.9 9.2 %collective-permute-start.16 = (f32[4,8,330]{2,1,0:T(8,128)S(1)}, f32[4,8,330]{2,1,0:T(8,128)S(1)}, u32[]{:S(2)}, u32[]{:S(2)}) collective-permute-start(f32[4,8,330]{2,1,0:T(8,128)S(1)} %get-tuple-element.22), channel_id=1, source_target_pairs={{0,32},{4,36},{8,40},{12,44},{16,48},{20,52},{24,56},{28,60},{32,0... | collective-permute-start | bytes 126728 | tf_op jit(solution)/shard_map/ppermute | solution.py:81
  94.4 7.7 %collective-permute-start.15 = (f32[4,8,330]{2,1,0:T(8,128)S(1)}, f32[4,8,330]{2,1,0:T(8,128)S(1)}, u32[]{:S(2)}, u32[]{:S(2)}) collective-permute-start(f32[4,8,330]{2,1,0:T(8,128)S(1)} %get-tuple-element.23), channel_id=1, source_target_pairs={{0,16},{4,20},{8,24},{12,28},{16,0},{20,4},{24,8},{28,12},{32,48},... | collective-permute-start | bytes 126728 | tf_op jit(solution)/shard_map/ppermute | solution.py:81
  103.1 20.0 %copy-start.4 = (bf16[4,8,320]{2,1,0:T(8,128)(2,1)S(1)}, bf16[4,8,320]{2,1,0:T(8,128)(2,1)}, u32[]{:S(2)}) copy-start(bf16[4,8,320]{2,1,0:T(8,128)(2,1)} %copy-done.3) | copy-start | bytes 61444
  103.2 19.9 %copy-start.15 = (pred[4]{0:T(512)(128)(4,1)S(1)}, pred[4]{0:T(512)(128)(4,1)}, u32[]{:S(2)}) copy-start(pred[4]{0:T(512)(128)(4,1)} %copy-done.14) | copy-start | bytes 16
  104.0 5.0 %collective-permute-start.20 = (f32[1,8,330]{2,1,0:T(8,128)S(1)}, f32[1,8,330]{2,1,0:T(8,128)S(1)}, u32[]{:S(2)}, u32[]{:S(2)}) collective-permute-start(f32[1,8,330]{2,1,0:T(8,128)S(1)} %get-tuple-element.29), channel_id=1, source_target_pairs={{0,192},{4,196},{8,200},{12,204},{16,208},{20,212},{24,216},{28,22... | collective-permute-start | bytes 31688 | tf_op jit(solution)/shard_map/ppermute | solution.py:81
  104.4 5.2 %collective-permute-start.19 = (f32[1,8,330]{2,1,0:T(8,128)S(1)}, f32[1,8,330]{2,1,0:T(8,128)S(1)}, u32[]{:S(2)}, u32[]{:S(2)}) collective-permute-start(f32[1,8,330]{2,1,0:T(8,128)S(1)} %get-tuple-element.30), channel_id=1, source_target_pairs={{0,128},{4,132},{8,136},{12,140},{16,144},{20,148},{24,152},{28,15... | collective-permute-start | bytes 31688 | tf_op jit(solution)/shard_map/ppermute | solution.py:81
  106.8 3.7 %collective-permute-start.18 = (f32[1,8,330]{2,1,0:T(8,128)S(1)}, f32[1,8,330]{2,1,0:T(8,128)S(1)}, u32[]{:S(2)}, u32[]{:S(2)}) collective-permute-start(f32[1,8,330]{2,1,0:T(8,128)S(1)} %get-tuple-element.31), channel_id=1, source_target_pairs={{0,64},{4,68},{8,72},{12,76},{16,80},{20,84},{24,88},{28,92},{32,9... | collective-permute-start | bytes 31688 | tf_op jit(solution)/shard_map/ppermute | solution.py:81
  112.9 5.7 %collective-permute-start.23 = (f32[8,1280]{1,0:T(8,128)S(1)}, f32[8,1280]{1,0:T(8,128)S(1)}, u32[]{:S(2)}, u32[]{:S(2)}) collective-permute-start(f32[8,1280]{1,0:T(8,128)S(1)} %fusion.28), channel_id=1, source_target_pairs={{0,3},{1,2},{2,1},{3,0},{4,7},{5,6},{6,5},{7,4},{8,11},{9,10},{10,... | collective-permute-start | bytes 122888 | tf_op jit(solution)/shard_map/ppermute | solution.py:43
  116.0 5.5 %collective-permute-start.22 = (f32[8,1280]{1,0:T(8,128)S(1)}, f32[8,1280]{1,0:T(8,128)S(1)}, u32[]{:S(2)}, u32[]{:S(2)}) collective-permute-start(f32[8,1280]{1,0:T(8,128)S(1)} %fusion.28), channel_id=1, source_target_pairs={{0,2},{1,3},{2,0},{3,1},{4,6},{5,7},{6,4},{7,5},{8,10},{9,11},{10,... | collective-permute-start | bytes 122888 | tf_op jit(solution)/shard_map/ppermute | solution.py:43
  116.6 4.9 %collective-permute-start.21 = (f32[8,1280]{1,0:T(8,128)S(1)}, f32[8,1280]{1,0:T(8,128)S(1)}, u32[]{:S(2)}, u32[]{:S(2)}) collective-permute-start(f32[8,1280]{1,0:T(8,128)S(1)} %fusion.28), channel_id=1, source_target_pairs={{0,1},{1,0},{2,3},{3,2},{4,5},{5,4},{6,7},{7,6},{8,9},{9,8},{10,11... | collective-permute-start | bytes 122888 | tf_op jit(solution)/shard_map/ppermute | solution.py:43

commit v4 on v3

--- a/solution.py
+++ b/solution.py
@@ -56,29 +56,31 @@
     return held
 
 
-def sum_radix(value, axis):
-    low = 0
-    for width in digit_groups(lax.axis_size(axis)):
-        stacked = exchange(value, axis, low, width)
-        value = stacked[0]
-        for digit in range(1, stacked.shape[0]):
-            value = value + stacked[digit]
-        low += width
-    return value
-
-
-def scatter_radix(packed, axis, width_acc, heads):
+def gather_xor(value, axis):
     size = lax.axis_size(axis)
-    index = lax.axis_index(axis)
+    held = value[None]
+    low = 0
+    for width in digit_groups(size):
+        got = [held] + [
+            lax.ppermute(held, axis, perm=xor_partner(axis, size, digit << low))
+            for digit in range(1, 1 << width)
+        ]
+        held = jnp.stack(got).reshape((-1,) + value.shape)
+        low += width
+    return held
+
+
+def scatter_xor(packed, axis, width_acc, heads):
+    size = lax.axis_size(axis)
     low = 0
     for width in digit_groups(size):
         count = 1 << width
-        mine = (index >> low) & (count - 1)
         grouped = packed.reshape((packed.shape[0] // count, count) + packed.shape[1:])
-        pieces = [lax.dynamic_index_in_dim(grouped, mine, 1, False)]
+        pieces = [grouped[:, 0]]
         for digit in range(1, count):
-            send = lax.dynamic_index_in_dim(grouped, mine ^ digit, 1, False)
-            pieces.append(lax.ppermute(send, axis, perm=xor_partner(axis, size, digit << low)))
+            pieces.append(
+                lax.ppermute(grouped[:, digit], axis, perm=xor_partner(axis, size, digit << low))
+            )
         stacked = jnp.stack(pieces)
         acc = stacked[..., :width_acc]
         total = stacked[..., width_acc : width_acc + heads]
@@ -90,6 +92,17 @@
         packed = jnp.concatenate([acc, total, top], axis=-1)
         low += width
     return packed[0]
+
+
+def sum_radix(value, axis):
+    low = 0
+    for width in digit_groups(lax.axis_size(axis)):
+        stacked = exchange(value, axis, low, width)
+        value = stacked[0]
+        for digit in range(1, stacked.shape[0]):
+            value = value + stacked[digit]
+        low += width
+    return value
 
 
 def local(
@@ -123,9 +136,14 @@
         axis=-1,
     ) / math.sqrt(HEAD_DIM)
 
-    all_queries = gather_radix(query, "seq").reshape(-1, width_local)
+    query, page_cache, page_request, page_number, lengths = lax.optimization_barrier(
+        (query, page_cache, page_request, page_number, lengths)
+    )
+    seq_index = lax.axis_index("seq")
+    all_queries = gather_xor(query, "seq").reshape(-1, width_local)
+    owner_place = ((page_request // rows) ^ seq_index) * rows + page_request % rows
     pages, page_len = (page_cache.shape[0], page_cache.shape[1])
-    owner_query = all_queries[page_request].reshape(pages, heads_local, HEAD_DIM)
+    owner_query = all_queries[owner_place].reshape(pages, heads_local, HEAD_DIM)
     keys_scaled = head_norm(page_cache[:, :, 0, :].astype(jnp.float32), score_gain).astype(
         jnp.bfloat16
     )
@@ -145,9 +163,9 @@
     ).reshape(pages, width_local)
 
     requests = lengths.shape[0]
-    onehot = page_request[:, None] == jnp.arange(requests, dtype=jnp.int32)[None, :]
+    onehot = owner_place[:, None] == jnp.arange(requests, dtype=jnp.int32)[None, :]
     request_max = jnp.max(jnp.where(onehot[:, :, None], page_max[:, None, :], far_below), axis=0)
-    factor = jnp.exp(page_max - request_max[page_request])
+    factor = jnp.exp(page_max - request_max[owner_place])
     selector = onehot.astype(jnp.float32)
     request_total = jnp.dot(selector.T, page_total * factor, precision=lax.Precision.HIGHEST)
     request_acc = jnp.dot(
@@ -155,7 +173,7 @@
     )
     packed = jnp.concatenate([request_acc, request_total, request_max], axis=1)
     packed = packed.reshape(lax.axis_size("seq"), rows, packed.shape[-1])
-    home = scatter_radix(packed, "seq", width_local, heads_local)
+    home = scatter_xor(packed, "seq", width_local, heads_local)
     home_acc = home[:, :width_local]
     home_total = home[:, width_local : width_local + heads_local]
     home_max = home[:, width_local + heads_local :]

time: 126 us -> 121 us (0.960)
  other arithmetic: 15.6 us -> 11.1 us
  local copies, waits for them, and re-layouts: 24.7 us -> 21.4 us
  starting transfers between devices: 35.7 us -> 38.9 us
    ppermute x9 -> x18, waiting for transfers between devices: 16.6 us -> 36 us  [the longest x9 19.7 us: scatter_xor(): lax.ppermute(grouped[:, digit], axis, perm=xor_partner(axis, size, digit...]
    ppermute x15 -> x6, waiting for transfers between devices: 24 us -> 4.68 us  [exchange(): lax.ppermute(held, axis, perm=xor_partner(axis, size, digit << low))]
    ppermute x9 -> x18, starting transfers between devices: 12.8 us -> 29.4 us  [the longest x9 15.4 us: gather_xor(): lax.ppermute(held, axis, perm=xor_partner(axis, size, digit << low))]
    ppermute x15 -> x6, starting transfers between devices: 22.9 us -> 9.44 us  [exchange(): lax.ppermute(held, axis, perm=xor_partner(axis, size, digit << low))]
    gather x6 -> x2, local copies, waits for them, and re-layouts: 5.95 us -> 1.24 us  [exchange(): return jnp.take(jnp.stack(got), order, axis=0)]
    gather x2, local copies, waits for them, and re-layouts: 1.19 us -> 2.47 us  [the longest x1 1.78 us: local(): owner_query = all_queries[owner_place].reshape(pages, heads_local, HEAD_DIM)]
    unnamed x40 -> x26, local copies, waits for them, and re-layouts: 2.66 us -> 1.89 us
  transfers between devices with their start and end apart: 24 -> 24, of which waited for: 14 -> 14; matrix products, arithmetic and copies ran while one was open for 9% -> 8% of each run, Pallas kernels for 0% -> 0%
where the time goes in v4:
time: 121 us; the launch traced here: 120 us
  waiting for transfers between devices  40.7 us (34%)
  starting transfers between devices  38.9 us (32%)
  local copies, waits for them, and re-layouts  21.4 us (18%)
  other arithmetic  11.1 us (9%)
  matrix products  7.72 us (6%)
    ppermute x9, waiting for transfers between devices, scatter_xor(): lax.ppermute(grouped[:, digit], axis, perm=xor_partner(axis, size, digit...  19.7 us
    ppermute x9, waiting for transfers between devices, gather_xor(): lax.ppermute(held, axis, perm=xor_partner(axis, size, digit << low))  16.3 us
    ppermute x9, starting transfers between devices, gather_xor(): lax.ppermute(held, axis, perm=xor_partner(axis, size, digit << low))  15.4 us
    ppermute x9, starting transfers between devices, scatter_xor(): lax.ppermute(grouped[:, digit], axis, perm=xor_partner(axis, size, digit...  14 us
    ppermute x6, starting transfers between devices, exchange(): lax.ppermute(held, axis, perm=xor_partner(axis, size, digit << low))  9.44 us
    mul x10, local copies, waits for them, and re-layouts, scale_heads(): return (shaped * factor[..., None]).reshape(summed.shape)  5.31 us
    ppermute x6, waiting for transfers between devices, exchange(): lax.ppermute(held, axis, perm=xor_partner(axis, size, digit << low))  4.68 us
    slice x1, local copies, waits for them, and re-layouts, local(): page_cache[:, :, 1, :].reshape(pages, page_len, heads_local, HEAD_DIM)  3.67 us
  transfers between devices with their start and end apart: 24, of which 14 were waited for; matrix products, arithmetic and copies ran while one was open for 8% of the time, Pallas kernels for 0%

profile of v4, /device:TPU:6, one launch (start us, length us, event | category | flops | bytes accessed | tf_op | source)
XLA Modules:
  0.0 120.2 jit_solution(16411005869218053896)
XLA Ops:
  0.0 1.6 %collective-permute-start = (bf16[1,8,320]{2,1,0:T(8,128)(2,1)}, bf16[1,8,320]{2,1,0:T(8,128)(2,1)S(1)}, u32[]{:S(2)}, u32[]{:S(2)}) collective-permute-start(bf16[1,8,320]{2,1,0:T(8,128)(2,1)} %bitcast.160), channel_id=1, source_target_pairs={{0,1},{1,0},{2,3},{3,2},{4,5},{5,4},{6,7},{7,6},{8,9},{9,8},{10,11... | collective-permute-start | bytes 15368 | tf_op jit(solution)/shard_map/ppermute | solution.py:43
  1.6 2.9 %collective-permute-start.1 = (bf16[1,8,320]{2,1,0:T(8,128)(2,1)}, bf16[1,8,320]{2,1,0:T(8,128)(2,1)S(1)}, u32[]{:S(2)}, u32[]{:S(2)}) collective-permute-start(bf16[1,8,320]{2,1,0:T(8,128)(2,1)} %bitcast.161), channel_id=1, source_target_pairs={{0,2},{1,3},{2,0},{3,1},{4,6},{5,7},{6,4},{7,5},{8,10},{9,11},{10,... | collective-permute-start | bytes 15368 | tf_op jit(solution)/shard_map/ppermute | solution.py:43
  4.8 0.8 mul.156
  5.5 1.4 %collective-permute-done.1 = bf16[1,8,320]{2,1,0:T(8,128)(2,1)S(1)} collective-permute-done((bf16[1,8,320]{2,1,0:T(8,128)(2,1)}, bf16[1,8,320]{2,1,0:T(8,128)(2,1)S(1)}, u32[]{:S(2)}, u32[]{:S(2)}) %collective-permute-start.1) | collective-permute-done | bytes 5152 | tf_op jit(solution)/shard_map/ppermute | solution.py:43
  6.9 2.6 %collective-permute-done.2 = bf16[1,8,320]{2,1,0:T(8,128)(2,1)S(1)} collective-permute-done((bf16[1,8,320]{2,1,0:T(8,128)(2,1)}, bf16[1,8,320]{2,1,0:T(8,128)(2,1)S(1)}, u32[]{:S(2)}, u32[]{:S(2)}) %collective-permute-start.2) | collective-permute-done | bytes 5152 | tf_op jit(solution)/shard_map/ppermute | solution.py:43
  11.0 0.7 fusion.43
  12.7 0.8 multiply_reduce_fusion.1
  13.5 1.9 %collective-permute-start.4 = (bf16[1,8,5,64]{3,2,1,0:T(8,128)(2,1)S(1)}, bf16[1,8,5,64]{3,2,1,0:T(8,128)(2,1)S(1)}, u32[]{:S(2)}, u32[]{:S(2)}) collective-permute-start(bf16[1,8,5,64]{3,2,1,0:T(8,128)(2,1)S(1)} %bitcast.139), channel_id=1, source_target_pairs={{0,8},{4,12},{8,0},{12,4},{16,24},{20,28},{24,16},{28,20},{32,40},... | collective-permute-start | bytes 15368 | tf_op jit(solution)/shard_map/ppermute | solution.py:65
  15.5 3.7 %fusion.41 = (bf16[24,128,1,320]{1,3,2,0:T(8,128)(2,1)}, bf16[24,128,1,320]{1,3,2,0:T(8,128)(2,1)S(1)}) fusion(bf16[24,128,2,320]{1,3,2,0:T(8,128)(2,1)} %param.17), kind=kLoop, calls=%fused_computation.129 | loop fusion | bytes 7864320 | tf_op jit(solution)/shard_map/slice | solution.py:150
  19.2 1.3 %copy-done.2 = bf16[24,128,1,320]{1,3,2,0:T(8,128)(2,1)} copy-done((bf16[24,128,1,320]{1,3,2,0:T(8,128)(2,1)}, bf16[24,128,1,320]{1,3,2,0:T(8,128)(2,1)S(1)}, u32[]{:S(2)}) %copy-start.2) | copy-done | bytes 1966104
  20.5 0.7 fusion
  22.6 0.7 gather_fusion.1
  23.4 3.4 %collective-permute-start.6 = (bf16[4,8,5,64]{3,2,1,0:T(8,128)(2,1)S(1)}, bf16[4,8,5,64]{3,2,1,0:T(8,128)(2,1)S(1)}, u32[]{:S(2)}, u32[]{:S(2)}) collective-permute-start(bf16[4,8,5,64]{3,2,1,0:T(8,128)(2,1)S(1)} %get-tuple-element.41), channel_id=1, source_target_pairs={{0,16},{4,20},{8,24},{12,28},{16,0},{20,4},{24,8},{28,12},{32,48},... | collective-permute-start | bytes 61448 | tf_op jit(solution)/shard_map/ppermute | solution.py:65
  26.7 5.2 %collective-permute-start.7 = (bf16[4,8,5,64]{3,2,1,0:T(8,128)(2,1)S(1)}, bf16[4,8,5,64]{3,2,1,0:T(8,128)(2,1)S(1)}, u32[]{:S(2)}, u32[]{:S(2)}) collective-permute-start(bf16[4,8,5,64]{3,2,1,0:T(8,128)(2,1)S(1)} %get-tuple-element.41), channel_id=1, source_target_pairs={{0,32},{4,36},{8,40},{12,44},{16,48},{20,52},{24,56},{28,60},{32,0... | collective-permute-start | bytes 61448 | tf_op jit(solution)/shard_map/ppermute | solution.py:65
  32.0 3.7 %collective-permute-done.7 = bf16[4,8,5,64]{3,2,1,0:T(8,128)(2,1)S(1)} collective-permute-done((bf16[4,8,5,64]{3,2,1,0:T(8,128)(2,1)S(1)}, bf16[4,8,5,64]{3,2,1,0:T(8,128)(2,1)S(1)}, u32[]{:S(2)}, u32[]{:S(2)}) %collective-permute-start.7) | collective-permute-done | bytes 20512 | tf_op jit(solution)/shard_map/ppermute | solution.py:65
  35.7 2.6 %collective-permute-done.8 = bf16[4,8,5,64]{3,2,1,0:T(8,128)(2,1)S(1)} collective-permute-done((bf16[4,8,5,64]{3,2,1,0:T(8,128)(2,1)S(1)}, bf16[4,8,5,64]{3,2,1,0:T(8,128)(2,1)S(1)}, u32[]{:S(2)}, u32[]{:S(2)}) %collective-permute-start.8) | collective-permute-done | bytes 20512 | tf_op jit(solution)/shard_map/ppermute | solution.py:65
  38.4 0.9 collective-permute-start.9
  39.3 1.1 collective-permute-start.10
  40.4 2.8 %collective-permute-start.11 = (bf16[16,8,5,64]{3,2,1,0:T(8,128)(2,1)S(1)}, bf16[16,8,5,64]{3,2,1,0:T(8,128)(2,1)S(1)}, u32[]{:S(2)}, u32[]{:S(2)}) collective-permute-start(bf16[16,8,5,64]{3,2,1,0:T(8,128)(2,1)S(1)} %bitcast.127), channel_id=1, source_target_pairs={{0,192},{4,196},{8,200},{12,204},{16,208},{20,212},{24,216},{28,22... | collective-permute-start | bytes 245768 | tf_op jit(solution)/shard_map/ppermute | solution.py:65
  43.8 3.9 %collective-permute-done.9 = bf16[16,8,5,64]{3,2,1,0:T(8,128)(2,1)S(1)} collective-permute-done((bf16[16,8,5,64]{3,2,1,0:T(8,128)(2,1)S(1)}, bf16[16,8,5,64]{3,2,1,0:T(8,128)(2,1)S(1)}, u32[]{:S(2)}, u32[]{:S(2)}) %collective-permute-start.9) | collective-permute-done | bytes 81952 | tf_op jit(solution)/shard_map/ppermute | solution.py:65
  47.7 3.5 %collective-permute-done.10 = bf16[16,8,5,64]{3,2,1,0:T(8,128)(2,1)S(1)} collective-permute-done((bf16[16,8,5,64]{3,2,1,0:T(8,128)(2,1)S(1)}, bf16[16,8,5,64]{3,2,1,0:T(8,128)(2,1)S(1)}, u32[]{:S(2)}, u32[]{:S(2)}) %collective-permute-start.10) | collective-permute-done | bytes 81952 | tf_op jit(solution)/shard_map/ppermute | solution.py:65
  51.2 2.6 %collective-permute-done.11 = bf16[16,8,5,64]{3,2,1,0:T(8,128)(2,1)S(1)} collective-permute-done((bf16[16,8,5,64]{3,2,1,0:T(8,128)(2,1)S(1)}, bf16[16,8,5,64]{3,2,1,0:T(8,128)(2,1)S(1)}, u32[]{:S(2)}, u32[]{:S(2)}) %collective-permute-start.11) | collective-permute-done | bytes 81952 | tf_op jit(solution)/shard_map/ppermute | solution.py:65
  54.1 1.3 %reshape_reshape.6 = bf16[512,320]{1,0:T(8,128)(2,1)} reshape(bf16[4,16,8,5,64]{4,3,2,1,0:T(8,128)(2,1)S(1)} %pad_maximum_fusion) | data formatting | bytes 655360 | tf_op jit(solution)/shard_map/reshape;reshape | solution.py:143
  55.4 1.8 %gather_fusion.2 = bf16[24,320]{1,0:T(8,128)(2,1)S(1)} fusion(bf16[512,320]{1,0:T(8,128)(2,1)} %reshape_reshape.6, s32[1024]{0:T(1024)} %pad_clamp_fusion), kind=kCustom, calls=%fused_computation.2 | custom fusion | bytes 30816 | tf_op jit(solution)/shard_map/gather | solution.py:146
  57.3 2.3 %fusion.3 = f32[24,5,1,128]{3,2,1,0:T(1,128)S(1)} fusion(bf16[24,5,64,1]{2,3,1,0:T(2,128)(2,1)S(1)} %reshape.281, bf16[24,128,5,64]{1,3,2,0:T(8,128)(2,1)} %bitcast.122, f32[5,64]{1,0:T(8,128)} %copy-done.5, f32[24,128,5]{1,2,0:T(8,128)} %add_sqrt_fusion), kind=kOutput, calls=%fused_computation.10 | convolution fusion | flops 5898240 | bytes 2105600 | tf_op jit(solution)/shard_map/sphd,shd->shp/dot_general | solution.py:151
  60.9 2.6 %fusion.9 = f32[24,5,1,64]{3,2,1,0:T(1,128)S(1)} fusion(bf16[24,128,5,64]{1,3,2,0:T(8,128)(2,1)} %bitcast.124, bf16[24,5,128,1]{2,0,1,3:T(8,128)(2,1)S(1)} %get-tuple-element.38), kind=kOutput, calls=%fused_computation.40 | convolution fusion | flops 1966080 | bytes 2027520 | tf_op jit(solution)/shard_map/shp,sphd->shd/dot_general | solution.py:161
  64.6 0.9 pad_maximum_fusion.2
  65.5 1.4 %copy.47 = f32[512,330]{1,0:T(8,128)S(1)} copy(f32[512,330]{0,1:T(8,128)} %pad_maximum_fusion.2) | data formatting | bytes 1351680 | tf_op jit(solution)/shard_map/concatenate | solution.py:174
  67.2 1.2 collective-permute-start.13
  69.0 6.0 %collective-permute-done.13 = f32[16,8,330]{2,1,0:T(8,128)S(1)} collective-permute-done((f32[16,8,330]{2,1,0:T(8,128)S(1)}, f32[16,8,330]{2,1,0:T(8,128)S(1)}, u32[]{:S(2)}, u32[]{:S(2)}) %collective-permute-start.13) | collective-permute-done | bytes 168992 | tf_op jit(solution)/shard_map/ppermute | solution.py:82
  75.1 3.1 %collective-permute-done.14 = f32[16,8,330]{2,1,0:T(8,128)S(1)} collective-permute-done((f32[16,8,330]{2,1,0:T(8,128)S(1)}, f32[16,8,330]{2,1,0:T(8,128)S(1)}, u32[]{:S(2)}, u32[]{:S(2)}) %collective-permute-start.14) | collective-permute-done | bytes 168992 | tf_op jit(solution)/shard_map/ppermute | solution.py:82
  78.5 2.0 %mul.167 = f32[4,16,8,5,64]{4,3,2,1,0:T(8,128)} broadcast(f32[4,16,8,5]{3,2,1,0:T(8,128)S(1)} %get-tuple-element.25), dimensions={0,1,2,3} | broadcast | bytes 665600 | tf_op jit(solution)/shard_map/mul | solution.py:23
  80.5 2.6 %mul.168 = f32[4,16,8,320]{3,2,1,0:T(8,128)} reshape(f32[4,16,8,5,64]{4,3,2,1,0:T(8,128)} %mul.167) | data formatting | bytes 1310720 | tf_op jit(solution)/shard_map/mul | solution.py:23
  83.1 1.2 %fusion.5 = f32[16,8,320]{2,1,0:T(8,128)S(1)} fusion(f32[4,16,8,320]{3,2,1,0:T(8,128)} %mul.168, f32[4,16,8,330]{3,2,1,0:T(8,128)S(1)} %pad_maximum_fusion.1), kind=kLoop, calls=%fused_computation.13 | loop fusion | flops 286720 | bytes 1474560 | tf_op jit(solution)/shard_map/reduce_sum | solution.py:90
  84.5 1.3 %collective-permute-start.15 = (f32[4,8,330]{2,1,0:T(8,128)S(1)}, f32[4,8,330]{2,1,0:T(8,128)S(1)}, u32[]{:S(2)}, u32[]{:S(2)}) collective-permute-start(f32[4,8,330]{2,1,0:T(8,128)S(1)} %get-tuple-element.35), channel_id=1, source_target_pairs={{0,16},{4,20},{8,24},{12,28},{16,0},{20,4},{24,8},{28,12},{32,48},... | collective-permute-start | bytes 126728 | tf_op jit(solution)/shard_map/ppermute | solution.py:82
  85.8 5.8 %collective-permute-start.16 = (f32[4,8,330]{2,1,0:T(8,128)S(1)}, f32[4,8,330]{2,1,0:T(8,128)S(1)}, u32[]{:S(2)}, u32[]{:S(2)}) collective-permute-start(f32[4,8,330]{2,1,0:T(8,128)S(1)} %get-tuple-element.37), channel_id=1, source_target_pairs={{0,32},{4,36},{8,40},{12,44},{16,48},{20,52},{24,56},{28,60},{32,0... | collective-permute-start | bytes 126728 | tf_op jit(solution)/shard_map/ppermute | solution.py:82
  91.6 3.2 %collective-permute-done.16 = f32[4,8,330]{2,1,0:T(8,128)S(1)} collective-permute-done((f32[4,8,330]{2,1,0:T(8,128)S(1)}, f32[4,8,330]{2,1,0:T(8,128)S(1)}, u32[]{:S(2)}, u32[]{:S(2)}) %collective-permute-start.16) | collective-permute-done | bytes 42272 | tf_op jit(solution)/shard_map/ppermute | solution.py:82
  94.7 3.0 %collective-permute-done.17 = f32[4,8,330]{2,1,0:T(8,128)S(1)} collective-permute-done((f32[4,8,330]{2,1,0:T(8,128)S(1)}, f32[4,8,330]{2,1,0:T(8,128)S(1)}, u32[]{:S(2)}, u32[]{:S(2)}) %collective-permute-start.17) | collective-permute-done | bytes 42272 | tf_op jit(solution)/shard_map/ppermute | solution.py:82
  98.5 4.2 %collective-permute-start.19 = (f32[1,8,330]{2,1,0:T(8,128)S(1)}, f32[1,8,330]{2,1,0:T(8,128)S(1)}, u32[]{:S(2)}, u32[]{:S(2)}) collective-permute-start(f32[1,8,330]{2,1,0:T(8,128)S(1)} %get-tuple-element.46), channel_id=1, source_target_pairs={{0,128},{4,132},{8,136},{12,140},{16,144},{20,148},{24,152},{28,15... | collective-permute-start | bytes 31688 | tf_op jit(solution)/shard_map/ppermute | solution.py:82
  103.2 1.3 %collective-permute-done.19 = f32[1,8,330]{2,1,0:T(8,128)S(1)} collective-permute-done((f32[1,8,330]{2,1,0:T(8,128)S(1)}, f32[1,8,330]{2,1,0:T(8,128)S(1)}, u32[]{:S(2)}, u32[]{:S(2)}) %collective-permute-start.19) | collective-permute-done | bytes 10592 | tf_op jit(solution)/shard_map/ppermute | solution.py:82
  104.5 3.1 %collective-permute-done.20 = f32[1,8,330]{2,1,0:T(8,128)S(1)} collective-permute-done((f32[1,8,330]{2,1,0:T(8,128)S(1)}, f32[1,8,330]{2,1,0:T(8,128)S(1)}, u32[]{:S(2)}, u32[]{:S(2)}) %collective-permute-start.20) | collective-permute-done | bytes 10592 | tf_op jit(solution)/shard_map/ppermute | solution.py:82
  108.6 1.4 %fusion.30 = f32[8,1280]{1,0:T(8,128)S(1)} fusion(bf16[320,1280]{1,0:T(8,128)(2,1)} %param.11, f32[8,320]{1,0:T(8,128)S(1)} %div.117, f32[8,320]{1,0:T(8,128)S(1)} %mul.187, f32[8,320]{1,0:T(8,128)S(1)} %mul.184, f32[8,330]{1,0:T(8,128)S(1)} %maximum_bitcast_fusion.2, f32[8,960]{1,0:T(8,128)} %copy-done.3), kind=kOutput, calls=%fused_computation.101 | convolution fusion | flops 6568960 | bytes 907584 | tf_op jit(solution)/shard_map/dot_general | solution.py:192
  110.1 1.7 %collective-permute-start.22 = (f32[8,1280]{1,0:T(8,128)S(1)}, f32[8,1280]{1,0:T(8,128)S(1)}, u32[]{:S(2)}, u32[]{:S(2)}) collective-permute-start(f32[8,1280]{1,0:T(8,128)S(1)} %fusion.30), channel_id=1, source_target_pairs={{0,2},{1,3},{2,0},{3,1},{4,6},{5,7},{6,4},{7,5},{8,10},{9,11},{10,... | collective-permute-start | bytes 122888 | tf_op jit(solution)/shard_map/ppermute | solution.py:43
  111.8 3.0 %collective-permute-start.23 = (f32[8,1280]{1,0:T(8,128)S(1)}, f32[8,1280]{1,0:T(8,128)S(1)}, u32[]{:S(2)}, u32[]{:S(2)}) collective-permute-start(f32[8,1280]{1,0:T(8,128)S(1)} %fusion.30), channel_id=1, source_target_pairs={{0,3},{1,2},{2,1},{3,0},{4,7},{5,6},{6,5},{7,4},{8,11},{9,10},{10,... | collective-permute-start | bytes 122888 | tf_op jit(solution)/shard_map/ppermute | solution.py:43
  114.8 0.8 mul.192
  115.5 0.8 dynamic-slice
  117.7 0.7 broadcast_select_fusion
  118.6 0.8 fusion.13
  (118 shorter events, 13.7 us)
Async XLA Ops:
  0.0 11.0 %copy-start = (bf16[1280,3,320]{0,2,1:T(8,128)(2,1)S(1)}, bf16[1280,3,320]{0,2,1:T(8,128)(2,1)}, u32[]{:S(2)}) copy-start(bf16[1280,3,320]{0,2,1:T(8,128)(2,1)} %param.10) | copy-start | bytes 7372804
  0.0 5.5 %collective-permute-start = (bf16[1,8,320]{2,1,0:T(8,128)(2,1)}, bf16[1,8,320]{2,1,0:T(8,128)(2,1)S(1)}, u32[]{:S(2)}, u32[]{:S(2)}) collective-permute-start(bf16[1,8,320]{2,1,0:T(8,128)(2,1)} %bitcast.160), channel_id=1, source_target_pairs={{0,1},{1,0},{2,3},{3,2},{4,5},{5,4},{6,7},{7,6},{8,9},{9,8},{10,11... | collective-permute-start | bytes 15368 | tf_op jit(solution)/shard_map/ppermute | solution.py:43
  1.6 5.3 %collective-permute-start.1 = (bf16[1,8,320]{2,1,0:T(8,128)(2,1)}, bf16[1,8,320]{2,1,0:T(8,128)(2,1)S(1)}, u32[]{:S(2)}, u32[]{:S(2)}) collective-permute-start(bf16[1,8,320]{2,1,0:T(8,128)(2,1)} %bitcast.161), channel_id=1, source_target_pairs={{0,2},{1,3},{2,0},{3,1},{4,6},{5,7},{6,4},{7,5},{8,10},{9,11},{10,... | collective-permute-start | bytes 15368 | tf_op jit(solution)/shard_map/ppermute | solution.py:43
  4.5 5.1 %collective-permute-start.2 = (bf16[1,8,320]{2,1,0:T(8,128)(2,1)}, bf16[1,8,320]{2,1,0:T(8,128)(2,1)S(1)}, u32[]{:S(2)}, u32[]{:S(2)}) collective-permute-start(bf16[1,8,320]{2,1,0:T(8,128)(2,1)} %bitcast.162), channel_id=1, source_target_pairs={{0,3},{1,2},{2,1},{3,0},{4,7},{5,6},{6,5},{7,4},{8,11},{9,10},{10,... | collective-permute-start | bytes 15368 | tf_op jit(solution)/shard_map/ppermute | solution.py:43
  4.7 7.1 %copy-start.7 = (s32[1024]{0:T(1024)}, s32[1024]{0:T(1024)S(1)}, u32[]{:S(2)}) copy-start(s32[1024]{0:T(1024)S(1)} %pad_clamp_fusion.2) | copy-start | bytes 12292
  4.7 7.8 %copy-start.8 = (pred[4]{0:T(512)(128)(4,1)}, pred[4]{0:T(512)(128)(4,1)S(1)}, u32[]{:S(2)}) copy-start(pred[4]{0:T(512)(128)(4,1)S(1)} %compare_and_fusion) | copy-start | bytes 16
  5.5 13.7 %copy-start.5 = (f32[5,64]{1,0:T(8,128)}, f32[5,64]{1,0:T(8,128)S(1)}, u32[]{:S(2)}) copy-start(f32[5,64]{1,0:T(8,128)S(1)} %mul.156) | copy-start | bytes 3844
  11.7 0.6 copy-start.3
  13.5 8.4 %copy-start.12 = (s32[24]{0:T(128)S(1)}, s32[24]{0:T(128)}, u32[]{:S(2)}) copy-start(s32[24]{0:T(128)} %param.16) | copy-start | bytes 292
  13.5 8.4 %copy-start.11 = (s32[24]{0:T(128)S(1)}, s32[24]{0:T(128)}, u32[]{:S(2)}) copy-start(s32[24]{0:T(128)} %param.15) | copy-start | bytes 292
  13.5 9.8 %collective-permute-start.3 = (bf16[1,8,5,64]{3,2,1,0:T(8,128)(2,1)S(1)}, bf16[1,8,5,64]{3,2,1,0:T(8,128)(2,1)S(1)}, u32[]{:S(2)}, u32[]{:S(2)}) collective-permute-start(bf16[1,8,5,64]{3,2,1,0:T(8,128)(2,1)S(1)} %bitcast.138), channel_id=1, source_target_pairs={{0,4},{4,0},{8,12},{12,8},{16,20},{20,16},{24,28},{28,24},{32,36},... | collective-permute-start | bytes 15368 | tf_op jit(solution)/shard_map/ppermute | solution.py:65
  13.5 9.8 %collective-permute-start.4 = (bf16[1,8,5,64]{3,2,1,0:T(8,128)(2,1)S(1)}, bf16[1,8,5,64]{3,2,1,0:T(8,128)(2,1)S(1)}, u32[]{:S(2)}, u32[]{:S(2)}) collective-permute-start(bf16[1,8,5,64]{3,2,1,0:T(8,128)(2,1)S(1)} %bitcast.139), channel_id=1, source_target_pairs={{0,8},{4,12},{8,0},{12,4},{16,24},{20,28},{24,16},{28,20},{32,40},... | collective-permute-start | bytes 15368 | tf_op jit(solution)/shard_map/ppermute | solution.py:65
  15.4 7.9 %collective-permute-start.5 = (bf16[1,8,5,64]{3,2,1,0:T(8,128)(2,1)S(1)}, bf16[1,8,5,64]{3,2,1,0:T(8,128)(2,1)S(1)}, u32[]{:S(2)}, u32[]{:S(2)}) collective-permute-start(bf16[1,8,5,64]{3,2,1,0:T(8,128)(2,1)S(1)} %bitcast.140), channel_id=1, source_target_pairs={{0,12},{4,8},{8,4},{12,0},{16,28},{20,24},{24,20},{28,16},{32,44},... | collective-permute-start | bytes 15368 | tf_op jit(solution)/shard_map/ppermute | solution.py:65
  19.2 1.3 %copy-start.2 = (bf16[24,128,1,320]{1,3,2,0:T(8,128)(2,1)}, bf16[24,128,1,320]{1,3,2,0:T(8,128)(2,1)S(1)}, u32[]{:S(2)}) copy-start(bf16[24,128,1,320]{1,3,2,0:T(8,128)(2,1)S(1)} %get-tuple-element.29) | copy-start | bytes 5898244
  19.2 3.4 %copy-start.1 = (s32[512]{0:T(512)S(1)}, s32[512]{0:T(512)}, u32[]{:S(2)}) copy-start(s32[512]{0:T(512)} %param.14) | copy-start | bytes 6148
  21.9 0.7 copy-start.9
  23.4 8.7 %collective-permute-start.6 = (bf16[4,8,5,64]{3,2,1,0:T(8,128)(2,1)S(1)}, bf16[4,8,5,64]{3,2,1,0:T(8,128)(2,1)S(1)}, u32[]{:S(2)}, u32[]{:S(2)}) collective-permute-start(bf16[4,8,5,64]{3,2,1,0:T(8,128)(2,1)S(1)} %get-tuple-element.41), channel_id=1, source_target_pairs={{0,16},{4,20},{8,24},{12,28},{16,0},{20,4},{24,8},{28,12},{32,48},... | collective-permute-start | bytes 61448 | tf_op jit(solution)/shard_map/ppermute | solution.py:65
  26.7 9.0 %collective-permute-start.7 = (bf16[4,8,5,64]{3,2,1,0:T(8,128)(2,1)S(1)}, bf16[4,8,5,64]{3,2,1,0:T(8,128)(2,1)S(1)}, u32[]{:S(2)}, u32[]{:S(2)}) collective-permute-start(bf16[4,8,5,64]{3,2,1,0:T(8,128)(2,1)S(1)} %get-tuple-element.41), channel_id=1, source_target_pairs={{0,32},{4,36},{8,40},{12,44},{16,48},{20,52},{24,56},{28,60},{32,0... | collective-permute-start | bytes 61448 | tf_op jit(solution)/shard_map/ppermute | solution.py:65
  31.9 6.4 %collective-permute-start.8 = (bf16[4,8,5,64]{3,2,1,0:T(8,128)(2,1)S(1)}, bf16[4,8,5,64]{3,2,1,0:T(8,128)(2,1)S(1)}, u32[]{:S(2)}, u32[]{:S(2)}) collective-permute-start(bf16[4,8,5,64]{3,2,1,0:T(8,128)(2,1)S(1)} %get-tuple-element.41), channel_id=1, source_target_pairs={{0,48},{4,52},{8,56},{12,60},{16,32},{20,36},{24,40},{28,44},{32,1... | collective-permute-start | bytes 61448 | tf_op jit(solution)/shard_map/ppermute | solution.py:65
  38.4 9.3 %collective-permute-start.9 = (bf16[16,8,5,64]{3,2,1,0:T(8,128)(2,1)S(1)}, bf16[16,8,5,64]{3,2,1,0:T(8,128)(2,1)S(1)}, u32[]{:S(2)}, u32[]{:S(2)}) collective-permute-start(bf16[16,8,5,64]{3,2,1,0:T(8,128)(2,1)S(1)} %bitcast.125), channel_id=1, source_target_pairs={{0,64},{4,68},{8,72},{12,76},{16,80},{20,84},{24,88},{28,92},{32,9... | collective-permute-start | bytes 245768 | tf_op jit(solution)/shard_map/ppermute | solution.py:65
  39.3 11.9 %collective-permute-start.10 = (bf16[16,8,5,64]{3,2,1,0:T(8,128)(2,1)S(1)}, bf16[16,8,5,64]{3,2,1,0:T(8,128)(2,1)S(1)}, u32[]{:S(2)}, u32[]{:S(2)}) collective-permute-start(bf16[16,8,5,64]{3,2,1,0:T(8,128)(2,1)S(1)} %bitcast.126), channel_id=1, source_target_pairs={{0,128},{4,132},{8,136},{12,140},{16,144},{20,148},{24,152},{28,15... | collective-permute-start | bytes 245768 | tf_op jit(solution)/shard_map/ppermute | solution.py:65
  40.4 13.3 %collective-permute-start.11 = (bf16[16,8,5,64]{3,2,1,0:T(8,128)(2,1)S(1)}, bf16[16,8,5,64]{3,2,1,0:T(8,128)(2,1)S(1)}, u32[]{:S(2)}, u32[]{:S(2)}) collective-permute-start(bf16[16,8,5,64]{3,2,1,0:T(8,128)(2,1)S(1)} %bitcast.127), channel_id=1, source_target_pairs={{0,192},{4,196},{8,200},{12,204},{16,208},{20,212},{24,216},{28,22... | collective-permute-start | bytes 245768 | tf_op jit(solution)/shard_map/ppermute | solution.py:65
  57.3 2.6 %copy-start.4 = (pred[24,512]{1,0:T(8,128)(4,1)S(1)}, pred[24,512]{1,0:T(8,128)(4,1)}, u32[]{:S(2)}) copy-start(pred[24,512]{1,0:T(8,128)(4,1)} %iota_compare_fusion) | copy-start | bytes 36868
  59.6 4.2 %copy-start.10 = (s32[24]{0:T(128)S(1)}, s32[24]{0:T(128)}, u32[]{:S(2)}) copy-start(s32[24]{0:T(128)} %copy-done.9) | copy-start | bytes 292
  66.9 2.1 %collective-permute-start.12 = (f32[16,8,330]{2,1,0:T(8,128)S(1)}, f32[16,8,330]{2,1,0:T(8,128)S(1)}, u32[]{:S(2)}, u32[]{:S(2)}) collective-permute-start(f32[16,8,330]{2,1,0:T(8,128)S(1)} %get-tuple-element.31), channel_id=1, source_target_pairs={{0,4},{4,0},{8,12},{12,8},{16,20},{20,16},{24,28},{28,24},{32,36},... | collective-permute-start | bytes 506888 | tf_op jit(solution)/shard_map/ppermute | solution.py:82
  67.2 7.9 %collective-permute-start.13 = (f32[16,8,330]{2,1,0:T(8,128)S(1)}, f32[16,8,330]{2,1,0:T(8,128)S(1)}, u32[]{:S(2)}, u32[]{:S(2)}) collective-permute-start(f32[16,8,330]{2,1,0:T(8,128)S(1)} %get-tuple-element.33), channel_id=1, source_target_pairs={{0,8},{4,12},{8,0},{12,4},{16,24},{20,28},{24,16},{28,20},{32,40},... | collective-permute-start | bytes 506888 | tf_op jit(solution)/shard_map/ppermute | solution.py:82
  68.3 9.8 %collective-permute-start.14 = (f32[16,8,330]{2,1,0:T(8,128)S(1)}, f32[16,8,330]{2,1,0:T(8,128)S(1)}, u32[]{:S(2)}, u32[]{:S(2)}) collective-permute-start(f32[16,8,330]{2,1,0:T(8,128)S(1)} %get-tuple-element.32), channel_id=1, source_target_pairs={{0,12},{4,8},{8,4},{12,0},{16,28},{20,24},{24,20},{28,16},{32,44},... | collective-permute-start | bytes 506888 | tf_op jit(solution)/shard_map/ppermute | solution.py:82
  84.3 23.8 %copy-start.6 = (f32[8,5]{1,0:T(8,128)S(1)}, f32[8,5]{1,0:T(8,128)}, u32[]{:S(2)}) copy-start(f32[8,5]{1,0:T(8,128)} %get-tuple-element.20) | copy-start | bytes 484
  84.5 7.1 %collective-permute-start.15 = (f32[4,8,330]{2,1,0:T(8,128)S(1)}, f32[4,8,330]{2,1,0:T(8,128)S(1)}, u32[]{:S(2)}, u32[]{:S(2)}) collective-permute-start(f32[4,8,330]{2,1,0:T(8,128)S(1)} %get-tuple-element.35), channel_id=1, source_target_pairs={{0,16},{4,20},{8,24},{12,28},{16,0},{20,4},{24,8},{28,12},{32,48},... | collective-permute-start | bytes 126728 | tf_op jit(solution)/shard_map/ppermute | solution.py:82
  85.8 8.9 %collective-permute-start.16 = (f32[4,8,330]{2,1,0:T(8,128)S(1)}, f32[4,8,330]{2,1,0:T(8,128)S(1)}, u32[]{:S(2)}, u32[]{:S(2)}) collective-permute-start(f32[4,8,330]{2,1,0:T(8,128)S(1)} %get-tuple-element.37), channel_id=1, source_target_pairs={{0,32},{4,36},{8,40},{12,44},{16,48},{20,52},{24,56},{28,60},{32,0... | collective-permute-start | bytes 126728 | tf_op jit(solution)/shard_map/ppermute | solution.py:82
  91.6 6.2 %collective-permute-start.17 = (f32[4,8,330]{2,1,0:T(8,128)S(1)}, f32[4,8,330]{2,1,0:T(8,128)S(1)}, u32[]{:S(2)}, u32[]{:S(2)}) collective-permute-start(f32[4,8,330]{2,1,0:T(8,128)S(1)} %get-tuple-element.36), channel_id=1, source_target_pairs={{0,48},{4,52},{8,56},{12,60},{16,32},{20,36},{24,40},{28,44},{32,1... | collective-permute-start | bytes 126728 | tf_op jit(solution)/shard_map/ppermute | solution.py:82
  98.4 4.8 %collective-permute-start.18 = (f32[1,8,330]{2,1,0:T(8,128)S(1)}, f32[1,8,330]{2,1,0:T(8,128)S(1)}, u32[]{:S(2)}, u32[]{:S(2)}) collective-permute-start(f32[1,8,330]{2,1,0:T(8,128)S(1)} %get-tuple-element.47), channel_id=1, source_target_pairs={{0,64},{4,68},{8,72},{12,76},{16,80},{20,84},{24,88},{28,92},{32,9... | collective-permute-start | bytes 31688 | tf_op jit(solution)/shard_map/ppermute | solution.py:82
  98.5 6.0 %collective-permute-start.19 = (f32[1,8,330]{2,1,0:T(8,128)S(1)}, f32[1,8,330]{2,1,0:T(8,128)S(1)}, u32[]{:S(2)}, u32[]{:S(2)}) collective-permute-start(f32[1,8,330]{2,1,0:T(8,128)S(1)} %get-tuple-element.46), channel_id=1, source_target_pairs={{0,128},{4,132},{8,136},{12,140},{16,144},{20,148},{24,152},{28,15... | collective-permute-start | bytes 31688 | tf_op jit(solution)/shard_map/ppermute | solution.py:82
  102.7 4.9 %collective-permute-start.20 = (f32[1,8,330]{2,1,0:T(8,128)S(1)}, f32[1,8,330]{2,1,0:T(8,128)S(1)}, u32[]{:S(2)}, u32[]{:S(2)}) collective-permute-start(f32[1,8,330]{2,1,0:T(8,128)S(1)} %get-tuple-element.45), channel_id=1, source_target_pairs={{0,192},{4,196},{8,200},{12,204},{16,208},{20,212},{24,216},{28,22... | collective-permute-start | bytes 31688 | tf_op jit(solution)/shard_map/ppermute | solution.py:82
  110.0 6.3 %collective-permute-start.21 = (f32[8,1280]{1,0:T(8,128)S(1)}, f32[8,1280]{1,0:T(8,128)S(1)}, u32[]{:S(2)}, u32[]{:S(2)}) collective-permute-start(f32[8,1280]{1,0:T(8,128)S(1)} %fusion.30), channel_id=1, source_target_pairs={{0,1},{1,0},{2,3},{3,2},{4,5},{5,4},{6,7},{7,6},{8,9},{9,8},{10,11... | collective-permute-start | bytes 122888 | tf_op jit(solution)/shard_map/ppermute | solution.py:43
  110.1 6.2 %collective-permute-start.22 = (f32[8,1280]{1,0:T(8,128)S(1)}, f32[8,1280]{1,0:T(8,128)S(1)}, u32[]{:S(2)}, u32[]{:S(2)}) collective-permute-start(f32[8,1280]{1,0:T(8,128)S(1)} %fusion.30), channel_id=1, source_target_pairs={{0,2},{1,3},{2,0},{3,1},{4,6},{5,7},{6,4},{7,5},{8,10},{9,11},{10,... | collective-permute-start | bytes 122888 | tf_op jit(solution)/shard_map/ppermute | solution.py:43
  111.8 5.2 %collective-permute-start.23 = (f32[8,1280]{1,0:T(8,128)S(1)}, f32[8,1280]{1,0:T(8,128)S(1)}, u32[]{:S(2)}, u32[]{:S(2)}) collective-permute-start(f32[8,1280]{1,0:T(8,128)S(1)} %fusion.30), channel_id=1, source_target_pairs={{0,3},{1,2},{2,1},{3,0},{4,7},{5,6},{6,5},{7,4},{8,11},{9,10},{10,... | collective-permute-start | bytes 122888 | tf_op jit(solution)/shard_map/ppermute | solution.py:43

commit v5 on v4

--- a/solution.py
+++ b/solution.py
@@ -21,6 +21,18 @@
 def scale_heads(summed, factor):
     shaped = summed.reshape(summed.shape[:-1] + (factor.shape[-1], -1))
     return (shaped * factor[..., None]).reshape(summed.shape)
+
+
+def head_spread(heads, width):
+    return (
+        jnp.arange(width, dtype=jnp.int32)[None, :] // HEAD_DIM
+        == jnp.arange(heads, dtype=jnp.int32)[:, None]
+    )
+
+
+def spread_heads(factor, width):
+    spread = head_spread(factor.shape[-1], width).astype(jnp.float32)
+    return jnp.dot(factor, spread, precision=lax.Precision.HIGHEST)
 
 
 def xor_partner(axis, size, bit):
@@ -87,7 +99,7 @@
         top_each = stacked[..., width_acc + heads :]
         top = jnp.max(top_each, axis=0)
         factor = jnp.exp(top_each - top[None])
-        acc = jnp.sum(scale_heads(acc, factor), axis=0)
+        acc = jnp.sum(acc * spread_heads(factor, width_acc), axis=0)
         total = jnp.sum(total * factor, axis=0)
         packed = jnp.concatenate([acc, total, top], axis=-1)
         low += width
@@ -143,13 +155,15 @@
     all_queries = gather_xor(query, "seq").reshape(-1, width_local)
     owner_place = ((page_request // rows) ^ seq_index) * rows + page_request % rows
     pages, page_len = (page_cache.shape[0], page_cache.shape[1])
-    owner_query = all_queries[owner_place].reshape(pages, heads_local, HEAD_DIM)
+    owner_query = all_queries[owner_place]
     keys_scaled = head_norm(page_cache[:, :, 0, :].astype(jnp.float32), score_gain).astype(
         jnp.bfloat16
-    )
-    values_paged = page_cache[:, :, 1, :].reshape(pages, page_len, heads_local, HEAD_DIM)
+    ).reshape(pages, page_len, width_local)
+    values_paged = page_cache[:, :, 1, :]
+    spread = head_spread(heads_local, width_local)
+    query_blocks = jnp.where(spread.T[None], owner_query[:, :, None], jnp.zeros((), jnp.bfloat16))
     scores = jnp.einsum(
-        "sphd,shd->shp", keys_scaled, owner_query, preferred_element_type=jnp.float32
+        "spf,sfh->shp", keys_scaled, query_blocks, preferred_element_type=jnp.float32
     ) / math.sqrt(HEAD_DIM)
     positions = page_number[:, None] * page_len + jnp.arange(page_len, dtype=jnp.int32)[None, :]
     live_mask = positions < lengths[page_request][:, None]
@@ -158,9 +172,10 @@
         jnp.bfloat16
     )
     page_total = jnp.sum(weights.astype(jnp.float32), axis=-1)
-    page_acc = jnp.einsum(
-        "shp,sphd->shd", weights, values_paged, preferred_element_type=jnp.float32
-    ).reshape(pages, width_local)
+    acc_blocks = jnp.einsum(
+        "shp,spf->shf", weights, values_paged, preferred_element_type=jnp.float32
+    )
+    page_acc = jnp.sum(jnp.where(spread[None], acc_blocks, 0.0), axis=1)
 
     requests = lengths.shape[0]
     onehot = owner_place[:, None] == jnp.arange(requests, dtype=jnp.int32)[None, :]

time: 121 us -> 114 us (0.942)
  local copies, waits for them, and re-layouts: 21.4 us -> 10 us
  other arithmetic: 11.1 us -> 19 us
  waiting for transfers between devices: 40.7 us -> 37.5 us
    mul x10 -> x6, local copies, waits for them, and re-layouts: 5.31 us -> 0.46 us  [scale_heads(): return (shaped * factor[..., None]).reshape(summed.shape)]
    mul x2 -> x1, other arithmetic: 0.2 us -> 3.88 us  [head_norm(): shaped * shaped]
    slice x1 -> x0, local copies, waits for them, and re-layouts: 3.67 us -> none  [local(): page_cache[:, :, 1, :].reshape(pages, page_len, heads_local, HEAD_DIM)]
    ppermute x9, waiting for transfers between devices: 16.3 us -> 12.9 us  [gather_xor(): lax.ppermute(held, axis, perm=xor_partner(axis, size, digit << low))]
    convert_element_type x1, other arithmetic: 0.17 us -> 3.48 us  [local(): head_norm(page_cache[:, :, 0, :].astype(jnp.float32), score_gain)]
    reduce_sum x3, other arithmetic: 0.9 us -> 2.86 us  [head_norm(): jnp.mean(shaped * shaped, axis=-1, keepdims=True) + epsilon]
    unnamed x26 -> x32, local copies, waits for them, and re-layouts: 1.89 us -> 0.62 us
    dot_general x2 -> x5, matrix products: 4.91 us -> 5.47 us  [the longest x1 2.35 us: local(): jnp.einsum('shp,spf->shf', weights, values_paged, preferred_element_type=...]
  transfers between devices with their start and end apart: 24 -> 24, of which waited for: 14 -> 15; matrix products, arithmetic and copies ran while one was open for 8% -> 13% of each run, Pallas kernels for 0% -> 0%
where the time goes in v5:
time: 114 us; the launch traced here: 113 us
  starting transfers between devices  38.7 us (34%)
  waiting for transfers between devices  37.5 us (33%)
  other arithmetic  19 us (17%)
  local copies, waits for them, and re-layouts  10 us (9%)
  matrix products  7.83 us (7%)
    ppermute x9, waiting for transfers between devices, scatter_xor(): lax.ppermute(grouped[:, digit], axis, perm=xor_partner(axis, size, digit...  19.7 us
    ppermute x9, starting transfers between devices, gather_xor(): lax.ppermute(held, axis, perm=xor_partner(axis, size, digit << low))  15.4 us
    ppermute x9, starting transfers between devices, scatter_xor(): lax.ppermute(grouped[:, digit], axis, perm=xor_partner(axis, size, digit...  13.8 us
    ppermute x9, waiting for transfers between devices, gather_xor(): lax.ppermute(held, axis, perm=xor_partner(axis, size, digit << low))  12.9 us
    ppermute x6, starting transfers between devices, exchange(): lax.ppermute(held, axis, perm=xor_partner(axis, size, digit << low))  9.44 us
    ppermute x6, waiting for transfers between devices, exchange(): lax.ppermute(held, axis, perm=xor_partner(axis, size, digit << low))  4.87 us
    mul x1, other arithmetic, head_norm(): shaped * shaped  3.88 us
    convert_element_type x1, other arithmetic, local(): head_norm(page_cache[:, :, 0, :].astype(jnp.float32), score_gain)  3.48 us
  transfers between devices with their start and end apart: 24, of which 15 were waited for; matrix products, arithmetic and copies ran while one was open for 13% of the time, Pallas kernels for 0%

profile of v5, /device:TPU:6, one launch (start us, length us, event | category | flops | bytes accessed | tf_op | source)
XLA Modules:
  0.0 113.4 jit_solution(14091431779696270211)
XLA Ops:
  0.0 1.6 %collective-permute-start = (bf16[1,8,320]{2,1,0:T(8,128)(2,1)}, bf16[1,8,320]{2,1,0:T(8,128)(2,1)S(1)}, u32[]{:S(2)}, u32[]{:S(2)}) collective-permute-start(bf16[1,8,320]{2,1,0:T(8,128)(2,1)} %bitcast.178), channel_id=1, source_target_pairs={{0,1},{1,0},{2,3},{3,2},{4,5},{5,4},{6,7},{7,6},{8,9},{9,8},{10,11... | collective-permute-start | bytes 15368 | tf_op jit(solution)/shard_map/ppermute | solution.py:55
  1.6 2.9 %collective-permute-start.1 = (bf16[1,8,320]{2,1,0:T(8,128)(2,1)}, bf16[1,8,320]{2,1,0:T(8,128)(2,1)S(1)}, u32[]{:S(2)}, u32[]{:S(2)}) collective-permute-start(bf16[1,8,320]{2,1,0:T(8,128)(2,1)} %bitcast.179), channel_id=1, source_target_pairs={{0,2},{1,3},{2,0},{3,1},{4,6},{5,7},{6,4},{7,5},{8,10},{9,11},{10,... | collective-permute-start | bytes 15368 | tf_op jit(solution)/shard_map/ppermute | solution.py:55
  5.9 0.8 mul.135
  6.9 2.6 %collective-permute-done.2 = bf16[1,8,320]{2,1,0:T(8,128)(2,1)S(1)} collective-permute-done((bf16[1,8,320]{2,1,0:T(8,128)(2,1)}, bf16[1,8,320]{2,1,0:T(8,128)(2,1)S(1)}, u32[]{:S(2)}, u32[]{:S(2)}) %collective-permute-start.2) | collective-permute-done | bytes 5152 | tf_op jit(solution)/shard_map/ppermute | solution.py:55
  9.5 0.7 maximum_bitcast_fusion.1
  11.0 0.7 fusion.62
  12.7 0.8 multiply_reduce_fusion.1
  13.5 2.0 %collective-permute-start.4 = (bf16[1,8,5,64]{3,2,1,0:T(8,128)(2,1)S(1)}, bf16[1,8,5,64]{3,2,1,0:T(8,128)(2,1)S(1)}, u32[]{:S(2)}, u32[]{:S(2)}) collective-permute-start(bf16[1,8,5,64]{3,2,1,0:T(8,128)(2,1)S(1)} %bitcast.157), channel_id=1, source_target_pairs={{0,8},{4,12},{8,0},{12,4},{16,24},{20,28},{24,16},{28,20},{32,40},... | collective-permute-start | bytes 15368 | tf_op jit(solution)/shard_map/ppermute | solution.py:77
  15.5 3.9 %convert_multiply_fusion = f32[24,128,1,320]{1,3,2,0:T(8,128)} fusion(bf16[24,128,2,320]{1,3,2,0:T(8,128)(2,1)} %param.17), kind=kLoop, calls=%fused_computation.5 | loop fusion | flops 1966080 | bytes 5898240 | tf_op jit(solution)/shard_map/mul | solution.py:17
  19.4 2.7 %reduce_sum.131 = f32[24,128,5]{1,2,0:T(8,128)S(1)} reduce(f32[24,128,5,64]{1,3,2,0:T(8,128)} %bitcast.141, f32[]{:T(128)} %constant.103.clone.1), dimensions={3}, to_apply=%region_1.2 | reduce | flops 967680 | bytes 3993604 | tf_op jit(solution)/shard_map/reduce_sum | solution.py:17
  22.2 0.7 iota_compare_fusion
  22.9 0.7 gather_fusion.1
  23.7 3.4 %collective-permute-start.6 = (bf16[4,8,5,64]{3,2,1,0:T(8,128)(2,1)S(1)}, bf16[4,8,5,64]{3,2,1,0:T(8,128)(2,1)S(1)}, u32[]{:S(2)}, u32[]{:S(2)}) collective-permute-start(bf16[4,8,5,64]{3,2,1,0:T(8,128)(2,1)S(1)} %get-tuple-element.33), channel_id=1, source_target_pairs={{0,16},{4,20},{8,24},{12,28},{16,0},{20,4},{24,8},{28,12},{32,48},... | collective-permute-start | bytes 61448 | tf_op jit(solution)/shard_map/ppermute | solution.py:77
  27.0 5.2 %collective-permute-start.7 = (bf16[4,8,5,64]{3,2,1,0:T(8,128)(2,1)S(1)}, bf16[4,8,5,64]{3,2,1,0:T(8,128)(2,1)S(1)}, u32[]{:S(2)}, u32[]{:S(2)}) collective-permute-start(bf16[4,8,5,64]{3,2,1,0:T(8,128)(2,1)S(1)} %get-tuple-element.33), channel_id=1, source_target_pairs={{0,32},{4,36},{8,40},{12,44},{16,48},{20,52},{24,56},{28,60},{32,0... | collective-permute-start | bytes 61448 | tf_op jit(solution)/shard_map/ppermute | solution.py:77
  32.3 3.5 %fusion.2 = bf16[24,128,320]{1,2,0:T(8,128)(2,1)} fusion(f32[320]{0:T(512)S(1)} %copy-done.8, f32[24,128,5]{1,2,0:T(8,128)S(1)} %add_sqrt_fusion, bf16[24,128,2,320]{1,3,2,0:T(8,128)(2,1)} %param.17), kind=kLoop, calls=%fused_computation.9 | loop fusion | flops 3932160 | bytes 3994880 | tf_op jit(solution)/shard_map/convert_element_type | solution.py:159
  36.1 2.5 %collective-permute-done.8 = bf16[4,8,5,64]{3,2,1,0:T(8,128)(2,1)S(1)} collective-permute-done((bf16[4,8,5,64]{3,2,1,0:T(8,128)(2,1)S(1)}, bf16[4,8,5,64]{3,2,1,0:T(8,128)(2,1)S(1)}, u32[]{:S(2)}, u32[]{:S(2)}) %collective-permute-start.8) | collective-permute-done | bytes 20512 | tf_op jit(solution)/shard_map/ppermute | solution.py:77
  38.7 0.9 collective-permute-start.9
  39.6 1.1 collective-permute-start.10
  40.7 2.8 %collective-permute-start.11 = (bf16[16,8,5,64]{3,2,1,0:T(8,128)(2,1)S(1)}, bf16[16,8,5,64]{3,2,1,0:T(8,128)(2,1)S(1)}, u32[]{:S(2)}, u32[]{:S(2)}) collective-permute-start(bf16[16,8,5,64]{3,2,1,0:T(8,128)(2,1)S(1)} %bitcast.145), channel_id=1, source_target_pairs={{0,192},{4,196},{8,200},{12,204},{16,208},{20,212},{24,216},{28,22... | collective-permute-start | bytes 245768 | tf_op jit(solution)/shard_map/ppermute | solution.py:77
  44.1 3.9 %collective-permute-done.9 = bf16[16,8,5,64]{3,2,1,0:T(8,128)(2,1)S(1)} collective-permute-done((bf16[16,8,5,64]{3,2,1,0:T(8,128)(2,1)S(1)}, bf16[16,8,5,64]{3,2,1,0:T(8,128)(2,1)S(1)}, u32[]{:S(2)}, u32[]{:S(2)}) %collective-permute-start.9) | collective-permute-done | bytes 81952 | tf_op jit(solution)/shard_map/ppermute | solution.py:77
  48.0 3.6 %collective-permute-done.10 = bf16[16,8,5,64]{3,2,1,0:T(8,128)(2,1)S(1)} collective-permute-done((bf16[16,8,5,64]{3,2,1,0:T(8,128)(2,1)S(1)}, bf16[16,8,5,64]{3,2,1,0:T(8,128)(2,1)S(1)}, u32[]{:S(2)}, u32[]{:S(2)}) %collective-permute-start.10) | collective-permute-done | bytes 81952 | tf_op jit(solution)/shard_map/ppermute | solution.py:77
  51.6 2.6 %collective-permute-done.11 = bf16[16,8,5,64]{3,2,1,0:T(8,128)(2,1)S(1)} collective-permute-done((bf16[16,8,5,64]{3,2,1,0:T(8,128)(2,1)S(1)}, bf16[16,8,5,64]{3,2,1,0:T(8,128)(2,1)S(1)}, u32[]{:S(2)}, u32[]{:S(2)}) %collective-permute-start.11) | collective-permute-done | bytes 81952 | tf_op jit(solution)/shard_map/ppermute | solution.py:77
  54.5 1.3 %reshape_reshape.6 = bf16[512,320]{1,0:T(8,128)(2,1)} reshape(bf16[4,16,8,5,64]{4,3,2,1,0:T(8,128)(2,1)S(1)} %pad_maximum_fusion) | data formatting | bytes 655360 | tf_op jit(solution)/shard_map/reshape;reshape | solution.py:155
  55.8 1.8 %gather_fusion.2 = bf16[24,320]{1,0:T(8,128)(2,1)S(1)} fusion(bf16[512,320]{1,0:T(8,128)(2,1)} %reshape_reshape.6, s32[1024]{0:T(1024)} %pad_clamp_fusion), kind=kCustom, calls=%fused_computation.2 | custom fusion | bytes 30816 | tf_op jit(solution)/shard_map/gather | solution.py:158
  57.6 2.0 %select_reduce_fusion.1 = (f32[24,5]{1,0:T(8,128)S(1)}, f32[24,5,128]{2,1,0:T(8,128)S(1)}) fusion(pred[24,128]{1,0:T(8,128)(4,1)S(1)} %add_compare_fusion, bf16[24,128,320]{1,2,0:T(8,128)(2,1)} %fusion.2, pred[320,5]{0,1:T(8,128)(4,1)} %iota_compare_fusion.3, bf16[24,320]{1,0:T(8,128)(2,1)S(1)} %gather_fusion.2), kind=kOutput, calls=%fused_computation.42 | convolution fusion | flops 9914760 | bytes 2048032 | tf_op jit(solution)/shard_map/spf,sfh->shp/dot_general | solution.py:165
  59.7 0.8 select_reduce_fusion
  60.7 0.7 gather_fusion.3
  61.8 2.3 %fusion.5 = f32[24,320]{1,0:T(8,128)S(1)} fusion(pred[5,320]{1,0:T(8,128)(4,1)} %iota_compare_fusion.4, f32[24,5,128]{2,1,0:T(8,128)S(1)} %get-tuple-element.42, f32[24,5]{1,0:T(8,128)S(1)} %get-tuple-element.41, pred[24,128]{1,0:T(8,128)(4,1)S(1)} %add_compare_fusion, bf16[24,128,2,320]{1,3,2,0:T(8,128)(2,1)} %param.17), kind=kOutput, calls=%fused_computation.13 | convolution fusion | flops 9945600 | bytes 2064864 | tf_op jit(solution)/shard_map/shp,spf->shf/dot_general | solution.py:175
  64.9 0.9 pad_maximum_fusion.2
  65.8 1.4 %copy.40 = f32[512,330]{1,0:T(8,128)S(1)} copy(f32[512,330]{0,1:T(8,128)} %pad_maximum_fusion.2) | data formatting | bytes 1351680 | tf_op jit(solution)/shard_map/concatenate | solution.py:189
  67.4 1.1 %collective-permute-start.13 = (f32[16,8,330]{2,1,0:T(8,128)S(1)}, f32[16,8,330]{2,1,0:T(8,128)S(1)}, u32[]{:S(2)}, u32[]{:S(2)}) collective-permute-start(f32[16,8,330]{2,1,0:T(8,128)S(1)} %get-tuple-element.25), channel_id=1, source_target_pairs={{0,8},{4,12},{8,0},{12,4},{16,24},{20,28},{24,16},{28,20},{32,40},... | collective-permute-start | bytes 506888 | tf_op jit(solution)/shard_map/ppermute | solution.py:94
  68.5 0.7 collective-permute-start.14
  69.2 6.0 %collective-permute-done.13 = f32[16,8,330]{2,1,0:T(8,128)S(1)} collective-permute-done((f32[16,8,330]{2,1,0:T(8,128)S(1)}, f32[16,8,330]{2,1,0:T(8,128)S(1)}, u32[]{:S(2)}, u32[]{:S(2)}) %collective-permute-start.13) | collective-permute-done | bytes 168992 | tf_op jit(solution)/shard_map/ppermute | solution.py:94
  75.2 3.1 %collective-permute-done.14 = f32[16,8,330]{2,1,0:T(8,128)S(1)} collective-permute-done((f32[16,8,330]{2,1,0:T(8,128)S(1)}, f32[16,8,330]{2,1,0:T(8,128)S(1)}, u32[]{:S(2)}, u32[]{:S(2)}) %collective-permute-start.14) | collective-permute-done | bytes 168992 | tf_op jit(solution)/shard_map/ppermute | solution.py:94
  79.4 1.3 %collective-permute-start.15 = (f32[4,8,330]{2,1,0:T(8,128)S(1)}, f32[4,8,330]{2,1,0:T(8,128)S(1)}, u32[]{:S(2)}, u32[]{:S(2)}) collective-permute-start(f32[4,8,330]{2,1,0:T(8,128)S(1)} %get-tuple-element.30), channel_id=1, source_target_pairs={{0,16},{4,20},{8,24},{12,28},{16,0},{20,4},{24,8},{28,12},{32,48},... | collective-permute-start | bytes 126728 | tf_op jit(solution)/shard_map/ppermute | solution.py:94
  80.8 5.8 %collective-permute-start.16 = (f32[4,8,330]{2,1,0:T(8,128)S(1)}, f32[4,8,330]{2,1,0:T(8,128)S(1)}, u32[]{:S(2)}, u32[]{:S(2)}) collective-permute-start(f32[4,8,330]{2,1,0:T(8,128)S(1)} %get-tuple-element.29), channel_id=1, source_target_pairs={{0,32},{4,36},{8,40},{12,44},{16,48},{20,52},{24,56},{28,60},{32,0... | collective-permute-start | bytes 126728 | tf_op jit(solution)/shard_map/ppermute | solution.py:94
  86.6 3.1 %collective-permute-done.16 = f32[4,8,330]{2,1,0:T(8,128)S(1)} collective-permute-done((f32[4,8,330]{2,1,0:T(8,128)S(1)}, f32[4,8,330]{2,1,0:T(8,128)S(1)}, u32[]{:S(2)}, u32[]{:S(2)}) %collective-permute-start.16) | collective-permute-done | bytes 42272 | tf_op jit(solution)/shard_map/ppermute | solution.py:94
  89.7 3.0 %collective-permute-done.17 = f32[4,8,330]{2,1,0:T(8,128)S(1)} collective-permute-done((f32[4,8,330]{2,1,0:T(8,128)S(1)}, f32[4,8,330]{2,1,0:T(8,128)S(1)}, u32[]{:S(2)}, u32[]{:S(2)}) %collective-permute-start.17) | collective-permute-done | bytes 42272 | tf_op jit(solution)/shard_map/ppermute | solution.py:94
  93.5 4.2 %collective-permute-start.19 = (f32[1,8,330]{2,1,0:T(8,128)S(1)}, f32[1,8,330]{2,1,0:T(8,128)S(1)}, u32[]{:S(2)}, u32[]{:S(2)}) collective-permute-start(f32[1,8,330]{2,1,0:T(8,128)S(1)} %get-tuple-element.36), channel_id=1, source_target_pairs={{0,128},{4,132},{8,136},{12,140},{16,144},{20,148},{24,152},{28,15... | collective-permute-start | bytes 31688 | tf_op jit(solution)/shard_map/ppermute | solution.py:94
  98.1 1.3 %collective-permute-done.19 = f32[1,8,330]{2,1,0:T(8,128)S(1)} collective-permute-done((f32[1,8,330]{2,1,0:T(8,128)S(1)}, f32[1,8,330]{2,1,0:T(8,128)S(1)}, u32[]{:S(2)}, u32[]{:S(2)}) %collective-permute-start.19) | collective-permute-done | bytes 10592 | tf_op jit(solution)/shard_map/ppermute | solution.py:94
  99.5 3.1 %collective-permute-done.20 = f32[1,8,330]{2,1,0:T(8,128)S(1)} collective-permute-done((f32[1,8,330]{2,1,0:T(8,128)S(1)}, f32[1,8,330]{2,1,0:T(8,128)S(1)}, u32[]{:S(2)}, u32[]{:S(2)}) %collective-permute-start.20) | collective-permute-done | bytes 10592 | tf_op jit(solution)/shard_map/ppermute | solution.py:94
  103.6 0.9 fusion.44
  104.6 1.7 %collective-permute-start.22 = (f32[8,1280]{1,0:T(8,128)S(1)}, f32[8,1280]{1,0:T(8,128)S(1)}, u32[]{:S(2)}, u32[]{:S(2)}) collective-permute-start(f32[8,1280]{1,0:T(8,128)S(1)} %fusion.44), channel_id=1, source_target_pairs={{0,2},{1,3},{2,0},{3,1},{4,6},{5,7},{6,4},{7,5},{8,10},{9,11},{10,... | collective-permute-start | bytes 122888 | tf_op jit(solution)/shard_map/ppermute | solution.py:55
  106.2 3.0 %collective-permute-start.23 = (f32[8,1280]{1,0:T(8,128)S(1)}, f32[8,1280]{1,0:T(8,128)S(1)}, u32[]{:S(2)}, u32[]{:S(2)}) collective-permute-start(f32[8,1280]{1,0:T(8,128)S(1)} %fusion.44), channel_id=1, source_target_pairs={{0,3},{1,2},{2,1},{3,0},{4,7},{5,6},{6,5},{7,4},{8,11},{9,10},{10,... | collective-permute-start | bytes 122888 | tf_op jit(solution)/shard_map/ppermute | solution.py:55
  109.4 0.7 collective-permute-done.22
  110.2 1.3 %collective-permute-done.23 = f32[8,1280]{1,0:T(8,128)S(1)} collective-permute-done((f32[8,1280]{1,0:T(8,128)S(1)}, f32[8,1280]{1,0:T(8,128)S(1)}, u32[]{:S(2)}, u32[]{:S(2)}) %collective-permute-start.23) | collective-permute-done | bytes 40992 | tf_op jit(solution)/shard_map/ppermute | solution.py:55
  111.5 0.7 gather_fusion.4
  112.7 0.7 fusion.37
  (119 shorter events, 10.3 us)
Async XLA Ops:
  0.0 11.0 %copy-start = (bf16[1280,3,320]{0,2,1:T(8,128)(2,1)S(1)}, bf16[1280,3,320]{0,2,1:T(8,128)(2,1)}, u32[]{:S(2)}) copy-start(bf16[1280,3,320]{0,2,1:T(8,128)(2,1)} %param.10) | copy-start | bytes 7372804
  0.0 6.7 %collective-permute-start = (bf16[1,8,320]{2,1,0:T(8,128)(2,1)}, bf16[1,8,320]{2,1,0:T(8,128)(2,1)S(1)}, u32[]{:S(2)}, u32[]{:S(2)}) collective-permute-start(bf16[1,8,320]{2,1,0:T(8,128)(2,1)} %bitcast.178), channel_id=1, source_target_pairs={{0,1},{1,0},{2,3},{3,2},{4,5},{5,4},{6,7},{7,6},{8,9},{9,8},{10,11... | collective-permute-start | bytes 15368 | tf_op jit(solution)/shard_map/ppermute | solution.py:55
  1.6 5.3 %collective-permute-start.1 = (bf16[1,8,320]{2,1,0:T(8,128)(2,1)}, bf16[1,8,320]{2,1,0:T(8,128)(2,1)S(1)}, u32[]{:S(2)}, u32[]{:S(2)}) collective-permute-start(bf16[1,8,320]{2,1,0:T(8,128)(2,1)} %bitcast.179), channel_id=1, source_target_pairs={{0,2},{1,3},{2,0},{3,1},{4,6},{5,7},{6,4},{7,5},{8,10},{9,11},{10,... | collective-permute-start | bytes 15368 | tf_op jit(solution)/shard_map/ppermute | solution.py:55
  4.5 5.1 %collective-permute-start.2 = (bf16[1,8,320]{2,1,0:T(8,128)(2,1)}, bf16[1,8,320]{2,1,0:T(8,128)(2,1)S(1)}, u32[]{:S(2)}, u32[]{:S(2)}) collective-permute-start(bf16[1,8,320]{2,1,0:T(8,128)(2,1)} %bitcast.180), channel_id=1, source_target_pairs={{0,3},{1,2},{2,1},{3,0},{4,7},{5,6},{6,5},{7,4},{8,11},{9,10},{10,... | collective-permute-start | bytes 15368 | tf_op jit(solution)/shard_map/ppermute | solution.py:55
  4.7 0.6 copy-start.4
  5.9 5.9 %copy-start.9 = (s32[1024]{0:T(1024)}, s32[1024]{0:T(1024)S(1)}, u32[]{:S(2)}) copy-start(s32[1024]{0:T(1024)S(1)} %pad_clamp_fusion.2) | copy-start | bytes 12292
  5.9 6.6 %copy-start.10 = (pred[4]{0:T(512)(128)(4,1)}, pred[4]{0:T(512)(128)(4,1)S(1)}, u32[]{:S(2)}) copy-start(pred[4]{0:T(512)(128)(4,1)S(1)} %compare_and_fusion) | copy-start | bytes 16
  11.7 0.6 copy-start.3
  13.5 8.7 %copy-start.15 = (s32[24]{0:T(128)S(1)}, s32[24]{0:T(128)}, u32[]{:S(2)}) copy-start(s32[24]{0:T(128)} %param.16) | copy-start | bytes 292
  13.5 8.7 %copy-start.14 = (s32[24]{0:T(128)S(1)}, s32[24]{0:T(128)}, u32[]{:S(2)}) copy-start(s32[24]{0:T(128)} %param.15) | copy-start | bytes 292
  13.5 9.4 %copy-start.1 = (s32[512]{0:T(512)S(1)}, s32[512]{0:T(512)}, u32[]{:S(2)}) copy-start(s32[512]{0:T(512)} %param.14) | copy-start | bytes 6148
  13.5 10.1 %collective-permute-start.3 = (bf16[1,8,5,64]{3,2,1,0:T(8,128)(2,1)S(1)}, bf16[1,8,5,64]{3,2,1,0:T(8,128)(2,1)S(1)}, u32[]{:S(2)}, u32[]{:S(2)}) collective-permute-start(bf16[1,8,5,64]{3,2,1,0:T(8,128)(2,1)S(1)} %bitcast.156), channel_id=1, source_target_pairs={{0,4},{4,0},{8,12},{12,8},{16,20},{20,16},{24,28},{28,24},{32,36},... | collective-permute-start | bytes 15368 | tf_op jit(solution)/shard_map/ppermute | solution.py:77
  13.5 10.1 %collective-permute-start.4 = (bf16[1,8,5,64]{3,2,1,0:T(8,128)(2,1)S(1)}, bf16[1,8,5,64]{3,2,1,0:T(8,128)(2,1)S(1)}, u32[]{:S(2)}, u32[]{:S(2)}) collective-permute-start(bf16[1,8,5,64]{3,2,1,0:T(8,128)(2,1)S(1)} %bitcast.157), channel_id=1, source_target_pairs={{0,8},{4,12},{8,0},{12,4},{16,24},{20,28},{24,16},{28,20},{32,40},... | collective-permute-start | bytes 15368 | tf_op jit(solution)/shard_map/ppermute | solution.py:77
  15.5 8.1 %collective-permute-start.5 = (bf16[1,8,5,64]{3,2,1,0:T(8,128)(2,1)S(1)}, bf16[1,8,5,64]{3,2,1,0:T(8,128)(2,1)S(1)}, u32[]{:S(2)}, u32[]{:S(2)}) collective-permute-start(bf16[1,8,5,64]{3,2,1,0:T(8,128)(2,1)S(1)} %bitcast.158), channel_id=1, source_target_pairs={{0,12},{4,8},{8,4},{12,0},{16,28},{20,24},{24,20},{28,16},{32,44},... | collective-permute-start | bytes 15368 | tf_op jit(solution)/shard_map/ppermute | solution.py:77
  19.4 12.9 %copy-start.8 = (f32[320]{0:T(512)S(1)}, f32[320]{0:T(512)}, u32[]{:S(2)}) copy-start(f32[320]{0:T(512)} %param.12) | copy-start | bytes 3844
  22.2 0.7 copy-start.12
  23.7 12.1 %collective-permute-start.6 = (bf16[4,8,5,64]{3,2,1,0:T(8,128)(2,1)S(1)}, bf16[4,8,5,64]{3,2,1,0:T(8,128)(2,1)S(1)}, u32[]{:S(2)}, u32[]{:S(2)}) collective-permute-start(bf16[4,8,5,64]{3,2,1,0:T(8,128)(2,1)S(1)} %get-tuple-element.33), channel_id=1, source_target_pairs={{0,16},{4,20},{8,24},{12,28},{16,0},{20,4},{24,8},{28,12},{32,48},... | collective-permute-start | bytes 61448 | tf_op jit(solution)/shard_map/ppermute | solution.py:77
  27.0 9.1 %collective-permute-start.7 = (bf16[4,8,5,64]{3,2,1,0:T(8,128)(2,1)S(1)}, bf16[4,8,5,64]{3,2,1,0:T(8,128)(2,1)S(1)}, u32[]{:S(2)}, u32[]{:S(2)}) collective-permute-start(bf16[4,8,5,64]{3,2,1,0:T(8,128)(2,1)S(1)} %get-tuple-element.33), channel_id=1, source_target_pairs={{0,32},{4,36},{8,40},{12,44},{16,48},{20,52},{24,56},{28,60},{32,0... | collective-permute-start | bytes 61448 | tf_op jit(solution)/shard_map/ppermute | solution.py:77
  32.2 6.4 %collective-permute-start.8 = (bf16[4,8,5,64]{3,2,1,0:T(8,128)(2,1)S(1)}, bf16[4,8,5,64]{3,2,1,0:T(8,128)(2,1)S(1)}, u32[]{:S(2)}, u32[]{:S(2)}) collective-permute-start(bf16[4,8,5,64]{3,2,1,0:T(8,128)(2,1)S(1)} %get-tuple-element.33), channel_id=1, source_target_pairs={{0,48},{4,52},{8,56},{12,60},{16,32},{20,36},{24,40},{28,44},{32,1... | collective-permute-start | bytes 61448 | tf_op jit(solution)/shard_map/ppermute | solution.py:77
  38.7 9.3 %collective-permute-start.9 = (bf16[16,8,5,64]{3,2,1,0:T(8,128)(2,1)S(1)}, bf16[16,8,5,64]{3,2,1,0:T(8,128)(2,1)S(1)}, u32[]{:S(2)}, u32[]{:S(2)}) collective-permute-start(bf16[16,8,5,64]{3,2,1,0:T(8,128)(2,1)S(1)} %bitcast.143), channel_id=1, source_target_pairs={{0,64},{4,68},{8,72},{12,76},{16,80},{20,84},{24,88},{28,92},{32,9... | collective-permute-start | bytes 245768 | tf_op jit(solution)/shard_map/ppermute | solution.py:77
  39.6 12.0 %collective-permute-start.10 = (bf16[16,8,5,64]{3,2,1,0:T(8,128)(2,1)S(1)}, bf16[16,8,5,64]{3,2,1,0:T(8,128)(2,1)S(1)}, u32[]{:S(2)}, u32[]{:S(2)}) collective-permute-start(bf16[16,8,5,64]{3,2,1,0:T(8,128)(2,1)S(1)} %bitcast.144), channel_id=1, source_target_pairs={{0,128},{4,132},{8,136},{12,140},{16,144},{20,148},{24,152},{28,15... | collective-permute-start | bytes 245768 | tf_op jit(solution)/shard_map/ppermute | solution.py:77
  40.7 13.4 %collective-permute-start.11 = (bf16[16,8,5,64]{3,2,1,0:T(8,128)(2,1)S(1)}, bf16[16,8,5,64]{3,2,1,0:T(8,128)(2,1)S(1)}, u32[]{:S(2)}, u32[]{:S(2)}) collective-permute-start(bf16[16,8,5,64]{3,2,1,0:T(8,128)(2,1)S(1)} %bitcast.145), channel_id=1, source_target_pairs={{0,192},{4,196},{8,200},{12,204},{16,208},{20,212},{24,216},{28,22... | collective-permute-start | bytes 245768 | tf_op jit(solution)/shard_map/ppermute | solution.py:77
  55.8 8.3 %copy-start.13 = (s32[24]{0:T(128)S(1)}, s32[24]{0:T(128)}, u32[]{:S(2)}) copy-start(s32[24]{0:T(128)} %copy-done.12) | copy-start | bytes 292
  64.2 14.4 %copy-start.5 = (s32[320]{0:T(512)S(1)}, s32[320]{0:T(512)}, u32[]{:S(2)}) copy-start(s32[320]{0:T(512)} %copy-done.4) | copy-start | bytes 3844
  67.2 35.9 %copy-start.6 = (f32[8,5]{1,0:T(8,128)S(1)}, f32[8,5]{1,0:T(8,128)}, u32[]{:S(2)}) copy-start(f32[8,5]{1,0:T(8,128)} %get-tuple-element.20) | copy-start | bytes 484
  67.2 42.1 %copy-start.7 = (f32[1280]{0:T(1024)S(1)}, f32[1280]{0:T(1024)}, u32[]{:S(2)}) copy-start(f32[1280]{0:T(1024)} %param.13) | copy-start | bytes 15364
  67.2 36.4 %copy-start.2 = (bf16[320,1280]{1,0:T(8,128)(2,1)S(1)}, bf16[320,1280]{1,0:T(8,128)(2,1)}, u32[]{:S(2)}) copy-start(bf16[320,1280]{1,0:T(8,128)(2,1)} %param.11) | copy-start | bytes 2457604
  67.2 44.9 %copy-start.11 = (pred[4]{0:T(512)(128)(4,1)S(1)}, pred[4]{0:T(512)(128)(4,1)}, u32[]{:S(2)}) copy-start(pred[4]{0:T(512)(128)(4,1)} %copy-done.10) | copy-start | bytes 16
  67.3 2.0 %collective-permute-start.12 = (f32[16,8,330]{2,1,0:T(8,128)S(1)}, f32[16,8,330]{2,1,0:T(8,128)S(1)}, u32[]{:S(2)}, u32[]{:S(2)}) collective-permute-start(f32[16,8,330]{2,1,0:T(8,128)S(1)} %get-tuple-element.26), channel_id=1, source_target_pairs={{0,4},{4,0},{8,12},{12,8},{16,20},{20,16},{24,28},{28,24},{32,36},... | collective-permute-start | bytes 506888 | tf_op jit(solution)/shard_map/ppermute | solution.py:94
  67.4 7.9 %collective-permute-start.13 = (f32[16,8,330]{2,1,0:T(8,128)S(1)}, f32[16,8,330]{2,1,0:T(8,128)S(1)}, u32[]{:S(2)}, u32[]{:S(2)}) collective-permute-start(f32[16,8,330]{2,1,0:T(8,128)S(1)} %get-tuple-element.25), channel_id=1, source_target_pairs={{0,8},{4,12},{8,0},{12,4},{16,24},{20,28},{24,16},{28,20},{32,40},... | collective-permute-start | bytes 506888 | tf_op jit(solution)/shard_map/ppermute | solution.py:94
  68.5 9.8 %collective-permute-start.14 = (f32[16,8,330]{2,1,0:T(8,128)S(1)}, f32[16,8,330]{2,1,0:T(8,128)S(1)}, u32[]{:S(2)}, u32[]{:S(2)}) collective-permute-start(f32[16,8,330]{2,1,0:T(8,128)S(1)} %get-tuple-element.27), channel_id=1, source_target_pairs={{0,12},{4,8},{8,4},{12,0},{16,28},{20,24},{24,20},{28,16},{32,44},... | collective-permute-start | bytes 506888 | tf_op jit(solution)/shard_map/ppermute | solution.py:94
  79.4 7.1 %collective-permute-start.15 = (f32[4,8,330]{2,1,0:T(8,128)S(1)}, f32[4,8,330]{2,1,0:T(8,128)S(1)}, u32[]{:S(2)}, u32[]{:S(2)}) collective-permute-start(f32[4,8,330]{2,1,0:T(8,128)S(1)} %get-tuple-element.30), channel_id=1, source_target_pairs={{0,16},{4,20},{8,24},{12,28},{16,0},{20,4},{24,8},{28,12},{32,48},... | collective-permute-start | bytes 126728 | tf_op jit(solution)/shard_map/ppermute | solution.py:94
  80.8 8.9 %collective-permute-start.16 = (f32[4,8,330]{2,1,0:T(8,128)S(1)}, f32[4,8,330]{2,1,0:T(8,128)S(1)}, u32[]{:S(2)}, u32[]{:S(2)}) collective-permute-start(f32[4,8,330]{2,1,0:T(8,128)S(1)} %get-tuple-element.29), channel_id=1, source_target_pairs={{0,32},{4,36},{8,40},{12,44},{16,48},{20,52},{24,56},{28,60},{32,0... | collective-permute-start | bytes 126728 | tf_op jit(solution)/shard_map/ppermute | solution.py:94
  86.5 6.2 %collective-permute-start.17 = (f32[4,8,330]{2,1,0:T(8,128)S(1)}, f32[4,8,330]{2,1,0:T(8,128)S(1)}, u32[]{:S(2)}, u32[]{:S(2)}) collective-permute-start(f32[4,8,330]{2,1,0:T(8,128)S(1)} %get-tuple-element.31), channel_id=1, source_target_pairs={{0,48},{4,52},{8,56},{12,60},{16,32},{20,36},{24,40},{28,44},{32,1... | collective-permute-start | bytes 126728 | tf_op jit(solution)/shard_map/ppermute | solution.py:94
  93.4 4.8 %collective-permute-start.18 = (f32[1,8,330]{2,1,0:T(8,128)S(1)}, f32[1,8,330]{2,1,0:T(8,128)S(1)}, u32[]{:S(2)}, u32[]{:S(2)}) collective-permute-start(f32[1,8,330]{2,1,0:T(8,128)S(1)} %get-tuple-element.37), channel_id=1, source_target_pairs={{0,64},{4,68},{8,72},{12,76},{16,80},{20,84},{24,88},{28,92},{32,9... | collective-permute-start | bytes 31688 | tf_op jit(solution)/shard_map/ppermute | solution.py:94
  93.5 6.0 %collective-permute-start.19 = (f32[1,8,330]{2,1,0:T(8,128)S(1)}, f32[1,8,330]{2,1,0:T(8,128)S(1)}, u32[]{:S(2)}, u32[]{:S(2)}) collective-permute-start(f32[1,8,330]{2,1,0:T(8,128)S(1)} %get-tuple-element.36), channel_id=1, source_target_pairs={{0,128},{4,132},{8,136},{12,140},{16,144},{20,148},{24,152},{28,15... | collective-permute-start | bytes 31688 | tf_op jit(solution)/shard_map/ppermute | solution.py:94
  97.7 4.9 %collective-permute-start.20 = (f32[1,8,330]{2,1,0:T(8,128)S(1)}, f32[1,8,330]{2,1,0:T(8,128)S(1)}, u32[]{:S(2)}, u32[]{:S(2)}) collective-permute-start(f32[1,8,330]{2,1,0:T(8,128)S(1)} %get-tuple-element.35), channel_id=1, source_target_pairs={{0,192},{4,196},{8,200},{12,204},{16,208},{20,212},{24,216},{28,22... | collective-permute-start | bytes 31688 | tf_op jit(solution)/shard_map/ppermute | solution.py:94
  104.5 4.9 %collective-permute-start.21 = (f32[8,1280]{1,0:T(8,128)S(1)}, f32[8,1280]{1,0:T(8,128)S(1)}, u32[]{:S(2)}, u32[]{:S(2)}) collective-permute-start(f32[8,1280]{1,0:T(8,128)S(1)} %fusion.44), channel_id=1, source_target_pairs={{0,1},{1,0},{2,3},{3,2},{4,5},{5,4},{6,7},{7,6},{8,9},{9,8},{10,11... | collective-permute-start | bytes 122888 | tf_op jit(solution)/shard_map/ppermute | solution.py:55
  104.6 5.6 %collective-permute-start.22 = (f32[8,1280]{1,0:T(8,128)S(1)}, f32[8,1280]{1,0:T(8,128)S(1)}, u32[]{:S(2)}, u32[]{:S(2)}) collective-permute-start(f32[8,1280]{1,0:T(8,128)S(1)} %fusion.44), channel_id=1, source_target_pairs={{0,2},{1,3},{2,0},{3,1},{4,6},{5,7},{6,4},{7,5},{8,10},{9,11},{10,... | collective-permute-start | bytes 122888 | tf_op jit(solution)/shard_map/ppermute | solution.py:55
  106.2 5.2 %collective-permute-start.23 = (f32[8,1280]{1,0:T(8,128)S(1)}, f32[8,1280]{1,0:T(8,128)S(1)}, u32[]{:S(2)}, u32[]{:S(2)}) collective-permute-start(f32[8,1280]{1,0:T(8,128)S(1)} %fusion.44), channel_id=1, source_target_pairs={{0,3},{1,2},{2,1},{3,0},{4,7},{5,6},{6,5},{7,4},{8,11},{9,10},{10,... | collective-permute-start | bytes 122888 | tf_op jit(solution)/shard_map/ppermute | solution.py:55

commit v6 on v5

--- a/solution.py
+++ b/solution.py
@@ -15,7 +15,7 @@
 def head_norm(values, gain):
     shaped = values.reshape(values.shape[:-1] + (-1, HEAD_DIM))
     normed = shaped / jnp.sqrt(jnp.mean(shaped * shaped, axis=-1, keepdims=True) + epsilon)
-    return normed * gain.reshape(-1, HEAD_DIM)
+    return (normed * gain.reshape(-1, HEAD_DIM)).reshape(values.shape)
 
 
 def scale_heads(summed, factor):
@@ -141,11 +141,10 @@
         jnp.bfloat16
     )
     value_own = projected[:, 2 * width_local :].astype(jnp.bfloat16)
-    own_score = jnp.sum(
-        (query.astype(jnp.float32) * key_new.astype(jnp.float32)).reshape(
-            rows, heads_local, HEAD_DIM
-        ),
-        axis=-1,
+    own_score = jnp.dot(
+        query.astype(jnp.float32) * key_new.astype(jnp.float32),
+        head_spread(heads_local, width_local).T.astype(jnp.float32),
+        precision=lax.Precision.HIGHEST,
     ) / math.sqrt(HEAD_DIM)
 
     query, page_cache, page_request, page_number, lengths = lax.optimization_barrier(
@@ -155,7 +154,11 @@
     all_queries = gather_xor(query, "seq").reshape(-1, width_local)
     owner_place = ((page_request // rows) ^ seq_index) * rows + page_request % rows
     pages, page_len = (page_cache.shape[0], page_cache.shape[1])
-    owner_query = all_queries[owner_place]
+    requests = lengths.shape[0]
+    onehot = owner_place[:, None] == jnp.arange(requests, dtype=jnp.int32)[None, :]
+    owner_query = jnp.dot(
+        onehot.astype(jnp.bfloat16), all_queries, preferred_element_type=jnp.float32
+    ).astype(jnp.bfloat16)
     keys_scaled = head_norm(page_cache[:, :, 0, :].astype(jnp.float32), score_gain).astype(
         jnp.bfloat16
     ).reshape(pages, page_len, width_local)
@@ -177,14 +180,12 @@
     )
     page_acc = jnp.sum(jnp.where(spread[None], acc_blocks, 0.0), axis=1)
 
-    requests = lengths.shape[0]
-    onehot = owner_place[:, None] == jnp.arange(requests, dtype=jnp.int32)[None, :]
     request_max = jnp.max(jnp.where(onehot[:, :, None], page_max[:, None, :], far_below), axis=0)
     factor = jnp.exp(page_max - request_max[owner_place])
     selector = onehot.astype(jnp.float32)
     request_total = jnp.dot(selector.T, page_total * factor, precision=lax.Precision.HIGHEST)
     request_acc = jnp.dot(
-        selector.T, scale_heads(page_acc, factor), precision=lax.Precision.HIGHEST
+        selector.T, page_acc * spread_heads(factor, width_local), precision=lax.Precision.HIGHEST
     )
     packed = jnp.concatenate([request_acc, request_total, request_max], axis=1)
     packed = packed.reshape(lax.axis_size("seq"), rows, packed.shape[-1])
@@ -195,15 +196,11 @@
     final_max = jnp.maximum(home_max, own_score)
     stored_factor = jnp.exp(home_max - final_max)
     total_stored = home_total * stored_factor
-    stored = scale_heads(home_acc, stored_factor)
+    stored = home_acc * spread_heads(stored_factor, width_local)
     own_factor = jnp.exp(own_score - final_max)
     total = total_stored + own_factor
-    summed = stored + scale_heads(value_own.astype(jnp.float32), own_factor)
-    attended = (
-        (summed.reshape(rows, heads_local, HEAD_DIM) / total[..., None])
-        .reshape(rows, width_local)
-        .astype(jnp.bfloat16)
-    )
+    summed = stored + value_own.astype(jnp.float32) * spread_heads(own_factor, width_local)
+    attended = (summed / spread_heads(total, width_local)).astype(jnp.bfloat16)
     partial_out = jnp.dot(attended, output_weight, preferred_element_type=jnp.float32)
     attn_out = sum_radix(partial_out, "tensor")
     width = attn_out.shape[1]

time: 114 us -> 99.9 us (0.88)
  waiting for transfers between devices: 37.5 us -> 27.1 us
  starting transfers between devices: 38.7 us -> 35.7 us
  local copies, waits for them, and re-layouts: 10 us -> 8.35 us
    ppermute x9, waiting for transfers between devices: 19.7 us -> 13.4 us  [scatter_xor(): lax.ppermute(grouped[:, digit], axis, perm=xor_partner(axis, size, digit...]
    ppermute x9, waiting for transfers between devices: 12.9 us -> 6.91 us  [gather_xor(): lax.ppermute(held, axis, perm=xor_partner(axis, size, digit << low))]
    another operation x3, other arithmetic: 0.07 us -> 2.03 us  [scatter_xor(): stacked = jnp.stack(pieces)]
    ppermute x6, waiting for transfers between devices: 4.87 us -> 6.74 us  [exchange(): lax.ppermute(held, axis, perm=xor_partner(axis, size, digit << low))]
    gather x1 -> x0, local copies, waits for them, and re-layouts: 1.78 us -> none  [local(): owner_query = all_queries[owner_place]]
    dot_general x1, matrix products: 2.04 us -> 0.5 us  [local(): jnp.einsum('spf,sfh->shp', keys_scaled, query_blocks, preferred_element_t...]
    another operation x2, local copies, waits for them, and re-layouts: 0.07 us -> 1.47 us  [scatter_xor(): stacked = jnp.stack(pieces)]
    mul x1 -> x3, other arithmetic: 3.88 us -> 5.24 us  [head_norm(): shaped * shaped]
  transfers between devices with their start and end apart: 24 -> 24, of which waited for: 15 -> 12; matrix products, arithmetic and copies ran while one was open for 13% -> 15% of each run, Pallas kernels for 0% -> 0%
where the time goes in v6:
time: 99.9 us; the launch traced here: 98.5 us
  starting transfers between devices  35.7 us (36%)
  waiting for transfers between devices  27.1 us (27%)
  other arithmetic  19.4 us (19%)
  local copies, waits for them, and re-layouts  8.35 us (8%)
  matrix products  7.51 us (8%)
    ppermute x9, starting transfers between devices, gather_xor(): lax.ppermute(held, axis, perm=xor_partner(axis, size, digit << low))  15 us
    ppermute x9, waiting for transfers between devices, scatter_xor(): lax.ppermute(grouped[:, digit], axis, perm=xor_partner(axis, size, digit...  13.4 us
    ppermute x9, starting transfers between devices, scatter_xor(): lax.ppermute(grouped[:, digit], axis, perm=xor_partner(axis, size, digit...  12.5 us
    ppermute x6, starting transfers between devices, exchange(): lax.ppermute(held, axis, perm=xor_partner(axis, size, digit << low))  8.24 us
    ppermute x9, waiting for transfers between devices, gather_xor(): lax.ppermute(held, axis, perm=xor_partner(axis, size, digit << low))  6.91 us
    ppermute x6, waiting for transfers between devices, exchange(): lax.ppermute(held, axis, perm=xor_partner(axis, size, digit << low))  6.74 us
    mul x3, other arithmetic, head_norm(): shaped * shaped  5.24 us
    reduce_sum x3, other arithmetic, head_norm(): jnp.mean(shaped * shaped, axis=-1, keepdims=True) + epsilon  4.23 us
  transfers between devices with their start and end apart: 24, of which 12 were waited for; matrix products, arithmetic and copies ran while one was open for 15% of the time, Pallas kernels for 0%

profile of v6, /device:TPU:6, one launch (start us, length us, event | category | flops | bytes accessed | tf_op | source)
XLA Modules:
  0.0 98.5 jit_solution(5704224125946381912)
XLA Ops:
  0.0 3.0 %collective-permute-start.2 = (bf16[1,8,320]{2,1,0:T(8,128)(2,1)}, bf16[1,8,320]{2,1,0:T(8,128)(2,1)S(1)}, u32[]{:S(2)}, u32[]{:S(2)}) collective-permute-start(bf16[1,8,320]{2,1,0:T(8,128)(2,1)} %bitcast.174), channel_id=1, source_target_pairs={{0,3},{1,2},{2,1},{3,0},{4,7},{5,6},{6,5},{7,4},{8,11},{9,10},{10,... | collective-permute-start | bytes 15368 | tf_op jit(solution)/shard_map/ppermute | solution.py:55
  4.2 0.9 collective-permute-done.2
  5.1 3.3 %collective-permute-done.1 = bf16[1,8,320]{2,1,0:T(8,128)(2,1)S(1)} collective-permute-done((bf16[1,8,320]{2,1,0:T(8,128)(2,1)}, bf16[1,8,320]{2,1,0:T(8,128)(2,1)S(1)}, u32[]{:S(2)}, u32[]{:S(2)}) %collective-permute-start.1) | collective-permute-done | bytes 5152 | tf_op jit(solution)/shard_map/ppermute | solution.py:55
  8.4 0.7 maximum_bitcast_fusion.1
  9.9 0.7 fusion.71
  11.0 1.4 %slice_multiply_fusion.6 = (f32[8,320]{1,0:T(8,128)}, bf16[8,320]{1,0:T(8,128)(2,1)S(1)}) fusion(f32[8,960]{1,0:T(8,128)S(1)} %fusion.71, f32[320]{0:T(512)} %param.12, f32[8,320]{1,0:T(8,128)S(1)} %div.143), kind=kLoop, calls=%fused_computation.116 | loop fusion | flops 10240 | bytes 47360 | tf_op jit(solution)/shard_map/mul | solution.py:17
  12.4 2.0 %collective-permute-start.4 = (bf16[1,8,320]{2,1,0:T(8,128)(2,1)S(1)}, bf16[1,8,320]{2,1,0:T(8,128)(2,1)S(1)}, u32[]{:S(2)}, u32[]{:S(2)}) collective-permute-start(bf16[1,8,320]{2,1,0:T(8,128)(2,1)S(1)} %bitcast.166), channel_id=1, source_target_pairs={{0,8},{4,12},{8,0},{12,4},{16,24},{20,28},{24,16},{28,20},{32,40},... | collective-permute-start | bytes 15368 | tf_op jit(solution)/shard_map/ppermute | solution.py:77
  14.5 3.9 %convert_multiply_fusion = f32[24,128,1,320]{1,3,2,0:T(8,128)} fusion(bf16[24,128,2,320]{1,3,2,0:T(8,128)(2,1)} %param.17), kind=kLoop, calls=%fused_computation.4 | loop fusion | flops 1966080 | bytes 5898240 | tf_op jit(solution)/shard_map/mul | solution.py:17
  18.3 2.7 %reduce_sum.122 = f32[24,128,5]{1,2,0:T(8,128)S(1)} reduce(f32[24,128,5,64]{1,3,2,0:T(8,128)} %bitcast.144, f32[]{:T(128)} %constant.113.clone.1), dimensions={3}, to_apply=%region_1.2 | reduce | flops 967680 | bytes 3993604 | tf_op jit(solution)/shard_map/reduce_sum | solution.py:17
  21.2 0.7 gather_fusion.1
  22.0 6.2 %collective-permute-start.8 = (bf16[4,8,320]{2,1,0:T(8,128)(2,1)S(1)}, bf16[4,8,320]{2,1,0:T(8,128)(2,1)S(1)}, u32[]{:S(2)}, u32[]{:S(2)}) collective-permute-start(bf16[4,8,320]{2,1,0:T(8,128)(2,1)S(1)} %get-tuple-element.34), channel_id=1, source_target_pairs={{0,48},{4,52},{8,56},{12,60},{16,32},{20,36},{24,40},{28,44},{32,1... | collective-permute-start | bytes 61448 | tf_op jit(solution)/shard_map/ppermute | solution.py:77
  28.2 1.0 %collective-permute-start.7 = (bf16[4,8,320]{2,1,0:T(8,128)(2,1)S(1)}, bf16[4,8,320]{2,1,0:T(8,128)(2,1)S(1)}, u32[]{:S(2)}, u32[]{:S(2)}) collective-permute-start(bf16[4,8,320]{2,1,0:T(8,128)(2,1)S(1)} %get-tuple-element.34), channel_id=1, source_target_pairs={{0,32},{4,36},{8,40},{12,44},{16,48},{20,52},{24,56},{28,60},{32,0... | collective-permute-start | bytes 61448 | tf_op jit(solution)/shard_map/ppermute | solution.py:77
  29.2 1.5 %collective-permute-start.6 = (bf16[4,8,320]{2,1,0:T(8,128)(2,1)S(1)}, bf16[4,8,320]{2,1,0:T(8,128)(2,1)S(1)}, u32[]{:S(2)}, u32[]{:S(2)}) collective-permute-start(bf16[4,8,320]{2,1,0:T(8,128)(2,1)S(1)} %get-tuple-element.34), channel_id=1, source_target_pairs={{0,16},{4,20},{8,24},{12,28},{16,0},{20,4},{24,8},{28,12},{32,48},... | collective-permute-start | bytes 61448 | tf_op jit(solution)/shard_map/ppermute | solution.py:77
  30.7 2.2 %fusion.2 = bf16[24,128,320]{1,2,0:T(8,128)(2,1)S(1)} fusion(f32[320]{0:T(512)S(1)} %copy-done.6, f32[24,128,5]{1,2,0:T(8,128)S(1)} %add_sqrt_fusion, bf16[24,128,2,320]{1,3,2,0:T(8,128)(2,1)} %param.17), kind=kLoop, calls=%fused_computation.8 | loop fusion | flops 3932160 | bytes 3994880 | tf_op jit(solution)/shard_map/convert_element_type | solution.py:162
  32.9 3.3 %collective-permute-done.7 = bf16[4,8,320]{2,1,0:T(8,128)(2,1)S(1)} collective-permute-done((bf16[4,8,320]{2,1,0:T(8,128)(2,1)S(1)}, bf16[4,8,320]{2,1,0:T(8,128)(2,1)S(1)}, u32[]{:S(2)}, u32[]{:S(2)}) %collective-permute-start.7) | collective-permute-done | bytes 20512 | tf_op jit(solution)/shard_map/ppermute | solution.py:77
  36.8 2.4 %collective-permute-start.10 = (bf16[16,8,320]{2,1,0:T(8,128)(2,1)S(1)}, bf16[16,8,320]{2,1,0:T(8,128)(2,1)S(1)}, u32[]{:S(2)}, u32[]{:S(2)}) collective-permute-start(bf16[16,8,320]{2,1,0:T(8,128)(2,1)S(1)} %bitcast.149), channel_id=1, source_target_pairs={{0,128},{4,132},{8,136},{12,140},{16,144},{20,148},{24,152},{28,15... | collective-permute-start | bytes 245768 | tf_op jit(solution)/shard_map/ppermute | solution.py:77
  39.2 1.2 %collective-permute-start.9 = (bf16[16,8,320]{2,1,0:T(8,128)(2,1)S(1)}, bf16[16,8,320]{2,1,0:T(8,128)(2,1)S(1)}, u32[]{:S(2)}, u32[]{:S(2)}) collective-permute-start(bf16[16,8,320]{2,1,0:T(8,128)(2,1)S(1)} %bitcast.150), channel_id=1, source_target_pairs={{0,64},{4,68},{8,72},{12,76},{16,80},{20,84},{24,88},{28,92},{32,9... | collective-permute-start | bytes 245768 | tf_op jit(solution)/shard_map/ppermute | solution.py:77
  40.4 2.8 %collective-permute-done.11 = bf16[16,8,320]{2,1,0:T(8,128)(2,1)S(1)} collective-permute-done((bf16[16,8,320]{2,1,0:T(8,128)(2,1)S(1)}, bf16[16,8,320]{2,1,0:T(8,128)(2,1)S(1)}, u32[]{:S(2)}, u32[]{:S(2)}) %collective-permute-start.11) | collective-permute-done | bytes 81952 | tf_op jit(solution)/shard_map/ppermute | solution.py:77
  43.2 0.9 collective-permute-done.9
  45.4 2.4 %fusion.5 = f32[24,320]{1,0:T(8,128)S(1)} fusion(pred[5,320]{1,0:T(8,128)(4,1)S(1)} %iota_compare_fusion.5, f32[24,5,128]{2,1,0:T(8,128)S(1)} %get-tuple-element.37, f32[24,5]{1,0:T(8,128)S(1)} %get-tuple-element.36, pred[24,128]{1,0:T(8,128)(4,1)S(1)} %add_compare_fusion, bf16[24,128,2,320]{1,3,2,0:T(8,128)(2,1)} %param.17), kind=kOutput, calls=%fused_computation.12 | convolution fusion | flops 9945600 | bytes 2063392 | tf_op jit(solution)/shard_map/shp,spf->shf/dot_general | solution.py:178
  49.2 0.9 pad_maximum_fusion.1
  50.1 1.4 %copy.40 = f32[512,330]{1,0:T(8,128)S(1)} copy(f32[512,330]{0,1:T(8,128)} %pad_maximum_fusion.1) | data formatting | bytes 1351680 | tf_op jit(solution)/shard_map/concatenate | solution.py:190
  51.5 0.8 slice_bitcast_fusion.9
  52.3 0.8 collective-permute-start.13
  53.2 1.0 %collective-permute-start.12 = (f32[16,8,330]{2,1,0:T(8,128)}, f32[16,8,330]{2,1,0:T(8,128)}, u32[]{:S(2)}, u32[]{:S(2)}) collective-permute-start(f32[16,8,330]{2,1,0:T(8,128)} %get-tuple-element.21), channel_id=1, source_target_pairs={{0,4},{4,0},{8,12},{12,8},{16,20},{20,16},{24,28},{28,24},{32,36},... | collective-permute-start | bytes 506888 | tf_op jit(solution)/shard_map/ppermute | solution.py:94
  54.2 1.4 %mul.135 = f32[8,5,64]{2,1,0:T(8,128)} reshape(f32[8,320]{1,0:T(8,128)} %get-tuple-element.31) | data formatting | bytes 20480 | tf_op jit(solution)/shard_map/mul | solution.py:17
  55.6 1.4 %reduce_sum.133 = f32[8,5]{1,0:T(8,128)} reduce(f32[8,5,64]{2,1,0:T(8,128)} %mul.135, f32[]{:T(128)} %constant.113.clone.1), dimensions={2}, to_apply=%region_15.16 | reduce | flops 2520 | bytes 10404 | tf_op jit(solution)/shard_map/reduce_sum | solution.py:17
  57.0 2.8 %collective-permute-done.14 = f32[16,8,330]{2,1,0:T(8,128)} collective-permute-done((f32[16,8,330]{2,1,0:T(8,128)}, f32[16,8,330]{2,1,0:T(8,128)}, u32[]{:S(2)}, u32[]{:S(2)}) %collective-permute-start.14) | collective-permute-done | bytes 168992 | tf_op jit(solution)/shard_map/ppermute | solution.py:94
  59.8 3.0 %collective-permute-done.13 = f32[16,8,330]{2,1,0:T(8,128)} collective-permute-done((f32[16,8,330]{2,1,0:T(8,128)}, f32[16,8,330]{2,1,0:T(8,128)}, u32[]{:S(2)}, u32[]{:S(2)}) %collective-permute-start.13) | collective-permute-done | bytes 168992 | tf_op jit(solution)/shard_map/ppermute | solution.py:94
  62.9 1.2 %pad_maximum_fusion = f32[4,16,8,330]{3,2,1,0:T(8,128)S(1)} fusion(f32[1,16,8,330]{3,2,1,0:T(8,128)} %bitcast.36, f32[1,16,8,330]{3,2,1,0:T(8,128)} %bitcast.34, f32[1,16,8,330]{3,2,1,0:T(8,128)} %bitcast.32, f32[1,16,8,330]{3,2,1,0:T(8,128)S(1)} %get-tuple-element.19), kind=kLoop, calls=%fused_computation.25 | loop fusion | flops 506880 | bytes 1351680 | tf_op jit(solution)/shard_map/stack | solution.py:96
  65.7 2.1 %collective-permute-start.17 = (f32[4,8,330]{2,1,0:T(8,128)}, f32[4,8,330]{2,1,0:T(8,128)S(1)}, u32[]{:S(2)}, u32[]{:S(2)}) collective-permute-start(f32[4,8,330]{2,1,0:T(8,128)} %get-tuple-element.26), channel_id=1, source_target_pairs={{0,48},{4,52},{8,56},{12,60},{16,32},{20,36},{24,40},{28,44},{32,1... | collective-permute-start | bytes 126728 | tf_op jit(solution)/shard_map/ppermute | solution.py:94
  67.8 3.9 %collective-permute-start.16 = (f32[4,8,330]{2,1,0:T(8,128)}, f32[4,8,330]{2,1,0:T(8,128)}, u32[]{:S(2)}, u32[]{:S(2)}) collective-permute-start(f32[4,8,330]{2,1,0:T(8,128)} %get-tuple-element.24), channel_id=1, source_target_pairs={{0,32},{4,36},{8,40},{12,44},{16,48},{20,52},{24,56},{28,60},{32,0... | collective-permute-start | bytes 126728 | tf_op jit(solution)/shard_map/ppermute | solution.py:94
  73.0 4.8 %collective-permute-done.16 = f32[4,8,330]{2,1,0:T(8,128)} collective-permute-done((f32[4,8,330]{2,1,0:T(8,128)}, f32[4,8,330]{2,1,0:T(8,128)}, u32[]{:S(2)}, u32[]{:S(2)}) %collective-permute-start.16) | collective-permute-done | bytes 42272 | tf_op jit(solution)/shard_map/ppermute | solution.py:94
  77.7 1.0 %collective-permute-done.15 = f32[4,8,330]{2,1,0:T(8,128)} collective-permute-done((f32[4,8,330]{2,1,0:T(8,128)S(1)}, f32[4,8,330]{2,1,0:T(8,128)}, u32[]{:S(2)}, u32[]{:S(2)}) %collective-permute-start.15) | collective-permute-done | bytes 42272 | tf_op jit(solution)/shard_map/ppermute | solution.py:94
  78.8 0.8 pad_maximum_fusion.4
  80.2 1.7 %collective-permute-start.20 = (f32[1,8,330]{2,1,0:T(8,128)S(1)}, f32[1,8,330]{2,1,0:T(8,128)S(1)}, u32[]{:S(2)}, u32[]{:S(2)}) collective-permute-start(f32[1,8,330]{2,1,0:T(8,128)S(1)} %get-tuple-element.28), channel_id=1, source_target_pairs={{0,192},{4,196},{8,200},{12,204},{16,208},{20,212},{24,216},{28,22... | collective-permute-start | bytes 31688 | tf_op jit(solution)/shard_map/ppermute | solution.py:94
  81.9 1.4 %collective-permute-start.19 = (f32[1,8,330]{2,1,0:T(8,128)S(1)}, f32[1,8,330]{2,1,0:T(8,128)S(1)}, u32[]{:S(2)}, u32[]{:S(2)}) collective-permute-start(f32[1,8,330]{2,1,0:T(8,128)S(1)} %get-tuple-element.29), channel_id=1, source_target_pairs={{0,128},{4,132},{8,136},{12,140},{16,144},{20,148},{24,152},{28,15... | collective-permute-start | bytes 31688 | tf_op jit(solution)/shard_map/ppermute | solution.py:94
  83.4 1.0 %collective-permute-start.18 = (f32[1,8,330]{2,1,0:T(8,128)S(1)}, f32[1,8,330]{2,1,0:T(8,128)S(1)}, u32[]{:S(2)}, u32[]{:S(2)}) collective-permute-start(f32[1,8,330]{2,1,0:T(8,128)S(1)} %get-tuple-element.30), channel_id=1, source_target_pairs={{0,64},{4,68},{8,72},{12,76},{16,80},{20,84},{24,88},{28,92},{32,9... | collective-permute-start | bytes 31688 | tf_op jit(solution)/shard_map/ppermute | solution.py:94
  84.4 0.9 convolution_multiply_fusion.4
  85.3 1.8 %collective-permute-done.19 = f32[1,8,330]{2,1,0:T(8,128)S(1)} collective-permute-done((f32[1,8,330]{2,1,0:T(8,128)S(1)}, f32[1,8,330]{2,1,0:T(8,128)S(1)}, u32[]{:S(2)}, u32[]{:S(2)}) %collective-permute-start.19) | collective-permute-done | bytes 10592 | tf_op jit(solution)/shard_map/ppermute | solution.py:94
  88.5 1.4 %collective-permute-start.23 = (f32[8,1280]{1,0:T(8,128)S(1)}, f32[8,1280]{1,0:T(8,128)S(1)}, u32[]{:S(2)}, u32[]{:S(2)}) collective-permute-start(f32[8,1280]{1,0:T(8,128)S(1)} %fusion.72), channel_id=1, source_target_pairs={{0,3},{1,2},{2,1},{3,0},{4,7},{5,6},{6,5},{7,4},{8,11},{9,10},{10,... | collective-permute-start | bytes 122888 | tf_op jit(solution)/shard_map/ppermute | solution.py:55
  89.8 0.9 collective-permute-start.22
  90.7 1.9 %collective-permute-start.21 = (f32[8,1280]{1,0:T(8,128)S(1)}, f32[8,1280]{1,0:T(8,128)S(1)}, u32[]{:S(2)}, u32[]{:S(2)}) collective-permute-start(f32[8,1280]{1,0:T(8,128)S(1)} %fusion.72), channel_id=1, source_target_pairs={{0,1},{1,0},{2,3},{3,2},{4,5},{5,4},{6,7},{7,6},{8,9},{9,8},{10,11... | collective-permute-start | bytes 122888 | tf_op jit(solution)/shard_map/ppermute | solution.py:55
  92.8 1.0 collective-permute-done.23
  93.7 1.6 %collective-permute-done.22 = f32[8,1280]{1,0:T(8,128)S(1)} collective-permute-done((f32[8,1280]{1,0:T(8,128)S(1)}, f32[8,1280]{1,0:T(8,128)S(1)}, u32[]{:S(2)}, u32[]{:S(2)}) %collective-permute-start.22) | collective-permute-done | bytes 40992 | tf_op jit(solution)/shard_map/ppermute | solution.py:55
  96.0 0.7 broadcast_select_fusion
  97.0 0.8 fusion.21
  97.8 0.7 fusion.43
  (106 shorter events, 11.9 us)
Async XLA Ops:
  0.0 9.8 %copy-start = (bf16[1280,3,320]{0,2,1:T(8,128)(2,1)S(1)}, bf16[1280,3,320]{0,2,1:T(8,128)(2,1)}, u32[]{:S(2)}) copy-start(bf16[1280,3,320]{0,2,1:T(8,128)(2,1)} %param.10) | copy-start | bytes 7372804
  0.0 5.1 %collective-permute-start.2 = (bf16[1,8,320]{2,1,0:T(8,128)(2,1)}, bf16[1,8,320]{2,1,0:T(8,128)(2,1)S(1)}, u32[]{:S(2)}, u32[]{:S(2)}) collective-permute-start(bf16[1,8,320]{2,1,0:T(8,128)(2,1)} %bitcast.174), channel_id=1, source_target_pairs={{0,3},{1,2},{2,1},{3,0},{4,7},{5,6},{6,5},{7,4},{8,11},{9,10},{10,... | collective-permute-start | bytes 15368 | tf_op jit(solution)/shard_map/ppermute | solution.py:55
  3.0 5.3 %collective-permute-start.1 = (bf16[1,8,320]{2,1,0:T(8,128)(2,1)}, bf16[1,8,320]{2,1,0:T(8,128)(2,1)S(1)}, u32[]{:S(2)}, u32[]{:S(2)}) collective-permute-start(bf16[1,8,320]{2,1,0:T(8,128)(2,1)} %bitcast.175), channel_id=1, source_target_pairs={{0,2},{1,3},{2,0},{3,1},{4,6},{5,7},{6,4},{7,5},{8,10},{9,11},{10,... | collective-permute-start | bytes 15368 | tf_op jit(solution)/shard_map/ppermute | solution.py:55
  3.6 4.7 %collective-permute-start = (bf16[1,8,320]{2,1,0:T(8,128)(2,1)}, bf16[1,8,320]{2,1,0:T(8,128)(2,1)S(1)}, u32[]{:S(2)}, u32[]{:S(2)}) collective-permute-start(bf16[1,8,320]{2,1,0:T(8,128)(2,1)} %bitcast.176), channel_id=1, source_target_pairs={{0,1},{1,0},{2,3},{3,2},{4,5},{5,4},{6,7},{7,6},{8,9},{9,8},{10,11... | collective-permute-start | bytes 15368 | tf_op jit(solution)/shard_map/ppermute | solution.py:55
  4.2 5.7 %copy-start.7 = (s32[1024]{0:T(1024)}, s32[1024]{0:T(1024)S(1)}, u32[]{:S(2)}) copy-start(s32[1024]{0:T(1024)S(1)} %pad_clamp_fusion.2) | copy-start | bytes 12292
  4.2 5.7 %copy-start.8 = (pred[4]{0:T(512)(128)(4,1)}, pred[4]{0:T(512)(128)(4,1)S(1)}, u32[]{:S(2)}) copy-start(pred[4]{0:T(512)(128)(4,1)S(1)} %compare_and_fusion) | copy-start | bytes 16
  12.3 9.6 %copy-start.3 = (bf16[8,320]{1,0:T(8,128)(2,1)}, bf16[8,320]{1,0:T(8,128)(2,1)S(1)}, u32[]{:S(2)}) copy-start(bf16[8,320]{1,0:T(8,128)(2,1)S(1)} %get-tuple-element.13) | copy-start | bytes 15364
  12.3 8.8 %copy-start.9 = (s32[24]{0:T(128)S(1)}, s32[24]{0:T(128)}, u32[]{:S(2)}) copy-start(s32[24]{0:T(128)} %param.15) | copy-start | bytes 292
  12.3 8.8 %copy-start.10 = (s32[24]{0:T(128)S(1)}, s32[24]{0:T(128)}, u32[]{:S(2)}) copy-start(s32[24]{0:T(128)} %param.16) | copy-start | bytes 292
  12.3 8.9 %copy-start.1 = (s32[512]{0:T(512)S(1)}, s32[512]{0:T(512)}, u32[]{:S(2)}) copy-start(s32[512]{0:T(512)} %param.14) | copy-start | bytes 6148
  12.3 18.4 %copy-start.6 = (f32[320]{0:T(512)S(1)}, f32[320]{0:T(512)}, u32[]{:S(2)}) copy-start(f32[320]{0:T(512)} %param.12) | copy-start | bytes 3844
  12.3 9.6 %collective-permute-start.5 = (bf16[1,8,320]{2,1,0:T(8,128)(2,1)S(1)}, bf16[1,8,320]{2,1,0:T(8,128)(2,1)S(1)}, u32[]{:S(2)}, u32[]{:S(2)}) collective-permute-start(bf16[1,8,320]{2,1,0:T(8,128)(2,1)S(1)} %bitcast.165), channel_id=1, source_target_pairs={{0,12},{4,8},{8,4},{12,0},{16,28},{20,24},{24,20},{28,16},{32,44},... | collective-permute-start | bytes 15368 | tf_op jit(solution)/shard_map/ppermute | solution.py:77
  12.4 9.5 %collective-permute-start.4 = (bf16[1,8,320]{2,1,0:T(8,128)(2,1)S(1)}, bf16[1,8,320]{2,1,0:T(8,128)(2,1)S(1)}, u32[]{:S(2)}, u32[]{:S(2)}) collective-permute-start(bf16[1,8,320]{2,1,0:T(8,128)(2,1)S(1)} %bitcast.166), channel_id=1, source_target_pairs={{0,8},{4,12},{8,0},{12,4},{16,24},{20,28},{24,16},{28,20},{32,40},... | collective-permute-start | bytes 15368 | tf_op jit(solution)/shard_map/ppermute | solution.py:77
  14.5 7.5 %collective-permute-start.3 = (bf16[1,8,320]{2,1,0:T(8,128)(2,1)S(1)}, bf16[1,8,320]{2,1,0:T(8,128)(2,1)S(1)}, u32[]{:S(2)}, u32[]{:S(2)}) collective-permute-start(bf16[1,8,320]{2,1,0:T(8,128)(2,1)S(1)} %bitcast.167), channel_id=1, source_target_pairs={{0,4},{4,0},{8,12},{12,8},{16,20},{20,16},{24,28},{28,24},{32,36},... | collective-permute-start | bytes 15368 | tf_op jit(solution)/shard_map/ppermute | solution.py:77
  22.0 11.0 %collective-permute-start.8 = (bf16[4,8,320]{2,1,0:T(8,128)(2,1)S(1)}, bf16[4,8,320]{2,1,0:T(8,128)(2,1)S(1)}, u32[]{:S(2)}, u32[]{:S(2)}) collective-permute-start(bf16[4,8,320]{2,1,0:T(8,128)(2,1)S(1)} %get-tuple-element.34), channel_id=1, source_target_pairs={{0,48},{4,52},{8,56},{12,60},{16,32},{20,36},{24,40},{28,44},{32,1... | collective-permute-start | bytes 61448 | tf_op jit(solution)/shard_map/ppermute | solution.py:77
  28.2 8.0 %collective-permute-start.7 = (bf16[4,8,320]{2,1,0:T(8,128)(2,1)S(1)}, bf16[4,8,320]{2,1,0:T(8,128)(2,1)S(1)}, u32[]{:S(2)}, u32[]{:S(2)}) collective-permute-start(bf16[4,8,320]{2,1,0:T(8,128)(2,1)S(1)} %get-tuple-element.34), channel_id=1, source_target_pairs={{0,32},{4,36},{8,40},{12,44},{16,48},{20,52},{24,56},{28,60},{32,0... | collective-permute-start | bytes 61448 | tf_op jit(solution)/shard_map/ppermute | solution.py:77
  29.2 7.0 %collective-permute-start.6 = (bf16[4,8,320]{2,1,0:T(8,128)(2,1)S(1)}, bf16[4,8,320]{2,1,0:T(8,128)(2,1)S(1)}, u32[]{:S(2)}, u32[]{:S(2)}) collective-permute-start(bf16[4,8,320]{2,1,0:T(8,128)(2,1)S(1)} %get-tuple-element.34), channel_id=1, source_target_pairs={{0,16},{4,20},{8,24},{12,28},{16,0},{20,4},{24,8},{28,12},{32,48},... | collective-permute-start | bytes 61448 | tf_op jit(solution)/shard_map/ppermute | solution.py:77
  36.2 7.0 %collective-permute-start.11 = (bf16[16,8,320]{2,1,0:T(8,128)(2,1)S(1)}, bf16[16,8,320]{2,1,0:T(8,128)(2,1)S(1)}, u32[]{:S(2)}, u32[]{:S(2)}) collective-permute-start(bf16[16,8,320]{2,1,0:T(8,128)(2,1)S(1)} %bitcast.148), channel_id=1, source_target_pairs={{0,192},{4,196},{8,200},{12,204},{16,208},{20,212},{24,216},{28,22... | collective-permute-start | bytes 245768 | tf_op jit(solution)/shard_map/ppermute | solution.py:77
  36.8 6.4 %collective-permute-start.10 = (bf16[16,8,320]{2,1,0:T(8,128)(2,1)S(1)}, bf16[16,8,320]{2,1,0:T(8,128)(2,1)S(1)}, u32[]{:S(2)}, u32[]{:S(2)}) collective-permute-start(bf16[16,8,320]{2,1,0:T(8,128)(2,1)S(1)} %bitcast.149), channel_id=1, source_target_pairs={{0,128},{4,132},{8,136},{12,140},{16,144},{20,148},{24,152},{28,15... | collective-permute-start | bytes 245768 | tf_op jit(solution)/shard_map/ppermute | solution.py:77
  39.2 4.8 %collective-permute-start.9 = (bf16[16,8,320]{2,1,0:T(8,128)(2,1)S(1)}, bf16[16,8,320]{2,1,0:T(8,128)(2,1)S(1)}, u32[]{:S(2)}, u32[]{:S(2)}) collective-permute-start(bf16[16,8,320]{2,1,0:T(8,128)(2,1)S(1)} %bitcast.150), channel_id=1, source_target_pairs={{0,64},{4,68},{8,72},{12,76},{16,80},{20,84},{24,88},{28,92},{32,9... | collective-permute-start | bytes 245768 | tf_op jit(solution)/shard_map/ppermute | solution.py:77
  52.3 35.9 %copy-start.2 = (bf16[320,1280]{1,0:T(8,128)(2,1)S(1)}, bf16[320,1280]{1,0:T(8,128)(2,1)}, u32[]{:S(2)}) copy-start(bf16[320,1280]{1,0:T(8,128)(2,1)} %param.11) | copy-start | bytes 2457604
  52.3 7.5 %collective-permute-start.14 = (f32[16,8,330]{2,1,0:T(8,128)}, f32[16,8,330]{2,1,0:T(8,128)}, u32[]{:S(2)}, u32[]{:S(2)}) collective-permute-start(f32[16,8,330]{2,1,0:T(8,128)} %get-tuple-element.22), channel_id=1, source_target_pairs={{0,12},{4,8},{8,4},{12,0},{16,28},{20,24},{24,20},{28,16},{32,44},... | collective-permute-start | bytes 506888 | tf_op jit(solution)/shard_map/ppermute | solution.py:94
  52.3 10.5 %collective-permute-start.13 = (f32[16,8,330]{2,1,0:T(8,128)}, f32[16,8,330]{2,1,0:T(8,128)}, u32[]{:S(2)}, u32[]{:S(2)}) collective-permute-start(f32[16,8,330]{2,1,0:T(8,128)} %get-tuple-element.20), channel_id=1, source_target_pairs={{0,8},{4,12},{8,0},{12,4},{16,24},{20,28},{24,16},{28,20},{32,40},... | collective-permute-start | bytes 506888 | tf_op jit(solution)/shard_map/ppermute | solution.py:94
  53.2 9.7 %collective-permute-start.12 = (f32[16,8,330]{2,1,0:T(8,128)}, f32[16,8,330]{2,1,0:T(8,128)}, u32[]{:S(2)}, u32[]{:S(2)}) collective-permute-start(f32[16,8,330]{2,1,0:T(8,128)} %get-tuple-element.21), channel_id=1, source_target_pairs={{0,4},{4,0},{8,12},{12,8},{16,20},{20,16},{24,28},{28,24},{32,36},... | collective-permute-start | bytes 506888 | tf_op jit(solution)/shard_map/ppermute | solution.py:94
  57.0 15.2 %copy-start.4 = (f32[8,5]{1,0:T(8,128)S(1)}, f32[8,5]{1,0:T(8,128)}, u32[]{:S(2)}) copy-start(f32[8,5]{1,0:T(8,128)} %reduce_sum.133) | copy-start | bytes 484
  64.0 28.6 %copy-start.5 = (f32[1280]{0:T(1024)S(1)}, f32[1280]{0:T(1024)}, u32[]{:S(2)}) copy-start(f32[1280]{0:T(1024)} %param.13) | copy-start | bytes 15364
  65.7 7.3 %collective-permute-start.17 = (f32[4,8,330]{2,1,0:T(8,128)}, f32[4,8,330]{2,1,0:T(8,128)S(1)}, u32[]{:S(2)}, u32[]{:S(2)}) collective-permute-start(f32[4,8,330]{2,1,0:T(8,128)} %get-tuple-element.26), channel_id=1, source_target_pairs={{0,48},{4,52},{8,56},{12,60},{16,32},{20,36},{24,40},{28,44},{32,1... | collective-permute-start | bytes 126728 | tf_op jit(solution)/shard_map/ppermute | solution.py:94
  67.8 9.9 %collective-permute-start.16 = (f32[4,8,330]{2,1,0:T(8,128)}, f32[4,8,330]{2,1,0:T(8,128)}, u32[]{:S(2)}, u32[]{:S(2)}) collective-permute-start(f32[4,8,330]{2,1,0:T(8,128)} %get-tuple-element.24), channel_id=1, source_target_pairs={{0,32},{4,36},{8,40},{12,44},{16,48},{20,52},{24,56},{28,60},{32,0... | collective-permute-start | bytes 126728 | tf_op jit(solution)/shard_map/ppermute | solution.py:94
  71.7 7.1 %collective-permute-start.15 = (f32[4,8,330]{2,1,0:T(8,128)S(1)}, f32[4,8,330]{2,1,0:T(8,128)}, u32[]{:S(2)}, u32[]{:S(2)}) collective-permute-start(f32[4,8,330]{2,1,0:T(8,128)S(1)} %get-tuple-element.25), channel_id=1, source_target_pairs={{0,16},{4,20},{8,24},{12,28},{16,0},{20,4},{24,8},{28,12},{32,48},... | collective-permute-start | bytes 126728 | tf_op jit(solution)/shard_map/ppermute | solution.py:94
  80.2 5.1 %collective-permute-start.20 = (f32[1,8,330]{2,1,0:T(8,128)S(1)}, f32[1,8,330]{2,1,0:T(8,128)S(1)}, u32[]{:S(2)}, u32[]{:S(2)}) collective-permute-start(f32[1,8,330]{2,1,0:T(8,128)S(1)} %get-tuple-element.28), channel_id=1, source_target_pairs={{0,192},{4,196},{8,200},{12,204},{16,208},{20,212},{24,216},{28,22... | collective-permute-start | bytes 31688 | tf_op jit(solution)/shard_map/ppermute | solution.py:94
  81.9 5.2 %collective-permute-start.19 = (f32[1,8,330]{2,1,0:T(8,128)S(1)}, f32[1,8,330]{2,1,0:T(8,128)S(1)}, u32[]{:S(2)}, u32[]{:S(2)}) collective-permute-start(f32[1,8,330]{2,1,0:T(8,128)S(1)} %get-tuple-element.29), channel_id=1, source_target_pairs={{0,128},{4,132},{8,136},{12,140},{16,144},{20,148},{24,152},{28,15... | collective-permute-start | bytes 31688 | tf_op jit(solution)/shard_map/ppermute | solution.py:94
  83.4 3.8 %collective-permute-start.18 = (f32[1,8,330]{2,1,0:T(8,128)S(1)}, f32[1,8,330]{2,1,0:T(8,128)S(1)}, u32[]{:S(2)}, u32[]{:S(2)}) collective-permute-start(f32[1,8,330]{2,1,0:T(8,128)S(1)} %get-tuple-element.30), channel_id=1, source_target_pairs={{0,64},{4,68},{8,72},{12,76},{16,80},{20,84},{24,88},{28,92},{32,9... | collective-permute-start | bytes 31688 | tf_op jit(solution)/shard_map/ppermute | solution.py:94
  88.5 5.3 %collective-permute-start.23 = (f32[8,1280]{1,0:T(8,128)S(1)}, f32[8,1280]{1,0:T(8,128)S(1)}, u32[]{:S(2)}, u32[]{:S(2)}) collective-permute-start(f32[8,1280]{1,0:T(8,128)S(1)} %fusion.72), channel_id=1, source_target_pairs={{0,3},{1,2},{2,1},{3,0},{4,7},{5,6},{6,5},{7,4},{8,11},{9,10},{10,... | collective-permute-start | bytes 122888 | tf_op jit(solution)/shard_map/ppermute | solution.py:55
  89.8 5.5 %collective-permute-start.22 = (f32[8,1280]{1,0:T(8,128)S(1)}, f32[8,1280]{1,0:T(8,128)S(1)}, u32[]{:S(2)}, u32[]{:S(2)}) collective-permute-start(f32[8,1280]{1,0:T(8,128)S(1)} %fusion.72), channel_id=1, source_target_pairs={{0,2},{1,3},{2,0},{3,1},{4,6},{5,7},{6,4},{7,5},{8,10},{9,11},{10,... | collective-permute-start | bytes 122888 | tf_op jit(solution)/shard_map/ppermute | solution.py:55
  90.7 4.6 %collective-permute-start.21 = (f32[8,1280]{1,0:T(8,128)S(1)}, f32[8,1280]{1,0:T(8,128)S(1)}, u32[]{:S(2)}, u32[]{:S(2)}) collective-permute-start(f32[8,1280]{1,0:T(8,128)S(1)} %fusion.72), channel_id=1, source_target_pairs={{0,1},{1,0},{2,3},{3,2},{4,5},{5,4},{6,7},{7,6},{8,9},{9,8},{10,11... | collective-permute-start | bytes 122888 | tf_op jit(solution)/shard_map/ppermute | solution.py:55

commit v7 on v6

--- a/solution.py
+++ b/solution.py
@@ -90,8 +90,11 @@
         grouped = packed.reshape((packed.shape[0] // count, count) + packed.shape[1:])
         pieces = [grouped[:, 0]]
         for digit in range(1, count):
+            sent = to_link(grouped[:, digit], width_acc, heads)
             pieces.append(
-                lax.ppermute(grouped[:, digit], axis, perm=xor_partner(axis, size, digit << low))
+                lax.ppermute(sent, axis, perm=xor_partner(axis, size, digit << low)).astype(
+                    jnp.float32
+                )
             )
         stacked = jnp.stack(pieces)
         acc = stacked[..., :width_acc]
@@ -104,6 +107,20 @@
         packed = jnp.concatenate([acc, total, top], axis=-1)
         low += width
     return packed[0]
+
+
+def to_link(piece, width_acc, heads):
+    top = piece[..., width_acc + heads :]
+    top_sent = top.astype(jnp.bfloat16).astype(jnp.float32)
+    shift = jnp.exp(jnp.where(top > 0.5 * far_below, top - top_sent, 0.0))
+    return jnp.concatenate(
+        [
+            piece[..., :width_acc] * spread_heads(shift, width_acc),
+            piece[..., width_acc : width_acc + heads] * shift,
+            top_sent,
+        ],
+        axis=-1,
+    ).astype(jnp.bfloat16)
 
 
 def sum_radix(value, axis):
@@ -182,10 +199,12 @@
 
     request_max = jnp.max(jnp.where(onehot[:, :, None], page_max[:, None, :], far_below), axis=0)
     factor = jnp.exp(page_max - request_max[owner_place])
-    selector = onehot.astype(jnp.float32)
-    request_total = jnp.dot(selector.T, page_total * factor, precision=lax.Precision.HIGHEST)
+    selector = (
+        jnp.arange(requests, dtype=jnp.int32)[:, None] == owner_place[None, :]
+    ).astype(jnp.float32)
+    request_total = jnp.dot(selector, page_total * factor, precision=lax.Precision.HIGHEST)
     request_acc = jnp.dot(
-        selector.T, page_acc * spread_heads(factor, width_local), precision=lax.Precision.HIGHEST
+        selector, page_acc * spread_heads(factor, width_local), precision=lax.Precision.HIGHEST
     )
     packed = jnp.concatenate([request_acc, request_total, request_max], axis=1)
     packed = packed.reshape(lax.axis_size("seq"), rows, packed.shape[-1])

time: 99.9 us -> 90.5 us (0.906)
  waiting for transfers between devices: 27.1 us -> 22.8 us
  other arithmetic: 19.4 us -> 15.9 us
  local copies, waits for them, and re-layouts: 8.35 us -> 4.91 us
  matrix products: 7.51 us -> 8.97 us
    ppermute x9, waiting for transfers between devices: 13.4 us -> 9.9 us  [scatter_xor(): lax.ppermute(sent, axis, perm=xor_partner(axis, size, digit << low))]
    dot_general x7 -> x16, matrix products: 1.88 us -> 4.06 us  [spread_heads(): return jnp.dot(factor, spread, precision=lax.Precision.HIGHEST)]
    another operation x3 -> x12, other arithmetic: 2.03 us -> 0.15 us  [scatter_xor(): stacked = jnp.stack(pieces)]
    another operation x2, local copies, waits for them, and re-layouts: 1.47 us -> 0.07 us  [scatter_xor(): stacked = jnp.stack(pieces)]
    reduce_sum x3, other arithmetic: 4.23 us -> 2.88 us  [head_norm(): jnp.mean(shaped * shaped, axis=-1, keepdims=True) + epsilon]
    mul x2, local copies, waits for them, and re-layouts: 1.45 us -> 0.15 us  [head_norm(): shaped * shaped]
  transfers between devices with their start and end apart: 24 -> 24, of which waited for: 12 -> 13; matrix products, arithmetic and copies ran while one was open for 15% -> 14% of each run, Pallas kernels for 0% -> 0%
where the time goes in v7:
time: 90.5 us; the launch traced here: 89.5 us
  starting transfers between devices  36.3 us (40%)
  waiting for transfers between devices  22.8 us (25%)
  other arithmetic  15.9 us (18%)
  matrix products  8.97 us (10%)
  local copies, waits for them, and re-layouts  4.91 us (5%)
    ppermute x9, starting transfers between devices, gather_xor(): lax.ppermute(held, axis, perm=xor_partner(axis, size, digit << low))  15 us
    ppermute x9, starting transfers between devices, scatter_xor(): lax.ppermute(sent, axis, perm=xor_partner(axis, size, digit << low))  13.1 us
    ppermute x9, waiting for transfers between devices, scatter_xor(): lax.ppermute(sent, axis, perm=xor_partner(axis, size, digit << low))  9.9 us
    ppermute x6, starting transfers between devices, exchange(): lax.ppermute(held, axis, perm=xor_partner(axis, size, digit << low))  8.24 us
    ppermute x6, waiting for transfers between devices, exchange(): lax.ppermute(held, axis, perm=xor_partner(axis, size, digit << low))  6.75 us
    ppermute x9, waiting for transfers between devices, gather_xor(): lax.ppermute(held, axis, perm=xor_partner(axis, size, digit << low))  6.2 us
    mul x3, other arithmetic, head_norm(): shaped * shaped  4.64 us
    dot_general x16, matrix products, spread_heads(): return jnp.dot(factor, spread, precision=lax.Precision.HIGHEST)  4.06 us
  transfers between devices with their start and end apart: 24, of which 13 were waited for; matrix products, arithmetic and copies ran while one was open for 14% of the time, Pallas kernels for 0%

profile of v7, /device:TPU:6, one launch (start us, length us, event | category | flops | bytes accessed | tf_op | source)
XLA Modules:
  0.0 89.5 jit_solution(3599664917805146434)
XLA Ops:
  0.0 3.0 %collective-permute-start.2 = (bf16[1,8,320]{2,1,0:T(8,128)(2,1)}, bf16[1,8,320]{2,1,0:T(8,128)(2,1)S(1)}, u32[]{:S(2)}, u32[]{:S(2)}) collective-permute-start(bf16[1,8,320]{2,1,0:T(8,128)(2,1)} %bitcast.215), channel_id=1, source_target_pairs={{0,3},{1,2},{2,1},{3,0},{4,7},{5,6},{6,5},{7,4},{8,11},{9,10},{10,... | collective-permute-start | bytes 15368 | tf_op jit(solution)/shard_map/ppermute | solution.py:55
  3.0 0.6 collective-permute-start.1
  4.2 0.9 collective-permute-done.2
  5.1 3.3 %collective-permute-done.1 = bf16[1,8,320]{2,1,0:T(8,128)(2,1)S(1)} collective-permute-done((bf16[1,8,320]{2,1,0:T(8,128)(2,1)}, bf16[1,8,320]{2,1,0:T(8,128)(2,1)S(1)}, u32[]{:S(2)}, u32[]{:S(2)}) %collective-permute-start.1) | collective-permute-done | bytes 5152 | tf_op jit(solution)/shard_map/ppermute | solution.py:55
  8.4 0.7 maximum_bitcast_fusion.1
  9.1 0.6 gather_fusion
  9.8 0.7 fusion.128
  10.9 0.8 slice_multiply_fusion.12
  11.8 2.0 %collective-permute-start.4 = (bf16[1,8,320]{2,1,0:T(8,128)(2,1)S(1)}, bf16[1,8,320]{2,1,0:T(8,128)(2,1)S(1)}, u32[]{:S(2)}, u32[]{:S(2)}) collective-permute-start(bf16[1,8,320]{2,1,0:T(8,128)(2,1)S(1)} %bitcast.210), channel_id=1, source_target_pairs={{0,8},{4,12},{8,0},{12,4},{16,24},{20,28},{24,16},{28,20},{32,40},... | collective-permute-start | bytes 15368 | tf_op jit(solution)/shard_map/ppermute | solution.py:77
  13.9 3.9 %convert_multiply_fusion = f32[24,128,1,320]{1,3,2,0:T(8,128)} fusion(bf16[24,128,2,320]{1,3,2,0:T(8,128)(2,1)} %param.17), kind=kLoop, calls=%fused_computation.4 | loop fusion | flops 1966080 | bytes 5898240 | tf_op jit(solution)/shard_map/mul | solution.py:17
  17.7 2.7 %reduce_sum.122 = f32[24,128,5]{1,2,0:T(8,128)S(1)} reduce(f32[24,128,5,64]{1,3,2,0:T(8,128)} %bitcast.189, f32[]{:T(128)} %constant.134.clone.1), dimensions={3}, to_apply=%region_1.2 | reduce | flops 967680 | bytes 3993604 | tf_op jit(solution)/shard_map/reduce_sum | solution.py:17
  21.2 6.2 %collective-permute-start.8 = (bf16[4,8,320]{2,1,0:T(8,128)(2,1)S(1)}, bf16[4,8,320]{2,1,0:T(8,128)(2,1)S(1)}, u32[]{:S(2)}, u32[]{:S(2)}) collective-permute-start(bf16[4,8,320]{2,1,0:T(8,128)(2,1)S(1)} %get-tuple-element.52), channel_id=1, source_target_pairs={{0,48},{4,52},{8,56},{12,60},{16,32},{20,36},{24,40},{28,44},{32,1... | collective-permute-start | bytes 61448 | tf_op jit(solution)/shard_map/ppermute | solution.py:77
  27.4 1.0 %collective-permute-start.7 = (bf16[4,8,320]{2,1,0:T(8,128)(2,1)S(1)}, bf16[4,8,320]{2,1,0:T(8,128)(2,1)S(1)}, u32[]{:S(2)}, u32[]{:S(2)}) collective-permute-start(bf16[4,8,320]{2,1,0:T(8,128)(2,1)S(1)} %get-tuple-element.52), channel_id=1, source_target_pairs={{0,32},{4,36},{8,40},{12,44},{16,48},{20,52},{24,56},{28,60},{32,0... | collective-permute-start | bytes 61448 | tf_op jit(solution)/shard_map/ppermute | solution.py:77
  28.4 1.5 %collective-permute-start.6 = (bf16[4,8,320]{2,1,0:T(8,128)(2,1)S(1)}, bf16[4,8,320]{2,1,0:T(8,128)(2,1)S(1)}, u32[]{:S(2)}, u32[]{:S(2)}) collective-permute-start(bf16[4,8,320]{2,1,0:T(8,128)(2,1)S(1)} %get-tuple-element.52), channel_id=1, source_target_pairs={{0,16},{4,20},{8,24},{12,28},{16,0},{20,4},{24,8},{28,12},{32,48},... | collective-permute-start | bytes 61448 | tf_op jit(solution)/shard_map/ppermute | solution.py:77
  29.8 0.7 gather_fusion.1
  30.6 4.8 %collective-permute-done.7 = bf16[4,8,320]{2,1,0:T(8,128)(2,1)S(1)} collective-permute-done((bf16[4,8,320]{2,1,0:T(8,128)(2,1)S(1)}, bf16[4,8,320]{2,1,0:T(8,128)(2,1)S(1)}, u32[]{:S(2)}, u32[]{:S(2)}) %collective-permute-start.7) | collective-permute-done | bytes 20512 | tf_op jit(solution)/shard_map/ppermute | solution.py:77
  35.4 0.6 collective-permute-start.11
  36.0 2.4 %collective-permute-start.10 = (bf16[16,8,320]{2,1,0:T(8,128)(2,1)S(1)}, bf16[16,8,320]{2,1,0:T(8,128)(2,1)S(1)}, u32[]{:S(2)}, u32[]{:S(2)}) collective-permute-start(bf16[16,8,320]{2,1,0:T(8,128)(2,1)S(1)} %bitcast.194), channel_id=1, source_target_pairs={{0,128},{4,132},{8,136},{12,140},{16,144},{20,148},{24,152},{28,15... | collective-permute-start | bytes 245768 | tf_op jit(solution)/shard_map/ppermute | solution.py:77
  38.4 1.2 %collective-permute-start.9 = (bf16[16,8,320]{2,1,0:T(8,128)(2,1)S(1)}, bf16[16,8,320]{2,1,0:T(8,128)(2,1)S(1)}, u32[]{:S(2)}, u32[]{:S(2)}) collective-permute-start(bf16[16,8,320]{2,1,0:T(8,128)(2,1)S(1)} %bitcast.195), channel_id=1, source_target_pairs={{0,64},{4,68},{8,72},{12,76},{16,80},{20,84},{24,88},{28,92},{32,9... | collective-permute-start | bytes 245768 | tf_op jit(solution)/shard_map/ppermute | solution.py:77
  39.7 2.2 %fusion.2 = bf16[24,128,320]{1,2,0:T(8,128)(2,1)S(1)} fusion(f32[320]{0:T(512)S(1)} %copy-done.4, f32[24,128,5]{1,2,0:T(8,128)S(1)} %add_sqrt_fusion, bf16[24,128,2,320]{1,3,2,0:T(8,128)(2,1)} %param.17), kind=kLoop, calls=%fused_computation.8 | loop fusion | flops 3932160 | bytes 3994880 | tf_op jit(solution)/shard_map/convert_element_type | solution.py:179
  41.9 0.5 collective-permute-done.11
  42.4 0.9 collective-permute-done.9
  43.6 0.5 select_reduce_fusion.1
  44.6 2.3 %fusion.5 = f32[24,320]{1,0:T(8,128)S(1)} fusion(pred[5,320]{1,0:T(8,128)(4,1)S(1)} %iota_compare_fusion.5, f32[24,5,128]{2,1,0:T(8,128)S(1)} %get-tuple-element.55, f32[24,5]{1,0:T(8,128)S(1)} %get-tuple-element.54, pred[24,128]{1,0:T(8,128)(4,1)S(1)} %add_compare_fusion, bf16[24,128,2,320]{1,3,2,0:T(8,128)(2,1)} %param.17), kind=kOutput, calls=%fused_computation.15 | convolution fusion | flops 9945600 | bytes 2063392 | tf_op jit(solution)/shard_map/shp,spf->shf/dot_general | solution.py:195
  47.0 0.6 gather_fusion.2
  48.4 0.9 %pad_maximum_fusion.1 = f32[512,330]{0,1:T(8,128)} fusion(f32[512,5]{0,1:T(8,128)S(1)} %select_reduce_fusion, f32[512,5]{0,1:T(8,128)S(1)} %fusion.22, f32[512,320]{0,1:T(8,128)S(1)} %fusion.23), kind=kLoop, calls=%fused_computation.47 | loop fusion | flops 337920 | bytes 1351680 | tf_op jit(solution)/shard_map/concatenate | solution.py:209
  49.3 1.4 %copy.34 = f32[512,330]{1,0:T(8,128)S(1)} copy(f32[512,330]{0,1:T(8,128)} %pad_maximum_fusion.1) | data formatting | bytes 1351680 | tf_op jit(solution)/shard_map/concatenate | solution.py:209
  52.1 0.9 %collective-permute-start.13 = (bf16[16,8,330]{2,1,0:T(8,128)(2,1)S(1)}, bf16[16,8,330]{2,1,0:T(8,128)(2,1)S(1)}, u32[]{:S(2)}, u32[]{:S(2)}) collective-permute-start(bf16[16,8,330]{2,1,0:T(8,128)(2,1)S(1)} %pad_maximum_fusion.8), channel_id=1, source_target_pairs={{0,8},{4,12},{8,0},{12,4},{16,24},{20,28},{24,16},{28,20},{32,40},... | collective-permute-start | bytes 253448 | tf_op jit(solution)/shard_map/ppermute | solution.py:95
  53.6 1.1 %collective-permute-start.12 = (bf16[16,8,330]{2,1,0:T(8,128)(2,1)S(1)}, bf16[16,8,330]{2,1,0:T(8,128)(2,1)S(1)}, u32[]{:S(2)}, u32[]{:S(2)}) collective-permute-start(bf16[16,8,330]{2,1,0:T(8,128)(2,1)S(1)} %pad_maximum_fusion.7), channel_id=1, source_target_pairs={{0,4},{4,0},{8,12},{12,8},{16,20},{20,16},{24,28},{28,24},{32,36},... | collective-permute-start | bytes 253448 | tf_op jit(solution)/shard_map/ppermute | solution.py:95
  54.7 1.7 %collective-permute-done.14 = bf16[16,8,330]{2,1,0:T(8,128)(2,1)S(1)} collective-permute-done((bf16[16,8,330]{2,1,0:T(8,128)(2,1)S(1)}, bf16[16,8,330]{2,1,0:T(8,128)(2,1)S(1)}, u32[]{:S(2)}, u32[]{:S(2)}) %collective-permute-start.14) | collective-permute-done | bytes 84512 | tf_op jit(solution)/shard_map/ppermute | solution.py:95
  56.4 1.5 %collective-permute-done.13 = bf16[16,8,330]{2,1,0:T(8,128)(2,1)S(1)} collective-permute-done((bf16[16,8,330]{2,1,0:T(8,128)(2,1)S(1)}, bf16[16,8,330]{2,1,0:T(8,128)(2,1)S(1)}, u32[]{:S(2)}, u32[]{:S(2)}) %collective-permute-start.13) | collective-permute-done | bytes 84512 | tf_op jit(solution)/shard_map/ppermute | solution.py:95
  58.3 0.6 fusion.20
  59.4 1.8 %collective-permute-start.17 = (bf16[4,8,330]{2,1,0:T(8,128)(2,1)S(1)}, bf16[4,8,330]{2,1,0:T(8,128)(2,1)S(1)}, u32[]{:S(2)}, u32[]{:S(2)}) collective-permute-start(bf16[4,8,330]{2,1,0:T(8,128)(2,1)S(1)} %pad_maximum_fusion.14), channel_id=1, source_target_pairs={{0,48},{4,52},{8,56},{12,60},{16,32},{20,36},{24,40},{28,44},{32,1... | collective-permute-start | bytes 63368 | tf_op jit(solution)/shard_map/ppermute | solution.py:95
  61.7 3.9 %collective-permute-start.16 = (bf16[4,8,330]{2,1,0:T(8,128)(2,1)S(1)}, bf16[4,8,330]{2,1,0:T(8,128)(2,1)S(1)}, u32[]{:S(2)}, u32[]{:S(2)}) collective-permute-start(bf16[4,8,330]{2,1,0:T(8,128)(2,1)S(1)} %pad_maximum_fusion.13), channel_id=1, source_target_pairs={{0,32},{4,36},{8,40},{12,44},{16,48},{20,52},{24,56},{28,60},{32,0... | collective-permute-start | bytes 63368 | tf_op jit(solution)/shard_map/ppermute | solution.py:95
  66.0 0.9 collective-permute-start.15
  66.8 2.6 %collective-permute-done.16 = bf16[4,8,330]{2,1,0:T(8,128)(2,1)S(1)} collective-permute-done((bf16[4,8,330]{2,1,0:T(8,128)(2,1)S(1)}, bf16[4,8,330]{2,1,0:T(8,128)(2,1)S(1)}, u32[]{:S(2)}, u32[]{:S(2)}) %collective-permute-start.16) | collective-permute-done | bytes 21152 | tf_op jit(solution)/shard_map/ppermute | solution.py:95
  69.4 1.6 %collective-permute-done.15 = bf16[4,8,330]{2,1,0:T(8,128)(2,1)S(1)} collective-permute-done((bf16[4,8,330]{2,1,0:T(8,128)(2,1)S(1)}, bf16[4,8,330]{2,1,0:T(8,128)(2,1)S(1)}, u32[]{:S(2)}, u32[]{:S(2)}) %collective-permute-start.15) | collective-permute-done | bytes 21152 | tf_op jit(solution)/shard_map/ppermute | solution.py:95
  72.0 1.7 %collective-permute-start.20 = (bf16[1,8,330]{2,1,0:T(8,128)(2,1)S(1)}, bf16[1,8,330]{2,1,0:T(8,128)(2,1)S(1)}, u32[]{:S(2)}, u32[]{:S(2)}) collective-permute-start(bf16[1,8,330]{2,1,0:T(8,128)(2,1)S(1)} %pad_maximum_fusion.17), channel_id=1, source_target_pairs={{0,192},{4,196},{8,200},{12,204},{16,208},{20,212},{24,216},{28,22... | collective-permute-start | bytes 15848 | tf_op jit(solution)/shard_map/ppermute | solution.py:95
  74.0 1.5 %collective-permute-start.19 = (bf16[1,8,330]{2,1,0:T(8,128)(2,1)S(1)}, bf16[1,8,330]{2,1,0:T(8,128)(2,1)S(1)}, u32[]{:S(2)}, u32[]{:S(2)}) collective-permute-start(bf16[1,8,330]{2,1,0:T(8,128)(2,1)S(1)} %pad_maximum_fusion.16), channel_id=1, source_target_pairs={{0,128},{4,132},{8,136},{12,140},{16,144},{20,148},{24,152},{28,15... | collective-permute-start | bytes 15848 | tf_op jit(solution)/shard_map/ppermute | solution.py:95
  75.8 1.1 %collective-permute-start.18 = (bf16[1,8,330]{2,1,0:T(8,128)(2,1)S(1)}, bf16[1,8,330]{2,1,0:T(8,128)(2,1)S(1)}, u32[]{:S(2)}, u32[]{:S(2)}) collective-permute-start(bf16[1,8,330]{2,1,0:T(8,128)(2,1)S(1)} %pad_maximum_fusion.15), channel_id=1, source_target_pairs={{0,64},{4,68},{8,72},{12,76},{16,80},{20,84},{24,88},{28,92},{32,9... | collective-permute-start | bytes 15848 | tf_op jit(solution)/shard_map/ppermute | solution.py:95
  76.9 2.3 %collective-permute-done.19 = bf16[1,8,330]{2,1,0:T(8,128)(2,1)S(1)} collective-permute-done((bf16[1,8,330]{2,1,0:T(8,128)(2,1)S(1)}, bf16[1,8,330]{2,1,0:T(8,128)(2,1)S(1)}, u32[]{:S(2)}, u32[]{:S(2)}) %collective-permute-start.19) | collective-permute-done | bytes 5312 | tf_op jit(solution)/shard_map/ppermute | solution.py:95
  80.8 1.4 %collective-permute-start.23 = (f32[8,1280]{1,0:T(8,128)S(1)}, f32[8,1280]{1,0:T(8,128)S(1)}, u32[]{:S(2)}, u32[]{:S(2)}) collective-permute-start(f32[8,1280]{1,0:T(8,128)S(1)} %fusion.129), channel_id=1, source_target_pairs={{0,3},{1,2},{2,1},{3,0},{4,7},{5,6},{6,5},{7,4},{8,11},{9,10},{10,... | collective-permute-start | bytes 122888 | tf_op jit(solution)/shard_map/ppermute | solution.py:55
  82.2 0.9 %collective-permute-start.22 = (f32[8,1280]{1,0:T(8,128)S(1)}, f32[8,1280]{1,0:T(8,128)S(1)}, u32[]{:S(2)}, u32[]{:S(2)}) collective-permute-start(f32[8,1280]{1,0:T(8,128)S(1)} %fusion.129), channel_id=1, source_target_pairs={{0,2},{1,3},{2,0},{3,1},{4,6},{5,7},{6,4},{7,5},{8,10},{9,11},{10,... | collective-permute-start | bytes 122888 | tf_op jit(solution)/shard_map/ppermute | solution.py:55
  83.1 1.9 %collective-permute-start.21 = (f32[8,1280]{1,0:T(8,128)S(1)}, f32[8,1280]{1,0:T(8,128)S(1)}, u32[]{:S(2)}, u32[]{:S(2)}) collective-permute-start(f32[8,1280]{1,0:T(8,128)S(1)} %fusion.129), channel_id=1, source_target_pairs={{0,1},{1,0},{2,3},{3,2},{4,5},{5,4},{6,7},{7,6},{8,9},{9,8},{10,11... | collective-permute-start | bytes 122888 | tf_op jit(solution)/shard_map/ppermute | solution.py:55
  85.1 1.0 %collective-permute-done.23 = f32[8,1280]{1,0:T(8,128)S(1)} collective-permute-done((f32[8,1280]{1,0:T(8,128)S(1)}, f32[8,1280]{1,0:T(8,128)S(1)}, u32[]{:S(2)}, u32[]{:S(2)}) %collective-permute-start.23) | collective-permute-done | bytes 40992 | tf_op jit(solution)/shard_map/ppermute | solution.py:55
  86.1 1.6 %collective-permute-done.22 = f32[8,1280]{1,0:T(8,128)S(1)} collective-permute-done((f32[8,1280]{1,0:T(8,128)S(1)}, f32[8,1280]{1,0:T(8,128)S(1)}, u32[]{:S(2)}, u32[]{:S(2)}) %collective-permute-start.22) | collective-permute-done | bytes 40992 | tf_op jit(solution)/shard_map/ppermute | solution.py:55
  87.7 0.6 gather_fusion.3
  88.8 0.7 fusion.67
  (134 shorter events, 11.3 us)
Async XLA Ops:
  0.0 9.8 %copy-start = (bf16[1280,3,320]{0,2,1:T(8,128)(2,1)S(1)}, bf16[1280,3,320]{0,2,1:T(8,128)(2,1)}, u32[]{:S(2)}) copy-start(bf16[1280,3,320]{0,2,1:T(8,128)(2,1)} %param.10) | copy-start | bytes 7372804
  0.0 5.1 %collective-permute-start.2 = (bf16[1,8,320]{2,1,0:T(8,128)(2,1)}, bf16[1,8,320]{2,1,0:T(8,128)(2,1)S(1)}, u32[]{:S(2)}, u32[]{:S(2)}) collective-permute-start(bf16[1,8,320]{2,1,0:T(8,128)(2,1)} %bitcast.215), channel_id=1, source_target_pairs={{0,3},{1,2},{2,1},{3,0},{4,7},{5,6},{6,5},{7,4},{8,11},{9,10},{10,... | collective-permute-start | bytes 15368 | tf_op jit(solution)/shard_map/ppermute | solution.py:55
  3.0 5.3 %collective-permute-start.1 = (bf16[1,8,320]{2,1,0:T(8,128)(2,1)}, bf16[1,8,320]{2,1,0:T(8,128)(2,1)S(1)}, u32[]{:S(2)}, u32[]{:S(2)}) collective-permute-start(bf16[1,8,320]{2,1,0:T(8,128)(2,1)} %bitcast.216), channel_id=1, source_target_pairs={{0,2},{1,3},{2,0},{3,1},{4,6},{5,7},{6,4},{7,5},{8,10},{9,11},{10,... | collective-permute-start | bytes 15368 | tf_op jit(solution)/shard_map/ppermute | solution.py:55
  3.6 4.7 %collective-permute-start = (bf16[1,8,320]{2,1,0:T(8,128)(2,1)}, bf16[1,8,320]{2,1,0:T(8,128)(2,1)S(1)}, u32[]{:S(2)}, u32[]{:S(2)}) collective-permute-start(bf16[1,8,320]{2,1,0:T(8,128)(2,1)} %bitcast.217), channel_id=1, source_target_pairs={{0,1},{1,0},{2,3},{3,2},{4,5},{5,4},{6,7},{7,6},{8,9},{9,8},{10,11... | collective-permute-start | bytes 15368 | tf_op jit(solution)/shard_map/ppermute | solution.py:55
  11.7 8.8 %copy-start.5 = (s32[24]{0:T(128)S(1)}, s32[24]{0:T(128)}, u32[]{:S(2)}) copy-start(s32[24]{0:T(128)} %param.15) | copy-start | bytes 292
  11.7 9.2 %copy-start.4 = (f32[320]{0:T(512)S(1)}, f32[320]{0:T(512)}, u32[]{:S(2)}) copy-start(f32[320]{0:T(512)} %param.12) | copy-start | bytes 3844
  11.7 9.4 %copy-start.6 = (s32[24]{0:T(128)S(1)}, s32[24]{0:T(128)}, u32[]{:S(2)}) copy-start(s32[24]{0:T(128)} %param.16) | copy-start | bytes 292
  11.7 18.1 %copy-start.1 = (s32[512]{0:T(512)S(1)}, s32[512]{0:T(512)}, u32[]{:S(2)}) copy-start(s32[512]{0:T(512)} %param.14) | copy-start | bytes 6148
  11.7 9.4 %collective-permute-start.5 = (bf16[1,8,320]{2,1,0:T(8,128)(2,1)S(1)}, bf16[1,8,320]{2,1,0:T(8,128)(2,1)S(1)}, u32[]{:S(2)}, u32[]{:S(2)}) collective-permute-start(bf16[1,8,320]{2,1,0:T(8,128)(2,1)S(1)} %bitcast.209), channel_id=1, source_target_pairs={{0,12},{4,8},{8,4},{12,0},{16,28},{20,24},{24,20},{28,16},{32,44},... | collective-permute-start | bytes 15368 | tf_op jit(solution)/shard_map/ppermute | solution.py:77
  11.8 9.3 %collective-permute-start.4 = (bf16[1,8,320]{2,1,0:T(8,128)(2,1)S(1)}, bf16[1,8,320]{2,1,0:T(8,128)(2,1)S(1)}, u32[]{:S(2)}, u32[]{:S(2)}) collective-permute-start(bf16[1,8,320]{2,1,0:T(8,128)(2,1)S(1)} %bitcast.210), channel_id=1, source_target_pairs={{0,8},{4,12},{8,0},{12,4},{16,24},{20,28},{24,16},{28,20},{32,40},... | collective-permute-start | bytes 15368 | tf_op jit(solution)/shard_map/ppermute | solution.py:77
  13.8 7.3 %collective-permute-start.3 = (bf16[1,8,320]{2,1,0:T(8,128)(2,1)S(1)}, bf16[1,8,320]{2,1,0:T(8,128)(2,1)S(1)}, u32[]{:S(2)}, u32[]{:S(2)}) collective-permute-start(bf16[1,8,320]{2,1,0:T(8,128)(2,1)S(1)} %bitcast.211), channel_id=1, source_target_pairs={{0,4},{4,0},{8,12},{12,8},{16,20},{20,16},{24,28},{28,24},{32,36},... | collective-permute-start | bytes 15368 | tf_op jit(solution)/shard_map/ppermute | solution.py:77
  21.2 9.4 %collective-permute-start.8 = (bf16[4,8,320]{2,1,0:T(8,128)(2,1)S(1)}, bf16[4,8,320]{2,1,0:T(8,128)(2,1)S(1)}, u32[]{:S(2)}, u32[]{:S(2)}) collective-permute-start(bf16[4,8,320]{2,1,0:T(8,128)(2,1)S(1)} %get-tuple-element.52), channel_id=1, source_target_pairs={{0,48},{4,52},{8,56},{12,60},{16,32},{20,36},{24,40},{28,44},{32,1... | collective-permute-start | bytes 61448 | tf_op jit(solution)/shard_map/ppermute | solution.py:77
  27.4 8.0 %collective-permute-start.7 = (bf16[4,8,320]{2,1,0:T(8,128)(2,1)S(1)}, bf16[4,8,320]{2,1,0:T(8,128)(2,1)S(1)}, u32[]{:S(2)}, u32[]{:S(2)}) collective-permute-start(bf16[4,8,320]{2,1,0:T(8,128)(2,1)S(1)} %get-tuple-element.52), channel_id=1, source_target_pairs={{0,32},{4,36},{8,40},{12,44},{16,48},{20,52},{24,56},{28,60},{32,0... | collective-permute-start | bytes 61448 | tf_op jit(solution)/shard_map/ppermute | solution.py:77
  28.4 7.0 %collective-permute-start.6 = (bf16[4,8,320]{2,1,0:T(8,128)(2,1)S(1)}, bf16[4,8,320]{2,1,0:T(8,128)(2,1)S(1)}, u32[]{:S(2)}, u32[]{:S(2)}) collective-permute-start(bf16[4,8,320]{2,1,0:T(8,128)(2,1)S(1)} %get-tuple-element.52), channel_id=1, source_target_pairs={{0,16},{4,20},{8,24},{12,28},{16,0},{20,4},{24,8},{28,12},{32,48},... | collective-permute-start | bytes 61448 | tf_op jit(solution)/shard_map/ppermute | solution.py:77
  35.4 7.0 %collective-permute-start.11 = (bf16[16,8,320]{2,1,0:T(8,128)(2,1)S(1)}, bf16[16,8,320]{2,1,0:T(8,128)(2,1)S(1)}, u32[]{:S(2)}, u32[]{:S(2)}) collective-permute-start(bf16[16,8,320]{2,1,0:T(8,128)(2,1)S(1)} %bitcast.193), channel_id=1, source_target_pairs={{0,192},{4,196},{8,200},{12,204},{16,208},{20,212},{24,216},{28,22... | collective-permute-start | bytes 245768 | tf_op jit(solution)/shard_map/ppermute | solution.py:77
  36.0 6.4 %collective-permute-start.10 = (bf16[16,8,320]{2,1,0:T(8,128)(2,1)S(1)}, bf16[16,8,320]{2,1,0:T(8,128)(2,1)S(1)}, u32[]{:S(2)}, u32[]{:S(2)}) collective-permute-start(bf16[16,8,320]{2,1,0:T(8,128)(2,1)S(1)} %bitcast.194), channel_id=1, source_target_pairs={{0,128},{4,132},{8,136},{12,140},{16,144},{20,148},{24,152},{28,15... | collective-permute-start | bytes 245768 | tf_op jit(solution)/shard_map/ppermute | solution.py:77
  38.4 4.8 %collective-permute-start.9 = (bf16[16,8,320]{2,1,0:T(8,128)(2,1)S(1)}, bf16[16,8,320]{2,1,0:T(8,128)(2,1)S(1)}, u32[]{:S(2)}, u32[]{:S(2)}) collective-permute-start(bf16[16,8,320]{2,1,0:T(8,128)(2,1)S(1)} %bitcast.195), channel_id=1, source_target_pairs={{0,64},{4,68},{8,72},{12,76},{16,80},{20,84},{24,88},{28,92},{32,9... | collective-permute-start | bytes 245768 | tf_op jit(solution)/shard_map/ppermute | solution.py:77
  51.3 5.1 %collective-permute-start.14 = (bf16[16,8,330]{2,1,0:T(8,128)(2,1)S(1)}, bf16[16,8,330]{2,1,0:T(8,128)(2,1)S(1)}, u32[]{:S(2)}, u32[]{:S(2)}) collective-permute-start(bf16[16,8,330]{2,1,0:T(8,128)(2,1)S(1)} %pad_maximum_fusion.9), channel_id=1, source_target_pairs={{0,12},{4,8},{8,4},{12,0},{16,28},{20,24},{24,20},{28,16},{32,44},... | collective-permute-start | bytes 253448 | tf_op jit(solution)/shard_map/ppermute | solution.py:95
  52.1 5.8 %collective-permute-start.13 = (bf16[16,8,330]{2,1,0:T(8,128)(2,1)S(1)}, bf16[16,8,330]{2,1,0:T(8,128)(2,1)S(1)}, u32[]{:S(2)}, u32[]{:S(2)}) collective-permute-start(bf16[16,8,330]{2,1,0:T(8,128)(2,1)S(1)} %pad_maximum_fusion.8), channel_id=1, source_target_pairs={{0,8},{4,12},{8,0},{12,4},{16,24},{20,28},{24,16},{28,20},{32,40},... | collective-permute-start | bytes 253448 | tf_op jit(solution)/shard_map/ppermute | solution.py:95
  53.5 27.1 %copy-start.2 = (bf16[320,1280]{1,0:T(8,128)(2,1)S(1)}, bf16[320,1280]{1,0:T(8,128)(2,1)}, u32[]{:S(2)}) copy-start(bf16[320,1280]{1,0:T(8,128)(2,1)} %param.11) | copy-start | bytes 2457604
  53.6 4.3 %collective-permute-start.12 = (bf16[16,8,330]{2,1,0:T(8,128)(2,1)S(1)}, bf16[16,8,330]{2,1,0:T(8,128)(2,1)S(1)}, u32[]{:S(2)}, u32[]{:S(2)}) collective-permute-start(bf16[16,8,330]{2,1,0:T(8,128)(2,1)S(1)} %pad_maximum_fusion.7), channel_id=1, source_target_pairs={{0,4},{4,0},{8,12},{12,8},{16,20},{20,16},{24,28},{28,24},{32,36},... | collective-permute-start | bytes 253448 | tf_op jit(solution)/shard_map/ppermute | solution.py:95
  57.9 27.1 %copy-start.3 = (f32[1280]{0:T(1024)S(1)}, f32[1280]{0:T(1024)}, u32[]{:S(2)}) copy-start(f32[1280]{0:T(1024)} %param.13) | copy-start | bytes 15364
  59.4 7.4 %collective-permute-start.17 = (bf16[4,8,330]{2,1,0:T(8,128)(2,1)S(1)}, bf16[4,8,330]{2,1,0:T(8,128)(2,1)S(1)}, u32[]{:S(2)}, u32[]{:S(2)}) collective-permute-start(bf16[4,8,330]{2,1,0:T(8,128)(2,1)S(1)} %pad_maximum_fusion.14), channel_id=1, source_target_pairs={{0,48},{4,52},{8,56},{12,60},{16,32},{20,36},{24,40},{28,44},{32,1... | collective-permute-start | bytes 63368 | tf_op jit(solution)/shard_map/ppermute | solution.py:95
  61.7 7.8 %collective-permute-start.16 = (bf16[4,8,330]{2,1,0:T(8,128)(2,1)S(1)}, bf16[4,8,330]{2,1,0:T(8,128)(2,1)S(1)}, u32[]{:S(2)}, u32[]{:S(2)}) collective-permute-start(bf16[4,8,330]{2,1,0:T(8,128)(2,1)S(1)} %pad_maximum_fusion.13), channel_id=1, source_target_pairs={{0,32},{4,36},{8,40},{12,44},{16,48},{20,52},{24,56},{28,60},{32,0... | collective-permute-start | bytes 63368 | tf_op jit(solution)/shard_map/ppermute | solution.py:95
  66.0 5.0 %collective-permute-start.15 = (bf16[4,8,330]{2,1,0:T(8,128)(2,1)S(1)}, bf16[4,8,330]{2,1,0:T(8,128)(2,1)S(1)}, u32[]{:S(2)}, u32[]{:S(2)}) collective-permute-start(bf16[4,8,330]{2,1,0:T(8,128)(2,1)S(1)} %pad_maximum_fusion.12), channel_id=1, source_target_pairs={{0,16},{4,20},{8,24},{12,28},{16,0},{20,4},{24,8},{28,12},{32,48},... | collective-permute-start | bytes 63368 | tf_op jit(solution)/shard_map/ppermute | solution.py:95
  72.0 4.9 %collective-permute-start.20 = (bf16[1,8,330]{2,1,0:T(8,128)(2,1)S(1)}, bf16[1,8,330]{2,1,0:T(8,128)(2,1)S(1)}, u32[]{:S(2)}, u32[]{:S(2)}) collective-permute-start(bf16[1,8,330]{2,1,0:T(8,128)(2,1)S(1)} %pad_maximum_fusion.17), channel_id=1, source_target_pairs={{0,192},{4,196},{8,200},{12,204},{16,208},{20,212},{24,216},{28,22... | collective-permute-start | bytes 15848 | tf_op jit(solution)/shard_map/ppermute | solution.py:95
  74.0 5.2 %collective-permute-start.19 = (bf16[1,8,330]{2,1,0:T(8,128)(2,1)S(1)}, bf16[1,8,330]{2,1,0:T(8,128)(2,1)S(1)}, u32[]{:S(2)}, u32[]{:S(2)}) collective-permute-start(bf16[1,8,330]{2,1,0:T(8,128)(2,1)S(1)} %pad_maximum_fusion.16), channel_id=1, source_target_pairs={{0,128},{4,132},{8,136},{12,140},{16,144},{20,148},{24,152},{28,15... | collective-permute-start | bytes 15848 | tf_op jit(solution)/shard_map/ppermute | solution.py:95
  75.8 3.7 %collective-permute-start.18 = (bf16[1,8,330]{2,1,0:T(8,128)(2,1)S(1)}, bf16[1,8,330]{2,1,0:T(8,128)(2,1)S(1)}, u32[]{:S(2)}, u32[]{:S(2)}) collective-permute-start(bf16[1,8,330]{2,1,0:T(8,128)(2,1)S(1)} %pad_maximum_fusion.15), channel_id=1, source_target_pairs={{0,64},{4,68},{8,72},{12,76},{16,80},{20,84},{24,88},{28,92},{32,9... | collective-permute-start | bytes 15848 | tf_op jit(solution)/shard_map/ppermute | solution.py:95
  80.8 5.3 %collective-permute-start.23 = (f32[8,1280]{1,0:T(8,128)S(1)}, f32[8,1280]{1,0:T(8,128)S(1)}, u32[]{:S(2)}, u32[]{:S(2)}) collective-permute-start(f32[8,1280]{1,0:T(8,128)S(1)} %fusion.129), channel_id=1, source_target_pairs={{0,3},{1,2},{2,1},{3,0},{4,7},{5,6},{6,5},{7,4},{8,11},{9,10},{10,... | collective-permute-start | bytes 122888 | tf_op jit(solution)/shard_map/ppermute | solution.py:55
  82.2 5.5 %collective-permute-start.22 = (f32[8,1280]{1,0:T(8,128)S(1)}, f32[8,1280]{1,0:T(8,128)S(1)}, u32[]{:S(2)}, u32[]{:S(2)}) collective-permute-start(f32[8,1280]{1,0:T(8,128)S(1)} %fusion.129), channel_id=1, source_target_pairs={{0,2},{1,3},{2,0},{3,1},{4,6},{5,7},{6,4},{7,5},{8,10},{9,11},{10,... | collective-permute-start | bytes 122888 | tf_op jit(solution)/shard_map/ppermute | solution.py:55
  83.1 4.6 %collective-permute-start.21 = (f32[8,1280]{1,0:T(8,128)S(1)}, f32[8,1280]{1,0:T(8,128)S(1)}, u32[]{:S(2)}, u32[]{:S(2)}) collective-permute-start(f32[8,1280]{1,0:T(8,128)S(1)} %fusion.129), channel_id=1, source_target_pairs={{0,1},{1,0},{2,3},{3,2},{4,5},{5,4},{6,7},{7,6},{8,9},{9,8},{10,11... | collective-permute-start | bytes 122888 | tf_op jit(solution)/shard_map/ppermute | solution.py:55

commit v8 on v7

--- a/solution.py
+++ b/solution.py
@@ -68,18 +68,20 @@
     return held
 
 
-def gather_xor(value, axis):
+def gather_xor(value, axis, riders=(), ride_after=0):
     size = lax.axis_size(axis)
     held = value[None]
     low = 0
-    for width in digit_groups(size):
+    for step, width in enumerate(digit_groups(size)):
         got = [held] + [
             lax.ppermute(held, axis, perm=xor_partner(axis, size, digit << low))
             for digit in range(1, 1 << width)
         ]
         held = jnp.stack(got).reshape((-1,) + value.shape)
-        low += width
-    return held
+        if step == ride_after:
+            held, riders = lax.optimization_barrier((held, riders))
+        low += width
+    return held, riders
 
 
 def scatter_xor(packed, axis, width_acc, heads):
@@ -124,12 +126,16 @@
 
 
 def sum_radix(value, axis):
-    low = 0
-    for width in digit_groups(lax.axis_size(axis)):
-        stacked = exchange(value, axis, low, width)
-        value = stacked[0]
-        for digit in range(1, stacked.shape[0]):
-            value = value + stacked[digit]
+    size = lax.axis_size(axis)
+    low = 0
+    for width in digit_groups(size):
+        got = [value] + [
+            lax.ppermute(value, axis, perm=xor_partner(axis, size, digit << low))
+            for digit in range(1, 1 << width)
+        ]
+        while len(got) > 1:
+            got = [got[i] + got[i + 1] for i in range(0, len(got), 2)]
+        value = got[0]
         low += width
     return value
 
@@ -164,11 +170,11 @@
         precision=lax.Precision.HIGHEST,
     ) / math.sqrt(HEAD_DIM)
 
-    query, page_cache, page_request, page_number, lengths = lax.optimization_barrier(
-        (query, page_cache, page_request, page_number, lengths)
-    )
     seq_index = lax.axis_index("seq")
-    all_queries = gather_xor(query, "seq").reshape(-1, width_local)
+    all_queries, (page_cache, page_request, page_number, lengths) = gather_xor(
+        query, "seq", (page_cache, page_request, page_number, lengths), 0
+    )
+    all_queries = all_queries.reshape(-1, width_local)
     owner_place = ((page_request // rows) ^ seq_index) * rows + page_request % rows
     pages, page_len = (page_cache.shape[0], page_cache.shape[1])
     requests = lengths.shape[0]
@@ -197,11 +203,10 @@
     )
     page_acc = jnp.sum(jnp.where(spread[None], acc_blocks, 0.0), axis=1)
 
-    request_max = jnp.max(jnp.where(onehot[:, :, None], page_max[:, None, :], far_below), axis=0)
+    chosen = jnp.arange(requests, dtype=jnp.int32)[:, None] == owner_place[None, :]
+    request_max = jnp.max(jnp.where(chosen[:, :, None], page_max[None, :, :], far_below), axis=1)
     factor = jnp.exp(page_max - request_max[owner_place])
-    selector = (
-        jnp.arange(requests, dtype=jnp.int32)[:, None] == owner_place[None, :]
-    ).astype(jnp.float32)
+    selector = chosen.astype(jnp.float32)
     request_total = jnp.dot(selector, page_total * factor, precision=lax.Precision.HIGHEST)
     request_acc = jnp.dot(
         selector, page_acc * spread_heads(factor, width_local), precision=lax.Precision.HIGHEST

time: 90.5 us -> 93 us (1.028)
  starting transfers between devices: 36.3 us -> 37.8 us
  waiting for transfers between devices: 22.8 us -> 24.1 us
    ppermute x0 -> x3, starting transfers between devices: none -> 4.74 us  [sum_radix(): lax.ppermute(value, axis, perm=xor_partner(axis, size, digit << low))]
    ppermute x9, waiting for transfers between devices: 9.9 us -> 13.7 us  [scatter_xor(): lax.ppermute(sent, axis, perm=xor_partner(axis, size, digit << low))]
    ppermute x6 -> x3, starting transfers between devices: 8.24 us -> 4.7 us  [exchange(): lax.ppermute(held, axis, perm=xor_partner(axis, size, digit << low))]
    ppermute x9, waiting for transfers between devices: 6.2 us -> 3.54 us  [gather_xor(): lax.ppermute(held, axis, perm=xor_partner(axis, size, digit << low))]
    ppermute x0 -> x3, waiting for transfers between devices: none -> 2.2 us  [sum_radix(): lax.ppermute(value, axis, perm=xor_partner(axis, size, digit << low))]
    ppermute x6 -> x3, waiting for transfers between devices: 6.75 us -> 4.75 us  [exchange(): lax.ppermute(held, axis, perm=xor_partner(axis, size, digit << low))]
  transfers between devices with their start and end apart: 24 -> 24, of which waited for: 13 -> 13; matrix products, arithmetic and copies ran while one was open for 14% -> 15% of each run, Pallas kernels for 0% -> 0%
where the time goes in v8:
time: 93 us; the launch traced here: 92.1 us
  starting transfers between devices  37.8 us (41%)
  waiting for transfers between devices  24.1 us (26%)
  other arithmetic  15.8 us (17%)
  matrix products  9.61 us (10%)
  local copies, waits for them, and re-layouts  4.11 us (4%)
    ppermute x9, starting transfers between devices, gather_xor(): lax.ppermute(held, axis, perm=xor_partner(axis, size, digit << low))  14.7 us
    ppermute x9, starting transfers between devices, scatter_xor(): lax.ppermute(sent, axis, perm=xor_partner(axis, size, digit << low))  13.7 us
    ppermute x9, waiting for transfers between devices, scatter_xor(): lax.ppermute(sent, axis, perm=xor_partner(axis, size, digit << low))  13.7 us
    ppermute x3, waiting for transfers between devices, exchange(): lax.ppermute(held, axis, perm=xor_partner(axis, size, digit << low))  4.75 us
    ppermute x3, starting transfers between devices, sum_radix(): lax.ppermute(value, axis, perm=xor_partner(axis, size, digit << low))  4.74 us
    ppermute x3, starting transfers between devices, exchange(): lax.ppermute(held, axis, perm=xor_partner(axis, size, digit << low))  4.7 us
    mul x3, other arithmetic, head_norm(): shaped * shaped  4.64 us
    dot_general x16, matrix products, spread_heads(): return jnp.dot(factor, spread, precision=lax.Precision.HIGHEST)  4.03 us
  transfers between devices with their start and end apart: 24, of which 13 were waited for; matrix products, arithmetic and copies ran while one was open for 15% of the time, Pallas kernels for 0%

profile of v8, /device:TPU:6, one launch (start us, length us, event | category | flops | bytes accessed | tf_op | source)
XLA Modules:
  0.0 92.1 jit_solution(9697161203631791083)
XLA Ops:
  0.0 1.6 %collective-permute-start = (bf16[1,8,320]{2,1,0:T(8,128)(2,1)}, bf16[1,8,320]{2,1,0:T(8,128)(2,1)S(1)}, u32[]{:S(2)}, u32[]{:S(2)}) collective-permute-start(bf16[1,8,320]{2,1,0:T(8,128)(2,1)} %bitcast.202), channel_id=1, source_target_pairs={{0,1},{1,0},{2,3},{3,2},{4,5},{5,4},{6,7},{7,6},{8,9},{9,8},{10,11... | collective-permute-start | bytes 15368 | tf_op jit(solution)/shard_map/ppermute | solution.py:55
  1.6 2.9 %collective-permute-start.1 = (bf16[1,8,320]{2,1,0:T(8,128)(2,1)}, bf16[1,8,320]{2,1,0:T(8,128)(2,1)S(1)}, u32[]{:S(2)}, u32[]{:S(2)}) collective-permute-start(bf16[1,8,320]{2,1,0:T(8,128)(2,1)} %bitcast.203), channel_id=1, source_target_pairs={{0,2},{1,3},{2,0},{3,1},{4,6},{5,7},{6,4},{7,5},{8,10},{9,11},{10,... | collective-permute-start | bytes 15368 | tf_op jit(solution)/shard_map/ppermute | solution.py:55
  4.8 2.1 %collective-permute-done.1 = bf16[1,8,320]{2,1,0:T(8,128)(2,1)S(1)} collective-permute-done((bf16[1,8,320]{2,1,0:T(8,128)(2,1)}, bf16[1,8,320]{2,1,0:T(8,128)(2,1)S(1)}, u32[]{:S(2)}, u32[]{:S(2)}) %collective-permute-start.1) | collective-permute-done | bytes 5152 | tf_op jit(solution)/shard_map/ppermute | solution.py:55
  6.9 2.6 %collective-permute-done.2 = bf16[1,8,320]{2,1,0:T(8,128)(2,1)S(1)} collective-permute-done((bf16[1,8,320]{2,1,0:T(8,128)(2,1)}, bf16[1,8,320]{2,1,0:T(8,128)(2,1)S(1)}, u32[]{:S(2)}, u32[]{:S(2)}) %collective-permute-start.2) | collective-permute-done | bytes 5152 | tf_op jit(solution)/shard_map/ppermute | solution.py:55
  9.5 0.7 maximum_bitcast_fusion.1
  10.2 0.6 gather_fusion
  11.0 0.7 fusion.123
  12.1 0.8 slice_multiply_fusion.12
  12.9 2.0 %collective-permute-start.4 = (bf16[1,8,320]{2,1,0:T(8,128)(2,1)S(1)}, bf16[1,8,320]{2,1,0:T(8,128)(2,1)S(1)}, u32[]{:S(2)}, u32[]{:S(2)}) collective-permute-start(bf16[1,8,320]{2,1,0:T(8,128)(2,1)S(1)} %bitcast.197), channel_id=1, source_target_pairs={{0,8},{4,12},{8,0},{12,4},{16,24},{20,28},{24,16},{28,20},{32,40},... | collective-permute-start | bytes 15368 | tf_op jit(solution)/shard_map/ppermute | solution.py:77
  15.3 0.9 convolution_multiply_fusion.10
  16.1 0.5 collective-permute-done.4
  16.6 1.3 %collective-permute-done.5 = bf16[1,8,320]{2,1,0:T(8,128)(2,1)S(1)} collective-permute-done((bf16[1,8,320]{2,1,0:T(8,128)(2,1)S(1)}, bf16[1,8,320]{2,1,0:T(8,128)(2,1)S(1)}, u32[]{:S(2)}, u32[]{:S(2)}) %collective-permute-start.5) | collective-permute-done | bytes 5152 | tf_op jit(solution)/shard_map/ppermute | solution.py:77
  18.0 3.4 %collective-permute-start.6 = (bf16[4,8,320]{2,1,0:T(8,128)(2,1)S(1)}, bf16[4,8,320]{2,1,0:T(8,128)(2,1)S(1)}, u32[]{:S(2)}, u32[]{:S(2)}) collective-permute-start(bf16[4,8,320]{2,1,0:T(8,128)(2,1)S(1)} %maximum_bitcast_fusion.2), channel_id=1, source_target_pairs={{0,16},{4,20},{8,24},{12,28},{16,0},{20,4},{24,8},{28,12},{32,48},... | collective-permute-start | bytes 61448 | tf_op jit(solution)/shard_map/ppermute | solution.py:77
  21.4 4.5 %collective-permute-start.7 = (bf16[4,8,320]{2,1,0:T(8,128)(2,1)S(1)}, bf16[4,8,320]{2,1,0:T(8,128)(2,1)S(1)}, u32[]{:S(2)}, u32[]{:S(2)}) collective-permute-start(bf16[4,8,320]{2,1,0:T(8,128)(2,1)S(1)} %maximum_bitcast_fusion.2), channel_id=1, source_target_pairs={{0,32},{4,36},{8,40},{12,44},{16,48},{20,52},{24,56},{28,60},{32,0... | collective-permute-start | bytes 61448 | tf_op jit(solution)/shard_map/ppermute | solution.py:77
  25.9 3.9 %convert_multiply_fusion = f32[24,128,1,320]{1,3,2,0:T(8,128)} fusion(bf16[24,128,2,320]{1,3,2,0:T(8,128)(2,1)} %param.17), kind=kLoop, calls=%fused_computation.3 | loop fusion | flops 1966080 | bytes 5898240 | tf_op jit(solution)/shard_map/mul | solution.py:17
  29.8 2.7 %reduce_sum.122 = f32[24,128,5]{1,2,0:T(8,128)S(1)} reduce(f32[24,128,5,64]{1,3,2,0:T(8,128)} %bitcast.180, f32[]{:T(128)} %constant.122.clone.1), dimensions={3}, to_apply=%region_1.2 | reduce | flops 967680 | bytes 3993604 | tf_op jit(solution)/shard_map/reduce_sum | solution.py:17
  32.6 0.7 gather_fusion.1
  33.4 0.9 collective-permute-start.9
  34.3 1.1 %collective-permute-start.10 = (bf16[16,8,320]{2,1,0:T(8,128)(2,1)S(1)}, bf16[16,8,320]{2,1,0:T(8,128)(2,1)S(1)}, u32[]{:S(2)}, u32[]{:S(2)}) collective-permute-start(bf16[16,8,320]{2,1,0:T(8,128)(2,1)S(1)} %bitcast.185), channel_id=1, source_target_pairs={{0,128},{4,132},{8,136},{12,140},{16,144},{20,148},{24,152},{28,15... | collective-permute-start | bytes 245768 | tf_op jit(solution)/shard_map/ppermute | solution.py:77
  35.4 2.8 %collective-permute-start.11 = (bf16[16,8,320]{2,1,0:T(8,128)(2,1)S(1)}, bf16[16,8,320]{2,1,0:T(8,128)(2,1)S(1)}, u32[]{:S(2)}, u32[]{:S(2)}) collective-permute-start(bf16[16,8,320]{2,1,0:T(8,128)(2,1)S(1)} %bitcast.186), channel_id=1, source_target_pairs={{0,192},{4,196},{8,200},{12,204},{16,208},{20,212},{24,216},{28,22... | collective-permute-start | bytes 245768 | tf_op jit(solution)/shard_map/ppermute | solution.py:77
  38.3 2.2 %fusion.2 = bf16[24,128,320]{1,2,0:T(8,128)(2,1)S(1)} fusion(f32[320]{0:T(512)S(1)} %copy-done.3, f32[24,128,5]{1,2,0:T(8,128)S(1)} %add_sqrt_fusion, bf16[24,128,2,320]{1,3,2,0:T(8,128)(2,1)} %param.17), kind=kLoop, calls=%fused_computation.7 | loop fusion | flops 3932160 | bytes 3994880 | tf_op jit(solution)/shard_map/convert_element_type | solution.py:185
  40.5 1.7 %collective-permute-done.11 = bf16[16,8,320]{2,1,0:T(8,128)(2,1)S(1)} collective-permute-done((bf16[16,8,320]{2,1,0:T(8,128)(2,1)S(1)}, bf16[16,8,320]{2,1,0:T(8,128)(2,1)S(1)}, u32[]{:S(2)}, u32[]{:S(2)}) %collective-permute-start.11) | collective-permute-done | bytes 81952 | tf_op jit(solution)/shard_map/ppermute | solution.py:77
  42.5 0.5 select_reduce_fusion.1
  43.3 2.3 %fusion.5 = f32[24,320]{1,0:T(8,128)S(1)} fusion(pred[5,320]{1,0:T(8,128)(4,1)S(1)} %iota_compare_fusion.6, f32[24,5,128]{2,1,0:T(8,128)S(1)} %get-tuple-element.55, f32[24,5]{1,0:T(8,128)S(1)} %get-tuple-element.54, pred[24,128]{1,0:T(8,128)(4,1)S(1)} %add_compare_fusion, bf16[24,128,2,320]{1,3,2,0:T(8,128)(2,1)} %param.17), kind=kOutput, calls=%fused_computation.14 | convolution fusion | flops 9945600 | bytes 2063392 | tf_op jit(solution)/shard_map/shp,spf->shf/dot_general | solution.py:201
  45.9 0.6 gather_fusion.2
  46.6 0.5 fusion.38
  47.4 0.9 pad_maximum_fusion.1
  48.3 1.4 %copy.32 = f32[512,330]{1,0:T(8,128)S(1)} copy(f32[512,330]{0,1:T(8,128)} %pad_maximum_fusion.1) | data formatting | bytes 1351680 | tf_op jit(solution)/shard_map/concatenate | solution.py:214
  49.8 0.3 fusion.6
  50.6 0.3 fusion.7
  51.0 1.1 %collective-permute-start.13 = (bf16[16,8,330]{2,1,0:T(8,128)(2,1)S(1)}, bf16[16,8,330]{2,1,0:T(8,128)(2,1)S(1)}, u32[]{:S(2)}, u32[]{:S(2)}) collective-permute-start(bf16[16,8,330]{2,1,0:T(8,128)(2,1)S(1)} %pad_maximum_fusion.7), channel_id=1, source_target_pairs={{0,8},{4,12},{8,0},{12,4},{16,24},{20,28},{24,16},{28,20},{32,40},... | collective-permute-start | bytes 253448 | tf_op jit(solution)/shard_map/ppermute | solution.py:97
  52.7 0.9 collective-permute-start.14
  53.6 3.2 %collective-permute-done.13 = bf16[16,8,330]{2,1,0:T(8,128)(2,1)S(1)} collective-permute-done((bf16[16,8,330]{2,1,0:T(8,128)(2,1)S(1)}, bf16[16,8,330]{2,1,0:T(8,128)(2,1)S(1)}, u32[]{:S(2)}, u32[]{:S(2)}) %collective-permute-start.13) | collective-permute-done | bytes 84512 | tf_op jit(solution)/shard_map/ppermute | solution.py:97
  56.8 1.1 %collective-permute-done.14 = bf16[16,8,330]{2,1,0:T(8,128)(2,1)S(1)} collective-permute-done((bf16[16,8,330]{2,1,0:T(8,128)(2,1)S(1)}, bf16[16,8,330]{2,1,0:T(8,128)(2,1)S(1)}, u32[]{:S(2)}, u32[]{:S(2)}) %collective-permute-start.14) | collective-permute-done | bytes 84512 | tf_op jit(solution)/shard_map/ppermute | solution.py:97
  58.2 0.6 fusion.20
  59.5 1.7 %collective-permute-start.15 = (bf16[4,8,330]{2,1,0:T(8,128)(2,1)S(1)}, bf16[4,8,330]{2,1,0:T(8,128)(2,1)S(1)}, u32[]{:S(2)}, u32[]{:S(2)}) collective-permute-start(bf16[4,8,330]{2,1,0:T(8,128)(2,1)S(1)} %pad_maximum_fusion.10), channel_id=1, source_target_pairs={{0,16},{4,20},{8,24},{12,28},{16,0},{20,4},{24,8},{28,12},{32,48},... | collective-permute-start | bytes 63368 | tf_op jit(solution)/shard_map/ppermute | solution.py:97
  61.6 4.5 %collective-permute-start.16 = (bf16[4,8,330]{2,1,0:T(8,128)(2,1)S(1)}, bf16[4,8,330]{2,1,0:T(8,128)(2,1)S(1)}, u32[]{:S(2)}, u32[]{:S(2)}) collective-permute-start(bf16[4,8,330]{2,1,0:T(8,128)(2,1)S(1)} %pad_maximum_fusion.11), channel_id=1, source_target_pairs={{0,32},{4,36},{8,40},{12,44},{16,48},{20,52},{24,56},{28,60},{32,0... | collective-permute-start | bytes 63368 | tf_op jit(solution)/shard_map/ppermute | solution.py:97
  66.6 0.3 collective-permute-start.17
  66.9 2.5 %collective-permute-done.16 = bf16[4,8,330]{2,1,0:T(8,128)(2,1)S(1)} collective-permute-done((bf16[4,8,330]{2,1,0:T(8,128)(2,1)S(1)}, bf16[4,8,330]{2,1,0:T(8,128)(2,1)S(1)}, u32[]{:S(2)}, u32[]{:S(2)}) %collective-permute-start.16) | collective-permute-done | bytes 21152 | tf_op jit(solution)/shard_map/ppermute | solution.py:97
  69.4 3.1 %collective-permute-done.17 = bf16[4,8,330]{2,1,0:T(8,128)(2,1)S(1)} collective-permute-done((bf16[4,8,330]{2,1,0:T(8,128)(2,1)S(1)}, bf16[4,8,330]{2,1,0:T(8,128)(2,1)S(1)}, u32[]{:S(2)}, u32[]{:S(2)}) %collective-permute-start.17) | collective-permute-done | bytes 21152 | tf_op jit(solution)/shard_map/ppermute | solution.py:97
  74.1 3.4 %collective-permute-start.19 = (bf16[1,8,330]{2,1,0:T(8,128)(2,1)S(1)}, bf16[1,8,330]{2,1,0:T(8,128)(2,1)S(1)}, u32[]{:S(2)}, u32[]{:S(2)}) collective-permute-start(bf16[1,8,330]{2,1,0:T(8,128)(2,1)S(1)} %pad_maximum_fusion.14), channel_id=1, source_target_pairs={{0,128},{4,132},{8,136},{12,140},{16,144},{20,148},{24,152},{28,15... | collective-permute-start | bytes 15848 | tf_op jit(solution)/shard_map/ppermute | solution.py:97
  77.9 1.2 %collective-permute-start.20 = (bf16[1,8,330]{2,1,0:T(8,128)(2,1)S(1)}, bf16[1,8,330]{2,1,0:T(8,128)(2,1)S(1)}, u32[]{:S(2)}, u32[]{:S(2)}) collective-permute-start(bf16[1,8,330]{2,1,0:T(8,128)(2,1)S(1)} %pad_maximum_fusion.15), channel_id=1, source_target_pairs={{0,192},{4,196},{8,200},{12,204},{16,208},{20,212},{24,216},{28,22... | collective-permute-start | bytes 15848 | tf_op jit(solution)/shard_map/ppermute | solution.py:97
  79.2 3.5 %collective-permute-done.20 = bf16[1,8,330]{2,1,0:T(8,128)(2,1)S(1)} collective-permute-done((bf16[1,8,330]{2,1,0:T(8,128)(2,1)S(1)}, bf16[1,8,330]{2,1,0:T(8,128)(2,1)S(1)}, u32[]{:S(2)}, u32[]{:S(2)}) %collective-permute-start.20) | collective-permute-done | bytes 5312 | tf_op jit(solution)/shard_map/ppermute | solution.py:97
  84.1 1.7 %collective-permute-start.22 = (f32[8,1280]{1,0:T(8,128)S(1)}, f32[8,1280]{1,0:T(8,128)S(1)}, u32[]{:S(2)}, u32[]{:S(2)}) collective-permute-start(f32[8,1280]{1,0:T(8,128)S(1)} %fusion.124), channel_id=1, source_target_pairs={{0,2},{1,3},{2,0},{3,1},{4,6},{5,7},{6,4},{7,5},{8,10},{9,11},{10,... | collective-permute-start | bytes 122888 | tf_op jit(solution)/shard_map/ppermute | solution.py:133
  85.8 3.0 %collective-permute-start.23 = (f32[8,1280]{1,0:T(8,128)S(1)}, f32[8,1280]{1,0:T(8,128)S(1)}, u32[]{:S(2)}, u32[]{:S(2)}) collective-permute-start(f32[8,1280]{1,0:T(8,128)S(1)} %fusion.124), channel_id=1, source_target_pairs={{0,3},{1,2},{2,1},{3,0},{4,7},{5,6},{6,5},{7,4},{8,11},{9,10},{10,... | collective-permute-start | bytes 122888 | tf_op jit(solution)/shard_map/ppermute | solution.py:133
  88.8 0.9 collective-permute-done.22
  89.7 1.3 %collective-permute-done.23 = f32[8,1280]{1,0:T(8,128)S(1)} collective-permute-done((f32[8,1280]{1,0:T(8,128)S(1)}, f32[8,1280]{1,0:T(8,128)S(1)}, u32[]{:S(2)}, u32[]{:S(2)}) %collective-permute-start.23) | collective-permute-done | bytes 40992 | tf_op jit(solution)/shard_map/ppermute | solution.py:133
  91.4 0.7 fusion.49
  (128 shorter events, 9.4 us)
Async XLA Ops:
  0.0 11.0 %copy-start = (bf16[1280,3,320]{0,2,1:T(8,128)(2,1)S(1)}, bf16[1280,3,320]{0,2,1:T(8,128)(2,1)}, u32[]{:S(2)}) copy-start(bf16[1280,3,320]{0,2,1:T(8,128)(2,1)} %param.10) | copy-start | bytes 7372804
  0.0 4.8 %collective-permute-start = (bf16[1,8,320]{2,1,0:T(8,128)(2,1)}, bf16[1,8,320]{2,1,0:T(8,128)(2,1)S(1)}, u32[]{:S(2)}, u32[]{:S(2)}) collective-permute-start(bf16[1,8,320]{2,1,0:T(8,128)(2,1)} %bitcast.202), channel_id=1, source_target_pairs={{0,1},{1,0},{2,3},{3,2},{4,5},{5,4},{6,7},{7,6},{8,9},{9,8},{10,11... | collective-permute-start | bytes 15368 | tf_op jit(solution)/shard_map/ppermute | solution.py:55
  1.6 5.3 %collective-permute-start.1 = (bf16[1,8,320]{2,1,0:T(8,128)(2,1)}, bf16[1,8,320]{2,1,0:T(8,128)(2,1)S(1)}, u32[]{:S(2)}, u32[]{:S(2)}) collective-permute-start(bf16[1,8,320]{2,1,0:T(8,128)(2,1)} %bitcast.203), channel_id=1, source_target_pairs={{0,2},{1,3},{2,0},{3,1},{4,6},{5,7},{6,4},{7,5},{8,10},{9,11},{10,... | collective-permute-start | bytes 15368 | tf_op jit(solution)/shard_map/ppermute | solution.py:55
  4.5 5.1 %collective-permute-start.2 = (bf16[1,8,320]{2,1,0:T(8,128)(2,1)}, bf16[1,8,320]{2,1,0:T(8,128)(2,1)S(1)}, u32[]{:S(2)}, u32[]{:S(2)}) collective-permute-start(bf16[1,8,320]{2,1,0:T(8,128)(2,1)} %bitcast.204), channel_id=1, source_target_pairs={{0,3},{1,2},{2,1},{3,0},{4,7},{5,6},{6,5},{7,4},{8,11},{9,10},{10,... | collective-permute-start | bytes 15368 | tf_op jit(solution)/shard_map/ppermute | solution.py:55
  12.9 3.3 %collective-permute-start.3 = (bf16[1,8,320]{2,1,0:T(8,128)(2,1)S(1)}, bf16[1,8,320]{2,1,0:T(8,128)(2,1)S(1)}, u32[]{:S(2)}, u32[]{:S(2)}) collective-permute-start(bf16[1,8,320]{2,1,0:T(8,128)(2,1)S(1)} %bitcast.196), channel_id=1, source_target_pairs={{0,4},{4,0},{8,12},{12,8},{16,20},{20,16},{24,28},{28,24},{32,36},... | collective-permute-start | bytes 15368 | tf_op jit(solution)/shard_map/ppermute | solution.py:77
  12.9 3.7 %collective-permute-start.4 = (bf16[1,8,320]{2,1,0:T(8,128)(2,1)S(1)}, bf16[1,8,320]{2,1,0:T(8,128)(2,1)S(1)}, u32[]{:S(2)}, u32[]{:S(2)}) collective-permute-start(bf16[1,8,320]{2,1,0:T(8,128)(2,1)S(1)} %bitcast.197), channel_id=1, source_target_pairs={{0,8},{4,12},{8,0},{12,4},{16,24},{20,28},{24,16},{28,20},{32,40},... | collective-permute-start | bytes 15368 | tf_op jit(solution)/shard_map/ppermute | solution.py:77
  14.9 3.1 %collective-permute-start.5 = (bf16[1,8,320]{2,1,0:T(8,128)(2,1)S(1)}, bf16[1,8,320]{2,1,0:T(8,128)(2,1)S(1)}, u32[]{:S(2)}, u32[]{:S(2)}) collective-permute-start(bf16[1,8,320]{2,1,0:T(8,128)(2,1)S(1)} %bitcast.198), channel_id=1, source_target_pairs={{0,12},{4,8},{8,4},{12,0},{16,28},{20,24},{24,20},{28,16},{32,44},... | collective-permute-start | bytes 15368 | tf_op jit(solution)/shard_map/ppermute | solution.py:77
  18.0 14.5 %copy-start.6 = (s32[24]{0:T(128)S(1)}, s32[24]{0:T(128)}, u32[]{:S(2)}) copy-start(s32[24]{0:T(128)} %param.16) | copy-start | bytes 292
  18.0 14.5 %copy-start.5 = (s32[24]{0:T(128)S(1)}, s32[24]{0:T(128)}, u32[]{:S(2)}) copy-start(s32[24]{0:T(128)} %param.15) | copy-start | bytes 292
  18.0 14.6 %copy-start.1 = (s32[512]{0:T(512)S(1)}, s32[512]{0:T(512)}, u32[]{:S(2)}) copy-start(s32[512]{0:T(512)} %param.14) | copy-start | bytes 6148
  18.0 15.3 %collective-permute-start.6 = (bf16[4,8,320]{2,1,0:T(8,128)(2,1)S(1)}, bf16[4,8,320]{2,1,0:T(8,128)(2,1)S(1)}, u32[]{:S(2)}, u32[]{:S(2)}) collective-permute-start(bf16[4,8,320]{2,1,0:T(8,128)(2,1)S(1)} %maximum_bitcast_fusion.2), channel_id=1, source_target_pairs={{0,16},{4,20},{8,24},{12,28},{16,0},{20,4},{24,8},{28,12},{32,48},... | collective-permute-start | bytes 61448 | tf_op jit(solution)/shard_map/ppermute | solution.py:77
  21.4 12.0 %collective-permute-start.7 = (bf16[4,8,320]{2,1,0:T(8,128)(2,1)S(1)}, bf16[4,8,320]{2,1,0:T(8,128)(2,1)S(1)}, u32[]{:S(2)}, u32[]{:S(2)}) collective-permute-start(bf16[4,8,320]{2,1,0:T(8,128)(2,1)S(1)} %maximum_bitcast_fusion.2), channel_id=1, source_target_pairs={{0,32},{4,36},{8,40},{12,44},{16,48},{20,52},{24,56},{28,60},{32,0... | collective-permute-start | bytes 61448 | tf_op jit(solution)/shard_map/ppermute | solution.py:77
  25.9 7.5 %collective-permute-start.8 = (bf16[4,8,320]{2,1,0:T(8,128)(2,1)S(1)}, bf16[4,8,320]{2,1,0:T(8,128)(2,1)S(1)}, u32[]{:S(2)}, u32[]{:S(2)}) collective-permute-start(bf16[4,8,320]{2,1,0:T(8,128)(2,1)S(1)} %maximum_bitcast_fusion.2), channel_id=1, source_target_pairs={{0,48},{4,52},{8,56},{12,60},{16,32},{20,36},{24,40},{28,44},{32,1... | collective-permute-start | bytes 61448 | tf_op jit(solution)/shard_map/ppermute | solution.py:77
  29.8 8.5 %copy-start.3 = (f32[320]{0:T(512)S(1)}, f32[320]{0:T(512)}, u32[]{:S(2)}) copy-start(f32[320]{0:T(512)} %param.12) | copy-start | bytes 3844
  33.4 7.1 %collective-permute-start.9 = (bf16[16,8,320]{2,1,0:T(8,128)(2,1)S(1)}, bf16[16,8,320]{2,1,0:T(8,128)(2,1)S(1)}, u32[]{:S(2)}, u32[]{:S(2)}) collective-permute-start(bf16[16,8,320]{2,1,0:T(8,128)(2,1)S(1)} %bitcast.184), channel_id=1, source_target_pairs={{0,64},{4,68},{8,72},{12,76},{16,80},{20,84},{24,88},{28,92},{32,9... | collective-permute-start | bytes 245768 | tf_op jit(solution)/shard_map/ppermute | solution.py:77
  34.3 6.2 %collective-permute-start.10 = (bf16[16,8,320]{2,1,0:T(8,128)(2,1)S(1)}, bf16[16,8,320]{2,1,0:T(8,128)(2,1)S(1)}, u32[]{:S(2)}, u32[]{:S(2)}) collective-permute-start(bf16[16,8,320]{2,1,0:T(8,128)(2,1)S(1)} %bitcast.185), channel_id=1, source_target_pairs={{0,128},{4,132},{8,136},{12,140},{16,144},{20,148},{24,152},{28,15... | collective-permute-start | bytes 245768 | tf_op jit(solution)/shard_map/ppermute | solution.py:77
  35.4 6.8 %collective-permute-start.11 = (bf16[16,8,320]{2,1,0:T(8,128)(2,1)S(1)}, bf16[16,8,320]{2,1,0:T(8,128)(2,1)S(1)}, u32[]{:S(2)}, u32[]{:S(2)}) collective-permute-start(bf16[16,8,320]{2,1,0:T(8,128)(2,1)S(1)} %bitcast.186), channel_id=1, source_target_pairs={{0,192},{4,196},{8,200},{12,204},{16,208},{20,212},{24,216},{28,22... | collective-permute-start | bytes 245768 | tf_op jit(solution)/shard_map/ppermute | solution.py:77
  50.2 3.4 %collective-permute-start.12 = (bf16[16,8,330]{2,1,0:T(8,128)(2,1)S(1)}, bf16[16,8,330]{2,1,0:T(8,128)(2,1)S(1)}, u32[]{:S(2)}, u32[]{:S(2)}) collective-permute-start(bf16[16,8,330]{2,1,0:T(8,128)(2,1)S(1)} %pad_maximum_fusion.6), channel_id=1, source_target_pairs={{0,4},{4,0},{8,12},{12,8},{16,20},{20,16},{24,28},{28,24},{32,36},... | collective-permute-start | bytes 253448 | tf_op jit(solution)/shard_map/ppermute | solution.py:97
  51.0 5.8 %collective-permute-start.13 = (bf16[16,8,330]{2,1,0:T(8,128)(2,1)S(1)}, bf16[16,8,330]{2,1,0:T(8,128)(2,1)S(1)}, u32[]{:S(2)}, u32[]{:S(2)}) collective-permute-start(bf16[16,8,330]{2,1,0:T(8,128)(2,1)S(1)} %pad_maximum_fusion.7), channel_id=1, source_target_pairs={{0,8},{4,12},{8,0},{12,4},{16,24},{20,28},{24,16},{28,20},{32,40},... | collective-permute-start | bytes 253448 | tf_op jit(solution)/shard_map/ppermute | solution.py:97
  52.6 31.3 %copy-start.2 = (bf16[320,1280]{1,0:T(8,128)(2,1)S(1)}, bf16[320,1280]{1,0:T(8,128)(2,1)}, u32[]{:S(2)}) copy-start(bf16[320,1280]{1,0:T(8,128)(2,1)} %param.11) | copy-start | bytes 2457604
  52.7 5.3 %collective-permute-start.14 = (bf16[16,8,330]{2,1,0:T(8,128)(2,1)S(1)}, bf16[16,8,330]{2,1,0:T(8,128)(2,1)S(1)}, u32[]{:S(2)}, u32[]{:S(2)}) collective-permute-start(bf16[16,8,330]{2,1,0:T(8,128)(2,1)S(1)} %pad_maximum_fusion.8), channel_id=1, source_target_pairs={{0,12},{4,8},{8,4},{12,0},{16,28},{20,24},{24,20},{28,16},{32,44},... | collective-permute-start | bytes 253448 | tf_op jit(solution)/shard_map/ppermute | solution.py:97
  58.0 33.2 %copy-start.4 = (f32[1280]{0:T(1024)S(1)}, f32[1280]{0:T(1024)}, u32[]{:S(2)}) copy-start(f32[1280]{0:T(1024)} %param.13) | copy-start | bytes 15364
  59.5 7.4 %collective-permute-start.15 = (bf16[4,8,330]{2,1,0:T(8,128)(2,1)S(1)}, bf16[4,8,330]{2,1,0:T(8,128)(2,1)S(1)}, u32[]{:S(2)}, u32[]{:S(2)}) collective-permute-start(bf16[4,8,330]{2,1,0:T(8,128)(2,1)S(1)} %pad_maximum_fusion.10), channel_id=1, source_target_pairs={{0,16},{4,20},{8,24},{12,28},{16,0},{20,4},{24,8},{28,12},{32,48},... | collective-permute-start | bytes 63368 | tf_op jit(solution)/shard_map/ppermute | solution.py:97
  61.6 7.8 %collective-permute-start.16 = (bf16[4,8,330]{2,1,0:T(8,128)(2,1)S(1)}, bf16[4,8,330]{2,1,0:T(8,128)(2,1)S(1)}, u32[]{:S(2)}, u32[]{:S(2)}) collective-permute-start(bf16[4,8,330]{2,1,0:T(8,128)(2,1)S(1)} %pad_maximum_fusion.11), channel_id=1, source_target_pairs={{0,32},{4,36},{8,40},{12,44},{16,48},{20,52},{24,56},{28,60},{32,0... | collective-permute-start | bytes 63368 | tf_op jit(solution)/shard_map/ppermute | solution.py:97
  66.6 6.0 %collective-permute-start.17 = (bf16[4,8,330]{2,1,0:T(8,128)(2,1)S(1)}, bf16[4,8,330]{2,1,0:T(8,128)(2,1)S(1)}, u32[]{:S(2)}, u32[]{:S(2)}) collective-permute-start(bf16[4,8,330]{2,1,0:T(8,128)(2,1)S(1)} %pad_maximum_fusion.12), channel_id=1, source_target_pairs={{0,48},{4,52},{8,56},{12,60},{16,32},{20,36},{24,40},{28,44},{32,1... | collective-permute-start | bytes 63368 | tf_op jit(solution)/shard_map/ppermute | solution.py:97
  73.5 5.5 %collective-permute-start.18 = (bf16[1,8,330]{2,1,0:T(8,128)(2,1)S(1)}, bf16[1,8,330]{2,1,0:T(8,128)(2,1)S(1)}, u32[]{:S(2)}, u32[]{:S(2)}) collective-permute-start(bf16[1,8,330]{2,1,0:T(8,128)(2,1)S(1)} %pad_maximum_fusion.13), channel_id=1, source_target_pairs={{0,64},{4,68},{8,72},{12,76},{16,80},{20,84},{24,88},{28,92},{32,9... | collective-permute-start | bytes 15848 | tf_op jit(solution)/shard_map/ppermute | solution.py:97
  74.1 5.2 %collective-permute-start.19 = (bf16[1,8,330]{2,1,0:T(8,128)(2,1)S(1)}, bf16[1,8,330]{2,1,0:T(8,128)(2,1)S(1)}, u32[]{:S(2)}, u32[]{:S(2)}) collective-permute-start(bf16[1,8,330]{2,1,0:T(8,128)(2,1)S(1)} %pad_maximum_fusion.14), channel_id=1, source_target_pairs={{0,128},{4,132},{8,136},{12,140},{16,144},{20,148},{24,152},{28,15... | collective-permute-start | bytes 15848 | tf_op jit(solution)/shard_map/ppermute | solution.py:97
  77.9 4.9 %collective-permute-start.20 = (bf16[1,8,330]{2,1,0:T(8,128)(2,1)S(1)}, bf16[1,8,330]{2,1,0:T(8,128)(2,1)S(1)}, u32[]{:S(2)}, u32[]{:S(2)}) collective-permute-start(bf16[1,8,330]{2,1,0:T(8,128)(2,1)S(1)} %pad_maximum_fusion.15), channel_id=1, source_target_pairs={{0,192},{4,196},{8,200},{12,204},{16,208},{20,212},{24,216},{28,22... | collective-permute-start | bytes 15848 | tf_op jit(solution)/shard_map/ppermute | solution.py:97
  84.1 4.8 %collective-permute-start.21 = (f32[8,1280]{1,0:T(8,128)S(1)}, f32[8,1280]{1,0:T(8,128)S(1)}, u32[]{:S(2)}, u32[]{:S(2)}) collective-permute-start(f32[8,1280]{1,0:T(8,128)S(1)} %fusion.124), channel_id=1, source_target_pairs={{0,1},{1,0},{2,3},{3,2},{4,5},{5,4},{6,7},{7,6},{8,9},{9,8},{10,11... | collective-permute-start | bytes 122888 | tf_op jit(solution)/shard_map/ppermute | solution.py:133
  84.1 5.6 %collective-permute-start.22 = (f32[8,1280]{1,0:T(8,128)S(1)}, f32[8,1280]{1,0:T(8,128)S(1)}, u32[]{:S(2)}, u32[]{:S(2)}) collective-permute-start(f32[8,1280]{1,0:T(8,128)S(1)} %fusion.124), channel_id=1, source_target_pairs={{0,2},{1,3},{2,0},{3,1},{4,6},{5,7},{6,4},{7,5},{8,10},{9,11},{10,... | collective-permute-start | bytes 122888 | tf_op jit(solution)/shard_map/ppermute | solution.py:133
  85.8 5.2 %collective-permute-start.23 = (f32[8,1280]{1,0:T(8,128)S(1)}, f32[8,1280]{1,0:T(8,128)S(1)}, u32[]{:S(2)}, u32[]{:S(2)}) collective-permute-start(f32[8,1280]{1,0:T(8,128)S(1)} %fusion.124), channel_id=1, source_target_pairs={{0,3},{1,2},{2,1},{3,0},{4,7},{5,6},{6,5},{7,4},{8,11},{9,10},{10,... | collective-permute-start | bytes 122888 | tf_op jit(solution)/shard_map/ppermute | solution.py:133

commit v9 on v8

--- a/solution.py
+++ b/solution.py
@@ -171,9 +171,10 @@
     ) / math.sqrt(HEAD_DIM)
 
     seq_index = lax.axis_index("seq")
-    all_queries, (page_cache, page_request, page_number, lengths) = gather_xor(
-        query, "seq", (page_cache, page_request, page_number, lengths), 0
-    )
+    query, page_cache, page_request, page_number, lengths = lax.optimization_barrier(
+        (query, page_cache, page_request, page_number, lengths)
+    )
+    all_queries, _ = gather_xor(query, "seq")
     all_queries = all_queries.reshape(-1, width_local)
     owner_place = ((page_request // rows) ^ seq_index) * rows + page_request % rows
     pages, page_len = (page_cache.shape[0], page_cache.shape[1])

time: 93 us -> 90.1 us (0.969)
  starting transfers between devices: 37.8 us -> 35.7 us
    ppermute x9, waiting for transfers between devices: 13.7 us -> 9.91 us  [scatter_xor(): lax.ppermute(sent, axis, perm=xor_partner(axis, size, digit << low))]
    ppermute x9, waiting for transfers between devices: 3.54 us -> 6.2 us  [gather_xor(): lax.ppermute(held, axis, perm=xor_partner(axis, size, digit << low))]
    ppermute x3, waiting for transfers between devices: 2.2 us -> 3.75 us  [sum_radix(): lax.ppermute(value, axis, perm=xor_partner(axis, size, digit << low))]
    ppermute x3, starting transfers between devices: 4.74 us -> 3.54 us  [sum_radix(): lax.ppermute(value, axis, perm=xor_partner(axis, size, digit << low))]
  transfers between devices with their start and end apart: 24 -> 24, of which waited for: 13 -> 13; matrix products, arithmetic and copies ran while one was open for 15% -> 14% of each run, Pallas kernels for 0% -> 0%
where the time goes in v9:
time: 90.1 us; the launch traced here: 89.1 us
  starting transfers between devices  35.7 us (40%)
  waiting for transfers between devices  24 us (27%)
  other arithmetic  15.8 us (18%)
  matrix products  8.93 us (10%)
  local copies, waits for them, and re-layouts  4.1 us (5%)
    ppermute x9, starting transfers between devices, gather_xor(): lax.ppermute(held, axis, perm=xor_partner(axis, size, digit << low))  15 us
    ppermute x9, starting transfers between devices, scatter_xor(): lax.ppermute(sent, axis, perm=xor_partner(axis, size, digit << low))  13.1 us
    ppermute x9, waiting for transfers between devices, scatter_xor(): lax.ppermute(sent, axis, perm=xor_partner(axis, size, digit << low))  9.91 us
    ppermute x9, waiting for transfers between devices, gather_xor(): lax.ppermute(held, axis, perm=xor_partner(axis, size, digit << low))  6.2 us
    mul x3, other arithmetic, head_norm(): shaped * shaped  4.64 us
    ppermute x3, waiting for transfers between devices, exchange(): lax.ppermute(held, axis, perm=xor_partner(axis, size, digit << low))  4.19 us
    ppermute x3, starting transfers between devices, exchange(): lax.ppermute(held, axis, perm=xor_partner(axis, size, digit << low))  4.09 us
    dot_general x16, matrix products, spread_heads(): return jnp.dot(factor, spread, precision=lax.Precision.HIGHEST)  4.03 us
  transfers between devices with their start and end apart: 24, of which 13 were waited for; matrix products, arithmetic and copies ran while one was open for 14% of the time, Pallas kernels for 0%

profile of v9, /device:TPU:6, one launch (start us, length us, event | category | flops | bytes accessed | tf_op | source)
XLA Modules:
  0.0 89.1 jit_solution(14236880018068764227)
XLA Ops:
  0.0 3.0 %collective-permute-start.2 = (bf16[1,8,320]{2,1,0:T(8,128)(2,1)}, bf16[1,8,320]{2,1,0:T(8,128)(2,1)S(1)}, u32[]{:S(2)}, u32[]{:S(2)}) collective-permute-start(bf16[1,8,320]{2,1,0:T(8,128)(2,1)} %bitcast.202), channel_id=1, source_target_pairs={{0,3},{1,2},{2,1},{3,0},{4,7},{5,6},{6,5},{7,4},{8,11},{9,10},{10,... | collective-permute-start | bytes 15368 | tf_op jit(solution)/shard_map/ppermute | solution.py:55
  3.0 0.6 collective-permute-start.1
  4.2 0.9 collective-permute-done.2
  5.1 3.3 %collective-permute-done.1 = bf16[1,8,320]{2,1,0:T(8,128)(2,1)S(1)} collective-permute-done((bf16[1,8,320]{2,1,0:T(8,128)(2,1)}, bf16[1,8,320]{2,1,0:T(8,128)(2,1)S(1)}, u32[]{:S(2)}, u32[]{:S(2)}) %collective-permute-start.1) | collective-permute-done | bytes 5152 | tf_op jit(solution)/shard_map/ppermute | solution.py:55
  8.4 0.7 maximum_bitcast_fusion.1
  9.1 0.6 gather_fusion
  9.8 0.7 fusion.123
  10.9 0.8 slice_multiply_fusion.12
  11.8 2.0 %collective-permute-start.4 = (bf16[1,8,320]{2,1,0:T(8,128)(2,1)S(1)}, bf16[1,8,320]{2,1,0:T(8,128)(2,1)S(1)}, u32[]{:S(2)}, u32[]{:S(2)}) collective-permute-start(bf16[1,8,320]{2,1,0:T(8,128)(2,1)S(1)} %bitcast.197), channel_id=1, source_target_pairs={{0,8},{4,12},{8,0},{12,4},{16,24},{20,28},{24,16},{28,20},{32,40},... | collective-permute-start | bytes 15368 | tf_op jit(solution)/shard_map/ppermute | solution.py:77
  13.9 3.9 %convert_multiply_fusion = f32[24,128,1,320]{1,3,2,0:T(8,128)} fusion(bf16[24,128,2,320]{1,3,2,0:T(8,128)(2,1)} %param.17), kind=kLoop, calls=%fused_computation.3 | loop fusion | flops 1966080 | bytes 5898240 | tf_op jit(solution)/shard_map/mul | solution.py:17
  17.7 2.7 %reduce_sum.122 = f32[24,128,5]{1,2,0:T(8,128)S(1)} reduce(f32[24,128,5,64]{1,3,2,0:T(8,128)} %bitcast.180, f32[]{:T(128)} %constant.122.clone.1), dimensions={3}, to_apply=%region_1.2 | reduce | flops 967680 | bytes 3993604 | tf_op jit(solution)/shard_map/reduce_sum | solution.py:17
  21.2 6.2 %collective-permute-start.8 = (bf16[4,8,320]{2,1,0:T(8,128)(2,1)S(1)}, bf16[4,8,320]{2,1,0:T(8,128)(2,1)S(1)}, u32[]{:S(2)}, u32[]{:S(2)}) collective-permute-start(bf16[4,8,320]{2,1,0:T(8,128)(2,1)S(1)} %maximum_bitcast_fusion.2), channel_id=1, source_target_pairs={{0,48},{4,52},{8,56},{12,60},{16,32},{20,36},{24,40},{28,44},{32,1... | collective-permute-start | bytes 61448 | tf_op jit(solution)/shard_map/ppermute | solution.py:77
  27.4 1.0 %collective-permute-start.7 = (bf16[4,8,320]{2,1,0:T(8,128)(2,1)S(1)}, bf16[4,8,320]{2,1,0:T(8,128)(2,1)S(1)}, u32[]{:S(2)}, u32[]{:S(2)}) collective-permute-start(bf16[4,8,320]{2,1,0:T(8,128)(2,1)S(1)} %maximum_bitcast_fusion.2), channel_id=1, source_target_pairs={{0,32},{4,36},{8,40},{12,44},{16,48},{20,52},{24,56},{28,60},{32,0... | collective-permute-start | bytes 61448 | tf_op jit(solution)/shard_map/ppermute | solution.py:77
  28.4 1.5 %collective-permute-start.6 = (bf16[4,8,320]{2,1,0:T(8,128)(2,1)S(1)}, bf16[4,8,320]{2,1,0:T(8,128)(2,1)S(1)}, u32[]{:S(2)}, u32[]{:S(2)}) collective-permute-start(bf16[4,8,320]{2,1,0:T(8,128)(2,1)S(1)} %maximum_bitcast_fusion.2), channel_id=1, source_target_pairs={{0,16},{4,20},{8,24},{12,28},{16,0},{20,4},{24,8},{28,12},{32,48},... | collective-permute-start | bytes 61448 | tf_op jit(solution)/shard_map/ppermute | solution.py:77
  29.8 0.7 gather_fusion.1
  30.6 4.8 %collective-permute-done.7 = bf16[4,8,320]{2,1,0:T(8,128)(2,1)S(1)} collective-permute-done((bf16[4,8,320]{2,1,0:T(8,128)(2,1)S(1)}, bf16[4,8,320]{2,1,0:T(8,128)(2,1)S(1)}, u32[]{:S(2)}, u32[]{:S(2)}) %collective-permute-start.7) | collective-permute-done | bytes 20512 | tf_op jit(solution)/shard_map/ppermute | solution.py:77
  35.4 0.6 collective-permute-start.11
  36.0 2.4 %collective-permute-start.10 = (bf16[16,8,320]{2,1,0:T(8,128)(2,1)S(1)}, bf16[16,8,320]{2,1,0:T(8,128)(2,1)S(1)}, u32[]{:S(2)}, u32[]{:S(2)}) collective-permute-start(bf16[16,8,320]{2,1,0:T(8,128)(2,1)S(1)} %bitcast.185), channel_id=1, source_target_pairs={{0,128},{4,132},{8,136},{12,140},{16,144},{20,148},{24,152},{28,15... | collective-permute-start | bytes 245768 | tf_op jit(solution)/shard_map/ppermute | solution.py:77
  38.4 1.2 %collective-permute-start.9 = (bf16[16,8,320]{2,1,0:T(8,128)(2,1)S(1)}, bf16[16,8,320]{2,1,0:T(8,128)(2,1)S(1)}, u32[]{:S(2)}, u32[]{:S(2)}) collective-permute-start(bf16[16,8,320]{2,1,0:T(8,128)(2,1)S(1)} %bitcast.186), channel_id=1, source_target_pairs={{0,64},{4,68},{8,72},{12,76},{16,80},{20,84},{24,88},{28,92},{32,9... | collective-permute-start | bytes 245768 | tf_op jit(solution)/shard_map/ppermute | solution.py:77
  39.7 2.2 %fusion.2 = bf16[24,128,320]{1,2,0:T(8,128)(2,1)S(1)} fusion(f32[320]{0:T(512)S(1)} %copy-done.3, f32[24,128,5]{1,2,0:T(8,128)S(1)} %add_sqrt_fusion, bf16[24,128,2,320]{1,3,2,0:T(8,128)(2,1)} %param.17), kind=kLoop, calls=%fused_computation.7 | loop fusion | flops 3932160 | bytes 3994880 | tf_op jit(solution)/shard_map/convert_element_type | solution.py:186
  41.9 0.5 collective-permute-done.11
  42.4 0.9 collective-permute-done.9
  43.6 0.5 select_reduce_fusion.1
  44.6 2.3 %fusion.5 = f32[24,320]{1,0:T(8,128)S(1)} fusion(pred[5,320]{1,0:T(8,128)(4,1)S(1)} %iota_compare_fusion.6, f32[24,5,128]{2,1,0:T(8,128)S(1)} %get-tuple-element.55, f32[24,5]{1,0:T(8,128)S(1)} %get-tuple-element.54, pred[24,128]{1,0:T(8,128)(4,1)S(1)} %add_compare_fusion, bf16[24,128,2,320]{1,3,2,0:T(8,128)(2,1)} %param.17), kind=kOutput, calls=%fused_computation.14 | convolution fusion | flops 9945600 | bytes 2063392 | tf_op jit(solution)/shard_map/shp,spf->shf/dot_general | solution.py:202
  47.0 0.6 gather_fusion.2
  47.9 0.5 fusion.38
  48.4 0.9 %pad_maximum_fusion.1 = f32[512,330]{0,1:T(8,128)} fusion(f32[512,5]{0,1:T(8,128)S(1)} %select_reduce_fusion, f32[512,5]{0,1:T(8,128)S(1)} %fusion.37, f32[512,320]{0,1:T(8,128)S(1)} %fusion.38), kind=kLoop, calls=%fused_computation.46 | loop fusion | flops 337920 | bytes 1351680 | tf_op jit(solution)/shard_map/concatenate | solution.py:215
  49.3 1.4 %copy.32 = f32[512,330]{1,0:T(8,128)S(1)} copy(f32[512,330]{0,1:T(8,128)} %pad_maximum_fusion.1) | data formatting | bytes 1351680 | tf_op jit(solution)/shard_map/concatenate | solution.py:215
  52.1 0.9 %collective-permute-start.13 = (bf16[16,8,330]{2,1,0:T(8,128)(2,1)S(1)}, bf16[16,8,330]{2,1,0:T(8,128)(2,1)S(1)}, u32[]{:S(2)}, u32[]{:S(2)}) collective-permute-start(bf16[16,8,330]{2,1,0:T(8,128)(2,1)S(1)} %pad_maximum_fusion.7), channel_id=1, source_target_pairs={{0,8},{4,12},{8,0},{12,4},{16,24},{20,28},{24,16},{28,20},{32,40},... | collective-permute-start | bytes 253448 | tf_op jit(solution)/shard_map/ppermute | solution.py:97
  53.5 1.1 %collective-permute-start.12 = (bf16[16,8,330]{2,1,0:T(8,128)(2,1)S(1)}, bf16[16,8,330]{2,1,0:T(8,128)(2,1)S(1)}, u32[]{:S(2)}, u32[]{:S(2)}) collective-permute-start(bf16[16,8,330]{2,1,0:T(8,128)(2,1)S(1)} %pad_maximum_fusion.6), channel_id=1, source_target_pairs={{0,4},{4,0},{8,12},{12,8},{16,20},{20,16},{24,28},{28,24},{32,36},... | collective-permute-start | bytes 253448 | tf_op jit(solution)/shard_map/ppermute | solution.py:97
  54.6 1.7 %collective-permute-done.14 = bf16[16,8,330]{2,1,0:T(8,128)(2,1)S(1)} collective-permute-done((bf16[16,8,330]{2,1,0:T(8,128)(2,1)S(1)}, bf16[16,8,330]{2,1,0:T(8,128)(2,1)S(1)}, u32[]{:S(2)}, u32[]{:S(2)}) %collective-permute-start.14) | collective-permute-done | bytes 84512 | tf_op jit(solution)/shard_map/ppermute | solution.py:97
  56.3 1.5 %collective-permute-done.13 = bf16[16,8,330]{2,1,0:T(8,128)(2,1)S(1)} collective-permute-done((bf16[16,8,330]{2,1,0:T(8,128)(2,1)S(1)}, bf16[16,8,330]{2,1,0:T(8,128)(2,1)S(1)}, u32[]{:S(2)}, u32[]{:S(2)}) %collective-permute-start.13) | collective-permute-done | bytes 84512 | tf_op jit(solution)/shard_map/ppermute | solution.py:97
  58.3 0.6 fusion.20
  59.4 1.8 %collective-permute-start.17 = (bf16[4,8,330]{2,1,0:T(8,128)(2,1)S(1)}, bf16[4,8,330]{2,1,0:T(8,128)(2,1)S(1)}, u32[]{:S(2)}, u32[]{:S(2)}) collective-permute-start(bf16[4,8,330]{2,1,0:T(8,128)(2,1)S(1)} %pad_maximum_fusion.12), channel_id=1, source_target_pairs={{0,48},{4,52},{8,56},{12,60},{16,32},{20,36},{24,40},{28,44},{32,1... | collective-permute-start | bytes 63368 | tf_op jit(solution)/shard_map/ppermute | solution.py:97
  61.6 3.9 %collective-permute-start.16 = (bf16[4,8,330]{2,1,0:T(8,128)(2,1)S(1)}, bf16[4,8,330]{2,1,0:T(8,128)(2,1)S(1)}, u32[]{:S(2)}, u32[]{:S(2)}) collective-permute-start(bf16[4,8,330]{2,1,0:T(8,128)(2,1)S(1)} %pad_maximum_fusion.11), channel_id=1, source_target_pairs={{0,32},{4,36},{8,40},{12,44},{16,48},{20,52},{24,56},{28,60},{32,0... | collective-permute-start | bytes 63368 | tf_op jit(solution)/shard_map/ppermute | solution.py:97
  65.9 0.8 collective-permute-start.15
  66.8 2.6 %collective-permute-done.16 = bf16[4,8,330]{2,1,0:T(8,128)(2,1)S(1)} collective-permute-done((bf16[4,8,330]{2,1,0:T(8,128)(2,1)S(1)}, bf16[4,8,330]{2,1,0:T(8,128)(2,1)S(1)}, u32[]{:S(2)}, u32[]{:S(2)}) %collective-permute-start.16) | collective-permute-done | bytes 21152 | tf_op jit(solution)/shard_map/ppermute | solution.py:97
  69.4 1.6 %collective-permute-done.15 = bf16[4,8,330]{2,1,0:T(8,128)(2,1)S(1)} collective-permute-done((bf16[4,8,330]{2,1,0:T(8,128)(2,1)S(1)}, bf16[4,8,330]{2,1,0:T(8,128)(2,1)S(1)}, u32[]{:S(2)}, u32[]{:S(2)}) %collective-permute-start.15) | collective-permute-done | bytes 21152 | tf_op jit(solution)/shard_map/ppermute | solution.py:97
  71.9 1.7 %collective-permute-start.20 = (bf16[1,8,330]{2,1,0:T(8,128)(2,1)S(1)}, bf16[1,8,330]{2,1,0:T(8,128)(2,1)S(1)}, u32[]{:S(2)}, u32[]{:S(2)}) collective-permute-start(bf16[1,8,330]{2,1,0:T(8,128)(2,1)S(1)} %pad_maximum_fusion.15), channel_id=1, source_target_pairs={{0,192},{4,196},{8,200},{12,204},{16,208},{20,212},{24,216},{28,22... | collective-permute-start | bytes 15848 | tf_op jit(solution)/shard_map/ppermute | solution.py:97
  74.0 1.4 %collective-permute-start.19 = (bf16[1,8,330]{2,1,0:T(8,128)(2,1)S(1)}, bf16[1,8,330]{2,1,0:T(8,128)(2,1)S(1)}, u32[]{:S(2)}, u32[]{:S(2)}) collective-permute-start(bf16[1,8,330]{2,1,0:T(8,128)(2,1)S(1)} %pad_maximum_fusion.14), channel_id=1, source_target_pairs={{0,128},{4,132},{8,136},{12,140},{16,144},{20,148},{24,152},{28,15... | collective-permute-start | bytes 15848 | tf_op jit(solution)/shard_map/ppermute | solution.py:97
  75.8 1.1 %collective-permute-start.18 = (bf16[1,8,330]{2,1,0:T(8,128)(2,1)S(1)}, bf16[1,8,330]{2,1,0:T(8,128)(2,1)S(1)}, u32[]{:S(2)}, u32[]{:S(2)}) collective-permute-start(bf16[1,8,330]{2,1,0:T(8,128)(2,1)S(1)} %pad_maximum_fusion.13), channel_id=1, source_target_pairs={{0,64},{4,68},{8,72},{12,76},{16,80},{20,84},{24,88},{28,92},{32,9... | collective-permute-start | bytes 15848 | tf_op jit(solution)/shard_map/ppermute | solution.py:97
  76.9 2.3 %collective-permute-done.19 = bf16[1,8,330]{2,1,0:T(8,128)(2,1)S(1)} collective-permute-done((bf16[1,8,330]{2,1,0:T(8,128)(2,1)S(1)}, bf16[1,8,330]{2,1,0:T(8,128)(2,1)S(1)}, u32[]{:S(2)}, u32[]{:S(2)}) %collective-permute-start.19) | collective-permute-done | bytes 5312 | tf_op jit(solution)/shard_map/ppermute | solution.py:97
  80.8 2.1 %collective-permute-start.22 = (f32[8,1280]{1,0:T(8,128)S(1)}, f32[8,1280]{1,0:T(8,128)S(1)}, u32[]{:S(2)}, u32[]{:S(2)}) collective-permute-start(f32[8,1280]{1,0:T(8,128)S(1)} %fusion.124), channel_id=1, source_target_pairs={{0,2},{1,3},{2,0},{3,1},{4,6},{5,7},{6,4},{7,5},{8,10},{9,11},{10,... | collective-permute-start | bytes 122888 | tf_op jit(solution)/shard_map/ppermute | solution.py:133
  82.8 0.8 collective-permute-start.23
  83.6 0.7 collective-permute-start.21
  84.3 2.0 %collective-permute-done.22 = f32[8,1280]{1,0:T(8,128)S(1)} collective-permute-done((f32[8,1280]{1,0:T(8,128)S(1)}, f32[8,1280]{1,0:T(8,128)S(1)}, u32[]{:S(2)}, u32[]{:S(2)}) %collective-permute-start.22) | collective-permute-done | bytes 40992 | tf_op jit(solution)/shard_map/ppermute | solution.py:133
  86.3 1.7 %collective-permute-done.23 = f32[8,1280]{1,0:T(8,128)S(1)} collective-permute-done((f32[8,1280]{1,0:T(8,128)S(1)}, f32[8,1280]{1,0:T(8,128)S(1)}, u32[]{:S(2)}, u32[]{:S(2)}) %collective-permute-start.23) | collective-permute-done | bytes 40992 | tf_op jit(solution)/shard_map/ppermute | solution.py:133
  88.4 0.7 fusion.49
  (128 shorter events, 10.4 us)
Async XLA Ops:
  0.0 9.8 %copy-start = (bf16[1280,3,320]{0,2,1:T(8,128)(2,1)S(1)}, bf16[1280,3,320]{0,2,1:T(8,128)(2,1)}, u32[]{:S(2)}) copy-start(bf16[1280,3,320]{0,2,1:T(8,128)(2,1)} %param.10) | copy-start | bytes 7372804
  0.0 5.1 %collective-permute-start.2 = (bf16[1,8,320]{2,1,0:T(8,128)(2,1)}, bf16[1,8,320]{2,1,0:T(8,128)(2,1)S(1)}, u32[]{:S(2)}, u32[]{:S(2)}) collective-permute-start(bf16[1,8,320]{2,1,0:T(8,128)(2,1)} %bitcast.202), channel_id=1, source_target_pairs={{0,3},{1,2},{2,1},{3,0},{4,7},{5,6},{6,5},{7,4},{8,11},{9,10},{10,... | collective-permute-start | bytes 15368 | tf_op jit(solution)/shard_map/ppermute | solution.py:55
  3.0 5.3 %collective-permute-start.1 = (bf16[1,8,320]{2,1,0:T(8,128)(2,1)}, bf16[1,8,320]{2,1,0:T(8,128)(2,1)S(1)}, u32[]{:S(2)}, u32[]{:S(2)}) collective-permute-start(bf16[1,8,320]{2,1,0:T(8,128)(2,1)} %bitcast.203), channel_id=1, source_target_pairs={{0,2},{1,3},{2,0},{3,1},{4,6},{5,7},{6,4},{7,5},{8,10},{9,11},{10,... | collective-permute-start | bytes 15368 | tf_op jit(solution)/shard_map/ppermute | solution.py:55
  3.6 4.7 %collective-permute-start = (bf16[1,8,320]{2,1,0:T(8,128)(2,1)}, bf16[1,8,320]{2,1,0:T(8,128)(2,1)S(1)}, u32[]{:S(2)}, u32[]{:S(2)}) collective-permute-start(bf16[1,8,320]{2,1,0:T(8,128)(2,1)} %bitcast.204), channel_id=1, source_target_pairs={{0,1},{1,0},{2,3},{3,2},{4,5},{5,4},{6,7},{7,6},{8,9},{9,8},{10,11... | collective-permute-start | bytes 15368 | tf_op jit(solution)/shard_map/ppermute | solution.py:55
  11.7 8.8 %copy-start.5 = (s32[24]{0:T(128)S(1)}, s32[24]{0:T(128)}, u32[]{:S(2)}) copy-start(s32[24]{0:T(128)} %param.15) | copy-start | bytes 292
  11.7 9.2 %copy-start.3 = (f32[320]{0:T(512)S(1)}, f32[320]{0:T(512)}, u32[]{:S(2)}) copy-start(f32[320]{0:T(512)} %param.12) | copy-start | bytes 3844
  11.7 9.4 %copy-start.6 = (s32[24]{0:T(128)S(1)}, s32[24]{0:T(128)}, u32[]{:S(2)}) copy-start(s32[24]{0:T(128)} %param.16) | copy-start | bytes 292
  11.7 18.1 %copy-start.1 = (s32[512]{0:T(512)S(1)}, s32[512]{0:T(512)}, u32[]{:S(2)}) copy-start(s32[512]{0:T(512)} %param.14) | copy-start | bytes 6148
  11.7 9.4 %collective-permute-start.5 = (bf16[1,8,320]{2,1,0:T(8,128)(2,1)S(1)}, bf16[1,8,320]{2,1,0:T(8,128)(2,1)S(1)}, u32[]{:S(2)}, u32[]{:S(2)}) collective-permute-start(bf16[1,8,320]{2,1,0:T(8,128)(2,1)S(1)} %bitcast.196), channel_id=1, source_target_pairs={{0,12},{4,8},{8,4},{12,0},{16,28},{20,24},{24,20},{28,16},{32,44},... | collective-permute-start | bytes 15368 | tf_op jit(solution)/shard_map/ppermute | solution.py:77
  11.8 9.3 %collective-permute-start.4 = (bf16[1,8,320]{2,1,0:T(8,128)(2,1)S(1)}, bf16[1,8,320]{2,1,0:T(8,128)(2,1)S(1)}, u32[]{:S(2)}, u32[]{:S(2)}) collective-permute-start(bf16[1,8,320]{2,1,0:T(8,128)(2,1)S(1)} %bitcast.197), channel_id=1, source_target_pairs={{0,8},{4,12},{8,0},{12,4},{16,24},{20,28},{24,16},{28,20},{32,40},... | collective-permute-start | bytes 15368 | tf_op jit(solution)/shard_map/ppermute | solution.py:77
  13.8 7.3 %collective-permute-start.3 = (bf16[1,8,320]{2,1,0:T(8,128)(2,1)S(1)}, bf16[1,8,320]{2,1,0:T(8,128)(2,1)S(1)}, u32[]{:S(2)}, u32[]{:S(2)}) collective-permute-start(bf16[1,8,320]{2,1,0:T(8,128)(2,1)S(1)} %bitcast.198), channel_id=1, source_target_pairs={{0,4},{4,0},{8,12},{12,8},{16,20},{20,16},{24,28},{28,24},{32,36},... | collective-permute-start | bytes 15368 | tf_op jit(solution)/shard_map/ppermute | solution.py:77
  21.2 9.4 %collective-permute-start.8 = (bf16[4,8,320]{2,1,0:T(8,128)(2,1)S(1)}, bf16[4,8,320]{2,1,0:T(8,128)(2,1)S(1)}, u32[]{:S(2)}, u32[]{:S(2)}) collective-permute-start(bf16[4,8,320]{2,1,0:T(8,128)(2,1)S(1)} %maximum_bitcast_fusion.2), channel_id=1, source_target_pairs={{0,48},{4,52},{8,56},{12,60},{16,32},{20,36},{24,40},{28,44},{32,1... | collective-permute-start | bytes 61448 | tf_op jit(solution)/shard_map/ppermute | solution.py:77
  27.4 8.0 %collective-permute-start.7 = (bf16[4,8,320]{2,1,0:T(8,128)(2,1)S(1)}, bf16[4,8,320]{2,1,0:T(8,128)(2,1)S(1)}, u32[]{:S(2)}, u32[]{:S(2)}) collective-permute-start(bf16[4,8,320]{2,1,0:T(8,128)(2,1)S(1)} %maximum_bitcast_fusion.2), channel_id=1, source_target_pairs={{0,32},{4,36},{8,40},{12,44},{16,48},{20,52},{24,56},{28,60},{32,0... | collective-permute-start | bytes 61448 | tf_op jit(solution)/shard_map/ppermute | solution.py:77
  28.4 7.0 %collective-permute-start.6 = (bf16[4,8,320]{2,1,0:T(8,128)(2,1)S(1)}, bf16[4,8,320]{2,1,0:T(8,128)(2,1)S(1)}, u32[]{:S(2)}, u32[]{:S(2)}) collective-permute-start(bf16[4,8,320]{2,1,0:T(8,128)(2,1)S(1)} %maximum_bitcast_fusion.2), channel_id=1, source_target_pairs={{0,16},{4,20},{8,24},{12,28},{16,0},{20,4},{24,8},{28,12},{32,48},... | collective-permute-start | bytes 61448 | tf_op jit(solution)/shard_map/ppermute | solution.py:77
  35.4 7.0 %collective-permute-start.11 = (bf16[16,8,320]{2,1,0:T(8,128)(2,1)S(1)}, bf16[16,8,320]{2,1,0:T(8,128)(2,1)S(1)}, u32[]{:S(2)}, u32[]{:S(2)}) collective-permute-start(bf16[16,8,320]{2,1,0:T(8,128)(2,1)S(1)} %bitcast.184), channel_id=1, source_target_pairs={{0,192},{4,196},{8,200},{12,204},{16,208},{20,212},{24,216},{28,22... | collective-permute-start | bytes 245768 | tf_op jit(solution)/shard_map/ppermute | solution.py:77
  36.0 6.4 %collective-permute-start.10 = (bf16[16,8,320]{2,1,0:T(8,128)(2,1)S(1)}, bf16[16,8,320]{2,1,0:T(8,128)(2,1)S(1)}, u32[]{:S(2)}, u32[]{:S(2)}) collective-permute-start(bf16[16,8,320]{2,1,0:T(8,128)(2,1)S(1)} %bitcast.185), channel_id=1, source_target_pairs={{0,128},{4,132},{8,136},{12,140},{16,144},{20,148},{24,152},{28,15... | collective-permute-start | bytes 245768 | tf_op jit(solution)/shard_map/ppermute | solution.py:77
  38.4 4.8 %collective-permute-start.9 = (bf16[16,8,320]{2,1,0:T(8,128)(2,1)S(1)}, bf16[16,8,320]{2,1,0:T(8,128)(2,1)S(1)}, u32[]{:S(2)}, u32[]{:S(2)}) collective-permute-start(bf16[16,8,320]{2,1,0:T(8,128)(2,1)S(1)} %bitcast.186), channel_id=1, source_target_pairs={{0,64},{4,68},{8,72},{12,76},{16,80},{20,84},{24,88},{28,92},{32,9... | collective-permute-start | bytes 245768 | tf_op jit(solution)/shard_map/ppermute | solution.py:77
  51.3 5.1 %collective-permute-start.14 = (bf16[16,8,330]{2,1,0:T(8,128)(2,1)S(1)}, bf16[16,8,330]{2,1,0:T(8,128)(2,1)S(1)}, u32[]{:S(2)}, u32[]{:S(2)}) collective-permute-start(bf16[16,8,330]{2,1,0:T(8,128)(2,1)S(1)} %pad_maximum_fusion.8), channel_id=1, source_target_pairs={{0,12},{4,8},{8,4},{12,0},{16,28},{20,24},{24,20},{28,16},{32,44},... | collective-permute-start | bytes 253448 | tf_op jit(solution)/shard_map/ppermute | solution.py:97
  52.1 5.8 %collective-permute-start.13 = (bf16[16,8,330]{2,1,0:T(8,128)(2,1)S(1)}, bf16[16,8,330]{2,1,0:T(8,128)(2,1)S(1)}, u32[]{:S(2)}, u32[]{:S(2)}) collective-permute-start(bf16[16,8,330]{2,1,0:T(8,128)(2,1)S(1)} %pad_maximum_fusion.7), channel_id=1, source_target_pairs={{0,8},{4,12},{8,0},{12,4},{16,24},{20,28},{24,16},{28,20},{32,40},... | collective-permute-start | bytes 253448 | tf_op jit(solution)/shard_map/ppermute | solution.py:97
  53.4 27.1 %copy-start.2 = (bf16[320,1280]{1,0:T(8,128)(2,1)S(1)}, bf16[320,1280]{1,0:T(8,128)(2,1)}, u32[]{:S(2)}) copy-start(bf16[320,1280]{1,0:T(8,128)(2,1)} %param.11) | copy-start | bytes 2457604
  53.5 4.3 %collective-permute-start.12 = (bf16[16,8,330]{2,1,0:T(8,128)(2,1)S(1)}, bf16[16,8,330]{2,1,0:T(8,128)(2,1)S(1)}, u32[]{:S(2)}, u32[]{:S(2)}) collective-permute-start(bf16[16,8,330]{2,1,0:T(8,128)(2,1)S(1)} %pad_maximum_fusion.6), channel_id=1, source_target_pairs={{0,4},{4,0},{8,12},{12,8},{16,20},{20,16},{24,28},{28,24},{32,36},... | collective-permute-start | bytes 253448 | tf_op jit(solution)/shard_map/ppermute | solution.py:97
  57.9 30.3 %copy-start.4 = (f32[1280]{0:T(1024)S(1)}, f32[1280]{0:T(1024)}, u32[]{:S(2)}) copy-start(f32[1280]{0:T(1024)} %param.13) | copy-start | bytes 15364
  59.4 7.4 %collective-permute-start.17 = (bf16[4,8,330]{2,1,0:T(8,128)(2,1)S(1)}, bf16[4,8,330]{2,1,0:T(8,128)(2,1)S(1)}, u32[]{:S(2)}, u32[]{:S(2)}) collective-permute-start(bf16[4,8,330]{2,1,0:T(8,128)(2,1)S(1)} %pad_maximum_fusion.12), channel_id=1, source_target_pairs={{0,48},{4,52},{8,56},{12,60},{16,32},{20,36},{24,40},{28,44},{32,1... | collective-permute-start | bytes 63368 | tf_op jit(solution)/shard_map/ppermute | solution.py:97
  61.6 7.8 %collective-permute-start.16 = (bf16[4,8,330]{2,1,0:T(8,128)(2,1)S(1)}, bf16[4,8,330]{2,1,0:T(8,128)(2,1)S(1)}, u32[]{:S(2)}, u32[]{:S(2)}) collective-permute-start(bf16[4,8,330]{2,1,0:T(8,128)(2,1)S(1)} %pad_maximum_fusion.11), channel_id=1, source_target_pairs={{0,32},{4,36},{8,40},{12,44},{16,48},{20,52},{24,56},{28,60},{32,0... | collective-permute-start | bytes 63368 | tf_op jit(solution)/shard_map/ppermute | solution.py:97
  65.9 5.0 %collective-permute-start.15 = (bf16[4,8,330]{2,1,0:T(8,128)(2,1)S(1)}, bf16[4,8,330]{2,1,0:T(8,128)(2,1)S(1)}, u32[]{:S(2)}, u32[]{:S(2)}) collective-permute-start(bf16[4,8,330]{2,1,0:T(8,128)(2,1)S(1)} %pad_maximum_fusion.10), channel_id=1, source_target_pairs={{0,16},{4,20},{8,24},{12,28},{16,0},{20,4},{24,8},{28,12},{32,48},... | collective-permute-start | bytes 63368 | tf_op jit(solution)/shard_map/ppermute | solution.py:97
  71.9 4.9 %collective-permute-start.20 = (bf16[1,8,330]{2,1,0:T(8,128)(2,1)S(1)}, bf16[1,8,330]{2,1,0:T(8,128)(2,1)S(1)}, u32[]{:S(2)}, u32[]{:S(2)}) collective-permute-start(bf16[1,8,330]{2,1,0:T(8,128)(2,1)S(1)} %pad_maximum_fusion.15), channel_id=1, source_target_pairs={{0,192},{4,196},{8,200},{12,204},{16,208},{20,212},{24,216},{28,22... | collective-permute-start | bytes 15848 | tf_op jit(solution)/shard_map/ppermute | solution.py:97
  74.0 5.2 %collective-permute-start.19 = (bf16[1,8,330]{2,1,0:T(8,128)(2,1)S(1)}, bf16[1,8,330]{2,1,0:T(8,128)(2,1)S(1)}, u32[]{:S(2)}, u32[]{:S(2)}) collective-permute-start(bf16[1,8,330]{2,1,0:T(8,128)(2,1)S(1)} %pad_maximum_fusion.14), channel_id=1, source_target_pairs={{0,128},{4,132},{8,136},{12,140},{16,144},{20,148},{24,152},{28,15... | collective-permute-start | bytes 15848 | tf_op jit(solution)/shard_map/ppermute | solution.py:97
  75.8 3.7 %collective-permute-start.18 = (bf16[1,8,330]{2,1,0:T(8,128)(2,1)S(1)}, bf16[1,8,330]{2,1,0:T(8,128)(2,1)S(1)}, u32[]{:S(2)}, u32[]{:S(2)}) collective-permute-start(bf16[1,8,330]{2,1,0:T(8,128)(2,1)S(1)} %pad_maximum_fusion.13), channel_id=1, source_target_pairs={{0,64},{4,68},{8,72},{12,76},{16,80},{20,84},{24,88},{28,92},{32,9... | collective-permute-start | bytes 15848 | tf_op jit(solution)/shard_map/ppermute | solution.py:97
  80.8 5.6 %collective-permute-start.22 = (f32[8,1280]{1,0:T(8,128)S(1)}, f32[8,1280]{1,0:T(8,128)S(1)}, u32[]{:S(2)}, u32[]{:S(2)}) collective-permute-start(f32[8,1280]{1,0:T(8,128)S(1)} %fusion.124), channel_id=1, source_target_pairs={{0,2},{1,3},{2,0},{3,1},{4,6},{5,7},{6,4},{7,5},{8,10},{9,11},{10,... | collective-permute-start | bytes 122888 | tf_op jit(solution)/shard_map/ppermute | solution.py:133
  82.8 5.2 %collective-permute-start.23 = (f32[8,1280]{1,0:T(8,128)S(1)}, f32[8,1280]{1,0:T(8,128)S(1)}, u32[]{:S(2)}, u32[]{:S(2)}) collective-permute-start(f32[8,1280]{1,0:T(8,128)S(1)} %fusion.124), channel_id=1, source_target_pairs={{0,3},{1,2},{2,1},{3,0},{4,7},{5,6},{6,5},{7,4},{8,11},{9,10},{10,... | collective-permute-start | bytes 122888 | tf_op jit(solution)/shard_map/ppermute | solution.py:133
  83.6 4.4 %collective-permute-start.21 = (f32[8,1280]{1,0:T(8,128)S(1)}, f32[8,1280]{1,0:T(8,128)S(1)}, u32[]{:S(2)}, u32[]{:S(2)}) collective-permute-start(f32[8,1280]{1,0:T(8,128)S(1)} %fusion.124), channel_id=1, source_target_pairs={{0,1},{1,0},{2,3},{3,2},{4,5},{5,4},{6,7},{7,6},{8,9},{9,8},{10,11... | collective-permute-start | bytes 122888 | tf_op jit(solution)/shard_map/ppermute | solution.py:133

commit v10 on v9

--- a/solution.py
+++ b/solution.py
@@ -129,8 +129,9 @@
     size = lax.axis_size(axis)
     low = 0
     for width in digit_groups(size):
+        sent = value.astype(jnp.bfloat16)
         got = [value] + [
-            lax.ppermute(value, axis, perm=xor_partner(axis, size, digit << low))
+            lax.ppermute(sent, axis, perm=xor_partner(axis, size, digit << low)).astype(value.dtype)
             for digit in range(1, 1 << width)
         ]
         while len(got) > 1:

time: 90.1 us -> 89.5 us (level)
  waiting for transfers between devices: 24 us -> 22.8 us
    ppermute x3, waiting for transfers between devices: 3.75 us -> 2.5 us  [sum_radix(): lax.ppermute(sent, axis, perm=xor_partner(axis, size, digit << low))]
where the time goes in v10:
time: 89.5 us; the launch traced here: 88.5 us
  starting transfers between devices  36.3 us (41%)
  waiting for transfers between devices  22.8 us (25%)
  other arithmetic  15.8 us (18%)
  matrix products  8.93 us (10%)
  local copies, waits for them, and re-layouts  4.1 us (5%)
    ppermute x9, starting transfers between devices, gather_xor(): lax.ppermute(held, axis, perm=xor_partner(axis, size, digit << low))  15 us
    ppermute x9, starting transfers between devices, scatter_xor(): lax.ppermute(sent, axis, perm=xor_partner(axis, size, digit << low))  13.1 us
    ppermute x9, waiting for transfers between devices, scatter_xor(): lax.ppermute(sent, axis, perm=xor_partner(axis, size, digit << low))  9.91 us
    ppermute x9, waiting for transfers between devices, gather_xor(): lax.ppermute(held, axis, perm=xor_partner(axis, size, digit << low))  6.2 us
    mul x3, other arithmetic, head_norm(): shaped * shaped  4.64 us
    ppermute x3, waiting for transfers between devices, exchange(): lax.ppermute(held, axis, perm=xor_partner(axis, size, digit << low))  4.19 us
    ppermute x3, starting transfers between devices, sum_radix(): lax.ppermute(sent, axis, perm=xor_partner(axis, size, digit << low))  4.16 us
    ppermute x3, starting transfers between devices, exchange(): lax.ppermute(held, axis, perm=xor_partner(axis, size, digit << low))  4.09 us
  transfers between devices with their start and end apart: 24, of which 13 were waited for; matrix products, arithmetic and copies ran while one was open for 14% of the time, Pallas kernels for 0%

profile of v10, /device:TPU:6, one launch (start us, length us, event | category | flops | bytes accessed | tf_op | source)
XLA Modules:
  0.0 88.5 jit_solution(7931322177474859515)
XLA Ops:
  0.0 3.0 %collective-permute-start.2 = (bf16[1,8,320]{2,1,0:T(8,128)(2,1)}, bf16[1,8,320]{2,1,0:T(8,128)(2,1)S(1)}, u32[]{:S(2)}, u32[]{:S(2)}) collective-permute-start(bf16[1,8,320]{2,1,0:T(8,128)(2,1)} %bitcast.202), channel_id=1, source_target_pairs={{0,3},{1,2},{2,1},{3,0},{4,7},{5,6},{6,5},{7,4},{8,11},{9,10},{10,... | collective-permute-start | bytes 15368 | tf_op jit(solution)/shard_map/ppermute | solution.py:55
  3.0 0.6 collective-permute-start.1
  4.2 0.9 collective-permute-done.2
  5.1 3.3 %collective-permute-done.1 = bf16[1,8,320]{2,1,0:T(8,128)(2,1)S(1)} collective-permute-done((bf16[1,8,320]{2,1,0:T(8,128)(2,1)}, bf16[1,8,320]{2,1,0:T(8,128)(2,1)S(1)}, u32[]{:S(2)}, u32[]{:S(2)}) %collective-permute-start.1) | collective-permute-done | bytes 5152 | tf_op jit(solution)/shard_map/ppermute | solution.py:55
  8.4 0.7 maximum_bitcast_fusion.1
  9.1 0.6 gather_fusion
  9.8 0.7 fusion.124
  10.9 0.8 slice_multiply_fusion.12
  11.8 2.0 %collective-permute-start.4 = (bf16[1,8,320]{2,1,0:T(8,128)(2,1)S(1)}, bf16[1,8,320]{2,1,0:T(8,128)(2,1)S(1)}, u32[]{:S(2)}, u32[]{:S(2)}) collective-permute-start(bf16[1,8,320]{2,1,0:T(8,128)(2,1)S(1)} %bitcast.197), channel_id=1, source_target_pairs={{0,8},{4,12},{8,0},{12,4},{16,24},{20,28},{24,16},{28,20},{32,40},... | collective-permute-start | bytes 15368 | tf_op jit(solution)/shard_map/ppermute | solution.py:77
  13.9 3.9 %convert_multiply_fusion = f32[24,128,1,320]{1,3,2,0:T(8,128)} fusion(bf16[24,128,2,320]{1,3,2,0:T(8,128)(2,1)} %param.17), kind=kLoop, calls=%fused_computation.3 | loop fusion | flops 1966080 | bytes 5898240 | tf_op jit(solution)/shard_map/mul | solution.py:17
  17.7 2.7 %reduce_sum.122 = f32[24,128,5]{1,2,0:T(8,128)S(1)} reduce(f32[24,128,5,64]{1,3,2,0:T(8,128)} %bitcast.180, f32[]{:T(128)} %constant.122.clone.1), dimensions={3}, to_apply=%region_1.2 | reduce | flops 967680 | bytes 3993604 | tf_op jit(solution)/shard_map/reduce_sum | solution.py:17
  21.2 6.2 %collective-permute-start.8 = (bf16[4,8,320]{2,1,0:T(8,128)(2,1)S(1)}, bf16[4,8,320]{2,1,0:T(8,128)(2,1)S(1)}, u32[]{:S(2)}, u32[]{:S(2)}) collective-permute-start(bf16[4,8,320]{2,1,0:T(8,128)(2,1)S(1)} %maximum_bitcast_fusion.2), channel_id=1, source_target_pairs={{0,48},{4,52},{8,56},{12,60},{16,32},{20,36},{24,40},{28,44},{32,1... | collective-permute-start | bytes 61448 | tf_op jit(solution)/shard_map/ppermute | solution.py:77
  27.4 1.0 %collective-permute-start.7 = (bf16[4,8,320]{2,1,0:T(8,128)(2,1)S(1)}, bf16[4,8,320]{2,1,0:T(8,128)(2,1)S(1)}, u32[]{:S(2)}, u32[]{:S(2)}) collective-permute-start(bf16[4,8,320]{2,1,0:T(8,128)(2,1)S(1)} %maximum_bitcast_fusion.2), channel_id=1, source_target_pairs={{0,32},{4,36},{8,40},{12,44},{16,48},{20,52},{24,56},{28,60},{32,0... | collective-permute-start | bytes 61448 | tf_op jit(solution)/shard_map/ppermute | solution.py:77
  28.4 1.5 %collective-permute-start.6 = (bf16[4,8,320]{2,1,0:T(8,128)(2,1)S(1)}, bf16[4,8,320]{2,1,0:T(8,128)(2,1)S(1)}, u32[]{:S(2)}, u32[]{:S(2)}) collective-permute-start(bf16[4,8,320]{2,1,0:T(8,128)(2,1)S(1)} %maximum_bitcast_fusion.2), channel_id=1, source_target_pairs={{0,16},{4,20},{8,24},{12,28},{16,0},{20,4},{24,8},{28,12},{32,48},... | collective-permute-start | bytes 61448 | tf_op jit(solution)/shard_map/ppermute | solution.py:77
  29.8 0.7 gather_fusion.1
  30.6 4.8 %collective-permute-done.7 = bf16[4,8,320]{2,1,0:T(8,128)(2,1)S(1)} collective-permute-done((bf16[4,8,320]{2,1,0:T(8,128)(2,1)S(1)}, bf16[4,8,320]{2,1,0:T(8,128)(2,1)S(1)}, u32[]{:S(2)}, u32[]{:S(2)}) %collective-permute-start.7) | collective-permute-done | bytes 20512 | tf_op jit(solution)/shard_map/ppermute | solution.py:77
  35.4 0.6 collective-permute-start.11
  36.0 2.4 %collective-permute-start.10 = (bf16[16,8,320]{2,1,0:T(8,128)(2,1)S(1)}, bf16[16,8,320]{2,1,0:T(8,128)(2,1)S(1)}, u32[]{:S(2)}, u32[]{:S(2)}) collective-permute-start(bf16[16,8,320]{2,1,0:T(8,128)(2,1)S(1)} %bitcast.185), channel_id=1, source_target_pairs={{0,128},{4,132},{8,136},{12,140},{16,144},{20,148},{24,152},{28,15... | collective-permute-start | bytes 245768 | tf_op jit(solution)/shard_map/ppermute | solution.py:77
  38.4 1.2 %collective-permute-start.9 = (bf16[16,8,320]{2,1,0:T(8,128)(2,1)S(1)}, bf16[16,8,320]{2,1,0:T(8,128)(2,1)S(1)}, u32[]{:S(2)}, u32[]{:S(2)}) collective-permute-start(bf16[16,8,320]{2,1,0:T(8,128)(2,1)S(1)} %bitcast.186), channel_id=1, source_target_pairs={{0,64},{4,68},{8,72},{12,76},{16,80},{20,84},{24,88},{28,92},{32,9... | collective-permute-start | bytes 245768 | tf_op jit(solution)/shard_map/ppermute | solution.py:77
  39.7 2.2 %fusion.2 = bf16[24,128,320]{1,2,0:T(8,128)(2,1)S(1)} fusion(f32[320]{0:T(512)S(1)} %copy-done.3, f32[24,128,5]{1,2,0:T(8,128)S(1)} %add_sqrt_fusion, bf16[24,128,2,320]{1,3,2,0:T(8,128)(2,1)} %param.17), kind=kLoop, calls=%fused_computation.7 | loop fusion | flops 3932160 | bytes 3994880 | tf_op jit(solution)/shard_map/convert_element_type | solution.py:187
  41.9 0.5 collective-permute-done.11
  42.4 0.9 collective-permute-done.9
  43.6 0.5 select_reduce_fusion.1
  44.6 2.3 %fusion.5 = f32[24,320]{1,0:T(8,128)S(1)} fusion(pred[5,320]{1,0:T(8,128)(4,1)S(1)} %iota_compare_fusion.6, f32[24,5,128]{2,1,0:T(8,128)S(1)} %get-tuple-element.53, f32[24,5]{1,0:T(8,128)S(1)} %get-tuple-element.52, pred[24,128]{1,0:T(8,128)(4,1)S(1)} %add_compare_fusion, bf16[24,128,2,320]{1,3,2,0:T(8,128)(2,1)} %param.17), kind=kOutput, calls=%fused_computation.14 | convolution fusion | flops 9945600 | bytes 2063392 | tf_op jit(solution)/shard_map/shp,spf->shf/dot_general | solution.py:203
  47.0 0.6 gather_fusion.2
  47.9 0.5 fusion.38
  48.4 0.9 %pad_maximum_fusion.1 = f32[512,330]{0,1:T(8,128)} fusion(f32[512,5]{0,1:T(8,128)S(1)} %select_reduce_fusion, f32[512,5]{0,1:T(8,128)S(1)} %fusion.37, f32[512,320]{0,1:T(8,128)S(1)} %fusion.38), kind=kLoop, calls=%fused_computation.46 | loop fusion | flops 337920 | bytes 1351680 | tf_op jit(solution)/shard_map/concatenate | solution.py:216
  49.3 1.4 %copy.32 = f32[512,330]{1,0:T(8,128)S(1)} copy(f32[512,330]{0,1:T(8,128)} %pad_maximum_fusion.1) | data formatting | bytes 1351680 | tf_op jit(solution)/shard_map/concatenate | solution.py:216
  52.1 0.9 %collective-permute-start.13 = (bf16[16,8,330]{2,1,0:T(8,128)(2,1)S(1)}, bf16[16,8,330]{2,1,0:T(8,128)(2,1)S(1)}, u32[]{:S(2)}, u32[]{:S(2)}) collective-permute-start(bf16[16,8,330]{2,1,0:T(8,128)(2,1)S(1)} %pad_maximum_fusion.7), channel_id=1, source_target_pairs={{0,8},{4,12},{8,0},{12,4},{16,24},{20,28},{24,16},{28,20},{32,40},... | collective-permute-start | bytes 253448 | tf_op jit(solution)/shard_map/ppermute | solution.py:97
  53.5 1.1 %collective-permute-start.12 = (bf16[16,8,330]{2,1,0:T(8,128)(2,1)S(1)}, bf16[16,8,330]{2,1,0:T(8,128)(2,1)S(1)}, u32[]{:S(2)}, u32[]{:S(2)}) collective-permute-start(bf16[16,8,330]{2,1,0:T(8,128)(2,1)S(1)} %pad_maximum_fusion.6), channel_id=1, source_target_pairs={{0,4},{4,0},{8,12},{12,8},{16,20},{20,16},{24,28},{28,24},{32,36},... | collective-permute-start | bytes 253448 | tf_op jit(solution)/shard_map/ppermute | solution.py:97
  54.6 1.7 %collective-permute-done.14 = bf16[16,8,330]{2,1,0:T(8,128)(2,1)S(1)} collective-permute-done((bf16[16,8,330]{2,1,0:T(8,128)(2,1)S(1)}, bf16[16,8,330]{2,1,0:T(8,128)(2,1)S(1)}, u32[]{:S(2)}, u32[]{:S(2)}) %collective-permute-start.14) | collective-permute-done | bytes 84512 | tf_op jit(solution)/shard_map/ppermute | solution.py:97
  56.3 1.5 %collective-permute-done.13 = bf16[16,8,330]{2,1,0:T(8,128)(2,1)S(1)} collective-permute-done((bf16[16,8,330]{2,1,0:T(8,128)(2,1)S(1)}, bf16[16,8,330]{2,1,0:T(8,128)(2,1)S(1)}, u32[]{:S(2)}, u32[]{:S(2)}) %collective-permute-start.13) | collective-permute-done | bytes 84512 | tf_op jit(solution)/shard_map/ppermute | solution.py:97
  58.3 0.6 fusion.20
  59.4 1.8 %collective-permute-start.17 = (bf16[4,8,330]{2,1,0:T(8,128)(2,1)S(1)}, bf16[4,8,330]{2,1,0:T(8,128)(2,1)S(1)}, u32[]{:S(2)}, u32[]{:S(2)}) collective-permute-start(bf16[4,8,330]{2,1,0:T(8,128)(2,1)S(1)} %pad_maximum_fusion.12), channel_id=1, source_target_pairs={{0,48},{4,52},{8,56},{12,60},{16,32},{20,36},{24,40},{28,44},{32,1... | collective-permute-start | bytes 63368 | tf_op jit(solution)/shard_map/ppermute | solution.py:97
  61.6 3.9 %collective-permute-start.16 = (bf16[4,8,330]{2,1,0:T(8,128)(2,1)S(1)}, bf16[4,8,330]{2,1,0:T(8,128)(2,1)S(1)}, u32[]{:S(2)}, u32[]{:S(2)}) collective-permute-start(bf16[4,8,330]{2,1,0:T(8,128)(2,1)S(1)} %pad_maximum_fusion.11), channel_id=1, source_target_pairs={{0,32},{4,36},{8,40},{12,44},{16,48},{20,52},{24,56},{28,60},{32,0... | collective-permute-start | bytes 63368 | tf_op jit(solution)/shard_map/ppermute | solution.py:97
  65.9 0.8 collective-permute-start.15
  66.8 2.6 %collective-permute-done.16 = bf16[4,8,330]{2,1,0:T(8,128)(2,1)S(1)} collective-permute-done((bf16[4,8,330]{2,1,0:T(8,128)(2,1)S(1)}, bf16[4,8,330]{2,1,0:T(8,128)(2,1)S(1)}, u32[]{:S(2)}, u32[]{:S(2)}) %collective-permute-start.16) | collective-permute-done | bytes 21152 | tf_op jit(solution)/shard_map/ppermute | solution.py:97
  69.4 1.6 %collective-permute-done.15 = bf16[4,8,330]{2,1,0:T(8,128)(2,1)S(1)} collective-permute-done((bf16[4,8,330]{2,1,0:T(8,128)(2,1)S(1)}, bf16[4,8,330]{2,1,0:T(8,128)(2,1)S(1)}, u32[]{:S(2)}, u32[]{:S(2)}) %collective-permute-start.15) | collective-permute-done | bytes 21152 | tf_op jit(solution)/shard_map/ppermute | solution.py:97
  71.9 1.7 %collective-permute-start.20 = (bf16[1,8,330]{2,1,0:T(8,128)(2,1)S(1)}, bf16[1,8,330]{2,1,0:T(8,128)(2,1)S(1)}, u32[]{:S(2)}, u32[]{:S(2)}) collective-permute-start(bf16[1,8,330]{2,1,0:T(8,128)(2,1)S(1)} %pad_maximum_fusion.15), channel_id=1, source_target_pairs={{0,192},{4,196},{8,200},{12,204},{16,208},{20,212},{24,216},{28,22... | collective-permute-start | bytes 15848 | tf_op jit(solution)/shard_map/ppermute | solution.py:97
  74.0 1.4 %collective-permute-start.19 = (bf16[1,8,330]{2,1,0:T(8,128)(2,1)S(1)}, bf16[1,8,330]{2,1,0:T(8,128)(2,1)S(1)}, u32[]{:S(2)}, u32[]{:S(2)}) collective-permute-start(bf16[1,8,330]{2,1,0:T(8,128)(2,1)S(1)} %pad_maximum_fusion.14), channel_id=1, source_target_pairs={{0,128},{4,132},{8,136},{12,140},{16,144},{20,148},{24,152},{28,15... | collective-permute-start | bytes 15848 | tf_op jit(solution)/shard_map/ppermute | solution.py:97
  75.8 1.1 %collective-permute-start.18 = (bf16[1,8,330]{2,1,0:T(8,128)(2,1)S(1)}, bf16[1,8,330]{2,1,0:T(8,128)(2,1)S(1)}, u32[]{:S(2)}, u32[]{:S(2)}) collective-permute-start(bf16[1,8,330]{2,1,0:T(8,128)(2,1)S(1)} %pad_maximum_fusion.13), channel_id=1, source_target_pairs={{0,64},{4,68},{8,72},{12,76},{16,80},{20,84},{24,88},{28,92},{32,9... | collective-permute-start | bytes 15848 | tf_op jit(solution)/shard_map/ppermute | solution.py:97
  76.9 2.3 %collective-permute-done.19 = bf16[1,8,330]{2,1,0:T(8,128)(2,1)S(1)} collective-permute-done((bf16[1,8,330]{2,1,0:T(8,128)(2,1)S(1)}, bf16[1,8,330]{2,1,0:T(8,128)(2,1)S(1)}, u32[]{:S(2)}, u32[]{:S(2)}) %collective-permute-start.19) | collective-permute-done | bytes 5312 | tf_op jit(solution)/shard_map/ppermute | solution.py:97
  80.8 1.4 %collective-permute-start.23 = (bf16[8,1280]{1,0:T(8,128)(2,1)S(1)}, bf16[8,1280]{1,0:T(8,128)(2,1)S(1)}, u32[]{:S(2)}, u32[]{:S(2)}) collective-permute-start(bf16[8,1280]{1,0:T(8,128)(2,1)S(1)} %get-tuple-element.54), channel_id=1, source_target_pairs={{0,3},{1,2},{2,1},{3,0},{4,7},{5,6},{6,5},{7,4},{8,11},{9,10},{10,... | collective-permute-start | bytes 61448 | tf_op jit(solution)/shard_map/ppermute | solution.py:134
  82.1 0.9 %collective-permute-start.22 = (bf16[8,1280]{1,0:T(8,128)(2,1)S(1)}, bf16[8,1280]{1,0:T(8,128)(2,1)S(1)}, u32[]{:S(2)}, u32[]{:S(2)}) collective-permute-start(bf16[8,1280]{1,0:T(8,128)(2,1)S(1)} %get-tuple-element.54), channel_id=1, source_target_pairs={{0,2},{1,3},{2,0},{3,1},{4,6},{5,7},{6,4},{7,5},{8,10},{9,11},{10,... | collective-permute-start | bytes 61448 | tf_op jit(solution)/shard_map/ppermute | solution.py:134
  83.0 1.9 %collective-permute-start.21 = (bf16[8,1280]{1,0:T(8,128)(2,1)S(1)}, bf16[8,1280]{1,0:T(8,128)(2,1)S(1)}, u32[]{:S(2)}, u32[]{:S(2)}) collective-permute-start(bf16[8,1280]{1,0:T(8,128)(2,1)S(1)} %get-tuple-element.54), channel_id=1, source_target_pairs={{0,1},{1,0},{2,3},{3,2},{4,5},{5,4},{6,7},{7,6},{8,9},{9,8},{10,11... | collective-permute-start | bytes 61448 | tf_op jit(solution)/shard_map/ppermute | solution.py:134
  84.9 0.9 %collective-permute-done.23 = bf16[8,1280]{1,0:T(8,128)(2,1)S(1)} collective-permute-done((bf16[8,1280]{1,0:T(8,128)(2,1)S(1)}, bf16[8,1280]{1,0:T(8,128)(2,1)S(1)}, u32[]{:S(2)}, u32[]{:S(2)}) %collective-permute-start.23) | collective-permute-done | bytes 20512 | tf_op jit(solution)/shard_map/ppermute | solution.py:134
  85.8 1.6 %collective-permute-done.22 = bf16[8,1280]{1,0:T(8,128)(2,1)S(1)} collective-permute-done((bf16[8,1280]{1,0:T(8,128)(2,1)S(1)}, bf16[8,1280]{1,0:T(8,128)(2,1)S(1)}, u32[]{:S(2)}, u32[]{:S(2)}) %collective-permute-start.22) | collective-permute-done | bytes 20512 | tf_op jit(solution)/shard_map/ppermute | solution.py:134
  87.8 0.7 fusion.49
  (128 shorter events, 10.4 us)
Async XLA Ops:
  0.0 9.8 %copy-start = (bf16[1280,3,320]{0,2,1:T(8,128)(2,1)S(1)}, bf16[1280,3,320]{0,2,1:T(8,128)(2,1)}, u32[]{:S(2)}) copy-start(bf16[1280,3,320]{0,2,1:T(8,128)(2,1)} %param.10) | copy-start | bytes 7372804
  0.0 5.1 %collective-permute-start.2 = (bf16[1,8,320]{2,1,0:T(8,128)(2,1)}, bf16[1,8,320]{2,1,0:T(8,128)(2,1)S(1)}, u32[]{:S(2)}, u32[]{:S(2)}) collective-permute-start(bf16[1,8,320]{2,1,0:T(8,128)(2,1)} %bitcast.202), channel_id=1, source_target_pairs={{0,3},{1,2},{2,1},{3,0},{4,7},{5,6},{6,5},{7,4},{8,11},{9,10},{10,... | collective-permute-start | bytes 15368 | tf_op jit(solution)/shard_map/ppermute | solution.py:55
  3.0 5.3 %collective-permute-start.1 = (bf16[1,8,320]{2,1,0:T(8,128)(2,1)}, bf16[1,8,320]{2,1,0:T(8,128)(2,1)S(1)}, u32[]{:S(2)}, u32[]{:S(2)}) collective-permute-start(bf16[1,8,320]{2,1,0:T(8,128)(2,1)} %bitcast.203), channel_id=1, source_target_pairs={{0,2},{1,3},{2,0},{3,1},{4,6},{5,7},{6,4},{7,5},{8,10},{9,11},{10,... | collective-permute-start | bytes 15368 | tf_op jit(solution)/shard_map/ppermute | solution.py:55
  3.6 4.7 %collective-permute-start = (bf16[1,8,320]{2,1,0:T(8,128)(2,1)}, bf16[1,8,320]{2,1,0:T(8,128)(2,1)S(1)}, u32[]{:S(2)}, u32[]{:S(2)}) collective-permute-start(bf16[1,8,320]{2,1,0:T(8,128)(2,1)} %bitcast.204), channel_id=1, source_target_pairs={{0,1},{1,0},{2,3},{3,2},{4,5},{5,4},{6,7},{7,6},{8,9},{9,8},{10,11... | collective-permute-start | bytes 15368 | tf_op jit(solution)/shard_map/ppermute | solution.py:55
  11.7 8.8 %copy-start.5 = (s32[24]{0:T(128)S(1)}, s32[24]{0:T(128)}, u32[]{:S(2)}) copy-start(s32[24]{0:T(128)} %param.15) | copy-start | bytes 292
  11.7 9.2 %copy-start.3 = (f32[320]{0:T(512)S(1)}, f32[320]{0:T(512)}, u32[]{:S(2)}) copy-start(f32[320]{0:T(512)} %param.12) | copy-start | bytes 3844
  11.7 9.4 %copy-start.6 = (s32[24]{0:T(128)S(1)}, s32[24]{0:T(128)}, u32[]{:S(2)}) copy-start(s32[24]{0:T(128)} %param.16) | copy-start | bytes 292
  11.7 18.1 %copy-start.1 = (s32[512]{0:T(512)S(1)}, s32[512]{0:T(512)}, u32[]{:S(2)}) copy-start(s32[512]{0:T(512)} %param.14) | copy-start | bytes 6148
  11.7 9.4 %collective-permute-start.5 = (bf16[1,8,320]{2,1,0:T(8,128)(2,1)S(1)}, bf16[1,8,320]{2,1,0:T(8,128)(2,1)S(1)}, u32[]{:S(2)}, u32[]{:S(2)}) collective-permute-start(bf16[1,8,320]{2,1,0:T(8,128)(2,1)S(1)} %bitcast.196), channel_id=1, source_target_pairs={{0,12},{4,8},{8,4},{12,0},{16,28},{20,24},{24,20},{28,16},{32,44},... | collective-permute-start | bytes 15368 | tf_op jit(solution)/shard_map/ppermute | solution.py:77
  11.8 9.3 %collective-permute-start.4 = (bf16[1,8,320]{2,1,0:T(8,128)(2,1)S(1)}, bf16[1,8,320]{2,1,0:T(8,128)(2,1)S(1)}, u32[]{:S(2)}, u32[]{:S(2)}) collective-permute-start(bf16[1,8,320]{2,1,0:T(8,128)(2,1)S(1)} %bitcast.197), channel_id=1, source_target_pairs={{0,8},{4,12},{8,0},{12,4},{16,24},{20,28},{24,16},{28,20},{32,40},... | collective-permute-start | bytes 15368 | tf_op jit(solution)/shard_map/ppermute | solution.py:77
  13.8 7.3 %collective-permute-start.3 = (bf16[1,8,320]{2,1,0:T(8,128)(2,1)S(1)}, bf16[1,8,320]{2,1,0:T(8,128)(2,1)S(1)}, u32[]{:S(2)}, u32[]{:S(2)}) collective-permute-start(bf16[1,8,320]{2,1,0:T(8,128)(2,1)S(1)} %bitcast.198), channel_id=1, source_target_pairs={{0,4},{4,0},{8,12},{12,8},{16,20},{20,16},{24,28},{28,24},{32,36},... | collective-permute-start | bytes 15368 | tf_op jit(solution)/shard_map/ppermute | solution.py:77
  21.2 9.4 %collective-permute-start.8 = (bf16[4,8,320]{2,1,0:T(8,128)(2,1)S(1)}, bf16[4,8,320]{2,1,0:T(8,128)(2,1)S(1)}, u32[]{:S(2)}, u32[]{:S(2)}) collective-permute-start(bf16[4,8,320]{2,1,0:T(8,128)(2,1)S(1)} %maximum_bitcast_fusion.2), channel_id=1, source_target_pairs={{0,48},{4,52},{8,56},{12,60},{16,32},{20,36},{24,40},{28,44},{32,1... | collective-permute-start | bytes 61448 | tf_op jit(solution)/shard_map/ppermute | solution.py:77
  27.4 8.0 %collective-permute-start.7 = (bf16[4,8,320]{2,1,0:T(8,128)(2,1)S(1)}, bf16[4,8,320]{2,1,0:T(8,128)(2,1)S(1)}, u32[]{:S(2)}, u32[]{:S(2)}) collective-permute-start(bf16[4,8,320]{2,1,0:T(8,128)(2,1)S(1)} %maximum_bitcast_fusion.2), channel_id=1, source_target_pairs={{0,32},{4,36},{8,40},{12,44},{16,48},{20,52},{24,56},{28,60},{32,0... | collective-permute-start | bytes 61448 | tf_op jit(solution)/shard_map/ppermute | solution.py:77
  28.4 7.0 %collective-permute-start.6 = (bf16[4,8,320]{2,1,0:T(8,128)(2,1)S(1)}, bf16[4,8,320]{2,1,0:T(8,128)(2,1)S(1)}, u32[]{:S(2)}, u32[]{:S(2)}) collective-permute-start(bf16[4,8,320]{2,1,0:T(8,128)(2,1)S(1)} %maximum_bitcast_fusion.2), channel_id=1, source_target_pairs={{0,16},{4,20},{8,24},{12,28},{16,0},{20,4},{24,8},{28,12},{32,48},... | collective-permute-start | bytes 61448 | tf_op jit(solution)/shard_map/ppermute | solution.py:77
  35.4 7.0 %collective-permute-start.11 = (bf16[16,8,320]{2,1,0:T(8,128)(2,1)S(1)}, bf16[16,8,320]{2,1,0:T(8,128)(2,1)S(1)}, u32[]{:S(2)}, u32[]{:S(2)}) collective-permute-start(bf16[16,8,320]{2,1,0:T(8,128)(2,1)S(1)} %bitcast.184), channel_id=1, source_target_pairs={{0,192},{4,196},{8,200},{12,204},{16,208},{20,212},{24,216},{28,22... | collective-permute-start | bytes 245768 | tf_op jit(solution)/shard_map/ppermute | solution.py:77
  36.0 6.4 %collective-permute-start.10 = (bf16[16,8,320]{2,1,0:T(8,128)(2,1)S(1)}, bf16[16,8,320]{2,1,0:T(8,128)(2,1)S(1)}, u32[]{:S(2)}, u32[]{:S(2)}) collective-permute-start(bf16[16,8,320]{2,1,0:T(8,128)(2,1)S(1)} %bitcast.185), channel_id=1, source_target_pairs={{0,128},{4,132},{8,136},{12,140},{16,144},{20,148},{24,152},{28,15... | collective-permute-start | bytes 245768 | tf_op jit(solution)/shard_map/ppermute | solution.py:77
  38.4 4.8 %collective-permute-start.9 = (bf16[16,8,320]{2,1,0:T(8,128)(2,1)S(1)}, bf16[16,8,320]{2,1,0:T(8,128)(2,1)S(1)}, u32[]{:S(2)}, u32[]{:S(2)}) collective-permute-start(bf16[16,8,320]{2,1,0:T(8,128)(2,1)S(1)} %bitcast.186), channel_id=1, source_target_pairs={{0,64},{4,68},{8,72},{12,76},{16,80},{20,84},{24,88},{28,92},{32,9... | collective-permute-start | bytes 245768 | tf_op jit(solution)/shard_map/ppermute | solution.py:77
  51.3 5.1 %collective-permute-start.14 = (bf16[16,8,330]{2,1,0:T(8,128)(2,1)S(1)}, bf16[16,8,330]{2,1,0:T(8,128)(2,1)S(1)}, u32[]{:S(2)}, u32[]{:S(2)}) collective-permute-start(bf16[16,8,330]{2,1,0:T(8,128)(2,1)S(1)} %pad_maximum_fusion.8), channel_id=1, source_target_pairs={{0,12},{4,8},{8,4},{12,0},{16,28},{20,24},{24,20},{28,16},{32,44},... | collective-permute-start | bytes 253448 | tf_op jit(solution)/shard_map/ppermute | solution.py:97
  52.1 5.8 %collective-permute-start.13 = (bf16[16,8,330]{2,1,0:T(8,128)(2,1)S(1)}, bf16[16,8,330]{2,1,0:T(8,128)(2,1)S(1)}, u32[]{:S(2)}, u32[]{:S(2)}) collective-permute-start(bf16[16,8,330]{2,1,0:T(8,128)(2,1)S(1)} %pad_maximum_fusion.7), channel_id=1, source_target_pairs={{0,8},{4,12},{8,0},{12,4},{16,24},{20,28},{24,16},{28,20},{32,40},... | collective-permute-start | bytes 253448 | tf_op jit(solution)/shard_map/ppermute | solution.py:97
  53.4 27.1 %copy-start.2 = (bf16[320,1280]{1,0:T(8,128)(2,1)S(1)}, bf16[320,1280]{1,0:T(8,128)(2,1)}, u32[]{:S(2)}) copy-start(bf16[320,1280]{1,0:T(8,128)(2,1)} %param.11) | copy-start | bytes 2457604
  53.5 4.3 %collective-permute-start.12 = (bf16[16,8,330]{2,1,0:T(8,128)(2,1)S(1)}, bf16[16,8,330]{2,1,0:T(8,128)(2,1)S(1)}, u32[]{:S(2)}, u32[]{:S(2)}) collective-permute-start(bf16[16,8,330]{2,1,0:T(8,128)(2,1)S(1)} %pad_maximum_fusion.6), channel_id=1, source_target_pairs={{0,4},{4,0},{8,12},{12,8},{16,20},{20,16},{24,28},{28,24},{32,36},... | collective-permute-start | bytes 253448 | tf_op jit(solution)/shard_map/ppermute | solution.py:97
  57.8 29.7 %copy-start.4 = (f32[1280]{0:T(1024)S(1)}, f32[1280]{0:T(1024)}, u32[]{:S(2)}) copy-start(f32[1280]{0:T(1024)} %param.13) | copy-start | bytes 15364
  59.4 7.4 %collective-permute-start.17 = (bf16[4,8,330]{2,1,0:T(8,128)(2,1)S(1)}, bf16[4,8,330]{2,1,0:T(8,128)(2,1)S(1)}, u32[]{:S(2)}, u32[]{:S(2)}) collective-permute-start(bf16[4,8,330]{2,1,0:T(8,128)(2,1)S(1)} %pad_maximum_fusion.12), channel_id=1, source_target_pairs={{0,48},{4,52},{8,56},{12,60},{16,32},{20,36},{24,40},{28,44},{32,1... | collective-permute-start | bytes 63368 | tf_op jit(solution)/shard_map/ppermute | solution.py:97
  61.6 7.8 %collective-permute-start.16 = (bf16[4,8,330]{2,1,0:T(8,128)(2,1)S(1)}, bf16[4,8,330]{2,1,0:T(8,128)(2,1)S(1)}, u32[]{:S(2)}, u32[]{:S(2)}) collective-permute-start(bf16[4,8,330]{2,1,0:T(8,128)(2,1)S(1)} %pad_maximum_fusion.11), channel_id=1, source_target_pairs={{0,32},{4,36},{8,40},{12,44},{16,48},{20,52},{24,56},{28,60},{32,0... | collective-permute-start | bytes 63368 | tf_op jit(solution)/shard_map/ppermute | solution.py:97
  65.9 5.0 %collective-permute-start.15 = (bf16[4,8,330]{2,1,0:T(8,128)(2,1)S(1)}, bf16[4,8,330]{2,1,0:T(8,128)(2,1)S(1)}, u32[]{:S(2)}, u32[]{:S(2)}) collective-permute-start(bf16[4,8,330]{2,1,0:T(8,128)(2,1)S(1)} %pad_maximum_fusion.10), channel_id=1, source_target_pairs={{0,16},{4,20},{8,24},{12,28},{16,0},{20,4},{24,8},{28,12},{32,48},... | collective-permute-start | bytes 63368 | tf_op jit(solution)/shard_map/ppermute | solution.py:97
  71.9 4.9 %collective-permute-start.20 = (bf16[1,8,330]{2,1,0:T(8,128)(2,1)S(1)}, bf16[1,8,330]{2,1,0:T(8,128)(2,1)S(1)}, u32[]{:S(2)}, u32[]{:S(2)}) collective-permute-start(bf16[1,8,330]{2,1,0:T(8,128)(2,1)S(1)} %pad_maximum_fusion.15), channel_id=1, source_target_pairs={{0,192},{4,196},{8,200},{12,204},{16,208},{20,212},{24,216},{28,22... | collective-permute-start | bytes 15848 | tf_op jit(solution)/shard_map/ppermute | solution.py:97
  74.0 5.2 %collective-permute-start.19 = (bf16[1,8,330]{2,1,0:T(8,128)(2,1)S(1)}, bf16[1,8,330]{2,1,0:T(8,128)(2,1)S(1)}, u32[]{:S(2)}, u32[]{:S(2)}) collective-permute-start(bf16[1,8,330]{2,1,0:T(8,128)(2,1)S(1)} %pad_maximum_fusion.14), channel_id=1, source_target_pairs={{0,128},{4,132},{8,136},{12,140},{16,144},{20,148},{24,152},{28,15... | collective-permute-start | bytes 15848 | tf_op jit(solution)/shard_map/ppermute | solution.py:97
  75.8 3.7 %collective-permute-start.18 = (bf16[1,8,330]{2,1,0:T(8,128)(2,1)S(1)}, bf16[1,8,330]{2,1,0:T(8,128)(2,1)S(1)}, u32[]{:S(2)}, u32[]{:S(2)}) collective-permute-start(bf16[1,8,330]{2,1,0:T(8,128)(2,1)S(1)} %pad_maximum_fusion.13), channel_id=1, source_target_pairs={{0,64},{4,68},{8,72},{12,76},{16,80},{20,84},{24,88},{28,92},{32,9... | collective-permute-start | bytes 15848 | tf_op jit(solution)/shard_map/ppermute | solution.py:97
  80.8 5.1 %collective-permute-start.23 = (bf16[8,1280]{1,0:T(8,128)(2,1)S(1)}, bf16[8,1280]{1,0:T(8,128)(2,1)S(1)}, u32[]{:S(2)}, u32[]{:S(2)}) collective-permute-start(bf16[8,1280]{1,0:T(8,128)(2,1)S(1)} %get-tuple-element.54), channel_id=1, source_target_pairs={{0,3},{1,2},{2,1},{3,0},{4,7},{5,6},{6,5},{7,4},{8,11},{9,10},{10,... | collective-permute-start | bytes 61448 | tf_op jit(solution)/shard_map/ppermute | solution.py:134
  82.1 5.3 %collective-permute-start.22 = (bf16[8,1280]{1,0:T(8,128)(2,1)S(1)}, bf16[8,1280]{1,0:T(8,128)(2,1)S(1)}, u32[]{:S(2)}, u32[]{:S(2)}) collective-permute-start(bf16[8,1280]{1,0:T(8,128)(2,1)S(1)} %get-tuple-element.54), channel_id=1, source_target_pairs={{0,2},{1,3},{2,0},{3,1},{4,6},{5,7},{6,4},{7,5},{8,10},{9,11},{10,... | collective-permute-start | bytes 61448 | tf_op jit(solution)/shard_map/ppermute | solution.py:134
  83.0 4.4 %collective-permute-start.21 = (bf16[8,1280]{1,0:T(8,128)(2,1)S(1)}, bf16[8,1280]{1,0:T(8,128)(2,1)S(1)}, u32[]{:S(2)}, u32[]{:S(2)}) collective-permute-start(bf16[8,1280]{1,0:T(8,128)(2,1)S(1)} %get-tuple-element.54), channel_id=1, source_target_pairs={{0,1},{1,0},{2,3},{3,2},{4,5},{5,4},{6,7},{7,6},{8,9},{9,8},{10,11... | collective-permute-start | bytes 61448 | tf_op jit(solution)/shard_map/ppermute | solution.py:134

commit v11 on v10

--- a/solution.py
+++ b/solution.py
@@ -175,7 +175,7 @@
     query, page_cache, page_request, page_number, lengths = lax.optimization_barrier(
         (query, page_cache, page_request, page_number, lengths)
     )
-    all_queries, _ = gather_xor(query, "seq")
+    all_queries, _ = gather_xor(query, "seq", (), -1)
     all_queries = all_queries.reshape(-1, width_local)
     owner_place = ((page_request // rows) ^ seq_index) * rows + page_request % rows
     pages, page_len = (page_cache.shape[0], page_cache.shape[1])

time: 89.5 us -> 89.5 us (level)
  no operation moved by 1% of the time
where the time goes in v11:
time: 89.5 us; the launch traced here: 88.5 us
  starting transfers between devices  36.3 us (41%)
  waiting for transfers between devices  22.8 us (25%)
  other arithmetic  15.8 us (18%)
  matrix products  8.93 us (10%)
  local copies, waits for them, and re-layouts  4.1 us (5%)
    ppermute x9, starting transfers between devices, gather_xor(): lax.ppermute(held, axis, perm=xor_partner(axis, size, digit << low))  15 us
    ppermute x9, starting transfers between devices, scatter_xor(): lax.ppermute(sent, axis, perm=xor_partner(axis, size, digit << low))  13.1 us
    ppermute x9, waiting for transfers between devices, scatter_xor(): lax.ppermute(sent, axis, perm=xor_partner(axis, size, digit << low))  9.9 us
    ppermute x9, waiting for transfers between devices, gather_xor(): lax.ppermute(held, axis, perm=xor_partner(axis, size, digit << low))  6.2 us
    mul x3, other arithmetic, head_norm(): shaped * shaped  4.64 us
    ppermute x3, waiting for transfers between devices, exchange(): lax.ppermute(held, axis, perm=xor_partner(axis, size, digit << low))  4.19 us
    ppermute x3, starting transfers between devices, sum_radix(): lax.ppermute(sent, axis, perm=xor_partner(axis, size, digit << low))  4.16 us
    ppermute x3, starting transfers between devices, exchange(): lax.ppermute(held, axis, perm=xor_partner(axis, size, digit << low))  4.09 us
  transfers between devices with their start and end apart: 24, of which 13 were waited for; matrix products, arithmetic and copies ran while one was open for 14% of the time, Pallas kernels for 0%

profile of v11, /device:TPU:6, one launch (start us, length us, event | category | flops | bytes accessed | tf_op | source)
XLA Modules:
  0.0 88.5 jit_solution(561610427751959565)
XLA Ops:
  0.0 3.0 %collective-permute-start.2 = (bf16[1,8,320]{2,1,0:T(8,128)(2,1)}, bf16[1,8,320]{2,1,0:T(8,128)(2,1)S(1)}, u32[]{:S(2)}, u32[]{:S(2)}) collective-permute-start(bf16[1,8,320]{2,1,0:T(8,128)(2,1)} %bitcast.202), channel_id=1, source_target_pairs={{0,3},{1,2},{2,1},{3,0},{4,7},{5,6},{6,5},{7,4},{8,11},{9,10},{10,... | collective-permute-start | bytes 15368 | tf_op jit(solution)/shard_map/ppermute | solution.py:55
  3.0 0.6 collective-permute-start.1
  4.2 0.9 collective-permute-done.2
  5.1 3.3 %collective-permute-done.1 = bf16[1,8,320]{2,1,0:T(8,128)(2,1)S(1)} collective-permute-done((bf16[1,8,320]{2,1,0:T(8,128)(2,1)}, bf16[1,8,320]{2,1,0:T(8,128)(2,1)S(1)}, u32[]{:S(2)}, u32[]{:S(2)}) %collective-permute-start.1) | collective-permute-done | bytes 5152 | tf_op jit(solution)/shard_map/ppermute | solution.py:55
  8.4 0.7 maximum_bitcast_fusion.1
  9.1 0.6 gather_fusion
  9.8 0.7 fusion.126
  10.9 0.8 slice_multiply_fusion.12
  11.8 2.0 %collective-permute-start.4 = (bf16[1,8,320]{2,1,0:T(8,128)(2,1)S(1)}, bf16[1,8,320]{2,1,0:T(8,128)(2,1)S(1)}, u32[]{:S(2)}, u32[]{:S(2)}) collective-permute-start(bf16[1,8,320]{2,1,0:T(8,128)(2,1)S(1)} %bitcast.197), channel_id=1, source_target_pairs={{0,8},{4,12},{8,0},{12,4},{16,24},{20,28},{24,16},{28,20},{32,40},... | collective-permute-start | bytes 15368 | tf_op jit(solution)/shard_map/ppermute | solution.py:77
  13.9 3.9 %convert_multiply_fusion = f32[24,128,1,320]{1,3,2,0:T(8,128)} fusion(bf16[24,128,2,320]{1,3,2,0:T(8,128)(2,1)} %param.17), kind=kLoop, calls=%fused_computation.3 | loop fusion | flops 1966080 | bytes 5898240 | tf_op jit(solution)/shard_map/mul | solution.py:17
  17.7 2.7 %reduce_sum.122 = f32[24,128,5]{1,2,0:T(8,128)S(1)} reduce(f32[24,128,5,64]{1,3,2,0:T(8,128)} %bitcast.181, f32[]{:T(128)} %constant.122.clone.1), dimensions={3}, to_apply=%region_1.2 | reduce | flops 967680 | bytes 3993604 | tf_op jit(solution)/shard_map/reduce_sum | solution.py:17
  21.2 6.2 %collective-permute-start.8 = (bf16[4,8,320]{2,1,0:T(8,128)(2,1)S(1)}, bf16[4,8,320]{2,1,0:T(8,128)(2,1)S(1)}, u32[]{:S(2)}, u32[]{:S(2)}) collective-permute-start(bf16[4,8,320]{2,1,0:T(8,128)(2,1)S(1)} %get-tuple-element.52), channel_id=1, source_target_pairs={{0,48},{4,52},{8,56},{12,60},{16,32},{20,36},{24,40},{28,44},{32,1... | collective-permute-start | bytes 61448 | tf_op jit(solution)/shard_map/ppermute | solution.py:77
  27.4 1.0 %collective-permute-start.7 = (bf16[4,8,320]{2,1,0:T(8,128)(2,1)S(1)}, bf16[4,8,320]{2,1,0:T(8,128)(2,1)S(1)}, u32[]{:S(2)}, u32[]{:S(2)}) collective-permute-start(bf16[4,8,320]{2,1,0:T(8,128)(2,1)S(1)} %get-tuple-element.52), channel_id=1, source_target_pairs={{0,32},{4,36},{8,40},{12,44},{16,48},{20,52},{24,56},{28,60},{32,0... | collective-permute-start | bytes 61448 | tf_op jit(solution)/shard_map/ppermute | solution.py:77
  28.4 1.5 %collective-permute-start.6 = (bf16[4,8,320]{2,1,0:T(8,128)(2,1)S(1)}, bf16[4,8,320]{2,1,0:T(8,128)(2,1)S(1)}, u32[]{:S(2)}, u32[]{:S(2)}) collective-permute-start(bf16[4,8,320]{2,1,0:T(8,128)(2,1)S(1)} %get-tuple-element.52), channel_id=1, source_target_pairs={{0,16},{4,20},{8,24},{12,28},{16,0},{20,4},{24,8},{28,12},{32,48},... | collective-permute-start | bytes 61448 | tf_op jit(solution)/shard_map/ppermute | solution.py:77
  29.8 0.7 gather_fusion.1
  30.6 4.8 %collective-permute-done.7 = bf16[4,8,320]{2,1,0:T(8,128)(2,1)S(1)} collective-permute-done((bf16[4,8,320]{2,1,0:T(8,128)(2,1)S(1)}, bf16[4,8,320]{2,1,0:T(8,128)(2,1)S(1)}, u32[]{:S(2)}, u32[]{:S(2)}) %collective-permute-start.7) | collective-permute-done | bytes 20512 | tf_op jit(solution)/shard_map/ppermute | solution.py:77
  35.4 0.6 collective-permute-start.11
  36.0 2.4 %collective-permute-start.10 = (bf16[16,8,320]{2,1,0:T(8,128)(2,1)S(1)}, bf16[16,8,320]{2,1,0:T(8,128)(2,1)S(1)}, u32[]{:S(2)}, u32[]{:S(2)}) collective-permute-start(bf16[16,8,320]{2,1,0:T(8,128)(2,1)S(1)} %bitcast.186), channel_id=1, source_target_pairs={{0,128},{4,132},{8,136},{12,140},{16,144},{20,148},{24,152},{28,15... | collective-permute-start | bytes 245768 | tf_op jit(solution)/shard_map/ppermute | solution.py:77
  38.4 1.2 %collective-permute-start.9 = (bf16[16,8,320]{2,1,0:T(8,128)(2,1)S(1)}, bf16[16,8,320]{2,1,0:T(8,128)(2,1)S(1)}, u32[]{:S(2)}, u32[]{:S(2)}) collective-permute-start(bf16[16,8,320]{2,1,0:T(8,128)(2,1)S(1)} %bitcast.187), channel_id=1, source_target_pairs={{0,64},{4,68},{8,72},{12,76},{16,80},{20,84},{24,88},{28,92},{32,9... | collective-permute-start | bytes 245768 | tf_op jit(solution)/shard_map/ppermute | solution.py:77
  39.7 2.2 %fusion.2 = bf16[24,128,320]{1,2,0:T(8,128)(2,1)S(1)} fusion(f32[320]{0:T(512)S(1)} %copy-done.3, f32[24,128,5]{1,2,0:T(8,128)S(1)} %add_sqrt_fusion, bf16[24,128,2,320]{1,3,2,0:T(8,128)(2,1)} %param.17), kind=kLoop, calls=%fused_computation.7 | loop fusion | flops 3932160 | bytes 3994880 | tf_op jit(solution)/shard_map/convert_element_type | solution.py:187
  41.9 0.5 collective-permute-done.11
  42.4 0.9 collective-permute-done.9
  43.6 0.5 select_reduce_fusion.1
  44.6 2.3 %fusion.5 = f32[24,320]{1,0:T(8,128)S(1)} fusion(pred[5,320]{1,0:T(8,128)(4,1)S(1)} %iota_compare_fusion.6, f32[24,5,128]{2,1,0:T(8,128)S(1)} %get-tuple-element.55, f32[24,5]{1,0:T(8,128)S(1)} %get-tuple-element.54, pred[24,128]{1,0:T(8,128)(4,1)S(1)} %add_compare_fusion, bf16[24,128,2,320]{1,3,2,0:T(8,128)(2,1)} %param.17), kind=kOutput, calls=%fused_computation.14 | convolution fusion | flops 9945600 | bytes 2063392 | tf_op jit(solution)/shard_map/shp,spf->shf/dot_general | solution.py:203
  47.0 0.6 gather_fusion.2
  47.9 0.5 fusion.38
  48.4 0.9 %pad_maximum_fusion.1 = f32[512,330]{0,1:T(8,128)} fusion(f32[512,5]{0,1:T(8,128)S(1)} %select_reduce_fusion, f32[512,5]{0,1:T(8,128)S(1)} %fusion.37, f32[512,320]{0,1:T(8,128)S(1)} %fusion.38), kind=kLoop, calls=%fused_computation.46 | loop fusion | flops 337920 | bytes 1351680 | tf_op jit(solution)/shard_map/concatenate | solution.py:216
  49.3 1.4 %copy.32 = f32[512,330]{1,0:T(8,128)S(1)} copy(f32[512,330]{0,1:T(8,128)} %pad_maximum_fusion.1) | data formatting | bytes 1351680 | tf_op jit(solution)/shard_map/concatenate | solution.py:216
  52.1 0.9 %collective-permute-start.13 = (bf16[16,8,330]{2,1,0:T(8,128)(2,1)S(1)}, bf16[16,8,330]{2,1,0:T(8,128)(2,1)S(1)}, u32[]{:S(2)}, u32[]{:S(2)}) collective-permute-start(bf16[16,8,330]{2,1,0:T(8,128)(2,1)S(1)} %pad_maximum_fusion.7), channel_id=1, source_target_pairs={{0,8},{4,12},{8,0},{12,4},{16,24},{20,28},{24,16},{28,20},{32,40},... | collective-permute-start | bytes 253448 | tf_op jit(solution)/shard_map/ppermute | solution.py:97
  53.5 1.1 %collective-permute-start.12 = (bf16[16,8,330]{2,1,0:T(8,128)(2,1)S(1)}, bf16[16,8,330]{2,1,0:T(8,128)(2,1)S(1)}, u32[]{:S(2)}, u32[]{:S(2)}) collective-permute-start(bf16[16,8,330]{2,1,0:T(8,128)(2,1)S(1)} %pad_maximum_fusion.6), channel_id=1, source_target_pairs={{0,4},{4,0},{8,12},{12,8},{16,20},{20,16},{24,28},{28,24},{32,36},... | collective-permute-start | bytes 253448 | tf_op jit(solution)/shard_map/ppermute | solution.py:97
  54.6 1.7 %collective-permute-done.14 = bf16[16,8,330]{2,1,0:T(8,128)(2,1)S(1)} collective-permute-done((bf16[16,8,330]{2,1,0:T(8,128)(2,1)S(1)}, bf16[16,8,330]{2,1,0:T(8,128)(2,1)S(1)}, u32[]{:S(2)}, u32[]{:S(2)}) %collective-permute-start.14) | collective-permute-done | bytes 84512 | tf_op jit(solution)/shard_map/ppermute | solution.py:97
  56.3 1.5 %collective-permute-done.13 = bf16[16,8,330]{2,1,0:T(8,128)(2,1)S(1)} collective-permute-done((bf16[16,8,330]{2,1,0:T(8,128)(2,1)S(1)}, bf16[16,8,330]{2,1,0:T(8,128)(2,1)S(1)}, u32[]{:S(2)}, u32[]{:S(2)}) %collective-permute-start.13) | collective-permute-done | bytes 84512 | tf_op jit(solution)/shard_map/ppermute | solution.py:97
  58.3 0.6 fusion.20
  59.4 1.8 %collective-permute-start.17 = (bf16[4,8,330]{2,1,0:T(8,128)(2,1)S(1)}, bf16[4,8,330]{2,1,0:T(8,128)(2,1)S(1)}, u32[]{:S(2)}, u32[]{:S(2)}) collective-permute-start(bf16[4,8,330]{2,1,0:T(8,128)(2,1)S(1)} %pad_maximum_fusion.13), channel_id=1, source_target_pairs={{0,48},{4,52},{8,56},{12,60},{16,32},{20,36},{24,40},{28,44},{32,1... | collective-permute-start | bytes 63368 | tf_op jit(solution)/shard_map/ppermute | solution.py:97
  61.6 3.9 %collective-permute-start.16 = (bf16[4,8,330]{2,1,0:T(8,128)(2,1)S(1)}, bf16[4,8,330]{2,1,0:T(8,128)(2,1)S(1)}, u32[]{:S(2)}, u32[]{:S(2)}) collective-permute-start(bf16[4,8,330]{2,1,0:T(8,128)(2,1)S(1)} %pad_maximum_fusion.12), channel_id=1, source_target_pairs={{0,32},{4,36},{8,40},{12,44},{16,48},{20,52},{24,56},{28,60},{32,0... | collective-permute-start | bytes 63368 | tf_op jit(solution)/shard_map/ppermute | solution.py:97
  66.0 0.8 collective-permute-start.15
  66.8 2.6 %collective-permute-done.16 = bf16[4,8,330]{2,1,0:T(8,128)(2,1)S(1)} collective-permute-done((bf16[4,8,330]{2,1,0:T(8,128)(2,1)S(1)}, bf16[4,8,330]{2,1,0:T(8,128)(2,1)S(1)}, u32[]{:S(2)}, u32[]{:S(2)}) %collective-permute-start.16) | collective-permute-done | bytes 21152 | tf_op jit(solution)/shard_map/ppermute | solution.py:97
  69.4 1.6 %collective-permute-done.15 = bf16[4,8,330]{2,1,0:T(8,128)(2,1)S(1)} collective-permute-done((bf16[4,8,330]{2,1,0:T(8,128)(2,1)S(1)}, bf16[4,8,330]{2,1,0:T(8,128)(2,1)S(1)}, u32[]{:S(2)}, u32[]{:S(2)}) %collective-permute-start.15) | collective-permute-done | bytes 21152 | tf_op jit(solution)/shard_map/ppermute | solution.py:97
  72.0 1.6 %collective-permute-start.20 = (bf16[1,8,330]{2,1,0:T(8,128)(2,1)S(1)}, bf16[1,8,330]{2,1,0:T(8,128)(2,1)S(1)}, u32[]{:S(2)}, u32[]{:S(2)}) collective-permute-start(bf16[1,8,330]{2,1,0:T(8,128)(2,1)S(1)} %pad_maximum_fusion.16), channel_id=1, source_target_pairs={{0,192},{4,196},{8,200},{12,204},{16,208},{20,212},{24,216},{28,22... | collective-permute-start | bytes 15848 | tf_op jit(solution)/shard_map/ppermute | solution.py:97
  74.0 1.4 %collective-permute-start.19 = (bf16[1,8,330]{2,1,0:T(8,128)(2,1)S(1)}, bf16[1,8,330]{2,1,0:T(8,128)(2,1)S(1)}, u32[]{:S(2)}, u32[]{:S(2)}) collective-permute-start(bf16[1,8,330]{2,1,0:T(8,128)(2,1)S(1)} %pad_maximum_fusion.15), channel_id=1, source_target_pairs={{0,128},{4,132},{8,136},{12,140},{16,144},{20,148},{24,152},{28,15... | collective-permute-start | bytes 15848 | tf_op jit(solution)/shard_map/ppermute | solution.py:97
  75.8 1.1 %collective-permute-start.18 = (bf16[1,8,330]{2,1,0:T(8,128)(2,1)S(1)}, bf16[1,8,330]{2,1,0:T(8,128)(2,1)S(1)}, u32[]{:S(2)}, u32[]{:S(2)}) collective-permute-start(bf16[1,8,330]{2,1,0:T(8,128)(2,1)S(1)} %pad_maximum_fusion.14), channel_id=1, source_target_pairs={{0,64},{4,68},{8,72},{12,76},{16,80},{20,84},{24,88},{28,92},{32,9... | collective-permute-start | bytes 15848 | tf_op jit(solution)/shard_map/ppermute | solution.py:97
  76.9 2.3 %collective-permute-done.19 = bf16[1,8,330]{2,1,0:T(8,128)(2,1)S(1)} collective-permute-done((bf16[1,8,330]{2,1,0:T(8,128)(2,1)S(1)}, bf16[1,8,330]{2,1,0:T(8,128)(2,1)S(1)}, u32[]{:S(2)}, u32[]{:S(2)}) %collective-permute-start.19) | collective-permute-done | bytes 5312 | tf_op jit(solution)/shard_map/ppermute | solution.py:97
  80.8 1.4 %collective-permute-start.23 = (bf16[8,1280]{1,0:T(8,128)(2,1)S(1)}, bf16[8,1280]{1,0:T(8,128)(2,1)S(1)}, u32[]{:S(2)}, u32[]{:S(2)}) collective-permute-start(bf16[8,1280]{1,0:T(8,128)(2,1)S(1)} %get-tuple-element.56), channel_id=1, source_target_pairs={{0,3},{1,2},{2,1},{3,0},{4,7},{5,6},{6,5},{7,4},{8,11},{9,10},{10,... | collective-permute-start | bytes 61448 | tf_op jit(solution)/shard_map/ppermute | solution.py:134
  82.1 0.9 %collective-permute-start.22 = (bf16[8,1280]{1,0:T(8,128)(2,1)S(1)}, bf16[8,1280]{1,0:T(8,128)(2,1)S(1)}, u32[]{:S(2)}, u32[]{:S(2)}) collective-permute-start(bf16[8,1280]{1,0:T(8,128)(2,1)S(1)} %get-tuple-element.56), channel_id=1, source_target_pairs={{0,2},{1,3},{2,0},{3,1},{4,6},{5,7},{6,4},{7,5},{8,10},{9,11},{10,... | collective-permute-start | bytes 61448 | tf_op jit(solution)/shard_map/ppermute | solution.py:134
  83.0 1.9 %collective-permute-start.21 = (bf16[8,1280]{1,0:T(8,128)(2,1)S(1)}, bf16[8,1280]{1,0:T(8,128)(2,1)S(1)}, u32[]{:S(2)}, u32[]{:S(2)}) collective-permute-start(bf16[8,1280]{1,0:T(8,128)(2,1)S(1)} %get-tuple-element.56), channel_id=1, source_target_pairs={{0,1},{1,0},{2,3},{3,2},{4,5},{5,4},{6,7},{7,6},{8,9},{9,8},{10,11... | collective-permute-start | bytes 61448 | tf_op jit(solution)/shard_map/ppermute | solution.py:134
  84.9 0.9 %collective-permute-done.23 = bf16[8,1280]{1,0:T(8,128)(2,1)S(1)} collective-permute-done((bf16[8,1280]{1,0:T(8,128)(2,1)S(1)}, bf16[8,1280]{1,0:T(8,128)(2,1)S(1)}, u32[]{:S(2)}, u32[]{:S(2)}) %collective-permute-start.23) | collective-permute-done | bytes 20512 | tf_op jit(solution)/shard_map/ppermute | solution.py:134
  85.8 1.6 %collective-permute-done.22 = bf16[8,1280]{1,0:T(8,128)(2,1)S(1)} collective-permute-done((bf16[8,1280]{1,0:T(8,128)(2,1)S(1)}, bf16[8,1280]{1,0:T(8,128)(2,1)S(1)}, u32[]{:S(2)}, u32[]{:S(2)}) %collective-permute-start.22) | collective-permute-done | bytes 20512 | tf_op jit(solution)/shard_map/ppermute | solution.py:134
  87.8 0.7 fusion.49
  (128 shorter events, 10.4 us)
Async XLA Ops:
  0.0 9.8 %copy-start = (bf16[1280,3,320]{0,2,1:T(8,128)(2,1)S(1)}, bf16[1280,3,320]{0,2,1:T(8,128)(2,1)}, u32[]{:S(2)}) copy-start(bf16[1280,3,320]{0,2,1:T(8,128)(2,1)} %param.10) | copy-start | bytes 7372804
  0.0 5.1 %collective-permute-start.2 = (bf16[1,8,320]{2,1,0:T(8,128)(2,1)}, bf16[1,8,320]{2,1,0:T(8,128)(2,1)S(1)}, u32[]{:S(2)}, u32[]{:S(2)}) collective-permute-start(bf16[1,8,320]{2,1,0:T(8,128)(2,1)} %bitcast.202), channel_id=1, source_target_pairs={{0,3},{1,2},{2,1},{3,0},{4,7},{5,6},{6,5},{7,4},{8,11},{9,10},{10,... | collective-permute-start | bytes 15368 | tf_op jit(solution)/shard_map/ppermute | solution.py:55
  3.0 5.3 %collective-permute-start.1 = (bf16[1,8,320]{2,1,0:T(8,128)(2,1)}, bf16[1,8,320]{2,1,0:T(8,128)(2,1)S(1)}, u32[]{:S(2)}, u32[]{:S(2)}) collective-permute-start(bf16[1,8,320]{2,1,0:T(8,128)(2,1)} %bitcast.203), channel_id=1, source_target_pairs={{0,2},{1,3},{2,0},{3,1},{4,6},{5,7},{6,4},{7,5},{8,10},{9,11},{10,... | collective-permute-start | bytes 15368 | tf_op jit(solution)/shard_map/ppermute | solution.py:55
  3.6 4.7 %collective-permute-start = (bf16[1,8,320]{2,1,0:T(8,128)(2,1)}, bf16[1,8,320]{2,1,0:T(8,128)(2,1)S(1)}, u32[]{:S(2)}, u32[]{:S(2)}) collective-permute-start(bf16[1,8,320]{2,1,0:T(8,128)(2,1)} %bitcast.204), channel_id=1, source_target_pairs={{0,1},{1,0},{2,3},{3,2},{4,5},{5,4},{6,7},{7,6},{8,9},{9,8},{10,11... | collective-permute-start | bytes 15368 | tf_op jit(solution)/shard_map/ppermute | solution.py:55
  11.7 8.8 %copy-start.5 = (s32[24]{0:T(128)S(1)}, s32[24]{0:T(128)}, u32[]{:S(2)}) copy-start(s32[24]{0:T(128)} %param.15) | copy-start | bytes 292
  11.7 9.2 %copy-start.3 = (f32[320]{0:T(512)S(1)}, f32[320]{0:T(512)}, u32[]{:S(2)}) copy-start(f32[320]{0:T(512)} %param.12) | copy-start | bytes 3844
  11.7 9.4 %copy-start.6 = (s32[24]{0:T(128)S(1)}, s32[24]{0:T(128)}, u32[]{:S(2)}) copy-start(s32[24]{0:T(128)} %param.16) | copy-start | bytes 292
  11.7 18.1 %copy-start.1 = (s32[512]{0:T(512)S(1)}, s32[512]{0:T(512)}, u32[]{:S(2)}) copy-start(s32[512]{0:T(512)} %param.14) | copy-start | bytes 6148
  11.7 9.4 %collective-permute-start.5 = (bf16[1,8,320]{2,1,0:T(8,128)(2,1)S(1)}, bf16[1,8,320]{2,1,0:T(8,128)(2,1)S(1)}, u32[]{:S(2)}, u32[]{:S(2)}) collective-permute-start(bf16[1,8,320]{2,1,0:T(8,128)(2,1)S(1)} %bitcast.196), channel_id=1, source_target_pairs={{0,12},{4,8},{8,4},{12,0},{16,28},{20,24},{24,20},{28,16},{32,44},... | collective-permute-start | bytes 15368 | tf_op jit(solution)/shard_map/ppermute | solution.py:77
  11.8 9.3 %collective-permute-start.4 = (bf16[1,8,320]{2,1,0:T(8,128)(2,1)S(1)}, bf16[1,8,320]{2,1,0:T(8,128)(2,1)S(1)}, u32[]{:S(2)}, u32[]{:S(2)}) collective-permute-start(bf16[1,8,320]{2,1,0:T(8,128)(2,1)S(1)} %bitcast.197), channel_id=1, source_target_pairs={{0,8},{4,12},{8,0},{12,4},{16,24},{20,28},{24,16},{28,20},{32,40},... | collective-permute-start | bytes 15368 | tf_op jit(solution)/shard_map/ppermute | solution.py:77
  13.8 7.3 %collective-permute-start.3 = (bf16[1,8,320]{2,1,0:T(8,128)(2,1)S(1)}, bf16[1,8,320]{2,1,0:T(8,128)(2,1)S(1)}, u32[]{:S(2)}, u32[]{:S(2)}) collective-permute-start(bf16[1,8,320]{2,1,0:T(8,128)(2,1)S(1)} %bitcast.198), channel_id=1, source_target_pairs={{0,4},{4,0},{8,12},{12,8},{16,20},{20,16},{24,28},{28,24},{32,36},... | collective-permute-start | bytes 15368 | tf_op jit(solution)/shard_map/ppermute | solution.py:77
  21.2 9.4 %collective-permute-start.8 = (bf16[4,8,320]{2,1,0:T(8,128)(2,1)S(1)}, bf16[4,8,320]{2,1,0:T(8,128)(2,1)S(1)}, u32[]{:S(2)}, u32[]{:S(2)}) collective-permute-start(bf16[4,8,320]{2,1,0:T(8,128)(2,1)S(1)} %get-tuple-element.52), channel_id=1, source_target_pairs={{0,48},{4,52},{8,56},{12,60},{16,32},{20,36},{24,40},{28,44},{32,1... | collective-permute-start | bytes 61448 | tf_op jit(solution)/shard_map/ppermute | solution.py:77
  27.4 8.0 %collective-permute-start.7 = (bf16[4,8,320]{2,1,0:T(8,128)(2,1)S(1)}, bf16[4,8,320]{2,1,0:T(8,128)(2,1)S(1)}, u32[]{:S(2)}, u32[]{:S(2)}) collective-permute-start(bf16[4,8,320]{2,1,0:T(8,128)(2,1)S(1)} %get-tuple-element.52), channel_id=1, source_target_pairs={{0,32},{4,36},{8,40},{12,44},{16,48},{20,52},{24,56},{28,60},{32,0... | collective-permute-start | bytes 61448 | tf_op jit(solution)/shard_map/ppermute | solution.py:77
  28.4 7.0 %collective-permute-start.6 = (bf16[4,8,320]{2,1,0:T(8,128)(2,1)S(1)}, bf16[4,8,320]{2,1,0:T(8,128)(2,1)S(1)}, u32[]{:S(2)}, u32[]{:S(2)}) collective-permute-start(bf16[4,8,320]{2,1,0:T(8,128)(2,1)S(1)} %get-tuple-element.52), channel_id=1, source_target_pairs={{0,16},{4,20},{8,24},{12,28},{16,0},{20,4},{24,8},{28,12},{32,48},... | collective-permute-start | bytes 61448 | tf_op jit(solution)/shard_map/ppermute | solution.py:77
  35.4 7.0 %collective-permute-start.11 = (bf16[16,8,320]{2,1,0:T(8,128)(2,1)S(1)}, bf16[16,8,320]{2,1,0:T(8,128)(2,1)S(1)}, u32[]{:S(2)}, u32[]{:S(2)}) collective-permute-start(bf16[16,8,320]{2,1,0:T(8,128)(2,1)S(1)} %bitcast.185), channel_id=1, source_target_pairs={{0,192},{4,196},{8,200},{12,204},{16,208},{20,212},{24,216},{28,22... | collective-permute-start | bytes 245768 | tf_op jit(solution)/shard_map/ppermute | solution.py:77
  36.0 6.4 %collective-permute-start.10 = (bf16[16,8,320]{2,1,0:T(8,128)(2,1)S(1)}, bf16[16,8,320]{2,1,0:T(8,128)(2,1)S(1)}, u32[]{:S(2)}, u32[]{:S(2)}) collective-permute-start(bf16[16,8,320]{2,1,0:T(8,128)(2,1)S(1)} %bitcast.186), channel_id=1, source_target_pairs={{0,128},{4,132},{8,136},{12,140},{16,144},{20,148},{24,152},{28,15... | collective-permute-start | bytes 245768 | tf_op jit(solution)/shard_map/ppermute | solution.py:77
  38.4 4.8 %collective-permute-start.9 = (bf16[16,8,320]{2,1,0:T(8,128)(2,1)S(1)}, bf16[16,8,320]{2,1,0:T(8,128)(2,1)S(1)}, u32[]{:S(2)}, u32[]{:S(2)}) collective-permute-start(bf16[16,8,320]{2,1,0:T(8,128)(2,1)S(1)} %bitcast.187), channel_id=1, source_target_pairs={{0,64},{4,68},{8,72},{12,76},{16,80},{20,84},{24,88},{28,92},{32,9... | collective-permute-start | bytes 245768 | tf_op jit(solution)/shard_map/ppermute | solution.py:77
  51.3 5.1 %collective-permute-start.14 = (bf16[16,8,330]{2,1,0:T(8,128)(2,1)S(1)}, bf16[16,8,330]{2,1,0:T(8,128)(2,1)S(1)}, u32[]{:S(2)}, u32[]{:S(2)}) collective-permute-start(bf16[16,8,330]{2,1,0:T(8,128)(2,1)S(1)} %pad_maximum_fusion.8), channel_id=1, source_target_pairs={{0,12},{4,8},{8,4},{12,0},{16,28},{20,24},{24,20},{28,16},{32,44},... | collective-permute-start | bytes 253448 | tf_op jit(solution)/shard_map/ppermute | solution.py:97
  52.1 5.8 %collective-permute-start.13 = (bf16[16,8,330]{2,1,0:T(8,128)(2,1)S(1)}, bf16[16,8,330]{2,1,0:T(8,128)(2,1)S(1)}, u32[]{:S(2)}, u32[]{:S(2)}) collective-permute-start(bf16[16,8,330]{2,1,0:T(8,128)(2,1)S(1)} %pad_maximum_fusion.7), channel_id=1, source_target_pairs={{0,8},{4,12},{8,0},{12,4},{16,24},{20,28},{24,16},{28,20},{32,40},... | collective-permute-start | bytes 253448 | tf_op jit(solution)/shard_map/ppermute | solution.py:97
  53.4 27.1 %copy-start.2 = (bf16[320,1280]{1,0:T(8,128)(2,1)S(1)}, bf16[320,1280]{1,0:T(8,128)(2,1)}, u32[]{:S(2)}) copy-start(bf16[320,1280]{1,0:T(8,128)(2,1)} %param.11) | copy-start | bytes 2457604
  53.5 4.3 %collective-permute-start.12 = (bf16[16,8,330]{2,1,0:T(8,128)(2,1)S(1)}, bf16[16,8,330]{2,1,0:T(8,128)(2,1)S(1)}, u32[]{:S(2)}, u32[]{:S(2)}) collective-permute-start(bf16[16,8,330]{2,1,0:T(8,128)(2,1)S(1)} %pad_maximum_fusion.6), channel_id=1, source_target_pairs={{0,4},{4,0},{8,12},{12,8},{16,20},{20,16},{24,28},{28,24},{32,36},... | collective-permute-start | bytes 253448 | tf_op jit(solution)/shard_map/ppermute | solution.py:97
  57.8 29.7 %copy-start.4 = (f32[1280]{0:T(1024)S(1)}, f32[1280]{0:T(1024)}, u32[]{:S(2)}) copy-start(f32[1280]{0:T(1024)} %param.13) | copy-start | bytes 15364
  59.4 7.4 %collective-permute-start.17 = (bf16[4,8,330]{2,1,0:T(8,128)(2,1)S(1)}, bf16[4,8,330]{2,1,0:T(8,128)(2,1)S(1)}, u32[]{:S(2)}, u32[]{:S(2)}) collective-permute-start(bf16[4,8,330]{2,1,0:T(8,128)(2,1)S(1)} %pad_maximum_fusion.13), channel_id=1, source_target_pairs={{0,48},{4,52},{8,56},{12,60},{16,32},{20,36},{24,40},{28,44},{32,1... | collective-permute-start | bytes 63368 | tf_op jit(solution)/shard_map/ppermute | solution.py:97
  61.6 7.8 %collective-permute-start.16 = (bf16[4,8,330]{2,1,0:T(8,128)(2,1)S(1)}, bf16[4,8,330]{2,1,0:T(8,128)(2,1)S(1)}, u32[]{:S(2)}, u32[]{:S(2)}) collective-permute-start(bf16[4,8,330]{2,1,0:T(8,128)(2,1)S(1)} %pad_maximum_fusion.12), channel_id=1, source_target_pairs={{0,32},{4,36},{8,40},{12,44},{16,48},{20,52},{24,56},{28,60},{32,0... | collective-permute-start | bytes 63368 | tf_op jit(solution)/shard_map/ppermute | solution.py:97
  66.0 5.0 %collective-permute-start.15 = (bf16[4,8,330]{2,1,0:T(8,128)(2,1)S(1)}, bf16[4,8,330]{2,1,0:T(8,128)(2,1)S(1)}, u32[]{:S(2)}, u32[]{:S(2)}) collective-permute-start(bf16[4,8,330]{2,1,0:T(8,128)(2,1)S(1)} %pad_maximum_fusion.11), channel_id=1, source_target_pairs={{0,16},{4,20},{8,24},{12,28},{16,0},{20,4},{24,8},{28,12},{32,48},... | collective-permute-start | bytes 63368 | tf_op jit(solution)/shard_map/ppermute | solution.py:97
  72.0 4.9 %collective-permute-start.20 = (bf16[1,8,330]{2,1,0:T(8,128)(2,1)S(1)}, bf16[1,8,330]{2,1,0:T(8,128)(2,1)S(1)}, u32[]{:S(2)}, u32[]{:S(2)}) collective-permute-start(bf16[1,8,330]{2,1,0:T(8,128)(2,1)S(1)} %pad_maximum_fusion.16), channel_id=1, source_target_pairs={{0,192},{4,196},{8,200},{12,204},{16,208},{20,212},{24,216},{28,22... | collective-permute-start | bytes 15848 | tf_op jit(solution)/shard_map/ppermute | solution.py:97
  74.0 5.2 %collective-permute-start.19 = (bf16[1,8,330]{2,1,0:T(8,128)(2,1)S(1)}, bf16[1,8,330]{2,1,0:T(8,128)(2,1)S(1)}, u32[]{:S(2)}, u32[]{:S(2)}) collective-permute-start(bf16[1,8,330]{2,1,0:T(8,128)(2,1)S(1)} %pad_maximum_fusion.15), channel_id=1, source_target_pairs={{0,128},{4,132},{8,136},{12,140},{16,144},{20,148},{24,152},{28,15... | collective-permute-start | bytes 15848 | tf_op jit(solution)/shard_map/ppermute | solution.py:97
  75.8 3.7 %collective-permute-start.18 = (bf16[1,8,330]{2,1,0:T(8,128)(2,1)S(1)}, bf16[1,8,330]{2,1,0:T(8,128)(2,1)S(1)}, u32[]{:S(2)}, u32[]{:S(2)}) collective-permute-start(bf16[1,8,330]{2,1,0:T(8,128)(2,1)S(1)} %pad_maximum_fusion.14), channel_id=1, source_target_pairs={{0,64},{4,68},{8,72},{12,76},{16,80},{20,84},{24,88},{28,92},{32,9... | collective-permute-start | bytes 15848 | tf_op jit(solution)/shard_map/ppermute | solution.py:97
  80.8 5.1 %collective-permute-start.23 = (bf16[8,1280]{1,0:T(8,128)(2,1)S(1)}, bf16[8,1280]{1,0:T(8,128)(2,1)S(1)}, u32[]{:S(2)}, u32[]{:S(2)}) collective-permute-start(bf16[8,1280]{1,0:T(8,128)(2,1)S(1)} %get-tuple-element.56), channel_id=1, source_target_pairs={{0,3},{1,2},{2,1},{3,0},{4,7},{5,6},{6,5},{7,4},{8,11},{9,10},{10,... | collective-permute-start | bytes 61448 | tf_op jit(solution)/shard_map/ppermute | solution.py:134
  82.1 5.3 %collective-permute-start.22 = (bf16[8,1280]{1,0:T(8,128)(2,1)S(1)}, bf16[8,1280]{1,0:T(8,128)(2,1)S(1)}, u32[]{:S(2)}, u32[]{:S(2)}) collective-permute-start(bf16[8,1280]{1,0:T(8,128)(2,1)S(1)} %get-tuple-element.56), channel_id=1, source_target_pairs={{0,2},{1,3},{2,0},{3,1},{4,6},{5,7},{6,4},{7,5},{8,10},{9,11},{10,... | collective-permute-start | bytes 61448 | tf_op jit(solution)/shard_map/ppermute | solution.py:134
  83.0 4.4 %collective-permute-start.21 = (bf16[8,1280]{1,0:T(8,128)(2,1)S(1)}, bf16[8,1280]{1,0:T(8,128)(2,1)S(1)}, u32[]{:S(2)}, u32[]{:S(2)}) collective-permute-start(bf16[8,1280]{1,0:T(8,128)(2,1)S(1)} %get-tuple-element.56), channel_id=1, source_target_pairs={{0,1},{1,0},{2,3},{3,2},{4,5},{5,4},{6,7},{7,6},{8,9},{9,8},{10,11... | collective-permute-start | bytes 61448 | tf_op jit(solution)/shard_map/ppermute | solution.py:134
